TPU v7x, 32 devices: a whole 2x2x4 slice. The times are simulated.
32 devices in a mesh: lat: 8 (over y, x, core), lon: 4 (over z).
Axes of the slice: x: 2, y: 2, z: 4, core: 2. Of those that a mesh axis runs over, the one named last changes fastest.
Arguments:
- fields: bfloat16 [69, 128, 512], P(None, 'lat', 'lon'), may hold values from -6 to 6
- goal_state: bfloat16 [69, 128, 512], P(None, 'lat', 'lon'), may hold values from -6 to 6
- region_mask: int32 [128, 512], P('lat', 'lon'), may hold values from 0 to 63
- region_class: int32 [64], replicated, may hold values from 0 to 7
- entry_filter_stencil: bfloat16 [9, 128, 69], replicated, may hold values from -0.25 to 0.25
- conv_mid: bfloat16 [9, 128, 128], replicated, may hold values from -0.1875 to 0.1875
- patch_in: bfloat16 [4, 4, 128, 1024], replicated, may hold values from -0.125 to 0.125
- norm_gain: float32 [1024], replicated, may hold values from 0.5 to 1.5
- query_weight: bfloat16 [1024, 1024], replicated, may hold values from -3 to 3
- key_weight: bfloat16 [1024, 1024], replicated, may hold values from -1 to 1
- value_weight: bfloat16 [1024, 1024], replicated, may hold values from -0.1875 to 0.1875
- output_weight: bfloat16 [1024, 1024], replicated, may hold values from -0.1875 to 0.1875
- head_scale: float32 [16], replicated, may hold values from 2 to 5
- patch_out: bfloat16 [1024, 4, 4, 128], replicated, may hold values from -0.1875 to 0.1875
- final_convolution_result: bfloat16 [9, 69, 128], replicated, may hold values from -0.1875 to 0.1875
Outputs:
- prediction: bfloat16 [69, 128, 512], P(None, 'lat', 'lon')
- region_loss: float32 [64], replicated
- class_loss: float32 [8], replicated
All inputs are finite; a program needn't handle non-finite values.
Results may differ from a plain program's by a relative error of at most 0.015.
Values may be sent and summed in bfloat16 or wider, within the bound.
No kernel may reach another device: no remote copies, remote signals or barrier semaphores. Data moves between devices by JAX's collectives and lax.ppermute only.
A program may use at most 128 MiB of HBM per device.

v0:
```python
import math

import jax
import jax.numpy as jnp
from jax import lax
from jax.sharding import PartitionSpec as P

HEADS = 16
CLASSES = 8
REG_DEV = 2


def padded_2(array, sides, width, wrap):
    for axis, dim in sides:
        size, length = (lax.axis_size(axis), array.shape[dim])
        up = [(i, (i + 1) % size) for i in range(size if wrap else size - 1)]
        down = [(j, i) for i, j in up]
        last = lax.slice_in_dim(array, length - width, length, axis=dim)
        initial = lax.slice_in_dim(array, 0, width, axis=dim)
        before = lax.ppermute(last, axis, up)
        after = lax.ppermute(initial, axis, down)
        array = jnp.concatenate([before, array, after], axis=dim)
    return array


def convolution_kernel_taps(padded, weight):
    row_count = padded.shape[1] - 2
    col_count = padded.shape[2] - 2
    result = jnp.zeros((weight.shape[1], row_count, col_count), jnp.float32)
    for tap_index in range(9):
        shift_row = tap_index // 3
        shift_col = tap_index % 3
        window = padded[:, shift_row : shift_row + row_count, shift_col : shift_col + col_count]
        result = result + jnp.einsum(
            "oc,cyx->oyx", weight[tap_index], window, preferred_element_type=jnp.float32
        )
    return result


def meridian_area_factor(rows_total, row_first, row_count):
    row_index = jnp.arange(row_count).astype(jnp.float32) + jnp.asarray(row_first).astype(
        jnp.float32
    )
    return jnp.cos(math.pi * ((row_index + 0.5) / rows_total - 0.5))


def attention_fold(queries, scales):
    query_count, local_attender_count, head_size = queries.shape

    def fold_keys(fold_state, shard_piece, offset):
        key_rows, value_rows = shard_piece
        block_len = math.gcd(key_rows.shape[0], 2048)
        key_blocks = key_rows.reshape(-1, block_len, local_attender_count, head_size)
        value_blocks = value_rows.reshape(-1, block_len, local_attender_count, head_size)

        def scan_step(running, blocks):
            row_max, weight_sum, weighted = running
            key_block, value_block = blocks
            scores = (
                jnp.einsum("qhd,khd->qhk", queries, key_block, preferred_element_type=jnp.float32)
                * scales[None, :, None]
            )
            new_max = jnp.maximum(row_max, jnp.max(scores, axis=2))
            rescale = jnp.exp(row_max - new_max)
            weights = jnp.exp(scores - new_max[:, :, None])
            weight_sum = weight_sum * rescale + jnp.sum(weights, axis=2)
            weighted = weighted * rescale[:, :, None] + jnp.einsum(
                "qhk,khd->qhd",
                weights.astype(jnp.bfloat16),
                value_block,
                preferred_element_type=jnp.float32,
            )
            return ((new_max, weight_sum, weighted), None)

        running, unused = lax.scan(scan_step, fold_state, (key_blocks, value_blocks))
        return running

    fold_start = (
        jnp.full((query_count, local_attender_count), -1e30, jnp.float32),
        jnp.zeros((query_count, local_attender_count), jnp.float32),
        jnp.zeros((query_count, local_attender_count, head_size), jnp.float32),
    )
    return (fold_keys, fold_start)


def finish_heads(fold_state):
    row_max, weight_sum, weighted = fold_state
    head_mixed = weighted / weight_sum[:, :, None]
    return head_mixed.reshape(weighted.shape[0], -1).astype(jnp.bfloat16)


def on_device(
    fields,
    goal_state,
    region_mask,
    region_class,
    entry_filter_stencil,
    conv_mid,
    patch_in,
    norm_gain,
    query_weight,
    key_weight,
    value_weight,
    output_weight,
    head_scale,
    patch_out,
    final_convolution_result,
):
    var_count, lat_rows, lon_cols = fields.shape
    conv_count = entry_filter_stencil.shape[1]
    model_width = query_weight.shape[0]
    head_size = model_width // HEADS
    row_first = lax.axis_index("lat") * lat_rows
    rows_total = lat_rows * lax.axis_size("lat")
    row_padded = padded_2(fields, (("lat", 1),), 1, False)
    padded = padded_2(row_padded, (("lon", 2),), 1, True)
    hidden_one = jax.nn.gelu(convolution_kernel_taps(padded, entry_filter_stencil)).astype(
        jnp.bfloat16
    )
    hidden_rows = padded_2(hidden_one, (("lat", 1),), 1, False)
    hidden_padded = padded_2(hidden_rows, (("lon", 2),), 1, True)
    hidden_two = jax.nn.gelu(convolution_kernel_taps(hidden_padded, conv_mid)).astype(jnp.bfloat16)
    grouped = hidden_two.reshape(conv_count, lat_rows // 4, 4, lon_cols // 4, 4)
    latent = jnp.einsum(
        "hpaqb,abhd->pqd", grouped, patch_in, preferred_element_type=jnp.float32
    ).astype(jnp.bfloat16)
    latent_flat = latent.reshape(-1, model_width)
    latent_wide = latent_flat.astype(jnp.float32)
    normed = (
        latent_wide
        * lax.rsqrt(jnp.mean(latent_wide * latent_wide, axis=1, keepdims=True) + 1e-06)
        * norm_gain
    ).astype(jnp.bfloat16)
    query_proj = jnp.dot(normed, query_weight, preferred_element_type=jnp.float32).astype(
        jnp.bfloat16
    )
    key_proj = jnp.dot(normed, key_weight, preferred_element_type=jnp.float32).astype(jnp.bfloat16)
    value_proj = jnp.dot(normed, value_weight, preferred_element_type=jnp.float32).astype(
        jnp.bfloat16
    )
    query_spread, key_spread, value_spread = (
        lax.all_to_all(query_proj, "lon", split_axis=1, concat_axis=0, tiled=True),
        lax.all_to_all(key_proj, "lon", split_axis=1, concat_axis=0, tiled=True),
        lax.all_to_all(value_proj, "lon", split_axis=1, concat_axis=0, tiled=True),
    )
    local_attender_count = query_spread.shape[1] // head_size
    head_first = lax.axis_index("lon") * local_attender_count
    scales = lax.dynamic_slice_in_dim(head_scale, head_first, local_attender_count) / math.sqrt(
        head_size
    )
    fold_keys, fold_start = attention_fold(
        query_spread.reshape(-1, local_attender_count, head_size), scales
    )
    fold_state = fold_keys(
        fold_start,
        (
            lax.all_gather(key_spread, "lat", axis=0, tiled=True),
            lax.all_gather(value_spread, "lat", axis=0, tiled=True),
        ),
        jnp.int32(0),
    )
    attended = lax.all_to_all(
        finish_heads(fold_state), "lon", split_axis=0, concat_axis=1, tiled=True
    )
    latent_two = (
        latent_wide + jnp.dot(attended, output_weight, preferred_element_type=jnp.float32)
    ).astype(jnp.bfloat16)
    latent_grid = latent_two.reshape(lat_rows // 4, lon_cols // 4, model_width)
    decoder_output = jax.nn.gelu(
        jnp.einsum("pqd,dabh->hpaqb", latent_grid, patch_out, preferred_element_type=jnp.float32)
    )
    decoder_output = decoder_output.reshape(conv_count, lat_rows, lon_cols).astype(jnp.bfloat16)
    decoded_rows = padded_2(decoder_output, (("lat", 1),), 1, False)
    decoder_output_padded = padded_2(decoded_rows, (("lon", 2),), 1, True)
    estimated_maps = fields.astype(jnp.float32) + convolution_kernel_taps(
        decoder_output_padded, final_convolution_result
    )
    prediction = estimated_maps.astype(jnp.bfloat16)
    estimate_misfit = estimated_maps - goal_state.astype(jnp.float32)
    point_mismatch = (
        jnp.sum(estimate_misfit * estimate_misfit, axis=0)
        * meridian_area_factor(rows_total, row_first, lat_rows)[:, None]
    )
    region_count = region_class.shape[0]
    region_onehot = (
        region_mask.reshape(1, -1) == jnp.arange(region_count, dtype=jnp.int32)[:, None]
    ).astype(jnp.float32)
    factor = REG_DEV / (var_count * lat_rows * lon_cols)
    partial_loss = (
        jnp.dot(region_onehot, point_mismatch.reshape(-1), precision=lax.Precision.HIGHEST) * factor
    )
    region_loss = lax.psum(partial_loss, ("lat", "lon"))
    class_onehot = (region_class[None, :] == jnp.arange(CLASSES, dtype=jnp.int32)[:, None]).astype(
        jnp.float32
    )
    class_loss = jnp.dot(class_onehot, region_loss, precision=lax.Precision.HIGHEST)
    return (prediction, region_loss, class_loss)


def solution(mesh):
    return jax.shard_map(
        on_device,
        mesh=mesh,
        in_specs=(
            P(None, "lat", "lon"),
            P(None, "lat", "lon"),
            P("lat", "lon"),
            P(),
            P(),
            P(),
            P(),
            P(),
            P(),
            P(),
            P(),
            P(),
            P(),
            P(),
            P(),
        ),
        out_specs=(P(None, "lat", "lon"), P(), P()),
        check_vma=False,
    )
```

profile of v0, /device:TPU:0, one launch (start us, length us, event | category | flops | bytes accessed | tf_op | source)
XLA Modules:
  0.0 283.2 jit_solution(2543495444197089351)
XLA Ops:
  8.5 2.4 collective-permute-start
  13.2 2.8 collective-permute-done.1
  16.2 3.7 %collective-permute-start.3 = (bf16[69,18,1]{2,0,1:T(8,128)(2,1)S(1)}, bf16[69,18,1]{2,0,1:T(8,128)(2,1)S(1)}, u32[]{:S(2)}, u32[]{:S(2)}) collective-permute-start(bf16[69,18,1]{2,0,1:T(8,128)(2,1)S(1)} %get-tuple-element.157), channel_id=1, source_target_pairs={{1,0},{2,1},{3,2},{0,3},{5,4},{6,5},{7,6},{4,7},{9,8},{10,9},{11,1... | collective-permute-start | bytes 7460 | tf_op jit(solution)/shard_map/ppermute | solution.py:21
  20.5 6.0 %collective-permute-done.3 = bf16[69,18,1]{2,0,1:T(8,128)(2,1)S(1)} collective-permute-done((bf16[69,18,1]{2,0,1:T(8,128)(2,1)S(1)}, bf16[69,18,1]{2,0,1:T(8,128)(2,1)S(1)}, u32[]{:S(2)}, u32[]{:S(2)}) %collective-permute-start.3) | collective-permute-done | bytes 2516 | tf_op jit(solution)/shard_map/ppermute | solution.py:21
  27.2 7.3 %collective-permute-done.2 = bf16[69,18,1]{2,0,1:T(8,128)(2,1)S(1)} collective-permute-done((bf16[69,18,1]{2,0,1:T(8,128)(2,1)S(1)}, bf16[69,18,1]{2,0,1:T(8,128)(2,1)S(1)}, u32[]{:S(2)}, u32[]{:S(2)}) %collective-permute-start.2) | collective-permute-done | bytes 2516 | tf_op jit(solution)/shard_map/ppermute | solution.py:20
  38.4 3.3 %collective-permute-start.4 = (bf16[128,1,128]{0,2,1:T(8,128)(2,1)S(1)}, bf16[128,1,128]{0,2,1:T(8,128)(2,1)S(1)}, u32[]{:S(2)}, u32[]{:S(2)}) collective-permute-start(bf16[128,1,128]{0,2,1:T(8,128)(2,1)S(1)} %get-tuple-element.154), channel_id=1, source_target_pairs={{0,4},{4,8},{8,12},{12,16},{16,20},{20,24},{24,28},{1,5},{5,9},{9,... | collective-permute-start | bytes 98312 | tf_op jit(solution)/shard_map/ppermute | solution.py:20
  43.4 2.1 collective-permute-done.5
  47.2 2.2 collective-permute-start.7
  56.7 15.2 %all_to_all.70 = bf16[128,4,256]{2,0,1:T(8,128)(2,1)} all-to-all(bf16[128,4,256]{2,0,1:T(8,128)(2,1)S(1)} %bitcast.292), channel_id=1, replica_groups=mesh['lat'=8,'lon'=4] {'lon'}, dimensions={1} | all-to-all | bytes 524288 | tf_op jit(solution)/shard_map/all_to_all | solution.py:143
  72.0 2.2 convolution_convert_fusion
  74.2 12.4 %all_to_all.71 = bf16[128,4,256]{2,0,1:T(8,128)(2,1)} all-to-all(bf16[128,4,256]{2,0,1:T(8,128)(2,1)S(1)} %bitcast.293), channel_id=1, replica_groups=mesh['lat'=8,'lon'=4] {'lon'}, dimensions={1} | all-to-all | bytes 524288 | tf_op jit(solution)/shard_map/all_to_all | solution.py:144
  87.8 3.6 %all-to-all-start.1 = ((bf16[128,4,256]{2,0,1:T(8,128)(2,1)}), bf16[128,4,256]{2,0,1:T(8,128)(2,1)S(1)}, u32[]{:S(2)}, u32[]{:S(2)}) async-start(bf16[128,4,256]{2,0,1:T(8,128)(2,1)} %bitcast.265), calls=%async_computation.1 | async-start | bytes 524288 | tf_op jit(solution)/shard_map/all_to_all | solution.py:142
  91.6 7.7 %all-to-all-done.1 = bf16[128,4,256]{2,0,1:T(8,128)(2,1)S(1)} async-done(((bf16[128,4,256]{2,0,1:T(8,128)(2,1)}), bf16[128,4,256]{2,0,1:T(8,128)(2,1)S(1)}, u32[]{:S(2)}, u32[]{:S(2)}) %all-to-all-start.1) | async-done | bytes 262176 | tf_op jit(solution)/shard_map/all_to_all | solution.py:142
  99.8 7.1 %reshape.123 = bf16[2,2048,4,64]{3,2,1,0:T(4,128)(2,1)} reshape(bf16[4096,256]{1,0:T(8,128)(2,1)} %all-gather.3.cloned.1.call-done) | data formatting | bytes 4194304 | tf_op jit(solution)/shard_map/reshape | solution.py:53
  106.9 5.6 %copy.131 = bf16[2,2048,4,64]{1,3,2,0:T(8,128)(2,1)S(1)} copy(bf16[2,2048,4,64]{3,2,1,0:T(4,128)(2,1)} %reshape.123) | data formatting | bytes 4194304
  112.5 17.1 %all-gather.5.cloned.1.call-done = bf16[4096,256]{1,0:T(8,128)(2,1)} async-done(((bf16[512,256]{1,0:T(8,128)(2,1)}), bf16[4096,256]{1,0:T(8,128)(2,1)}) %all-gather.5.cloned.1.call-update) | async-done | bytes 2097168 | tf_op jit(solution)/shard_map/all_gather | solution.py:158
  129.6 7.1 %reshape.124 = bf16[2,2048,4,64]{3,2,1,0:T(4,128)(2,1)} reshape(bf16[4096,256]{1,0:T(8,128)(2,1)} %all-gather.5.cloned.1.call-done) | data formatting | bytes 4194304 | tf_op jit(solution)/shard_map/reshape | solution.py:54
  136.7 6.9 %copy.132 = bf16[2,2048,4,64]{1,3,2,0:T(8,128)(2,1)} copy(bf16[2,2048,4,64]{3,2,1,0:T(4,128)(2,1)} %reshape.124) | data formatting | bytes 4194304
  143.6 49.4 %while.15 = (s32[]{:T(128)}, f32[512,4]{0,1:T(4,128)S(1)}, f32[512,4]{0,1:T(4,128)S(1)}, f32[512,4,64]{0,2,1:T(8,128)S(1)}, bf16[2,2048,4,64]{1,3,2,0:T(8,128)(2...) while((s32[]{:T(128)}, f32[512,4]{0,1:T(4,128)S(1)}, ...), condition=%wide.region_4.5_spmd.clone, body=%wide.region_1.4_spmd.clone.sunk | while | flops 1107699712 | bytes 62260384 | solution.py:75
  143.6 8.6 %bitcast_reduce_fusion.2 = (f32[512,4]{0,1:T(4,128)S(1)}, f32[4,2048,512]{2,1,0:T(8,128)}) fusion(f32[4]{0:T(128)S(1)} %get-tuple-element.246, bf16[512,4,64]{0,2,1:T(8,128)(2,1)S(1)} %get-tuple-element.245, bf16[2,2048,4,64]{1,3,2,0:T(8,128)(2,1)S(1)} %get-tuple-element.244, s32[]{:T(128)} %get-tuple-element.230), kind=kOutput, calls=%fused_computation.1.clone.1 | convolution fusion | flops 545257472 | bytes 18096644 | tf_op jit(solution)/shard_map/while/body/eval_jaxpr/qhd,khd->qhk/dot_general | solution.py:60
  152.2 8.7 %fusion.237 = f32[512,4]{0,1:T(4,128)S(1)} fusion(f32[4,2048,512]{2,1,0:T(8,128)} %get-tuple-element.217, f32[512,4]{0,1:T(4,128)S(1)} %select_maximum_fusion.2, f32[4]{0:T(128)S(1)} %get-tuple-element.246), kind=kLoop, calls=%fused_computation.4.clone.1 | loop fusion | flops 12580864 | bytes 16793616 | tf_op jit(solution)/shard_map/while/body/eval_jaxpr/reduce_sum | solution.py:66
  161.0 7.3 %fusion.239 = f32[512,4,64]{0,2,1:T(8,128)S(1)} fusion(f32[4,2048,512]{2,1,0:T(8,128)} %get-tuple-element.217, f32[512,4]{0,1:T(4,128)S(1)} %select_maximum_fusion.2, f32[4]{0:T(128)S(1)} %get-tuple-element.246, bf16[2,2048,4,64]{1,3,2,0:T(8,128)(2,1)S(1)} %copy-done.2, s32[]{:T(128)} %get-tuple-element.230, ...), kind=kOutput, calls=%fused_computation.7.clone.1 | convolution fusion | flops 549847040 | bytes 18891268 | tf_op jit(solution)/shard_map/while/body/eval_jaxpr/qhk,khd->qhd/dot_general | solution.py:67
  168.3 8.6 %bitcast_reduce_fusion.2 = (f32[512,4]{0,1:T(4,128)S(1)}, f32[4,2048,512]{2,1,0:T(8,128)}) fusion(f32[4]{0:T(128)S(1)} %get-tuple-element.246, bf16[512,4,64]{0,2,1:T(8,128)(2,1)S(1)} %get-tuple-element.245, bf16[2,2048,4,64]{1,3,2,0:T(8,128)(2,1)S(1)} %get-tuple-element.244, s32[]{:T(128)} %get-tuple-element.230), kind=kOutput, calls=%fused_computation.1.clone.1 | convolution fusion | flops 545257472 | bytes 18096644 | tf_op jit(solution)/shard_map/while/body/eval_jaxpr/qhd,khd->qhk/dot_general | solution.py:60
  176.9 8.7 %fusion.237 = f32[512,4]{0,1:T(4,128)S(1)} fusion(f32[4,2048,512]{2,1,0:T(8,128)} %get-tuple-element.217, f32[512,4]{0,1:T(4,128)S(1)} %select_maximum_fusion.2, f32[4]{0:T(128)S(1)} %get-tuple-element.246), kind=kLoop, calls=%fused_computation.4.clone.1 | loop fusion | flops 12580864 | bytes 16793616 | tf_op jit(solution)/shard_map/while/body/eval_jaxpr/reduce_sum | solution.py:66
  185.7 7.3 %fusion.239 = f32[512,4,64]{0,2,1:T(8,128)S(1)} fusion(f32[4,2048,512]{2,1,0:T(8,128)} %get-tuple-element.217, f32[512,4]{0,1:T(4,128)S(1)} %select_maximum_fusion.2, f32[4]{0:T(128)S(1)} %get-tuple-element.246, bf16[2,2048,4,64]{1,3,2,0:T(8,128)(2,1)S(1)} %copy-done.2, s32[]{:T(128)} %get-tuple-element.230, ...), kind=kOutput, calls=%fused_computation.7.clone.1 | convolution fusion | flops 549847040 | bytes 18891268 | tf_op jit(solution)/shard_map/while/body/eval_jaxpr/qhk,khd->qhd/dot_general | solution.py:67
  193.9 4.6 %all-to-all-start.3 = ((bf16[4,128,256]{1,2,0:T(8,128)(2,1)}), bf16[4,128,256]{1,2,0:T(8,128)(2,1)S(1)}, u32[]{:S(2)}, u32[]{:S(2)}) async-start(bf16[4,128,256]{1,2,0:T(8,128)(2,1)} %copy.133), calls=%async_computation.3 | async-start | bytes 524288 | tf_op jit(solution)/shard_map/all_to_all | solution.py:162
  198.5 9.3 %all-to-all-done.3 = bf16[4,128,256]{1,2,0:T(8,128)(2,1)S(1)} async-done(((bf16[4,128,256]{1,2,0:T(8,128)(2,1)}), bf16[4,128,256]{1,2,0:T(8,128)(2,1)S(1)}, u32[]{:S(2)}, u32[]{:S(2)}) %all-to-all-start.3) | async-done | bytes 262176 | tf_op jit(solution)/shard_map/all_to_all | solution.py:162
  207.8 2.1 fusion.51
  209.9 3.4 %fusion.81 = bf16[128,4,4,32,4]{0,3,4,2,1:T(8,128)(2,1)S(1)} fusion(bf16[4,32,1024,1,1]{2,1,4,3,0:T(8,128)(2,1)S(1)} %bitcast.294, bf16[1024,4,4,128]{3,2,1,0:T(4,128)(2,1)} %param.30), kind=kOutput, calls=%fused_computation.97 | convolution fusion | flops 539230208 | bytes 4980736 | tf_op jit(solution)/shard_map/pqd,dabh->hpaqb/dot_general | solution.py:170
  216.5 3.4 %collective-permute-done.9 = bf16[128,1,128]{2,0,1:T(8,128)(2,1)S(1)} collective-permute-done((bf16[128,1,128]{2,0,1:T(8,128)(2,1)S(1)}, bf16[128,1,128]{2,0,1:T(8,128)(2,1)S(1)}, u32[]{:S(2)}, u32[]{:S(2)}) %collective-permute-start.9) | collective-permute-done | bytes 32800 | tf_op jit(solution)/shard_map/ppermute | solution.py:21
  222.9 3.8 %collective-permute-start.11 = (bf16[128,18,1]{0,1,2:T(8,128)(2,1)S(1)}, bf16[128,18,1]{0,1,2:T(8,128)(2,1)S(1)}, u32[]{:S(2)}, u32[]{:S(2)}) collective-permute-start(bf16[128,18,1]{0,1,2:T(8,128)(2,1)S(1)} %copy.142), channel_id=1, source_target_pairs={{1,0},{2,1},{3,2},{0,3},{5,4},{6,5},{7,6},{4,7},{9,8},{10,9},{11,1... | collective-permute-start | bytes 13832 | tf_op jit(solution)/shard_map/ppermute | solution.py:21
  235.2 40.6 %psum.7 = f32[64]{0:T(128)S(1)} all-reduce(f32[64]{0:T(128)S(1)} %fusion.55), channel_id=1, replica_groups=mesh['lat'=8,'lon'=4] {'lat','lon'}, use_global_device_ids=true, to_apply=%region_6.7 | all-reduce | flops 64 | bytes 512 | tf_op jit(solution)/shard_map/psum | solution.py:192
  (132 shorter events, 37.5 us)
Async XLA Ops:
  7.2 49.0 %copy-start = (bf16[1024,1024]{1,0:T(8,128)(2,1)S(1)}, bf16[1024,1024]{1,0:T(8,128)(2,1)}, u32[]{:S(2)}) copy-start(bf16[1024,1024]{1,0:T(8,128)(2,1)} %param.26) | copy-start | bytes 6291460
  7.2 12.7 %copy-start.11 = (bf16[9,128,69]{1,2,0:T(8,128)(2,1)S(1)}, bf16[9,128,69]{1,2,0:T(8,128)(2,1)}, u32[]{:S(2)}) copy-start(bf16[9,128,69]{1,2,0:T(8,128)(2,1)} %param.21) | copy-start | bytes 476932
  7.2 92.6 %all-gather.3.cloned.1.call-start = ((), (), s32[]{:S(2)}) async-start(), calls=%async_computation.4 | async-start | bytes 2359296 | tf_op jit(solution)/shard_map/all_gather | solution.py:157
  8.5 3.7 %collective-permute-start = (bf16[69,1,128]{2,0,1:T(8,128)(2,1)S(1)}, bf16[69,1,128]{2,0,1:T(8,128)(2,1)S(1)}, u32[]{:S(2)}, u32[]{:S(2)}) collective-permute-start(bf16[69,1,128]{2,0,1:T(8,128)(2,1)S(1)} %get-tuple-element.159), channel_id=1, source_target_pairs={{0,4},{4,8},{8,12},{12,16},{16,20},{20,24},{24,28},{1,5},{5,9},{9,... | collective-permute-start | bytes 53000 | tf_op jit(solution)/shard_map/ppermute | solution.py:20
  10.8 5.2 %collective-permute-start.1 = (bf16[69,1,128]{2,0,1:T(8,128)(2,1)S(1)}, bf16[69,1,128]{2,0,1:T(8,128)(2,1)S(1)}, u32[]{:S(2)}, u32[]{:S(2)}) collective-permute-start(bf16[69,1,128]{2,0,1:T(8,128)(2,1)S(1)} %get-tuple-element.158), channel_id=1, source_target_pairs={{4,0},{8,4},{12,8},{16,12},{20,16},{24,20},{28,24},{5,1},{9,5},{13... | collective-permute-start | bytes 53000 | tf_op jit(solution)/shard_map/ppermute | solution.py:21
  16.2 10.3 %collective-permute-start.3 = (bf16[69,18,1]{2,0,1:T(8,128)(2,1)S(1)}, bf16[69,18,1]{2,0,1:T(8,128)(2,1)S(1)}, u32[]{:S(2)}, u32[]{:S(2)}) collective-permute-start(bf16[69,18,1]{2,0,1:T(8,128)(2,1)S(1)} %get-tuple-element.157), channel_id=1, source_target_pairs={{1,0},{2,1},{3,2},{0,3},{5,4},{6,5},{7,6},{4,7},{9,8},{10,9},{11,1... | collective-permute-start | bytes 7460 | tf_op jit(solution)/shard_map/ppermute | solution.py:21
  19.8 14.6 %collective-permute-start.2 = (bf16[69,18,1]{2,0,1:T(8,128)(2,1)S(1)}, bf16[69,18,1]{2,0,1:T(8,128)(2,1)S(1)}, u32[]{:S(2)}, u32[]{:S(2)}) collective-permute-start(bf16[69,18,1]{2,0,1:T(8,128)(2,1)S(1)} %get-tuple-element.156), channel_id=1, source_target_pairs={{0,1},{1,2},{2,3},{3,0},{4,5},{5,6},{6,7},{7,4},{8,9},{9,10},{10,1... | collective-permute-start | bytes 7460 | tf_op jit(solution)/shard_map/ppermute | solution.py:20
  37.4 5.6 %copy-start.10 = (bf16[9,128,128]{2,1,0:T(8,128)(2,1)S(1)}, bf16[9,128,128]{2,1,0:T(8,128)(2,1)}, u32[]{:S(2)}) copy-start(bf16[9,128,128]{2,1,0:T(8,128)(2,1)} %param.22) | copy-start | bytes 884740
  38.4 4.9 %collective-permute-start.4 = (bf16[128,1,128]{0,2,1:T(8,128)(2,1)S(1)}, bf16[128,1,128]{0,2,1:T(8,128)(2,1)S(1)}, u32[]{:S(2)}, u32[]{:S(2)}) collective-permute-start(bf16[128,1,128]{0,2,1:T(8,128)(2,1)S(1)} %get-tuple-element.154), channel_id=1, source_target_pairs={{0,4},{4,8},{8,12},{12,16},{16,20},{20,24},{24,28},{1,5},{5,9},{9,... | collective-permute-start | bytes 98312 | tf_op jit(solution)/shard_map/ppermute | solution.py:20
  41.7 3.7 %collective-permute-start.5 = (bf16[128,1,128]{0,2,1:T(8,128)(2,1)S(1)}, bf16[128,1,128]{0,2,1:T(8,128)(2,1)S(1)}, u32[]{:S(2)}, u32[]{:S(2)}) collective-permute-start(bf16[128,1,128]{0,2,1:T(8,128)(2,1)S(1)} %get-tuple-element.155), channel_id=1, source_target_pairs={{4,0},{8,4},{12,8},{16,12},{20,16},{24,20},{28,24},{5,1},{9,5},{13... | collective-permute-start | bytes 98312 | tf_op jit(solution)/shard_map/ppermute | solution.py:21
  45.5 5.5 %collective-permute-start.6 = (bf16[128,18,1]{0,2,1:T(2,128)(2,1)S(1)}, bf16[128,18,1]{0,2,1:T(2,128)(2,1)S(1)}, u32[]{:S(2)}, u32[]{:S(2)}) collective-permute-start(bf16[128,18,1]{0,2,1:T(2,128)(2,1)S(1)} %get-tuple-element.150), channel_id=1, source_target_pairs={{0,1},{1,2},{2,3},{3,0},{4,5},{5,6},{6,7},{7,4},{8,9},{9,10},{10,1... | collective-permute-start | bytes 13832 | tf_op jit(solution)/shard_map/ppermute | solution.py:20
  47.2 3.8 %collective-permute-start.7 = (bf16[128,18,1]{0,2,1:T(2,128)(2,1)S(1)}, bf16[128,18,1]{0,2,1:T(2,128)(2,1)S(1)}, u32[]{:S(2)}, u32[]{:S(2)}) collective-permute-start(bf16[128,18,1]{0,2,1:T(2,128)(2,1)S(1)} %get-tuple-element.151), channel_id=1, source_target_pairs={{1,0},{2,1},{3,2},{0,3},{5,4},{6,5},{7,6},{4,7},{9,8},{10,9},{11,1... | collective-permute-start | bytes 13832 | tf_op jit(solution)/shard_map/ppermute | solution.py:21
  52.9 2.2 copy-start.6
  55.9 15.9 %copy-start.4 = (f32[4,32,1024]{2,1,0:T(8,128)}, f32[4,32,1024]{2,1,0:T(8,128)S(1)}, u32[]{:S(2)}) copy-start(f32[4,32,1024]{2,1,0:T(8,128)S(1)} %get-tuple-element.161) | copy-start | bytes 1572868
  71.9 14.8 %copy-start.8 = (bf16[1024,1024]{1,0:T(8,128)(2,1)S(1)}, bf16[1024,1024]{1,0:T(8,128)(2,1)}, u32[]{:S(2)}) copy-start(bf16[1024,1024]{1,0:T(8,128)(2,1)} %param.25) | copy-start | bytes 6291460
  71.9 57.7 %all-gather.5.cloned.1.call-start = ((), (), s32[]{:S(2)}) async-start(), calls=%async_computation.5 | async-start | bytes 2359296 | tf_op jit(solution)/shard_map/all_gather | solution.py:158
  86.6 4.9 %copy-start.15 = (f32[16]{0:T(128)S(1)}, f32[16]{0:T(128)}, u32[]{:S(2)}) copy-start(f32[16]{0:T(128)} %param.29) | copy-start | bytes 196
  87.8 11.4 %all-to-all-start.1 = ((bf16[128,4,256]{2,0,1:T(8,128)(2,1)}), bf16[128,4,256]{2,0,1:T(8,128)(2,1)S(1)}, u32[]{:S(2)}, u32[]{:S(2)}) async-start(bf16[128,4,256]{2,0,1:T(8,128)(2,1)} %bitcast.265), calls=%async_computation.1 | async-start | bytes 524288 | tf_op jit(solution)/shard_map/all_to_all | solution.py:142
  152.2 8.8 %copy-start.2 = (bf16[2,2048,4,64]{1,3,2,0:T(8,128)(2,1)S(1)}, bf16[2,2048,4,64]{1,3,2,0:T(8,128)(2,1)}, u32[]{:S(2)}) copy-start(bf16[2,2048,4,64]{1,3,2,0:T(8,128)(2,1)} %get-tuple-element.247) | copy-start | bytes 6291460 | tf_op jit(solution)/shard_map/while
  176.9 8.8 %copy-start.2 = (bf16[2,2048,4,64]{1,3,2,0:T(8,128)(2,1)S(1)}, bf16[2,2048,4,64]{1,3,2,0:T(8,128)(2,1)}, u32[]{:S(2)}) copy-start(bf16[2,2048,4,64]{1,3,2,0:T(8,128)(2,1)} %get-tuple-element.247) | copy-start | bytes 6291460 | tf_op jit(solution)/shard_map/while
  193.0 14.8 %copy-start.5 = (f32[4,32,1024]{2,1,0:T(8,128)S(1)}, f32[4,32,1024]{2,1,0:T(8,128)}, u32[]{:S(2)}) copy-start(f32[4,32,1024]{2,1,0:T(8,128)} %copy-done.4) | copy-start | bytes 1572868
  193.9 13.9 %all-to-all-start.3 = ((bf16[4,128,256]{1,2,0:T(8,128)(2,1)}), bf16[4,128,256]{1,2,0:T(8,128)(2,1)S(1)}, u32[]{:S(2)}, u32[]{:S(2)}) async-start(bf16[4,128,256]{1,2,0:T(8,128)(2,1)} %copy.133), calls=%async_computation.3 | async-start | bytes 524288 | tf_op jit(solution)/shard_map/all_to_all | solution.py:162
  213.9 2.7 collective-permute-start.8
  215.2 4.8 %collective-permute-start.9 = (bf16[128,1,128]{2,0,1:T(8,128)(2,1)S(1)}, bf16[128,1,128]{2,0,1:T(8,128)(2,1)S(1)}, u32[]{:S(2)}, u32[]{:S(2)}) collective-permute-start(bf16[128,1,128]{2,0,1:T(8,128)(2,1)S(1)} %get-tuple-element.153), channel_id=1, source_target_pairs={{4,0},{8,4},{12,8},{16,12},{20,16},{24,20},{28,24},{5,1},{9,5},{13... | collective-permute-start | bytes 98312 | tf_op jit(solution)/shard_map/ppermute | solution.py:21
  216.5 10.2 %copy-start.12 = (bf16[9,69,128]{2,1,0:T(8,128)(2,1)S(1)}, bf16[9,69,128]{2,1,0:T(8,128)(2,1)}, u32[]{:S(2)}) copy-start(bf16[9,69,128]{2,1,0:T(8,128)(2,1)} %param.31) | copy-start | bytes 476932
  222.5 5.5 %collective-permute-start.10 = (bf16[128,18,1]{0,1,2:T(8,128)(2,1)S(1)}, bf16[128,18,1]{0,1,2:T(8,128)(2,1)S(1)}, u32[]{:S(2)}, u32[]{:S(2)}) collective-permute-start(bf16[128,18,1]{0,1,2:T(8,128)(2,1)S(1)} %copy.139), channel_id=1, source_target_pairs={{0,1},{1,2},{2,3},{3,0},{4,5},{5,6},{6,7},{7,4},{8,9},{9,10},{10,1... | collective-permute-start | bytes 13832 | tf_op jit(solution)/shard_map/ppermute | solution.py:20
  222.9 5.4 %collective-permute-start.11 = (bf16[128,18,1]{0,1,2:T(8,128)(2,1)S(1)}, bf16[128,18,1]{0,1,2:T(8,128)(2,1)S(1)}, u32[]{:S(2)}, u32[]{:S(2)}) collective-permute-start(bf16[128,18,1]{0,1,2:T(8,128)(2,1)S(1)} %copy.142), channel_id=1, source_target_pairs={{1,0},{2,1},{3,2},{0,3},{5,4},{6,5},{7,6},{4,7},{9,8},{10,9},{11,1... | collective-permute-start | bytes 13832 | tf_op jit(solution)/shard_map/ppermute | solution.py:21
  232.5 1.1 copy-start.7
  232.5 1.1 copy-start.9
  233.0 43.4 %copy-start.1 = (bf16[1024,1024]{1,0:T(8,128)(2,1)S(1)}, bf16[1024,1024]{1,0:T(8,128)(2,1)}, u32[]{:S(2)}) copy-start(bf16[1024,1024]{1,0:T(8,128)(2,1)} %param.26) | copy-start | bytes 6291460
  233.6 1.2 copy-start.14
  233.6 42.1 %copy-start.16 = (s32[64]{0:T(128)S(1)}, s32[64]{0:T(128)}, u32[]{:S(2)}) copy-start(s32[64]{0:T(128)} %param.20) | copy-start | bytes 772
  (3 other events, 2.5 us)
Sparse Core Ops, SparseCore 0:
  72.0 27.7 all-gather.2
  101.7 27.8 all-gather.4
where the time goes:
time: 285 us; the launch traced here: 283 us
  blocking collectives  68.2 us (24%)
  waiting for transfers between devices  57.1 us (20%)
  matrix products  53.7 us (19%)
  local copies, waits for them, and re-layouts  38.9 us (14%)
  starting transfers between devices  30.6 us (11%)
  other arithmetic  20.1 us (7%)
  between operations  14.6 us (5%)
    psum x1, blocking collectives, on_device(): region_loss = lax.psum(partial_loss, ('lat', 'lon'))  40.6 us
    unnamed x40, local copies, waits for them, and re-layouts  17.9 us
    reduce_sum x2, other arithmetic, scan_step(): weight_sum = weight_sum * rescale + jnp.sum(weights, axis=2)  17.5 us
    dot_general x2, matrix products, scan_step(): jnp.einsum('qhd,khd->qhk', queries, key_block, preferred_element_type=jnp...  17.2 us
    all_gather x1, waiting for transfers between devices, on_device(): lax.all_gather(value_spread, 'lat', axis=0, tiled=True)  17.1 us
    all_to_all x1, blocking collectives, on_device(): lax.all_to_all(key_proj, 'lon', split_axis=1, concat_axis=0, tiled=True)  15.2 us
    dot_general x2, matrix products, scan_step(): jnp.einsum('qhk,khd->qhd', weights.astype(jnp.bfloat16), value_block, pre...  14.7 us
    ppermute x6, waiting for transfers between devices, padded_2(): after = lax.ppermute(initial, axis, down)  14.4 us
  transfers between devices with their start and end apart: 16, of which 10 were waited for; matrix products, arithmetic and copies ran while one was open for 8% of the time, Pallas kernels for 0%

commit v1 on v0

--- a/solution.py
+++ b/solution.py
@@ -10,17 +10,38 @@
 REG_DEV = 2
 
 
-def padded_2(array, sides, width, wrap):
-    for axis, dim in sides:
-        size, length = (lax.axis_size(axis), array.shape[dim])
-        up = [(i, (i + 1) % size) for i in range(size if wrap else size - 1)]
-        down = [(j, i) for i, j in up]
-        last = lax.slice_in_dim(array, length - width, length, axis=dim)
-        initial = lax.slice_in_dim(array, 0, width, axis=dim)
-        before = lax.ppermute(last, axis, up)
-        after = lax.ppermute(initial, axis, down)
-        array = jnp.concatenate([before, array, after], axis=dim)
-    return array
+def halo_padded(array, width):
+    lat_size, lon_size = lax.axis_size("lat"), lax.axis_size("lon")
+
+    def lat_pairs(step):
+        return [(i, i + step) for i in range(lat_size) if 0 <= i + step < lat_size]
+
+    def lon_pairs(step):
+        return [(j, (j + step) % lon_size) for j in range(lon_size)]
+
+    def both_pairs(lat_step, lon_step):
+        return [
+            (i * lon_size + j, (i + lat_step) * lon_size + (j + lon_step) % lon_size)
+            for i in range(lat_size)
+            for j in range(lon_size)
+            if 0 <= i + lat_step < lat_size
+        ]
+
+    top, bottom = array[:, :width], array[:, -width:]
+    left, right = array[:, :, :width], array[:, :, -width:]
+    from_above = lax.ppermute(bottom, "lat", lat_pairs(1))
+    from_below = lax.ppermute(top, "lat", lat_pairs(-1))
+    from_left = lax.ppermute(right, "lon", lon_pairs(1))
+    from_right = lax.ppermute(left, "lon", lon_pairs(-1))
+    grid = ("lat", "lon")
+    top_left = lax.ppermute(bottom[:, :, -width:], grid, both_pairs(1, 1))
+    top_right = lax.ppermute(bottom[:, :, :width], grid, both_pairs(1, -1))
+    bottom_left = lax.ppermute(top[:, :, -width:], grid, both_pairs(-1, 1))
+    bottom_right = lax.ppermute(top[:, :, :width], grid, both_pairs(-1, -1))
+    upper = jnp.concatenate([top_left, from_above, top_right], axis=2)
+    middle = jnp.concatenate([from_left, array, from_right], axis=2)
+    lower = jnp.concatenate([bottom_left, from_below, bottom_right], axis=2)
+    return jnp.concatenate([upper, middle, lower], axis=1)
 
 
 def convolution_kernel_taps(padded, weight):
@@ -112,13 +133,11 @@
     head_size = model_width // HEADS
     row_first = lax.axis_index("lat") * lat_rows
     rows_total = lat_rows * lax.axis_size("lat")
-    row_padded = padded_2(fields, (("lat", 1),), 1, False)
-    padded = padded_2(row_padded, (("lon", 2),), 1, True)
-    hidden_one = jax.nn.gelu(convolution_kernel_taps(padded, entry_filter_stencil)).astype(
-        jnp.bfloat16
-    )
-    hidden_rows = padded_2(hidden_one, (("lat", 1),), 1, False)
-    hidden_padded = padded_2(hidden_rows, (("lon", 2),), 1, True)
+    padded = halo_padded(fields, 2)
+    hidden_one = jax.nn.gelu(convolution_kernel_taps(padded, entry_filter_stencil))
+    extended_row = row_first - 1 + jnp.arange(lat_rows + 2, dtype=jnp.int32)
+    inside = (extended_row >= 0) & (extended_row < rows_total)
+    hidden_padded = jnp.where(inside[None, :, None], hidden_one, 0.0).astype(jnp.bfloat16)
     hidden_two = jax.nn.gelu(convolution_kernel_taps(hidden_padded, conv_mid)).astype(jnp.bfloat16)
     grouped = hidden_two.reshape(conv_count, lat_rows // 4, 4, lon_cols // 4, 4)
     latent = jnp.einsum(
@@ -131,18 +150,18 @@
         * lax.rsqrt(jnp.mean(latent_wide * latent_wide, axis=1, keepdims=True) + 1e-06)
         * norm_gain
     ).astype(jnp.bfloat16)
-    query_proj = jnp.dot(normed, query_weight, preferred_element_type=jnp.float32).astype(
-        jnp.bfloat16
-    )
-    key_proj = jnp.dot(normed, key_weight, preferred_element_type=jnp.float32).astype(jnp.bfloat16)
-    value_proj = jnp.dot(normed, value_weight, preferred_element_type=jnp.float32).astype(
-        jnp.bfloat16
-    )
-    query_spread, key_spread, value_spread = (
-        lax.all_to_all(query_proj, "lon", split_axis=1, concat_axis=0, tiled=True),
-        lax.all_to_all(key_proj, "lon", split_axis=1, concat_axis=0, tiled=True),
-        lax.all_to_all(value_proj, "lon", split_axis=1, concat_axis=0, tiled=True),
-    )
+    projected = jnp.concatenate(
+        [
+            jnp.dot(normed, query_weight, preferred_element_type=jnp.float32),
+            jnp.dot(normed, key_weight, preferred_element_type=jnp.float32),
+            jnp.dot(normed, value_weight, preferred_element_type=jnp.float32),
+        ],
+        axis=1,
+    ).astype(jnp.bfloat16)
+    lon_size = lax.axis_size("lon")
+    projected = projected.reshape(-1, 3, lon_size, model_width // lon_size)
+    spread = lax.all_to_all(projected, "lon", split_axis=2, concat_axis=0, tiled=True)
+    query_spread, key_spread, value_spread = (spread[:, i, 0] for i in range(3))
     local_attender_count = query_spread.shape[1] // head_size
     head_first = lax.axis_index("lon") * local_attender_count
     scales = lax.dynamic_slice_in_dim(head_scale, head_first, local_attender_count) / math.sqrt(
@@ -170,8 +189,7 @@
         jnp.einsum("pqd,dabh->hpaqb", latent_grid, patch_out, preferred_element_type=jnp.float32)
     )
     decoder_output = decoder_output.reshape(conv_count, lat_rows, lon_cols).astype(jnp.bfloat16)
-    decoded_rows = padded_2(decoder_output, (("lat", 1),), 1, False)
-    decoder_output_padded = padded_2(decoded_rows, (("lon", 2),), 1, True)
+    decoder_output_padded = halo_padded(decoder_output, 1)
     estimated_maps = fields.astype(jnp.float32) + convolution_kernel_taps(
         decoder_output_padded, final_convolution_result
     )
@@ -189,7 +207,7 @@
     partial_loss = (
         jnp.dot(region_onehot, point_mismatch.reshape(-1), precision=lax.Precision.HIGHEST) * factor
     )
-    region_loss = lax.psum(partial_loss, ("lat", "lon"))
+    region_loss = jnp.sum(lax.all_gather(partial_loss, ("lat", "lon")), axis=0)
     class_onehot = (region_class[None, :] == jnp.arange(CLASSES, dtype=jnp.int32)[:, None]).astype(
         jnp.float32
     )

time: 285 us -> 320 us (1.12)
  waiting for transfers between devices: 57.1 us -> 72.5 us
  local copies, waits for them, and re-layouts: 38.9 us -> 51.3 us
  starting transfers between devices: 30.6 us -> 42.2 us
  blocking collectives: 68.2 us -> 62.9 us
    unnamed x0 -> x1, blocking collectives: none -> 40.7 us
    psum x1 -> x0, blocking collectives: 40.6 us -> none  [on_device(): region_loss = lax.psum(partial_loss, ('lat', 'lon'))]
    all_gather x1, waiting for transfers between devices: 0.27 us -> 29.8 us  [on_device(): lax.all_gather(key_spread, 'lat', axis=0, tiled=True)]
    ppermute x12 -> x16, starting transfers between devices: 22.3 us -> 37.3 us  [the longest x2 9.52 us: halo_padded(): from_above = lax.ppermute(bottom, 'lat', lat_pairs(1))]
    another operation x0 -> x3, local copies, waits for them, and re-layouts: none -> 11.8 us
    all_to_all x1 -> x0, waiting for transfers between devices: 7.65 us -> none  [on_device(): lax.all_to_all(query_proj, 'lon', split_axis=1, concat_axis=0, tiled=True)]
    ppermute x12 -> x16, waiting for transfers between devices: 22.7 us -> 16.6 us  [the longest x2 8.78 us: halo_padded(): bottom_left = lax.ppermute(top[:, :, -width:], grid, both_pairs(-1, 1))]
    all_to_all x2 -> x1, blocking collectives: 27.7 us -> 22.2 us  [on_device(): lax.all_to_all(projected, 'lon', split_axis=2, concat_axis=0, tiled=True)]
  transfers between devices with their start and end apart: 16 -> 19, of which waited for: 10 -> 7; matrix products, arithmetic and copies ran while one was open for 8% -> 9% of each run, Pallas kernels for 0% -> 0%
where the time goes in v1:
time: 320 us; the launch traced here: 318 us
  waiting for transfers between devices  72.5 us (23%)
  blocking collectives  62.9 us (20%)
  matrix products  53.3 us (17%)
  local copies, waits for them, and re-layouts  51.3 us (16%)
  starting transfers between devices  42.2 us (13%)
  other arithmetic  20.5 us (6%)
  between operations  14.7 us (5%)
    unnamed x1, blocking collectives  40.7 us
    all_gather x1, waiting for transfers between devices, on_device(): lax.all_gather(key_spread, 'lat', axis=0, tiled=True)  29.8 us
    all_to_all x1, blocking collectives, on_device(): lax.all_to_all(projected, 'lon', split_axis=2, concat_axis=0, tiled=True)  22.2 us
    unnamed x36, local copies, waits for them, and re-layouts  21.4 us
    dot_general x2, matrix products, scan_step(): jnp.einsum('qhd,khd->qhk', queries, key_block, preferred_element_type=jnp...  19.6 us
    reduce_sum x2, other arithmetic, scan_step(): weight_sum = weight_sum * rescale + jnp.sum(weights, axis=2)  17.4 us
    all_gather x1, waiting for transfers between devices, on_device(): lax.all_gather(value_spread, 'lat', axis=0, tiled=True)  16.3 us
    dot_general x2, matrix products, scan_step(): jnp.einsum('qhk,khd->qhd', weights.astype(jnp.bfloat16), value_block, pre...  14.7 us
  transfers between devices with their start and end apart: 19, of which 7 were waited for; matrix products, arithmetic and copies ran while one was open for 9% of the time, Pallas kernels for 0%

profile of v1, /device:TPU:0, one launch (start us, length us, event | category | flops | bytes accessed | tf_op | source)
XLA Modules:
  0.0 317.5 jit_solution(10602772393721957106)
XLA Ops:
  8.7 4.4 %collective-permute-start = (bf16[69,2,2]{0,2,1:T(2,128)(2,1)S(1)}, bf16[69,2,2]{0,2,1:T(2,128)(2,1)S(1)}, u32[]{:S(2)}, u32[]{:S(2)}) collective-permute-start(bf16[69,2,2]{0,2,1:T(2,128)(2,1)S(1)} %get-tuple-element.184), channel_id=1, source_target_pairs={{0,5},{1,6},{2,7},{3,4},{4,9},{5,10},{6,11},{7,8},{8,13},{9,14},{1... | collective-permute-start | bytes 1664 | tf_op jit(solution)/shard_map/ppermute | solution.py:37
  13.1 5.4 %collective-permute-start.2 = (bf16[69,2,2]{0,2,1:T(2,128)(2,1)S(1)}, bf16[69,2,2]{0,2,1:T(2,128)(2,1)S(1)}, u32[]{:S(2)}, u32[]{:S(2)}) collective-permute-start(bf16[69,2,2]{0,2,1:T(2,128)(2,1)S(1)} %get-tuple-element.183), channel_id=1, source_target_pairs={{0,7},{1,4},{2,5},{3,6},{4,11},{5,8},{6,9},{7,10},{8,15},{9,12},{1... | collective-permute-start | bytes 1664 | tf_op jit(solution)/shard_map/ppermute | solution.py:38
  21.1 4.4 %collective-permute-start.1 = (bf16[69,2,128]{0,2,1:T(8,128)(2,1)S(1)}, bf16[69,2,128]{0,2,1:T(8,128)(2,1)S(1)}, u32[]{:S(2)}, u32[]{:S(2)}) collective-permute-start(bf16[69,2,128]{0,2,1:T(8,128)(2,1)S(1)} %get-tuple-element.186), channel_id=1, source_target_pairs={{0,4},{4,8},{8,12},{12,16},{16,20},{20,24},{24,28},{1,5},{5,9},{9,... | collective-permute-start | bytes 105992 | tf_op jit(solution)/shard_map/ppermute | solution.py:32
  27.2 3.6 %collective-permute-start.4 = (bf16[69,16,2]{0,2,1:T(2,128)(2,1)S(1)}, bf16[69,16,2]{0,2,1:T(2,128)(2,1)S(1)}, u32[]{:S(2)}, u32[]{:S(2)}) collective-permute-start(bf16[69,16,2]{0,2,1:T(2,128)(2,1)S(1)} %get-tuple-element.188), channel_id=1, source_target_pairs={{0,3},{1,0},{2,1},{3,2},{4,7},{5,4},{6,5},{7,6},{8,11},{9,8},{10,9... | collective-permute-start | bytes 13256 | tf_op jit(solution)/shard_map/ppermute | solution.py:35
  30.8 4.0 %copy.266 = bf16[1024,1024]{1,0:T(8,128)(2,1)} copy(bf16[1024,1024]{0,1:T(8,128)(2,1)} %bitcast.280) | data formatting | bytes 4194304 | tf_op jit(solution)/shard_map/reshape.85
  34.7 4.0 %copy.267 = bf16[1024,1024]{1,0:T(8,128)(2,1)} copy(bf16[1024,1024]{0,1:T(8,128)(2,1)} %bitcast.281) | data formatting | bytes 4194304 | tf_op jit(solution)/shard_map/reshape.89
  38.7 3.9 %copy.268 = bf16[1024,1024]{1,0:T(8,128)(2,1)} copy(bf16[1024,1024]{0,1:T(8,128)(2,1)} %bitcast.282) | data formatting | bytes 4194304 | tf_op jit(solution)/shard_map/reshape.93
  58.7 22.2 %all_to_all.34 = bf16[128,3,4,256]{3,0,1,2:T(8,128)(2,1)S(1)} all-to-all(bf16[128,3,4,256]{3,0,1,2:T(8,128)(2,1)S(1)} %copy.238), channel_id=1, replica_groups=mesh['lat'=8,'lon'=4] {'lon'}, dimensions={2} | all-to-all | bytes 1572864 | tf_op jit(solution)/shard_map/all_to_all | solution.py:163
  83.9 29.8 %all-gather.6.cloned.1.call-done = bf16[4096,1,1,256]{3,0,1,2:T(8,128)(2,1)} async-done(((bf16[512,1,1,256]{3,0,1,2:T(8,128)(2,1)}), bf16[4096,1,1,256]{3,0,1,2:T(8,128)(2,1)}) %all-gather.6.cloned.1.call-update) | async-done | bytes 2097168 | tf_op jit(solution)/shard_map/all_gather | solution.py:176
  113.6 7.1 %reshape.174 = bf16[2,2048,4,64]{3,2,1,0:T(4,128)(2,1)} reshape(bf16[4096,1,1,256]{3,0,1,2:T(8,128)(2,1)} %all-gather.6.cloned.1.call-done) | data formatting | bytes 4194304 | tf_op jit(solution)/shard_map/reshape | solution.py:74
  120.7 7.0 %copy.243 = bf16[2,2048,4,64]{1,3,2,0:T(8,128)(2,1)} copy(bf16[2,2048,4,64]{3,2,1,0:T(4,128)(2,1)} %reshape.174) | data formatting | bytes 4194304
  127.7 16.3 %all-gather.8.cloned.1.call-done = bf16[4096,1,1,256]{3,0,1,2:T(8,128)(2,1)} async-done(((bf16[512,1,1,256]{3,0,1,2:T(8,128)(2,1)}), bf16[4096,1,1,256]{3,0,1,2:T(8,128)(2,1)}) %all-gather.8.cloned.1.call-update) | async-done | bytes 2097168 | tf_op jit(solution)/shard_map/all_gather | solution.py:177
  144.0 7.1 %reshape.175 = bf16[2,2048,4,64]{3,2,1,0:T(4,128)(2,1)} reshape(bf16[4096,1,1,256]{3,0,1,2:T(8,128)(2,1)} %all-gather.8.cloned.1.call-done) | data formatting | bytes 4194304 | tf_op jit(solution)/shard_map/reshape | solution.py:75
  151.1 7.0 %copy.244 = bf16[2,2048,4,64]{1,3,2,0:T(8,128)(2,1)} copy(bf16[2,2048,4,64]{3,2,1,0:T(4,128)(2,1)} %reshape.175) | data formatting | bytes 4194304
  158.1 51.9 %while.15 = (s32[]{:T(128)}, f32[512,4]{0,1:T(4,128)S(1)}, f32[512,4]{0,1:T(4,128)S(1)}, f32[512,4,64]{0,2,1:T(8,128)S(1)}, bf16[2,2048,4,64]{1,3,2,0:T(8,128)(2...) while((s32[]{:T(128)}, f32[512,4]{0,1:T(4,128)S(1)}, ...), condition=%wide.region_4.5_spmd.clone, body=%wide.region_1.4_spmd.clone.sunk | while | flops 1107699712 | bytes 62260396 | solution.py:96
  158.1 9.8 %bitcast_reduce_fusion.2 = (f32[512,4]{0,1:T(4,128)S(1)}, f32[4,2048,512]{2,1,0:T(8,128)}) fusion(f32[4]{0:T(128)S(1)} %get-tuple-element.275, bf16[512,4,64]{0,2,1:T(8,128)(2,1)S(1)} %get-tuple-element.274, bf16[2,2048,4,64]{1,3,2,0:T(8,128)(2,1)} %get-tuple-element.273, s32[]{:T(128)} %get-tuple-element.259), kind=kOutput, calls=%fused_computation.1.clone.1 | convolution fusion | flops 545257472 | bytes 18096656 | tf_op jit(solution)/shard_map/while/body/eval_jaxpr/qhd,khd->qhk/dot_general | solution.py:81
  168.0 8.7 %fusion.195 = f32[512,4]{0,1:T(4,128)S(1)} fusion(f32[4,2048,512]{2,1,0:T(8,128)} %get-tuple-element.246, f32[512,4]{0,1:T(4,128)S(1)} %select_maximum_fusion.2, f32[4]{0:T(128)S(1)} %get-tuple-element.275), kind=kLoop, calls=%fused_computation.4.clone.1 | loop fusion | flops 12580864 | bytes 16793616 | tf_op jit(solution)/shard_map/while/body/eval_jaxpr/reduce_sum | solution.py:87
  176.7 7.3 %fusion.197 = f32[512,4,64]{0,2,1:T(8,128)S(1)} fusion(f32[4,2048,512]{2,1,0:T(8,128)} %get-tuple-element.246, f32[512,4]{0,1:T(4,128)S(1)} %select_maximum_fusion.2, f32[4]{0:T(128)S(1)} %get-tuple-element.275, bf16[2,2048,4,64]{1,3,2,0:T(8,128)(2,1)S(1)} %copy-done.1, s32[]{:T(128)} %get-tuple-element.259, ...), kind=kOutput, calls=%fused_computation.7.clone.1 | convolution fusion | flops 549847040 | bytes 18891268 | tf_op jit(solution)/shard_map/while/body/eval_jaxpr/qhk,khd->qhd/dot_general | solution.py:88
  184.1 9.8 %bitcast_reduce_fusion.2 = (f32[512,4]{0,1:T(4,128)S(1)}, f32[4,2048,512]{2,1,0:T(8,128)}) fusion(f32[4]{0:T(128)S(1)} %get-tuple-element.275, bf16[512,4,64]{0,2,1:T(8,128)(2,1)S(1)} %get-tuple-element.274, bf16[2,2048,4,64]{1,3,2,0:T(8,128)(2,1)} %get-tuple-element.273, s32[]{:T(128)} %get-tuple-element.259), kind=kOutput, calls=%fused_computation.1.clone.1 | convolution fusion | flops 545257472 | bytes 18096656 | tf_op jit(solution)/shard_map/while/body/eval_jaxpr/qhd,khd->qhk/dot_general | solution.py:81
  193.9 8.7 %fusion.195 = f32[512,4]{0,1:T(4,128)S(1)} fusion(f32[4,2048,512]{2,1,0:T(8,128)} %get-tuple-element.246, f32[512,4]{0,1:T(4,128)S(1)} %select_maximum_fusion.2, f32[4]{0:T(128)S(1)} %get-tuple-element.275), kind=kLoop, calls=%fused_computation.4.clone.1 | loop fusion | flops 12580864 | bytes 16793616 | tf_op jit(solution)/shard_map/while/body/eval_jaxpr/reduce_sum | solution.py:87
  202.7 7.3 %fusion.197 = f32[512,4,64]{0,2,1:T(8,128)S(1)} fusion(f32[4,2048,512]{2,1,0:T(8,128)} %get-tuple-element.246, f32[512,4]{0,1:T(4,128)S(1)} %select_maximum_fusion.2, f32[4]{0:T(128)S(1)} %get-tuple-element.275, bf16[2,2048,4,64]{1,3,2,0:T(8,128)(2,1)S(1)} %copy-done.1, s32[]{:T(128)} %get-tuple-element.259, ...), kind=kOutput, calls=%fused_computation.7.clone.1 | convolution fusion | flops 549847040 | bytes 18891268 | tf_op jit(solution)/shard_map/while/body/eval_jaxpr/qhk,khd->qhd/dot_general | solution.py:88
  210.9 4.6 %all-to-all-start.1 = ((bf16[4,128,256]{1,2,0:T(8,128)(2,1)}), bf16[4,128,256]{1,2,0:T(8,128)(2,1)S(1)}, u32[]{:S(2)}, u32[]{:S(2)}) async-start(bf16[4,128,256]{1,2,0:T(8,128)(2,1)} %copy.245), calls=%async_computation.1 | async-start | bytes 524288 | tf_op jit(solution)/shard_map/all_to_all | solution.py:181
  215.5 9.3 %all-to-all-done.1 = bf16[4,128,256]{1,2,0:T(8,128)(2,1)S(1)} async-done(((bf16[4,128,256]{1,2,0:T(8,128)(2,1)}), bf16[4,128,256]{1,2,0:T(8,128)(2,1)S(1)}, u32[]{:S(2)}, u32[]{:S(2)}) %all-to-all-start.1) | async-done | bytes 262176 | tf_op jit(solution)/shard_map/all_to_all | solution.py:181
  225.3 3.4 %fusion.73 = bf16[128,4,4,32,4]{0,3,4,2,1:T(8,128)(2,1)S(1)} fusion(bf16[4,32,1024,1,1]{2,1,4,3,0:T(8,128)(2,1)S(1)} %bitcast.285, bf16[1024,4,4,128]{3,2,1,0:T(4,128)(2,1)} %param.30), kind=kOutput, calls=%fused_computation.97 | convolution fusion | flops 539230208 | bytes 4980736 | tf_op jit(solution)/shard_map/pqd,dabh->hpaqb/dot_general | solution.py:189
  229.7 3.0 collective-permute-start.10
  232.7 2.2 collective-permute-start.12
  237.4 5.4 %collective-permute-done.10 = bf16[128,1,1]{2,0,1:T(8,128)(2,1)S(1)} collective-permute-done((bf16[128,1,1]{2,0,1:T(8,128)(2,1)S(1)}, bf16[128,1,1]{2,0,1:T(8,128)(2,1)S(1)}, u32[]{:S(2)}, u32[]{:S(2)}) %collective-permute-start.10) | collective-permute-done | bytes 288 | tf_op jit(solution)/shard_map/ppermute | solution.py:38
  244.1 8.8 %collective-permute-done.13 = bf16[128,1,1]{2,0,1:T(8,128)(2,1)S(1)} collective-permute-done((bf16[128,1,1]{2,0,1:T(8,128)(2,1)S(1)}, bf16[128,1,1]{2,0,1:T(8,128)(2,1)S(1)}, u32[]{:S(2)}, u32[]{:S(2)}) %collective-permute-start.13) | collective-permute-done | bytes 288 | tf_op jit(solution)/shard_map/ppermute | solution.py:39
  254.1 2.1 collective-permute-done.15
  256.2 5.1 %collective-permute-start.9 = (bf16[128,1,128]{2,0,1:T(8,128)(2,1)S(1)}, bf16[128,1,128]{2,0,1:T(8,128)(2,1)S(1)}, u32[]{:S(2)}, u32[]{:S(2)}) collective-permute-start(bf16[128,1,128]{2,0,1:T(8,128)(2,1)S(1)} %get-tuple-element.177), channel_id=1, source_target_pairs={{0,4},{4,8},{8,12},{12,16},{16,20},{20,24},{24,28},{1,5},{5,9},{9,... | collective-permute-start | bytes 98312 | tf_op jit(solution)/shard_map/ppermute | solution.py:32
  262.2 2.0 maximum_maximum_fusion
  269.2 40.7 %all-reduce = f32[2048]{0:T(1024)S(1)} all-reduce(f32[2048]{0:T(1024)S(1)} %dynamic-update-slice), channel_id=4, replica_groups=mesh['lat'=8,'lon'=4] {'lat','lon'}, use_global_device_ids=true, to_apply=%add | all-reduce | flops 2048 | bytes 16384
  (133 shorter events, 38.6 us)
Async XLA Ops:
  7.2 217.6 %copy-start = (bf16[1024,1024]{1,0:T(8,128)(2,1)S(1)}, bf16[1024,1024]{1,0:T(8,128)(2,1)}, u32[]{:S(2)}) copy-start(bf16[1024,1024]{1,0:T(8,128)(2,1)} %param.28) | copy-start | bytes 6291460
  7.2 106.5 %all-gather.6.cloned.1.call-start = ((), (), s32[]{:S(2)}) async-start(), calls=%async_computation.2 | async-start | bytes 2359296 | tf_op jit(solution)/shard_map/all_gather | solution.py:176
  8.7 16.9 %collective-permute-start = (bf16[69,2,2]{0,2,1:T(2,128)(2,1)S(1)}, bf16[69,2,2]{0,2,1:T(2,128)(2,1)S(1)}, u32[]{:S(2)}, u32[]{:S(2)}) collective-permute-start(bf16[69,2,2]{0,2,1:T(2,128)(2,1)S(1)} %get-tuple-element.184), channel_id=1, source_target_pairs={{0,5},{1,6},{2,7},{3,4},{4,9},{5,10},{6,11},{7,8},{8,13},{9,14},{1... | collective-permute-start | bytes 1664 | tf_op jit(solution)/shard_map/ppermute | solution.py:37
  13.1 13.8 %collective-permute-start.2 = (bf16[69,2,2]{0,2,1:T(2,128)(2,1)S(1)}, bf16[69,2,2]{0,2,1:T(2,128)(2,1)S(1)}, u32[]{:S(2)}, u32[]{:S(2)}) collective-permute-start(bf16[69,2,2]{0,2,1:T(2,128)(2,1)S(1)} %get-tuple-element.183), channel_id=1, source_target_pairs={{0,7},{1,4},{2,5},{3,6},{4,11},{5,8},{6,9},{7,10},{8,15},{9,12},{1... | collective-permute-start | bytes 1664 | tf_op jit(solution)/shard_map/ppermute | solution.py:38
  18.5 8.7 %collective-permute-start.5 = (bf16[69,2,2]{0,2,1:T(2,128)(2,1)S(1)}, bf16[69,2,2]{0,2,1:T(2,128)(2,1)S(1)}, u32[]{:S(2)}, u32[]{:S(2)}) collective-permute-start(bf16[69,2,2]{0,2,1:T(2,128)(2,1)S(1)} %get-tuple-element.181), channel_id=1, source_target_pairs={{4,1},{5,2},{6,3},{7,0},{8,5},{9,6},{10,7},{11,4},{12,9},{13,10},{... | collective-permute-start | bytes 1664 | tf_op jit(solution)/shard_map/ppermute | solution.py:39
  19.8 22.9 %collective-permute-start.7 = (bf16[69,2,2]{0,2,1:T(2,128)(2,1)S(1)}, bf16[69,2,2]{0,2,1:T(2,128)(2,1)S(1)}, u32[]{:S(2)}, u32[]{:S(2)}) collective-permute-start(bf16[69,2,2]{0,2,1:T(2,128)(2,1)S(1)} %get-tuple-element.182), channel_id=1, source_target_pairs={{4,3},{5,0},{6,1},{7,2},{8,7},{9,4},{10,5},{11,6},{12,11},{13,8},{... | collective-permute-start | bytes 1664 | tf_op jit(solution)/shard_map/ppermute | solution.py:40
  21.1 21.6 %collective-permute-start.1 = (bf16[69,2,128]{0,2,1:T(8,128)(2,1)S(1)}, bf16[69,2,128]{0,2,1:T(8,128)(2,1)S(1)}, u32[]{:S(2)}, u32[]{:S(2)}) collective-permute-start(bf16[69,2,128]{0,2,1:T(8,128)(2,1)S(1)} %get-tuple-element.186), channel_id=1, source_target_pairs={{0,4},{4,8},{8,12},{12,16},{16,20},{20,24},{24,28},{1,5},{5,9},{9,... | collective-permute-start | bytes 105992 | tf_op jit(solution)/shard_map/ppermute | solution.py:32
  25.6 17.1 %collective-permute-start.6 = (bf16[69,2,128]{0,2,1:T(8,128)(2,1)S(1)}, bf16[69,2,128]{0,2,1:T(8,128)(2,1)S(1)}, u32[]{:S(2)}, u32[]{:S(2)}) collective-permute-start(bf16[69,2,128]{0,2,1:T(8,128)(2,1)S(1)} %get-tuple-element.185), channel_id=1, source_target_pairs={{4,0},{8,4},{12,8},{16,12},{20,16},{24,20},{28,24},{5,1},{9,5},{13... | collective-permute-start | bytes 105992 | tf_op jit(solution)/shard_map/ppermute | solution.py:33
  26.9 15.7 %collective-permute-start.3 = (bf16[69,16,2]{0,2,1:T(2,128)(2,1)S(1)}, bf16[69,16,2]{0,2,1:T(2,128)(2,1)S(1)}, u32[]{:S(2)}, u32[]{:S(2)}) collective-permute-start(bf16[69,16,2]{0,2,1:T(2,128)(2,1)S(1)} %get-tuple-element.187), channel_id=1, source_target_pairs={{0,1},{1,2},{2,3},{3,0},{4,5},{5,6},{6,7},{7,4},{8,9},{9,10},{10,1... | collective-permute-start | bytes 13256 | tf_op jit(solution)/shard_map/ppermute | solution.py:34
  27.2 15.5 %collective-permute-start.4 = (bf16[69,16,2]{0,2,1:T(2,128)(2,1)S(1)}, bf16[69,16,2]{0,2,1:T(2,128)(2,1)S(1)}, u32[]{:S(2)}, u32[]{:S(2)}) collective-permute-start(bf16[69,16,2]{0,2,1:T(2,128)(2,1)S(1)} %get-tuple-element.188), channel_id=1, source_target_pairs={{0,3},{1,0},{2,1},{3,2},{4,7},{5,4},{6,5},{7,6},{8,11},{9,8},{10,9... | collective-permute-start | bytes 13256 | tf_op jit(solution)/shard_map/ppermute | solution.py:35
  47.6 1.0 copy-start.8
  50.7 2.2 copy-start.5
  52.9 1.6 copy-start.4
  54.5 1.6 copy-start.3
  56.1 1.6 copy-start.2
  81.0 1.7 copy-start.14
  81.9 62.1 %all-gather.8.cloned.1.call-start = ((), (), s32[]{:S(2)}) async-start(), calls=%async_computation.3 | async-start | bytes 2359296 | tf_op jit(solution)/shard_map/all_gather | solution.py:177
  167.9 8.8 %copy-start.1 = (bf16[2,2048,4,64]{1,3,2,0:T(8,128)(2,1)S(1)}, bf16[2,2048,4,64]{1,3,2,0:T(8,128)(2,1)}, u32[]{:S(2)}) copy-start(bf16[2,2048,4,64]{1,3,2,0:T(8,128)(2,1)} %get-tuple-element.276) | copy-start | bytes 6291460 | tf_op jit(solution)/shard_map/while
  193.9 8.8 %copy-start.1 = (bf16[2,2048,4,64]{1,3,2,0:T(8,128)(2,1)S(1)}, bf16[2,2048,4,64]{1,3,2,0:T(8,128)(2,1)}, u32[]{:S(2)}) copy-start(bf16[2,2048,4,64]{1,3,2,0:T(8,128)(2,1)} %get-tuple-element.276) | copy-start | bytes 6291460 | tf_op jit(solution)/shard_map/while
  210.9 13.9 %all-to-all-start.1 = ((bf16[4,128,256]{1,2,0:T(8,128)(2,1)}), bf16[4,128,256]{1,2,0:T(8,128)(2,1)S(1)}, u32[]{:S(2)}, u32[]{:S(2)}) async-start(bf16[4,128,256]{1,2,0:T(8,128)(2,1)} %copy.245), calls=%async_computation.1 | async-start | bytes 524288 | tf_op jit(solution)/shard_map/all_to_all | solution.py:181
  229.2 32.1 %copy-start.9 = (bf16[9,69,128]{2,1,0:T(8,128)(2,1)S(1)}, bf16[9,69,128]{2,1,0:T(8,128)(2,1)}, u32[]{:S(2)}) copy-start(bf16[9,69,128]{2,1,0:T(8,128)(2,1)} %param.31) | copy-start | bytes 476932
  229.6 32.2 %collective-permute-start.11 = (bf16[128,16,1]{2,0,1:T(8,128)(2,1)S(1)}, bf16[128,16,1]{2,0,1:T(8,128)(2,1)S(1)}, u32[]{:S(2)}, u32[]{:S(2)}) collective-permute-start(bf16[128,16,1]{2,0,1:T(8,128)(2,1)S(1)} %get-tuple-element.179), channel_id=1, source_target_pairs={{0,1},{1,2},{2,3},{3,0},{4,5},{5,6},{6,7},{7,4},{8,9},{9,10},{10,1... | collective-permute-start | bytes 12296 | tf_op jit(solution)/shard_map/ppermute | solution.py:34
  229.7 13.1 %collective-permute-start.10 = (bf16[128,1,1]{2,0,1:T(8,128)(2,1)S(1)}, bf16[128,1,1]{2,0,1:T(8,128)(2,1)S(1)}, u32[]{:S(2)}, u32[]{:S(2)}) collective-permute-start(bf16[128,1,1]{2,0,1:T(8,128)(2,1)S(1)} %get-tuple-element.176), channel_id=1, source_target_pairs={{0,7},{1,4},{2,5},{3,6},{4,11},{5,8},{6,9},{7,10},{8,15},{9,12},{1... | collective-permute-start | bytes 776 | tf_op jit(solution)/shard_map/ppermute | solution.py:38
  232.7 29.1 %collective-permute-start.12 = (bf16[128,16,1]{2,0,1:T(8,128)(2,1)S(1)}, bf16[128,16,1]{2,0,1:T(8,128)(2,1)S(1)}, u32[]{:S(2)}, u32[]{:S(2)}) collective-permute-start(bf16[128,16,1]{2,0,1:T(8,128)(2,1)S(1)} %get-tuple-element.180), channel_id=1, source_target_pairs={{0,3},{1,0},{2,1},{3,2},{4,7},{5,4},{6,5},{7,6},{8,11},{9,8},{10,9... | collective-permute-start | bytes 12296 | tf_op jit(solution)/shard_map/ppermute | solution.py:35
  234.8 18.0 %collective-permute-start.13 = (bf16[128,1,1]{2,0,1:T(8,128)(2,1)S(1)}, bf16[128,1,1]{2,0,1:T(8,128)(2,1)S(1)}, u32[]{:S(2)}, u32[]{:S(2)}) collective-permute-start(bf16[128,1,1]{2,0,1:T(8,128)(2,1)S(1)} %get-tuple-element.175), channel_id=1, source_target_pairs={{4,1},{5,2},{6,3},{7,0},{8,5},{9,6},{10,7},{11,4},{12,9},{13,10},{... | collective-permute-start | bytes 776 | tf_op jit(solution)/shard_map/ppermute | solution.py:39
  236.1 20.1 %collective-permute-start.15 = (bf16[128,1,1]{2,0,1:T(8,128)(2,1)S(1)}, bf16[128,1,1]{2,0,1:T(8,128)(2,1)S(1)}, u32[]{:S(2)}, u32[]{:S(2)}) collective-permute-start(bf16[128,1,1]{2,0,1:T(8,128)(2,1)S(1)} %get-tuple-element.174), channel_id=1, source_target_pairs={{4,3},{5,0},{6,1},{7,2},{8,7},{9,4},{10,5},{11,6},{12,11},{13,8},{... | collective-permute-start | bytes 776 | tf_op jit(solution)/shard_map/ppermute | solution.py:40
  242.8 19.0 %collective-permute-start.8 = (bf16[128,1,1]{2,0,1:T(8,128)(2,1)S(1)}, bf16[128,1,1]{2,0,1:T(8,128)(2,1)S(1)}, u32[]{:S(2)}, u32[]{:S(2)}) collective-permute-start(bf16[128,1,1]{2,0,1:T(8,128)(2,1)S(1)} %get-tuple-element.173), channel_id=1, source_target_pairs={{0,5},{1,6},{2,7},{3,4},{4,9},{5,10},{6,11},{7,8},{8,13},{9,14},{1... | collective-permute-start | bytes 776 | tf_op jit(solution)/shard_map/ppermute | solution.py:37
  252.8 9.0 %collective-permute-start.14 = (bf16[128,1,128]{2,0,1:T(8,128)(2,1)S(1)}, bf16[128,1,128]{2,0,1:T(8,128)(2,1)S(1)}, u32[]{:S(2)}, u32[]{:S(2)}) collective-permute-start(bf16[128,1,128]{2,0,1:T(8,128)(2,1)S(1)} %get-tuple-element.178), channel_id=1, source_target_pairs={{4,0},{8,4},{12,8},{16,12},{20,16},{24,20},{28,24},{5,1},{9,5},{13... | collective-permute-start | bytes 98312 | tf_op jit(solution)/shard_map/ppermute | solution.py:33
  256.2 5.9 %collective-permute-start.9 = (bf16[128,1,128]{2,0,1:T(8,128)(2,1)S(1)}, bf16[128,1,128]{2,0,1:T(8,128)(2,1)S(1)}, u32[]{:S(2)}, u32[]{:S(2)}) collective-permute-start(bf16[128,1,128]{2,0,1:T(8,128)(2,1)S(1)} %get-tuple-element.177), channel_id=1, source_target_pairs={{0,4},{4,8},{8,12},{12,16},{16,20},{20,24},{24,28},{1,5},{5,9},{9,... | collective-permute-start | bytes 98312 | tf_op jit(solution)/shard_map/ppermute | solution.py:32
  266.3 1.1 copy-start.7
  267.4 1.3 copy-start.13
  267.4 42.6 %copy-start.15 = (s32[64]{0:T(128)S(1)}, s32[64]{0:T(128)}, u32[]{:S(2)}) copy-start(s32[64]{0:T(128)} %param.20) | copy-start | bytes 772
  (4 other events, 3.4 us)
Sparse Core Ops, SparseCore 0:
  82.0 31.5 all-gather.5
  116.1 27.8 all-gather.7

commit v2 on v1

v2 whole, which is shorter than its diff:
```python
import functools
import math

import jax
import jax.numpy as jnp
from jax import lax
from jax.experimental import pallas as pl
from jax.experimental.pallas import tpu as pltpu
from jax.sharding import PartitionSpec as P

HEADS = 16
CLASSES = 8
REG_DEV = 2


def halo_padded(array, width):
    lat_size, lon_size = lax.axis_size("lat"), lax.axis_size("lon")
    down = [(i, i + 1) for i in range(lat_size - 1)]
    up = [(i + 1, i) for i in range(lat_size - 1)]
    from_above = lax.ppermute(array[:, -width:], "lat", down)
    from_below = lax.ppermute(array[:, :width], "lat", up)
    array = jnp.concatenate([from_above, array, from_below], axis=1)
    right = [(j, (j + 1) % lon_size) for j in range(lon_size)]
    left = [((j + 1) % lon_size, j) for j in range(lon_size)]
    from_left = lax.ppermute(array[:, :, -width:], "lon", right)
    from_right = lax.ppermute(array[:, :, :width], "lon", left)
    return jnp.concatenate([from_left, array, from_right], axis=2)


def butterfly_sum(value, axis):
    size, step = lax.axis_size(axis), 1
    while step < size:
        partner = [(i, i ^ step) for i in range(size) if (i ^ step) < size]
        value = value + lax.ppermute(value, axis, partner)
        step *= 2
    return value


def convolution_kernel_taps(padded, weight):
    row_count = padded.shape[1] - 2
    col_count = padded.shape[2] - 2
    result = jnp.zeros((weight.shape[1], row_count, col_count), jnp.float32)
    for tap_index in range(9):
        shift_row = tap_index // 3
        shift_col = tap_index % 3
        window = padded[:, shift_row : shift_row + row_count, shift_col : shift_col + col_count]
        result = result + jnp.einsum(
            "oc,cyx->oyx", weight[tap_index], window, preferred_element_type=jnp.float32
        )
    return result


def meridian_area_factor(rows_total, row_first, row_count):
    row_index = jnp.arange(row_count).astype(jnp.float32) + jnp.asarray(row_first).astype(
        jnp.float32
    )
    return jnp.cos(math.pi * ((row_index + 0.5) / rows_total - 0.5))


def attention_kernel(scale_ref, q_ref, k_ref, v_ref, o_ref, *, head_size):
    queries = q_ref[...]
    keys = k_ref[...]
    values = v_ref[...]
    column_head = lax.broadcasted_iota(jnp.int32, queries.shape, 1) // head_size
    total = jnp.zeros(queries.shape, jnp.float32)
    for head in range(queries.shape[1] // head_size):
        in_head = column_head == head
        masked = jnp.where(in_head, queries, jnp.zeros_like(queries))
        scores = lax.dot_general(
            masked, keys, (((1,), (1,)), ((), ())), preferred_element_type=jnp.float32
        ) * scale_ref[head]
        row_max = jnp.max(scores, axis=1, keepdims=True)
        weights = jnp.exp(scores - row_max)
        weight_sum = jnp.sum(weights, axis=1, keepdims=True)
        weighted = jnp.dot(
            weights.astype(jnp.bfloat16), values, preferred_element_type=jnp.float32
        )
        total = jnp.where(in_head, weighted / weight_sum, total)
    o_ref[...] = total.astype(o_ref.dtype)


def attend(queries, keys, values, scales, head_size):
    query_count, width = queries.shape
    key_count = keys.shape[0]
    block = math.gcd(query_count, 256)
    heads = width // head_size
    return pl.pallas_call(
        functools.partial(attention_kernel, head_size=head_size),
        out_shape=jax.ShapeDtypeStruct((query_count, width), jnp.bfloat16),
        grid=(query_count // block,),
        in_specs=[
            pl.BlockSpec(memory_space=pltpu.SMEM),
            pl.BlockSpec((block, width), lambda i: (i, 0)),
            pl.BlockSpec((key_count, width), lambda i: (0, 0)),
            pl.BlockSpec((key_count, width), lambda i: (0, 0)),
        ],
        out_specs=pl.BlockSpec((block, width), lambda i: (i, 0)),
        compiler_params=pltpu.CompilerParams(vmem_limit_bytes=48 * 1024 * 1024),
        cost_estimate=pl.CostEstimate(
            flops=4 * query_count * key_count * width,
            transcendentals=query_count * key_count * heads,
            bytes_accessed=2 * (2 * query_count * width + 2 * key_count * width),
        ),
    )(scales, queries, keys, values)


def on_device(
    fields,
    goal_state,
    region_mask,
    region_class,
    entry_filter_stencil,
    conv_mid,
    patch_in,
    norm_gain,
    query_weight,
    key_weight,
    value_weight,
    output_weight,
    head_scale,
    patch_out,
    final_convolution_result,
):
    var_count, lat_rows, lon_cols = fields.shape
    conv_count = entry_filter_stencil.shape[1]
    model_width = query_weight.shape[0]
    head_size = model_width // HEADS
    row_first = lax.axis_index("lat") * lat_rows
    rows_total = lat_rows * lax.axis_size("lat")
    padded = halo_padded(fields, 2)
    hidden_one = jax.nn.gelu(convolution_kernel_taps(padded, entry_filter_stencil))
    extended_row = row_first - 1 + jnp.arange(lat_rows + 2, dtype=jnp.int32)
    inside = (extended_row >= 0) & (extended_row < rows_total)
    hidden_padded = jnp.where(inside[None, :, None], hidden_one, 0.0).astype(jnp.bfloat16)
    hidden_two = jax.nn.gelu(convolution_kernel_taps(hidden_padded, conv_mid)).astype(jnp.bfloat16)
    grouped = hidden_two.reshape(conv_count, lat_rows // 4, 4, lon_cols // 4, 4)
    latent = jnp.einsum(
        "hpaqb,abhd->pqd", grouped, patch_in, preferred_element_type=jnp.float32
    ).astype(jnp.bfloat16)
    latent_flat = latent.reshape(-1, model_width)
    latent_wide = latent_flat.astype(jnp.float32)
    normed = (
        latent_wide
        * lax.rsqrt(jnp.mean(latent_wide * latent_wide, axis=1, keepdims=True) + 1e-06)
        * norm_gain
    ).astype(jnp.bfloat16)
    lon_size = lax.axis_size("lon")
    group_width = model_width // lon_size
    projections = lax.optimization_barrier(
        tuple(
            jnp.dot(normed, weight, preferred_element_type=jnp.float32).astype(jnp.bfloat16)
            for weight in (query_weight, key_weight, value_weight)
        )
    )
    projected = jnp.stack(
        [p.reshape(-1, lon_size, group_width).transpose(1, 0, 2) for p in projections]
    )
    spread = lax.all_to_all(projected, "lon", split_axis=1, concat_axis=2, tiled=True)
    query_spread, key_spread, value_spread = (spread[i, 0] for i in range(3))
    local_attender_count = query_spread.shape[1] // head_size
    head_first = lax.axis_index("lon") * local_attender_count
    scales = lax.dynamic_slice_in_dim(head_scale, head_first, local_attender_count) / math.sqrt(
        head_size
    )
    attended_heads = attend(
        query_spread,
        lax.all_gather(key_spread, "lat", axis=0, tiled=True),
        lax.all_gather(value_spread, "lat", axis=0, tiled=True),
        scales,
        head_size,
    )
    attended = lax.all_to_all(attended_heads, "lon", split_axis=0, concat_axis=1, tiled=True)
    latent_two = (
        latent_wide + jnp.dot(attended, output_weight, preferred_element_type=jnp.float32)
    ).astype(jnp.bfloat16)
    latent_grid = latent_two.reshape(lat_rows // 4, lon_cols // 4, model_width)
    decoder_output = jax.nn.gelu(
        jnp.einsum("pqd,dabh->hpaqb", latent_grid, patch_out, preferred_element_type=jnp.float32)
    )
    decoder_output = decoder_output.reshape(conv_count, lat_rows, lon_cols).astype(jnp.bfloat16)
    decoder_output_padded = halo_padded(decoder_output, 1)
    estimated_maps = fields.astype(jnp.float32) + convolution_kernel_taps(
        decoder_output_padded, final_convolution_result
    )
    prediction = estimated_maps.astype(jnp.bfloat16)
    estimate_misfit = estimated_maps - goal_state.astype(jnp.float32)
    point_mismatch = (
        jnp.sum(estimate_misfit * estimate_misfit, axis=0)
        * meridian_area_factor(rows_total, row_first, lat_rows)[:, None]
    )
    region_count = region_class.shape[0]
    region_onehot = (
        region_mask.reshape(1, -1) == jnp.arange(region_count, dtype=jnp.int32)[:, None]
    ).astype(jnp.float32)
    factor = REG_DEV / (var_count * lat_rows * lon_cols)
    partial_loss = (
        jnp.dot(region_onehot, point_mismatch.reshape(-1), precision=lax.Precision.HIGHEST) * factor
    )
    region_loss = butterfly_sum(butterfly_sum(partial_loss, "lon"), "lat")
    class_onehot = (region_class[None, :] == jnp.arange(CLASSES, dtype=jnp.int32)[:, None]).astype(
        jnp.float32
    )
    class_loss = jnp.dot(class_onehot, region_loss, precision=lax.Precision.HIGHEST)
    return (prediction, region_loss, class_loss)


def solution(mesh):
    return jax.shard_map(
        on_device,
        mesh=mesh,
        in_specs=(
            P(None, "lat", "lon"),
            P(None, "lat", "lon"),
            P("lat", "lon"),
            P(),
            P(),
            P(),
            P(),
            P(),
            P(),
            P(),
            P(),
            P(),
            P(),
            P(),
            P(),
        ),
        out_specs=(P(None, "lat", "lon"), P(), P()),
        check_vma=False,
    )
```

time: 320 us -> 212 us (0.66)
  blocking collectives: 62.9 us -> 26.1 us
  matrix products: 53.3 us -> 21 us
  local copies, waits for them, and re-layouts: 51.3 us -> 19 us
  starting transfers between devices: 42.2 us -> 22.4 us
  other arithmetic: 20.5 us -> 2.76 us
  waiting for transfers between devices: 72.5 us -> 90.2 us
  Pallas kernels: 0 us -> 14.8 us
    unnamed x1 -> x0, blocking collectives: 40.7 us -> none
    dot_general x7 -> x3, matrix products: 36.8 us -> 1.34 us  [on_device(): jnp.dot(normed, weight, preferred_element_type=jnp.float32)]
    ppermute x16 -> x13, starting transfers between devices: 37.3 us -> 17.5 us  [the longest x5 5.35 us: butterfly_sum(): value = value + lax.ppermute(value, axis, partner)]
    reduce_sum x3 -> x0, other arithmetic: 17.5 us -> none  [the longest x2 17.4 us: scan_step(): weight_sum = weight_sum * rescale + jnp.sum(weights, axis=2)]
    pallas_call x0 -> x1, Pallas kernels: none -> 14.8 us  [attend(): pl.pallas_call(functools.partial(attention_kernel, head_size=head_size),...]
    reshape x2 -> x1, local copies, waits for them, and re-layouts: 14.2 us -> 0.02 us  [on_device(): p.reshape(-1, lon_size, group_width).transpose(1, 0, 2)]
    all_gather x1, waiting for transfers between devices: 16.3 us -> 30.4 us  [on_device(): lax.all_gather(value_spread, 'lat', axis=0, tiled=True)]
    another operation x3 -> x1, local copies, waits for them, and re-layouts: 11.8 us -> 0.04 us  [on_device(): jnp.stack([p.reshape(-1, lon_size, group_width).transpose(1, 0, 2) for p...]
  transfers between devices with their start and end apart: 19 -> 16, of which waited for: 7 -> 12; matrix products, arithmetic and copies ran while one was open for 9% -> 2% of each run, Pallas kernels for 0% -> 0%
where the time goes in v2:
time: 212 us; the launch traced here: 211 us
  waiting for transfers between devices  90.2 us (43%)
  blocking collectives  26.1 us (12%)
  starting transfers between devices  22.4 us (11%)
  matrix products  21 us (10%)
  local copies, waits for them, and re-layouts  19 us (9%)
  Pallas kernels  14.8 us (7%)
  between operations  14.5 us (7%)
  other arithmetic  2.76 us (1%)
    all_gather x1, waiting for transfers between devices, on_device(): lax.all_gather(value_spread, 'lat', axis=0, tiled=True)  30.4 us
    all_gather x1, waiting for transfers between devices, on_device(): lax.all_gather(key_spread, 'lat', axis=0, tiled=True)  26.8 us
    all_to_all x1, blocking collectives, on_device(): lax.all_to_all(projected, 'lon', split_axis=1, concat_axis=2, tiled=True)  26.1 us
    pallas_call x1, Pallas kernels, attend(): pl.pallas_call(functools.partial(attention_kernel, head_size=head_size),...  14.8 us
    dot_general x27, matrix products, convolution_kernel_taps(): jnp.einsum('oc,cyx->oyx', weight[tap_index], window, preferred_element_ty...  12.4 us
    ppermute x5, waiting for transfers between devices, butterfly_sum(): value = value + lax.ppermute(value, axis, partner)  11.4 us
    unnamed x38, local copies, waits for them, and re-layouts  10.3 us
    all_to_all x1, waiting for transfers between devices, on_device(): lax.all_to_all(attended_heads, 'lon', split_axis=0, concat_axis=1, tiled=...  9.32 us
  transfers between devices with their start and end apart: 16, of which 12 were waited for; matrix products, arithmetic and copies ran while one was open for 2% of the time, Pallas kernels for 0%

profile of v2, /device:TPU:0, one launch (start us, length us, event | category | flops | bytes accessed | tf_op | source)
XLA Modules:
  0.0 210.7 jit_solution(18266060446519497179)
XLA Ops:
  7.2 1.5 copy.49
  8.8 2.4 %collective-permute-start = (bf16[69,2,128]{0,2,1:T(8,128)(2,1)S(1)}, bf16[69,2,128]{0,2,1:T(8,128)(2,1)S(1)}, u32[]{:S(2)}, u32[]{:S(2)}) collective-permute-start(bf16[69,2,128]{0,2,1:T(8,128)(2,1)S(1)} %get-tuple-element.31), channel_id=1, source_target_pairs={{0,4},{4,8},{8,12},{12,16},{16,20},{20,24},{24,28},{1,5},{5,9},{9,... | collective-permute-start | bytes 105992 | tf_op jit(solution)/shard_map/ppermute | solution.py:20
  11.1 1.3 collective-permute-start.1
  12.4 3.9 %collective-permute-done.1 = bf16[69,2,128]{0,2,1:T(8,128)(2,1)S(1)} collective-permute-done((bf16[69,2,128]{0,2,1:T(8,128)(2,1)S(1)}, bf16[69,2,128]{0,2,1:T(8,128)(2,1)S(1)}, u32[]{:S(2)}, u32[]{:S(2)}) %collective-permute-start.1) | collective-permute-done | bytes 35360 | tf_op jit(solution)/shard_map/ppermute | solution.py:21
  16.4 1.6 collective-permute-start.2
  18.0 2.2 %collective-permute-start.3 = (bf16[69,20,2]{0,2,1:T(2,128)(2,1)S(1)}, bf16[69,20,2]{0,2,1:T(2,128)(2,1)S(1)}, u32[]{:S(2)}, u32[]{:S(2)}) collective-permute-start(bf16[69,20,2]{0,2,1:T(2,128)(2,1)S(1)} %get-tuple-element.22), channel_id=1, source_target_pairs={{1,0},{2,1},{3,2},{0,3},{5,4},{6,5},{7,6},{4,7},{9,8},{10,9},{11,1... | collective-permute-start | bytes 16568 | tf_op jit(solution)/shard_map/ppermute | solution.py:26
  20.3 1.6 collective-permute-done.2
  30.3 1.3 copy-done.3
  36.4 26.1 %all_to_all.28 = bf16[3,4,128,256]{3,2,0,1:T(8,128)(2,1)S(1)} all-to-all(bf16[3,4,128,256]{3,2,0,1:T(8,128)(2,1)S(1)} %pad_maximum_fusion.1), channel_id=1, replica_groups=mesh['lat'=8,'lon'=4] {'lon'}, dimensions={1} | all-to-all | bytes 1572864 | tf_op jit(solution)/shard_map/all_to_all | solution.py:158
  64.3 26.8 %all-gather.3.cloned.1.call-done.k_ref = bf16[4096,256]{1,0:T(8,128)(2,1)} async-done(((bf16[512,256]{1,0:T(8,128)(2,1)}), bf16[4096,256]{1,0:T(8,128)(2,1)}) %all-gather.3.cloned.1.call-update) | async-done | bytes 2097168 | tf_op jit(solution)/shard_map/all_gather | solution.py:167
  91.1 30.4 %all-gather.5.cloned.1.call-done.v_ref = bf16[4096,256]{1,0:T(8,128)(2,1)} async-done(((bf16[512,256]{1,0:T(8,128)(2,1)}), bf16[4096,256]{1,0:T(8,128)(2,1)}) %all-gather.5.cloned.1.call-update) | async-done | bytes 2097168 | tf_op jit(solution)/shard_map/all_gather | solution.py:168
  121.5 1.6 copy-done.1
  123.1 1.6 copy-done.2
  124.7 14.8 %shard_map.166 = bf16[512,256]{1,0:T(8,128)(2,1)S(1)} custom-call(f32[4]{0:T(128)S(1)} %dynamic-slice_multiply_fusion.scale_ref, bf16[512,256]{1,0:T(8,128)(2,1)S(1)} %bitcast.226, bf16[4096,256]{1,0:T(8,128)(2,1)S(1)} %copy-done.1, bf16[4096,256]{1,0:T(8,128)(2,1)S(1)} %copy-done.2), custom_call_target="tpu_custom_call" | custom-call | flops 2147483648 | bytes 4718592 | tf_op jit(solution)/shard_map/pallas_call | solution.py:87
  140.3 4.6 %all-to-all-start.1 = ((bf16[4,128,256]{1,2,0:T(8,128)(2,1)}), bf16[4,128,256]{1,2,0:T(8,128)(2,1)S(1)}, u32[]{:S(2)}, u32[]{:S(2)}) async-start(bf16[4,128,256]{1,2,0:T(8,128)(2,1)} %copy.56), calls=%async_computation.1 | async-start | bytes 524288 | tf_op jit(solution)/shard_map/all_to_all | solution.py:172
  144.9 9.3 %all-to-all-done.1 = bf16[4,128,256]{1,2,0:T(8,128)(2,1)S(1)} async-done(((bf16[4,128,256]{1,2,0:T(8,128)(2,1)}), bf16[4,128,256]{1,2,0:T(8,128)(2,1)S(1)}, u32[]{:S(2)}, u32[]{:S(2)}) %all-to-all-start.1) | async-done | bytes 262176 | tf_op jit(solution)/shard_map/all_to_all | solution.py:172
  154.2 2.1 fusion.36
  156.3 3.4 %fusion.58 = bf16[128,4,4,32,4]{0,3,4,2,1:T(8,128)(2,1)S(1)} fusion(bf16[4,32,1024,1,1]{2,1,4,3,0:T(8,128)(2,1)S(1)} %bitcast.238, bf16[1024,4,4,128]{3,2,1,0:T(4,128)(2,1)} %param.28), kind=kOutput, calls=%fused_computation.74 | convolution fusion | flops 539230208 | bytes 4980736 | tf_op jit(solution)/shard_map/pqd,dabh->hpaqb/dot_general | solution.py:178
  160.3 1.3 collective-permute-start.4
  161.6 1.3 collective-permute-start.5
  162.9 3.5 %collective-permute-done.5 = bf16[128,1,128]{2,0,1:T(8,128)(2,1)S(1)} collective-permute-done((bf16[128,1,128]{2,0,1:T(8,128)(2,1)S(1)}, bf16[128,1,128]{2,0,1:T(8,128)(2,1)S(1)}, u32[]{:S(2)}, u32[]{:S(2)}) %collective-permute-start.5) | collective-permute-done | bytes 32800 | tf_op jit(solution)/shard_map/ppermute | solution.py:21
  166.5 1.3 fusion.160
  167.7 1.4 copy.62
  169.1 1.4 copy.65
  170.4 1.5 collective-permute-start.7
  174.7 2.7 %collective-permute-done.6 = bf16[128,18,1]{0,1,2:T(8,128)(2,1)S(1)} collective-permute-done((bf16[128,18,1]{0,1,2:T(8,128)(2,1)S(1)}, bf16[128,18,1]{0,1,2:T(8,128)(2,1)S(1)}, u32[]{:S(2)}, u32[]{:S(2)}) %collective-permute-start.6) | collective-permute-done | bytes 4640 | tf_op jit(solution)/shard_map/ppermute | solution.py:25
  179.6 2.0 maximum_maximum_fusion
  185.7 3.6 %collective-permute-done.8 = f32[64]{0:T(128)S(1)} collective-permute-done((f32[64]{0:T(128)S(1)}, f32[64]{0:T(128)S(1)}, u32[]{:S(2)}, u32[]{:S(2)}) %collective-permute-start.8) | collective-permute-done | bytes 288 | tf_op jit(solution)/shard_map/ppermute | solution.py:34
  189.3 4.4 %collective-permute-done.9 = f32[64]{0:T(128)S(1)} collective-permute-done((f32[64]{0:T(128)S(1)}, f32[64]{0:T(128)S(1)}, u32[]{:S(2)}, u32[]{:S(2)}) %collective-permute-start.9) | collective-permute-done | bytes 288 | tf_op jit(solution)/shard_map/ppermute | solution.py:34
  194.9 2.5 %collective-permute-start.11 = (f32[64]{0:T(128)S(1)}, f32[64]{0:T(128)S(1)}, u32[]{:S(2)}, u32[]{:S(2)}) collective-permute-start(f32[64]{0:T(128)S(1)} %add.234), channel_id=1, source_target_pairs={{0,8},{4,12},{8,0},{12,4},{16,24},{20,28},{24,16},{28,20},{1,9},{5... | collective-permute-start | bytes 776 | tf_op jit(solution)/shard_map/ppermute | solution.py:34
  197.4 1.5 collective-permute-done.11
  198.9 2.8 %collective-permute-start.12 = (f32[64]{0:T(128)S(1)}, f32[64]{0:T(128)S(1)}, u32[]{:S(2)}, u32[]{:S(2)}) collective-permute-start(f32[64]{0:T(128)S(1)} %add.235), channel_id=1, source_target_pairs={{0,16},{4,20},{8,24},{12,28},{16,0},{20,4},{24,8},{28,12},{1,17},{... | collective-permute-start | bytes 776 | tf_op jit(solution)/shard_map/ppermute | solution.py:34
  (107 shorter events, 28.6 us)
Async XLA Ops:
  7.2 25.4 %copy-start = (bf16[1024,1024]{1,0:T(8,128)(2,1)S(1)}, bf16[1024,1024]{1,0:T(8,128)(2,1)}, u32[]{:S(2)}) copy-start(bf16[1024,1024]{1,0:T(8,128)(2,1)} %param.25) | copy-start | bytes 6291460
  7.2 15.0 %copy-start.12 = (bf16[9,128,69]{1,2,0:T(8,128)(2,1)S(1)}, bf16[9,128,69]{1,2,0:T(8,128)(2,1)}, u32[]{:S(2)}) copy-start(bf16[9,128,69]{1,2,0:T(8,128)(2,1)} %param.19) | copy-start | bytes 476932
  7.2 83.9 %all-gather.3.cloned.1.call-start = ((), (), s32[]{:S(2)}) async-start(), calls=%async_computation.2 | async-start | bytes 2359296 | tf_op jit(solution)/shard_map/all_gather | solution.py:167
  8.8 3.7 %collective-permute-start = (bf16[69,2,128]{0,2,1:T(8,128)(2,1)S(1)}, bf16[69,2,128]{0,2,1:T(8,128)(2,1)S(1)}, u32[]{:S(2)}, u32[]{:S(2)}) collective-permute-start(bf16[69,2,128]{0,2,1:T(8,128)(2,1)S(1)} %get-tuple-element.31), channel_id=1, source_target_pairs={{0,4},{4,8},{8,12},{12,16},{16,20},{20,24},{24,28},{1,5},{5,9},{9,... | collective-permute-start | bytes 105992 | tf_op jit(solution)/shard_map/ppermute | solution.py:20
  11.1 5.3 %collective-permute-start.1 = (bf16[69,2,128]{0,2,1:T(8,128)(2,1)S(1)}, bf16[69,2,128]{0,2,1:T(8,128)(2,1)S(1)}, u32[]{:S(2)}, u32[]{:S(2)}) collective-permute-start(bf16[69,2,128]{0,2,1:T(8,128)(2,1)S(1)} %get-tuple-element.32), channel_id=1, source_target_pairs={{4,0},{8,4},{12,8},{16,12},{20,16},{24,20},{28,24},{5,1},{9,5},{13... | collective-permute-start | bytes 105992 | tf_op jit(solution)/shard_map/ppermute | solution.py:21
  16.4 5.5 %collective-permute-start.2 = (bf16[69,20,2]{0,2,1:T(2,128)(2,1)S(1)}, bf16[69,20,2]{0,2,1:T(2,128)(2,1)S(1)}, u32[]{:S(2)}, u32[]{:S(2)}) collective-permute-start(bf16[69,20,2]{0,2,1:T(2,128)(2,1)S(1)} %get-tuple-element.21), channel_id=1, source_target_pairs={{0,1},{1,2},{2,3},{3,0},{4,5},{5,6},{6,7},{7,4},{8,9},{9,10},{10,1... | collective-permute-start | bytes 16568 | tf_op jit(solution)/shard_map/ppermute | solution.py:25
  18.0 3.9 %collective-permute-start.3 = (bf16[69,20,2]{0,2,1:T(2,128)(2,1)S(1)}, bf16[69,20,2]{0,2,1:T(2,128)(2,1)S(1)}, u32[]{:S(2)}, u32[]{:S(2)}) collective-permute-start(bf16[69,20,2]{0,2,1:T(2,128)(2,1)S(1)} %get-tuple-element.22), channel_id=1, source_target_pairs={{1,0},{2,1},{3,2},{0,3},{5,4},{6,5},{7,6},{4,7},{9,8},{10,9},{11,1... | collective-permute-start | bytes 16568 | tf_op jit(solution)/shard_map/ppermute | solution.py:26
  26.0 1.2 copy-start.10
  29.3 2.2 %copy-start.3 = (bf16[4,4,128,1024]{3,2,1,0:T(8,128)(2,1)S(1)}, bf16[4,4,128,1024]{3,2,1,0:T(8,128)(2,1)}, u32[]{:S(2)}) copy-start(bf16[4,4,128,1024]{3,2,1,0:T(8,128)(2,1)} %param.21) | copy-start | bytes 12582916
  31.5 0.9 copy-start.13
  32.6 1.6 copy-start.6
  34.2 1.6 copy-start.7
  62.5 1.6 copy-start.15
  63.4 58.1 %all-gather.5.cloned.1.call-start = ((), (), s32[]{:S(2)}) async-start(), calls=%async_computation.3 | async-start | bytes 2359296 | tf_op jit(solution)/shard_map/all_gather | solution.py:168
  121.5 1.6 copy-start.1
  123.1 1.6 copy-start.2
  140.3 13.9 %all-to-all-start.1 = ((bf16[4,128,256]{1,2,0:T(8,128)(2,1)}), bf16[4,128,256]{1,2,0:T(8,128)(2,1)S(1)}, u32[]{:S(2)}, u32[]{:S(2)}) async-start(bf16[4,128,256]{1,2,0:T(8,128)(2,1)} %copy.56), calls=%async_computation.1 | async-start | bytes 524288 | tf_op jit(solution)/shard_map/all_to_all | solution.py:172
  160.3 2.6 %collective-permute-start.4 = (bf16[128,1,128]{2,0,1:T(8,128)(2,1)S(1)}, bf16[128,1,128]{2,0,1:T(8,128)(2,1)S(1)}, u32[]{:S(2)}, u32[]{:S(2)}) collective-permute-start(bf16[128,1,128]{2,0,1:T(8,128)(2,1)S(1)} %get-tuple-element.29), channel_id=1, source_target_pairs={{0,4},{4,8},{8,12},{12,16},{16,20},{20,24},{24,28},{1,5},{5,9},{9,... | collective-permute-start | bytes 98312 | tf_op jit(solution)/shard_map/ppermute | solution.py:20
  161.6 4.8 %collective-permute-start.5 = (bf16[128,1,128]{2,0,1:T(8,128)(2,1)S(1)}, bf16[128,1,128]{2,0,1:T(8,128)(2,1)S(1)}, u32[]{:S(2)}, u32[]{:S(2)}) collective-permute-start(bf16[128,1,128]{2,0,1:T(8,128)(2,1)S(1)} %get-tuple-element.30), channel_id=1, source_target_pairs={{4,0},{8,4},{12,8},{16,12},{20,16},{24,20},{28,24},{5,1},{9,5},{13... | collective-permute-start | bytes 98312 | tf_op jit(solution)/shard_map/ppermute | solution.py:21
  166.4 6.1 %copy-start.11 = (bf16[9,69,128]{2,1,0:T(8,128)(2,1)S(1)}, bf16[9,69,128]{2,1,0:T(8,128)(2,1)}, u32[]{:S(2)}) copy-start(bf16[9,69,128]{2,1,0:T(8,128)(2,1)} %param.29) | copy-start | bytes 476932
  170.4 8.0 %collective-permute-start.7 = (bf16[128,18,1]{0,1,2:T(8,128)(2,1)S(1)}, bf16[128,18,1]{0,1,2:T(8,128)(2,1)S(1)}, u32[]{:S(2)}, u32[]{:S(2)}) collective-permute-start(bf16[128,18,1]{0,1,2:T(8,128)(2,1)S(1)} %copy.65), channel_id=1, source_target_pairs={{1,0},{2,1},{3,2},{0,3},{5,4},{6,5},{7,6},{4,7},{9,8},{10,9},{11,1... | collective-permute-start | bytes 13832 | tf_op jit(solution)/shard_map/ppermute | solution.py:26
  171.9 5.4 %collective-permute-start.6 = (bf16[128,18,1]{0,1,2:T(8,128)(2,1)S(1)}, bf16[128,18,1]{0,1,2:T(8,128)(2,1)S(1)}, u32[]{:S(2)}, u32[]{:S(2)}) collective-permute-start(bf16[128,18,1]{0,1,2:T(8,128)(2,1)S(1)} %copy.62), channel_id=1, source_target_pairs={{0,1},{1,2},{2,3},{3,0},{4,5},{5,6},{6,7},{7,4},{8,9},{9,10},{10,1... | collective-permute-start | bytes 13832 | tf_op jit(solution)/shard_map/ppermute | solution.py:25
  181.6 1.1 copy-start.5
  183.5 1.1 copy-start.4
  183.5 1.1 copy-start.8
  183.5 1.2 copy-start.9
  184.7 18.6 %copy-start.16 = (s32[64]{0:T(128)S(1)}, s32[64]{0:T(128)}, u32[]{:S(2)}) copy-start(s32[64]{0:T(128)} %param.18) | copy-start | bytes 772
  185.7 3.6 %collective-permute-start.8 = (f32[64]{0:T(128)S(1)}, f32[64]{0:T(128)S(1)}, u32[]{:S(2)}, u32[]{:S(2)}) collective-permute-start(f32[64]{0:T(128)S(1)} %fusion.40), channel_id=1, source_target_pairs={{0,1},{1,0},{2,3},{3,2},{4,5},{5,4},{6,7},{7,6},{8,9},{9,8},{10,11... | collective-permute-start | bytes 776 | tf_op jit(solution)/shard_map/ppermute | solution.py:34
  189.3 4.4 %collective-permute-start.9 = (f32[64]{0:T(128)S(1)}, f32[64]{0:T(128)S(1)}, u32[]{:S(2)}, u32[]{:S(2)}) collective-permute-start(f32[64]{0:T(128)S(1)} %add.232), channel_id=1, source_target_pairs={{0,2},{1,3},{2,0},{3,1},{4,6},{5,7},{6,4},{7,5},{8,10},{9,11},{10,... | collective-permute-start | bytes 776 | tf_op jit(solution)/shard_map/ppermute | solution.py:34
  193.7 1.1 collective-permute-start.10
  194.9 4.0 %collective-permute-start.11 = (f32[64]{0:T(128)S(1)}, f32[64]{0:T(128)S(1)}, u32[]{:S(2)}, u32[]{:S(2)}) collective-permute-start(f32[64]{0:T(128)S(1)} %add.234), channel_id=1, source_target_pairs={{0,8},{4,12},{8,0},{12,4},{16,24},{20,28},{24,16},{28,20},{1,9},{5... | collective-permute-start | bytes 776 | tf_op jit(solution)/shard_map/ppermute | solution.py:34
  198.9 4.3 %collective-permute-start.12 = (f32[64]{0:T(128)S(1)}, f32[64]{0:T(128)S(1)}, u32[]{:S(2)}, u32[]{:S(2)}) collective-permute-start(f32[64]{0:T(128)S(1)} %add.235), channel_id=1, source_target_pairs={{0,16},{4,20},{8,24},{12,28},{16,0},{20,4},{24,8},{28,12},{1,17},{... | collective-permute-start | bytes 776 | tf_op jit(solution)/shard_map/ppermute | solution.py:34
  (2 other events, 1.3 us)
Sparse Core Ops, SparseCore 0:
  63.5 27.5 all-gather.2
  93.6 27.8 all-gather.4

commit v3 on v2

--- a/solution.py
+++ b/solution.py
@@ -82,7 +82,7 @@
 def attend(queries, keys, values, scales, head_size):
     query_count, width = queries.shape
     key_count = keys.shape[0]
-    block = math.gcd(query_count, 256)
+    block = math.gcd(query_count, max(8, (1 << 20) // key_count))
     heads = width // head_size
     return pl.pallas_call(
         functools.partial(attention_kernel, head_size=head_size),
@@ -157,17 +157,34 @@
     )
     spread = lax.all_to_all(projected, "lon", split_axis=1, concat_axis=2, tiled=True)
     query_spread, key_spread, value_spread = (spread[i, 0] for i in range(3))
-    local_attender_count = query_spread.shape[1] // head_size
-    head_first = lax.axis_index("lon") * local_attender_count
-    scales = lax.dynamic_slice_in_dim(head_scale, head_first, local_attender_count) / math.sqrt(
-        head_size
-    )
-    attended_heads = attend(
-        query_spread,
-        lax.all_gather(key_spread, "lat", axis=0, tiled=True),
-        lax.all_gather(value_spread, "lat", axis=0, tiled=True),
-        scales,
-        head_size,
+    lat_size = lax.axis_size("lat")
+    core = lax.axis_index("lat") % 2
+    half = group_width // 2
+    stacked = jnp.stack([query_spread, key_spread, value_spread])
+    low, high = stacked[..., :half], stacked[..., half:]
+    mine = jnp.where(core == 0, low, high)
+    theirs = jnp.where(core == 0, high, low)
+    partner = [(i, i ^ 1) for i in range(lat_size)]
+    pair_tokens = jnp.concatenate([mine, lax.ppermute(theirs, "lat", partner)], axis=1)
+    key_value = pair_tokens[1:]
+    chunks = [key_value] + [
+        lax.ppermute(key_value, "lat", [(i, i ^ (2 * d)) for i in range(lat_size)])
+        for d in range(1, lat_size // 2)
+    ]
+    all_key_value = jnp.concatenate(chunks, axis=1)
+    local_heads = half // head_size
+    head_first = (lax.axis_index("lon") * 2 + core) * local_heads
+    scales = lax.dynamic_slice_in_dim(head_scale, head_first, local_heads) / math.sqrt(head_size)
+    pair_attended = attend(
+        pair_tokens[0], all_key_value[0], all_key_value[1], scales, head_size
+    )
+    token_count = query_spread.shape[0]
+    own_part = pair_attended[:token_count]
+    returned = lax.ppermute(pair_attended[token_count:], "lat", partner)
+    attended_heads = jnp.where(
+        core == 0,
+        jnp.concatenate([own_part, returned], axis=1),
+        jnp.concatenate([returned, own_part], axis=1),
     )
     attended = lax.all_to_all(attended_heads, "lon", split_axis=0, concat_axis=1, tiled=True)
     latent_two = (

time: 212 us -> 169 us (0.80)
  blocking collectives: 26.1 us -> 0 us
  between operations: 14.5 us -> 1.18 us
  waiting for transfers between devices: 90.2 us -> 78.6 us
  starting transfers between devices: 22.4 us -> 29.8 us
  other arithmetic: 2.76 us -> 7.03 us
  local copies, waits for them, and re-layouts: 19 us -> 15.2 us
    all_gather x2 -> x0, waiting for transfers between devices: 57.2 us -> none  [the longest x1 30.4 us: on_device(): lax.all_gather(value_spread, 'lat', axis=0, tiled=True)]
    all_to_all x1 -> x0, blocking collectives: 26.1 us -> none  [on_device(): lax.all_to_all(projected, 'lon', split_axis=1, concat_axis=2, tiled=True)]
    ppermute x0 -> x5, waiting for transfers between devices: none -> 24.2 us  [the longest x3 21.4 us: on_device(): lax.ppermute(key_value, 'lat', [(i, i ^ 2 * d) for i in range(lat_size)])]
    all_to_all x0 -> x1, waiting for transfers between devices: none -> 21.2 us  [on_device(): lax.all_to_all(projected, 'lon', split_axis=1, concat_axis=2, tiled=True)]
    all_to_all x0 -> x1, starting transfers between devices: none -> 5.13 us  [on_device(): lax.all_to_all(projected, 'lon', split_axis=1, concat_axis=2, tiled=True)]
    ppermute x0 -> x5, starting transfers between devices: none -> 4.24 us  [the longest x3 3.95 us: on_device(): lax.ppermute(key_value, 'lat', [(i, i ^ 2 * d) for i in range(lat_size)])]
    unnamed x38 -> x36, local copies, waits for them, and re-layouts: 10.3 us -> 7.8 us
  transfers between devices with their start and end apart: 16 -> 20, of which waited for: 12 -> 16; matrix products, arithmetic and copies ran while one was open for 2% -> 3% of each run, Pallas kernels for 0% -> 0%
where the time goes in v3:
time: 169 us; the launch traced here: 168 us
  waiting for transfers between devices  78.6 us (47%)
  starting transfers between devices  29.8 us (18%)
  matrix products  21 us (12%)
  local copies, waits for them, and re-layouts  15.2 us (9%)
  Pallas kernels  15.1 us (9%)
  other arithmetic  7.03 us (4%)
    ppermute x3, waiting for transfers between devices, on_device(): lax.ppermute(key_value, 'lat', [(i, i ^ 2 * d) for i in range(lat_size)])  21.4 us
    all_to_all x1, waiting for transfers between devices, on_device(): lax.all_to_all(projected, 'lon', split_axis=1, concat_axis=2, tiled=True)  21.2 us
    pallas_call x1, Pallas kernels, attend(): pl.pallas_call(functools.partial(attention_kernel, head_size=head_size),...  15.1 us
    dot_general x27, matrix products, convolution_kernel_taps(): jnp.einsum('oc,cyx->oyx', weight[tap_index], window, preferred_element_ty...  12.4 us
    ppermute x5, waiting for transfers between devices, butterfly_sum(): value = value + lax.ppermute(value, axis, partner)  11.4 us
    all_to_all x1, waiting for transfers between devices, on_device(): lax.all_to_all(attended_heads, 'lon', split_axis=0, concat_axis=1, tiled=...  9.42 us
    ppermute x2, waiting for transfers between devices, halo_padded(): from_below = lax.ppermute(array[:, :width], 'lat', up)  7.96 us
    unnamed x36, local copies, waits for them, and re-layouts  7.8 us
  transfers between devices with their start and end apart: 20, of which 16 were waited for; matrix products, arithmetic and copies ran while one was open for 3% of the time, Pallas kernels for 0%

profile of v3, /device:TPU:0, one launch (start us, length us, event | category | flops | bytes accessed | tf_op | source)
XLA Modules:
  0.0 167.8 jit_solution(1648750266230108536)
XLA Ops:
  0.7 1.5 copy.52
  2.2 2.4 %collective-permute-start = (bf16[69,2,128]{0,2,1:T(8,128)(2,1)S(1)}, bf16[69,2,128]{0,2,1:T(8,128)(2,1)S(1)}, u32[]{:S(2)}, u32[]{:S(2)}) collective-permute-start(bf16[69,2,128]{0,2,1:T(8,128)(2,1)S(1)} %get-tuple-element.35), channel_id=1, source_target_pairs={{0,4},{4,8},{8,12},{12,16},{16,20},{20,24},{24,28},{1,5},{5,9},{9,... | collective-permute-start | bytes 105992 | tf_op jit(solution)/shard_map/ppermute | solution.py:20
  4.5 1.3 collective-permute-start.1
  5.9 3.9 %collective-permute-done.1 = bf16[69,2,128]{0,2,1:T(8,128)(2,1)S(1)} collective-permute-done((bf16[69,2,128]{0,2,1:T(8,128)(2,1)S(1)}, bf16[69,2,128]{0,2,1:T(8,128)(2,1)S(1)}, u32[]{:S(2)}, u32[]{:S(2)}) %collective-permute-start.1) | collective-permute-done | bytes 35360 | tf_op jit(solution)/shard_map/ppermute | solution.py:21
  9.8 1.6 collective-permute-start.2
  11.5 2.2 %collective-permute-start.3 = (bf16[69,20,2]{0,2,1:T(2,128)(2,1)S(1)}, bf16[69,20,2]{0,2,1:T(2,128)(2,1)S(1)}, u32[]{:S(2)}, u32[]{:S(2)}) collective-permute-start(bf16[69,20,2]{0,2,1:T(2,128)(2,1)S(1)} %get-tuple-element.26), channel_id=1, source_target_pairs={{1,0},{2,1},{3,2},{0,3},{5,4},{6,5},{7,6},{4,7},{9,8},{10,9},{11,1... | collective-permute-start | bytes 16568 | tf_op jit(solution)/shard_map/ppermute | solution.py:26
  13.7 1.6 collective-permute-done.2
  30.7 5.1 %all-to-all-start = ((bf16[3,4,128,256]{3,2,0,1:T(8,128)(2,1)}), bf16[3,4,128,256]{3,2,0,1:T(8,128)(2,1)S(1)}, u32[]{:S(2)}, u32[]{:S(2)}) async-start(bf16[3,4,128,256]{3,2,0,1:T(8,128)(2,1)} %pad_maximum_fusion.2), calls=%async_computation | async-start | bytes 1572864 | tf_op jit(solution)/shard_map/all_to_all | solution.py:158
  35.8 21.2 %all-to-all-done = bf16[3,4,128,256]{3,2,0,1:T(8,128)(2,1)S(1)} async-done(((bf16[3,4,128,256]{3,2,0,1:T(8,128)(2,1)}), bf16[3,4,128,256]{3,2,0,1:T(8,128)(2,1)S(1)}, u32[]{:S(2)}, u32[]{:S(2)}) %all-to-all-start) | async-done | bytes 786464 | tf_op jit(solution)/shard_map/all_to_all | solution.py:158
  57.5 1.6 collective-permute-done.4
  59.8 3.9 %collective-permute-start.6 = (bf16[2,1024,128]{2,1,0:T(8,128)(2,1)S(1)}, bf16[2,1024,128]{2,1,0:T(8,128)(2,1)}, u32[]{:S(2)}, u32[]{:S(2)}) collective-permute-start(bf16[2,1024,128]{2,1,0:T(8,128)(2,1)S(1)} %pad_maximum_fusion.7), channel_id=1, source_target_pairs={{0,16},{4,20},{8,24},{12,28},{16,0},{20,4},{24,8},{28,12},{1,17},{... | collective-permute-start | bytes 1572872 | tf_op jit(solution)/shard_map/ppermute | solution.py:171
  64.7 10.3 %collective-permute-done.7 = bf16[2,1024,128]{2,1,0:T(8,128)(2,1)} collective-permute-done((bf16[2,1024,128]{2,1,0:T(8,128)(2,1)S(1)}, bf16[2,1024,128]{2,1,0:T(8,128)(2,1)}, u32[]{:S(2)}, u32[]{:S(2)}) %collective-permute-start.7) | collective-permute-done | bytes 524320 | tf_op jit(solution)/shard_map/ppermute | solution.py:171
  75.0 10.4 %collective-permute-done.6 = bf16[2,1024,128]{2,1,0:T(8,128)(2,1)} collective-permute-done((bf16[2,1024,128]{2,1,0:T(8,128)(2,1)S(1)}, bf16[2,1024,128]{2,1,0:T(8,128)(2,1)}, u32[]{:S(2)}, u32[]{:S(2)}) %collective-permute-start.6) | collective-permute-done | bytes 524320 | tf_op jit(solution)/shard_map/ppermute | solution.py:171
  86.1 1.5 pad_maximum_fusion
  87.8 15.1 %shard_map.166 = bf16[1024,128]{1,0:T(8,128)(2,1)S(1)} custom-call(f32[2]{0:T(128)S(1)} %dynamic-slice_multiply_fusion.scale_ref, bf16[1024,128]{1,0:T(8,128)(2,1)S(1)} %maximum_bitcast_fusion.q_ref, bf16[4096,128]{1,0:T(8,128)(2,1)S(1)} %get-tuple-element.19.k_ref, bf16[4096,128]{1,0:T(8,128)(2,1)S(1)} %get-tuple-element.18.v_ref), custom_call_target="tpu_custom_call" | custom-call | flops 2147483648 | bytes 2621440 | tf_op jit(solution)/shard_map/pallas_call | solution.py:87
  105.2 3.4 %all-to-all-start.1 = ((bf16[4,128,256]{1,2,0:T(8,128)(2,1)}), bf16[4,128,256]{1,2,0:T(8,128)(2,1)S(1)}, u32[]{:S(2)}, u32[]{:S(2)}) async-start(bf16[4,128,256]{1,2,0:T(8,128)(2,1)} %maximum_select_fusion), calls=%async_computation.1 | async-start | bytes 524288 | tf_op jit(solution)/shard_map/all_to_all | solution.py:189
  108.6 9.4 %all-to-all-done.1 = bf16[4,128,256]{1,2,0:T(8,128)(2,1)S(1)} async-done(((bf16[4,128,256]{1,2,0:T(8,128)(2,1)}), bf16[4,128,256]{1,2,0:T(8,128)(2,1)S(1)}, u32[]{:S(2)}, u32[]{:S(2)}) %all-to-all-start.1) | async-done | bytes 262176 | tf_op jit(solution)/shard_map/all_to_all | solution.py:189
  118.1 2.1 %fusion.36 = bf16[128,1024]{1,0:T(8,128)(2,1)S(1)} fusion(f32[128,1024]{1,0:T(8,128)S(1)} %bitcast.232, bf16[128,1024]{0,1:T(8,128)(2,1)S(1)} %bitcast.235, bf16[1024,1024]{1,0:T(8,128)(2,1)} %param.26), kind=kOutput, calls=%fused_computation.53 | convolution fusion | flops 268697600 | bytes 3145728 | tf_op jit(solution)/shard_map/dot_general | solution.py:191
  120.1 3.4 %fusion.58 = bf16[128,4,4,32,4]{0,3,4,2,1:T(8,128)(2,1)S(1)} fusion(bf16[4,32,1024,1,1]{2,1,4,3,0:T(8,128)(2,1)S(1)} %bitcast.245, bf16[1024,4,4,128]{3,2,1,0:T(4,128)(2,1)} %param.28), kind=kOutput, calls=%fused_computation.75 | convolution fusion | flops 539230208 | bytes 4980736 | tf_op jit(solution)/shard_map/pqd,dabh->hpaqb/dot_general | solution.py:195
  124.1 1.3 collective-permute-start.9
  125.4 1.3 collective-permute-start.10
  126.7 4.0 %collective-permute-done.10 = bf16[128,1,128]{2,0,1:T(8,128)(2,1)S(1)} collective-permute-done((bf16[128,1,128]{2,0,1:T(8,128)(2,1)S(1)}, bf16[128,1,128]{2,0,1:T(8,128)(2,1)S(1)}, u32[]{:S(2)}, u32[]{:S(2)}) %collective-permute-start.10) | collective-permute-done | bytes 32800 | tf_op jit(solution)/shard_map/ppermute | solution.py:21
  132.1 1.4 copy.68
  133.5 1.4 copy.71
  134.8 1.5 collective-permute-start.12
  139.0 2.7 %collective-permute-done.11 = bf16[128,18,1]{0,1,2:T(8,128)(2,1)S(1)} collective-permute-done((bf16[128,18,1]{0,1,2:T(8,128)(2,1)S(1)}, bf16[128,18,1]{0,1,2:T(8,128)(2,1)S(1)}, u32[]{:S(2)}, u32[]{:S(2)}) %collective-permute-start.11) | collective-permute-done | bytes 4640 | tf_op jit(solution)/shard_map/ppermute | solution.py:25
  144.0 2.0 %maximum_maximum_fusion = (bf16[128,18,129]{2,0,1:T(8,128)(2,1)S(1)}, bf16[128,18,129]{2,0,1:T(8,128)(2,1)S(1)}) fusion(bf16[128,1,128]{2,0,1:T(8,128)(2,1)S(1)} %collective-permute-done.10, bf16[128,16,128]{2,0,1:T(8,128)(2,1)S(1)} %copy.65, bf16[128,1,128]{2,0,1:T(8,128)(2,1)S(1)} %collective-permute-done.9, bf16[128,18,1]{2,0,1:T(8,128)(2,1)} %copy.69, ...), kind=kLoop, calls=%fused_computation.55 | loop fusion | flops 4755456 | bytes 1787904 | tf_op jit(solution)/shard_map/concatenate | solution.py:27
  150.1 3.6 %collective-permute-done.13 = f32[64]{0:T(128)S(1)} collective-permute-done((f32[64]{0:T(128)S(1)}, f32[64]{0:T(128)S(1)}, u32[]{:S(2)}, u32[]{:S(2)}) %collective-permute-start.13) | collective-permute-done | bytes 288 | tf_op jit(solution)/shard_map/ppermute | solution.py:34
  153.7 4.4 %collective-permute-done.14 = f32[64]{0:T(128)S(1)} collective-permute-done((f32[64]{0:T(128)S(1)}, f32[64]{0:T(128)S(1)}, u32[]{:S(2)}, u32[]{:S(2)}) %collective-permute-start.14) | collective-permute-done | bytes 288 | tf_op jit(solution)/shard_map/ppermute | solution.py:34
  159.2 2.5 %collective-permute-start.16 = (f32[64]{0:T(128)S(1)}, f32[64]{0:T(128)S(1)}, u32[]{:S(2)}, u32[]{:S(2)}) collective-permute-start(f32[64]{0:T(128)S(1)} %add.243), channel_id=1, source_target_pairs={{0,8},{4,12},{8,0},{12,4},{16,24},{20,28},{24,16},{28,20},{1,9},{5... | collective-permute-start | bytes 776 | tf_op jit(solution)/shard_map/ppermute | solution.py:34
  161.8 1.5 collective-permute-done.16
  163.3 2.3 %collective-permute-start.17 = (f32[64]{0:T(128)S(1)}, f32[64]{0:T(128)S(1)}, u32[]{:S(2)}, u32[]{:S(2)}) collective-permute-start(f32[64]{0:T(128)S(1)} %add.244), channel_id=1, source_target_pairs={{0,16},{4,20},{8,24},{12,28},{16,0},{20,4},{24,8},{28,12},{1,17},{... | collective-permute-start | bytes 776 | tf_op jit(solution)/shard_map/ppermute | solution.py:34
  (119 shorter events, 34.8 us)
Async XLA Ops:
  0.6 25.4 %copy-start = (bf16[1024,1024]{1,0:T(8,128)(2,1)S(1)}, bf16[1024,1024]{1,0:T(8,128)(2,1)}, u32[]{:S(2)}) copy-start(bf16[1024,1024]{1,0:T(8,128)(2,1)} %param.25) | copy-start | bytes 6291460
  0.6 15.0 %copy-start.11 = (bf16[9,128,69]{1,2,0:T(8,128)(2,1)S(1)}, bf16[9,128,69]{1,2,0:T(8,128)(2,1)}, u32[]{:S(2)}) copy-start(bf16[9,128,69]{1,2,0:T(8,128)(2,1)} %param.19) | copy-start | bytes 476932
  2.2 3.7 %collective-permute-start = (bf16[69,2,128]{0,2,1:T(8,128)(2,1)S(1)}, bf16[69,2,128]{0,2,1:T(8,128)(2,1)S(1)}, u32[]{:S(2)}, u32[]{:S(2)}) collective-permute-start(bf16[69,2,128]{0,2,1:T(8,128)(2,1)S(1)} %get-tuple-element.35), channel_id=1, source_target_pairs={{0,4},{4,8},{8,12},{12,16},{16,20},{20,24},{24,28},{1,5},{5,9},{9,... | collective-permute-start | bytes 105992 | tf_op jit(solution)/shard_map/ppermute | solution.py:20
  4.5 5.3 %collective-permute-start.1 = (bf16[69,2,128]{0,2,1:T(8,128)(2,1)S(1)}, bf16[69,2,128]{0,2,1:T(8,128)(2,1)S(1)}, u32[]{:S(2)}, u32[]{:S(2)}) collective-permute-start(bf16[69,2,128]{0,2,1:T(8,128)(2,1)S(1)} %get-tuple-element.36), channel_id=1, source_target_pairs={{4,0},{8,4},{12,8},{16,12},{20,16},{24,20},{28,24},{5,1},{9,5},{13... | collective-permute-start | bytes 105992 | tf_op jit(solution)/shard_map/ppermute | solution.py:21
  9.8 5.5 %collective-permute-start.2 = (bf16[69,20,2]{0,2,1:T(2,128)(2,1)S(1)}, bf16[69,20,2]{0,2,1:T(2,128)(2,1)S(1)}, u32[]{:S(2)}, u32[]{:S(2)}) collective-permute-start(bf16[69,20,2]{0,2,1:T(2,128)(2,1)S(1)} %get-tuple-element.25), channel_id=1, source_target_pairs={{0,1},{1,2},{2,3},{3,0},{4,5},{5,6},{6,7},{7,4},{8,9},{9,10},{10,1... | collective-permute-start | bytes 16568 | tf_op jit(solution)/shard_map/ppermute | solution.py:25
  11.5 3.9 %collective-permute-start.3 = (bf16[69,20,2]{0,2,1:T(2,128)(2,1)S(1)}, bf16[69,20,2]{0,2,1:T(2,128)(2,1)S(1)}, u32[]{:S(2)}, u32[]{:S(2)}) collective-permute-start(bf16[69,20,2]{0,2,1:T(2,128)(2,1)S(1)} %get-tuple-element.26), channel_id=1, source_target_pairs={{1,0},{2,1},{3,2},{0,3},{5,4},{6,5},{7,6},{4,7},{9,8},{10,9},{11,1... | collective-permute-start | bytes 16568 | tf_op jit(solution)/shard_map/ppermute | solution.py:26
  19.4 1.2 copy-start.9
  22.8 2.2 %copy-start.1 = (bf16[4,4,128,1024]{3,2,1,0:T(8,128)(2,1)S(1)}, bf16[4,4,128,1024]{3,2,1,0:T(8,128)(2,1)}, u32[]{:S(2)}) copy-start(bf16[4,4,128,1024]{3,2,1,0:T(8,128)(2,1)} %param.21) | copy-start | bytes 12582916
  26.0 1.6 copy-start.4
  27.6 1.6 copy-start.5
  30.7 26.3 %all-to-all-start = ((bf16[3,4,128,256]{3,2,0,1:T(8,128)(2,1)}), bf16[3,4,128,256]{3,2,0,1:T(8,128)(2,1)S(1)}, u32[]{:S(2)}, u32[]{:S(2)}) async-start(bf16[3,4,128,256]{3,2,0,1:T(8,128)(2,1)} %pad_maximum_fusion.2), calls=%async_computation | async-start | bytes 1572864 | tf_op jit(solution)/shard_map/all_to_all | solution.py:158
  57.2 6.5 %copy-start.14 = (f32[16]{0:T(128)S(1)}, f32[16]{0:T(128)}, u32[]{:S(2)}) copy-start(f32[16]{0:T(128)} %param.27) | copy-start | bytes 196
  57.3 1.8 %collective-permute-start.4 = (bf16[3,512,128]{2,1,0:T(8,128)(2,1)S(1)}, bf16[3,512,128]{2,1,0:T(8,128)(2,1)S(1)}, u32[]{:S(2)}, u32[]{:S(2)}) collective-permute-start(bf16[3,512,128]{2,1,0:T(8,128)(2,1)S(1)} %get-tuple-element.21), channel_id=1, source_target_pairs={{0,4},{4,0},{8,12},{12,8},{16,20},{20,16},{24,28},{28,24},{1,5},{5... | collective-permute-start | bytes 1179656 | tf_op jit(solution)/shard_map/ppermute | solution.py:168
  59.1 15.9 %collective-permute-start.7 = (bf16[2,1024,128]{2,1,0:T(8,128)(2,1)S(1)}, bf16[2,1024,128]{2,1,0:T(8,128)(2,1)}, u32[]{:S(2)}, u32[]{:S(2)}) collective-permute-start(bf16[2,1024,128]{2,1,0:T(8,128)(2,1)S(1)} %pad_maximum_fusion.7), channel_id=1, source_target_pairs={{0,24},{4,28},{8,16},{12,20},{16,8},{20,12},{24,0},{28,4},{1,25},{... | collective-permute-start | bytes 1572872 | tf_op jit(solution)/shard_map/ppermute | solution.py:171
  59.8 25.6 %collective-permute-start.6 = (bf16[2,1024,128]{2,1,0:T(8,128)(2,1)S(1)}, bf16[2,1024,128]{2,1,0:T(8,128)(2,1)}, u32[]{:S(2)}, u32[]{:S(2)}) collective-permute-start(bf16[2,1024,128]{2,1,0:T(8,128)(2,1)S(1)} %pad_maximum_fusion.7), channel_id=1, source_target_pairs={{0,16},{4,20},{8,24},{12,28},{16,0},{20,4},{24,8},{28,12},{1,17},{... | collective-permute-start | bytes 1572872 | tf_op jit(solution)/shard_map/ppermute | solution.py:171
  63.7 22.4 %collective-permute-start.5 = (bf16[2,1024,128]{2,1,0:T(8,128)(2,1)S(1)}, bf16[2,1024,128]{2,1,0:T(8,128)(2,1)}, u32[]{:S(2)}, u32[]{:S(2)}) collective-permute-start(bf16[2,1024,128]{2,1,0:T(8,128)(2,1)S(1)} %pad_maximum_fusion.7), channel_id=1, source_target_pairs={{0,8},{4,12},{8,0},{12,4},{16,24},{20,28},{24,16},{28,20},{1,9},{5... | collective-permute-start | bytes 1572872 | tf_op jit(solution)/shard_map/ppermute | solution.py:171
  102.9 1.4 collective-permute-start.8
  105.2 12.8 %all-to-all-start.1 = ((bf16[4,128,256]{1,2,0:T(8,128)(2,1)}), bf16[4,128,256]{1,2,0:T(8,128)(2,1)S(1)}, u32[]{:S(2)}, u32[]{:S(2)}) async-start(bf16[4,128,256]{1,2,0:T(8,128)(2,1)} %maximum_select_fusion), calls=%async_computation.1 | async-start | bytes 524288 | tf_op jit(solution)/shard_map/all_to_all | solution.py:189
  124.1 2.6 %collective-permute-start.9 = (bf16[128,1,128]{2,0,1:T(8,128)(2,1)S(1)}, bf16[128,1,128]{2,0,1:T(8,128)(2,1)S(1)}, u32[]{:S(2)}, u32[]{:S(2)}) collective-permute-start(bf16[128,1,128]{2,0,1:T(8,128)(2,1)S(1)} %get-tuple-element.33), channel_id=1, source_target_pairs={{0,4},{4,8},{8,12},{12,16},{16,20},{20,24},{24,28},{1,5},{5,9},{9,... | collective-permute-start | bytes 98312 | tf_op jit(solution)/shard_map/ppermute | solution.py:20
  125.4 5.4 %collective-permute-start.10 = (bf16[128,1,128]{2,0,1:T(8,128)(2,1)S(1)}, bf16[128,1,128]{2,0,1:T(8,128)(2,1)S(1)}, u32[]{:S(2)}, u32[]{:S(2)}) collective-permute-start(bf16[128,1,128]{2,0,1:T(8,128)(2,1)S(1)} %get-tuple-element.34), channel_id=1, source_target_pairs={{4,0},{8,4},{12,8},{16,12},{20,16},{24,20},{28,24},{5,1},{9,5},{13... | collective-permute-start | bytes 98312 | tf_op jit(solution)/shard_map/ppermute | solution.py:21
  130.9 6.0 %copy-start.10 = (bf16[9,69,128]{2,1,0:T(8,128)(2,1)S(1)}, bf16[9,69,128]{2,1,0:T(8,128)(2,1)}, u32[]{:S(2)}) copy-start(bf16[9,69,128]{2,1,0:T(8,128)(2,1)} %param.29) | copy-start | bytes 476932
  134.8 8.0 %collective-permute-start.12 = (bf16[128,18,1]{0,1,2:T(8,128)(2,1)S(1)}, bf16[128,18,1]{0,1,2:T(8,128)(2,1)S(1)}, u32[]{:S(2)}, u32[]{:S(2)}) collective-permute-start(bf16[128,18,1]{0,1,2:T(8,128)(2,1)S(1)} %copy.71), channel_id=1, source_target_pairs={{1,0},{2,1},{3,2},{0,3},{5,4},{6,5},{7,6},{4,7},{9,8},{10,9},{11,1... | collective-permute-start | bytes 13832 | tf_op jit(solution)/shard_map/ppermute | solution.py:26
  136.3 5.4 %collective-permute-start.11 = (bf16[128,18,1]{0,1,2:T(8,128)(2,1)S(1)}, bf16[128,18,1]{0,1,2:T(8,128)(2,1)S(1)}, u32[]{:S(2)}, u32[]{:S(2)}) collective-permute-start(bf16[128,18,1]{0,1,2:T(8,128)(2,1)S(1)} %copy.68), channel_id=1, source_target_pairs={{0,1},{1,2},{2,3},{3,0},{4,5},{5,6},{6,7},{7,4},{8,9},{9,10},{10,1... | collective-permute-start | bytes 13832 | tf_op jit(solution)/shard_map/ppermute | solution.py:25
  145.9 1.1 copy-start.3
  147.9 1.1 copy-start.7
  147.9 1.2 copy-start.8
  149.1 18.0 %copy-start.15 = (s32[64]{0:T(128)S(1)}, s32[64]{0:T(128)}, u32[]{:S(2)}) copy-start(s32[64]{0:T(128)} %param.18) | copy-start | bytes 772
  150.1 3.6 %collective-permute-start.13 = (f32[64]{0:T(128)S(1)}, f32[64]{0:T(128)S(1)}, u32[]{:S(2)}, u32[]{:S(2)}) collective-permute-start(f32[64]{0:T(128)S(1)} %fusion.40), channel_id=1, source_target_pairs={{0,1},{1,0},{2,3},{3,2},{4,5},{5,4},{6,7},{7,6},{8,9},{9,8},{10,11... | collective-permute-start | bytes 776 | tf_op jit(solution)/shard_map/ppermute | solution.py:34
  153.7 4.4 %collective-permute-start.14 = (f32[64]{0:T(128)S(1)}, f32[64]{0:T(128)S(1)}, u32[]{:S(2)}, u32[]{:S(2)}) collective-permute-start(f32[64]{0:T(128)S(1)} %add.241), channel_id=1, source_target_pairs={{0,2},{1,3},{2,0},{3,1},{4,6},{5,7},{6,4},{7,5},{8,10},{9,11},{10,... | collective-permute-start | bytes 776 | tf_op jit(solution)/shard_map/ppermute | solution.py:34
  158.1 1.1 collective-permute-start.15
  159.2 4.0 %collective-permute-start.16 = (f32[64]{0:T(128)S(1)}, f32[64]{0:T(128)S(1)}, u32[]{:S(2)}, u32[]{:S(2)}) collective-permute-start(f32[64]{0:T(128)S(1)} %add.243), channel_id=1, source_target_pairs={{0,8},{4,12},{8,0},{12,4},{16,24},{20,28},{24,16},{28,20},{1,9},{5... | collective-permute-start | bytes 776 | tf_op jit(solution)/shard_map/ppermute | solution.py:34
  163.3 3.8 %collective-permute-start.17 = (f32[64]{0:T(128)S(1)}, f32[64]{0:T(128)S(1)}, u32[]{:S(2)}, u32[]{:S(2)}) collective-permute-start(f32[64]{0:T(128)S(1)} %add.244), channel_id=1, source_target_pairs={{0,16},{4,20},{8,24},{12,28},{16,0},{20,4},{24,8},{28,12},{1,17},{... | collective-permute-start | bytes 776 | tf_op jit(solution)/shard_map/ppermute | solution.py:34
  (5 other events, 4.1 us)

commit v4 on v3

--- a/solution.py
+++ b/solution.py
@@ -152,31 +152,35 @@
             for weight in (query_weight, key_weight, value_weight)
         )
     )
-    projected = jnp.stack(
-        [p.reshape(-1, lon_size, group_width).transpose(1, 0, 2) for p in projections]
-    )
-    spread = lax.all_to_all(projected, "lon", split_axis=1, concat_axis=2, tiled=True)
-    query_spread, key_spread, value_spread = (spread[i, 0] for i in range(3))
+    by_group = [p.reshape(-1, lon_size, group_width).transpose(1, 0, 2) for p in projections]
+    key_value_spread = lax.all_to_all(
+        jnp.stack(by_group[1:]), "lon", split_axis=1, concat_axis=2, tiled=True
+    )
+    query_spread = lax.all_to_all(by_group[0], "lon", split_axis=0, concat_axis=1, tiled=True)[0]
+    key_spread, value_spread = key_value_spread[0, 0], key_value_spread[1, 0]
     lat_size = lax.axis_size("lat")
     core = lax.axis_index("lat") % 2
     half = group_width // 2
-    stacked = jnp.stack([query_spread, key_spread, value_spread])
-    low, high = stacked[..., :half], stacked[..., half:]
-    mine = jnp.where(core == 0, low, high)
-    theirs = jnp.where(core == 0, high, low)
     partner = [(i, i ^ 1) for i in range(lat_size)]
-    pair_tokens = jnp.concatenate([mine, lax.ppermute(theirs, "lat", partner)], axis=1)
-    key_value = pair_tokens[1:]
+
+    def with_partner(spread):
+        low, high = spread[..., :half], spread[..., half:]
+        mine = jnp.where(core == 0, low, high)
+        theirs = jnp.where(core == 0, high, low)
+        return jnp.concatenate([mine, lax.ppermute(theirs, "lat", partner)], axis=-2)
+
+    key_value = with_partner(jnp.stack([key_spread, value_spread]))
     chunks = [key_value] + [
         lax.ppermute(key_value, "lat", [(i, i ^ (2 * d)) for i in range(lat_size)])
         for d in range(1, lat_size // 2)
     ]
     all_key_value = jnp.concatenate(chunks, axis=1)
+    pair_queries = with_partner(query_spread)
     local_heads = half // head_size
     head_first = (lax.axis_index("lon") * 2 + core) * local_heads
     scales = lax.dynamic_slice_in_dim(head_scale, head_first, local_heads) / math.sqrt(head_size)
     pair_attended = attend(
-        pair_tokens[0], all_key_value[0], all_key_value[1], scales, head_size
+        pair_queries, all_key_value[0], all_key_value[1], scales, head_size
     )
     token_count = query_spread.shape[0]
     own_part = pair_attended[:token_count]

time: 169 us -> 170 us (level)
  waiting for transfers between devices: 78.6 us -> 70 us
  local copies, waits for them, and re-layouts: 15.2 us -> 22.2 us
  starting transfers between devices: 29.8 us -> 33.8 us
    ppermute x3, waiting for transfers between devices: 21.4 us -> 15.9 us  [on_device(): lax.ppermute(key_value, 'lat', [(i, i ^ 2 * d) for i in range(lat_size)])]
    unnamed x36 -> x37, local copies, waits for them, and re-layouts: 7.8 us -> 11.8 us
    all_to_all x1 -> x2, starting transfers between devices: 5.13 us -> 8.72 us  [the longest x1 5.13 us: on_device(): lax.all_to_all(jnp.stack(by_group[1:]), 'lon', split_axis=1, concat_axis=...]
    all_to_all x1 -> x2, waiting for transfers between devices: 21.2 us -> 17.8 us  [the longest x1 14.9 us: on_device(): lax.all_to_all(jnp.stack(by_group[1:]), 'lon', split_axis=1, concat_axis=...]
  transfers between devices with their start and end apart: 20 -> 22, of which waited for: 16 -> 17; matrix products, arithmetic and copies ran while one was open for 3% -> 7% of each run, Pallas kernels for 0% -> 0%
where the time goes in v4:
time: 170 us; the launch traced here: 169 us
  waiting for transfers between devices  70 us (41%)
  starting transfers between devices  33.8 us (20%)
  local copies, waits for them, and re-layouts  22.2 us (13%)
  matrix products  20.9 us (12%)
  Pallas kernels  15.1 us (9%)
  other arithmetic  6.03 us (4%)
    ppermute x3, waiting for transfers between devices, on_device(): lax.ppermute(key_value, 'lat', [(i, i ^ 2 * d) for i in range(lat_size)])  15.9 us
    pallas_call x1, Pallas kernels, attend(): pl.pallas_call(functools.partial(attention_kernel, head_size=head_size),...  15.1 us
    all_to_all x1, waiting for transfers between devices, on_device(): lax.all_to_all(jnp.stack(by_group[1:]), 'lon', split_axis=1, concat_axis=...  14.9 us
    dot_general x27, matrix products, convolution_kernel_taps(): jnp.einsum('oc,cyx->oyx', weight[tap_index], window, preferred_element_ty...  12.4 us
    unnamed x37, local copies, waits for them, and re-layouts  11.8 us
    ppermute x5, waiting for transfers between devices, butterfly_sum(): value = value + lax.ppermute(value, axis, partner)  11.4 us
    all_to_all x1, waiting for transfers between devices, on_device(): lax.all_to_all(attended_heads, 'lon', split_axis=0, concat_axis=1, tiled=...  9.23 us
    ppermute x2, waiting for transfers between devices, halo_padded(): from_below = lax.ppermute(array[:, :width], 'lat', up)  7.62 us
  transfers between devices with their start and end apart: 22, of which 17 were waited for; matrix products, arithmetic and copies ran while one was open for 7% of the time, Pallas kernels for 0%

profile of v4, /device:TPU:0, one launch (start us, length us, event | category | flops | bytes accessed | tf_op | source)
XLA Modules:
  0.0 169.2 jit_solution(1324207980267689257)
XLA Ops:
  0.7 1.5 copy.52
  2.2 2.4 %collective-permute-start = (bf16[69,2,128]{0,2,1:T(8,128)(2,1)S(1)}, bf16[69,2,128]{0,2,1:T(8,128)(2,1)S(1)}, u32[]{:S(2)}, u32[]{:S(2)}) collective-permute-start(bf16[69,2,128]{0,2,1:T(8,128)(2,1)S(1)} %get-tuple-element.35), channel_id=1, source_target_pairs={{0,4},{4,8},{8,12},{12,16},{16,20},{20,24},{24,28},{1,5},{5,9},{9,... | collective-permute-start | bytes 105992 | tf_op jit(solution)/shard_map/ppermute | solution.py:20
  5.9 3.9 %collective-permute-done.1 = bf16[69,2,128]{0,2,1:T(8,128)(2,1)S(1)} collective-permute-done((bf16[69,2,128]{0,2,1:T(8,128)(2,1)S(1)}, bf16[69,2,128]{0,2,1:T(8,128)(2,1)S(1)}, u32[]{:S(2)}, u32[]{:S(2)}) %collective-permute-start.1) | collective-permute-done | bytes 35360 | tf_op jit(solution)/shard_map/ppermute | solution.py:21
  9.8 1.6 collective-permute-start.2
  11.5 2.2 %collective-permute-start.3 = (bf16[69,20,2]{0,2,1:T(2,128)(2,1)S(1)}, bf16[69,20,2]{0,2,1:T(2,128)(2,1)S(1)}, u32[]{:S(2)}, u32[]{:S(2)}) collective-permute-start(bf16[69,20,2]{0,2,1:T(2,128)(2,1)S(1)} %get-tuple-element.23), channel_id=1, source_target_pairs={{1,0},{2,1},{3,2},{0,3},{5,4},{6,5},{7,6},{4,7},{9,8},{10,9},{11,1... | collective-permute-start | bytes 16568 | tf_op jit(solution)/shard_map/ppermute | solution.py:26
  13.7 1.6 collective-permute-done.2
  30.5 5.1 %all-to-all-start.1 = ((bf16[2,4,128,256]{3,2,0,1:T(8,128)(2,1)}), bf16[2,4,128,256]{3,2,0,1:T(8,128)(2,1)S(1)}, u32[]{:S(2)}, u32[]{:S(2)}) async-start(bf16[2,4,128,256]{3,2,0,1:T(8,128)(2,1)} %pad_maximum_fusion.4), calls=%async_computation.1 | async-start | bytes 1048576 | tf_op jit(solution)/shard_map/all_to_all | solution.py:156
  36.4 14.9 %all-to-all-done.1 = bf16[2,4,128,256]{3,2,0,1:T(8,128)(2,1)S(1)} async-done(((bf16[2,4,128,256]{3,2,0,1:T(8,128)(2,1)}), bf16[2,4,128,256]{3,2,0,1:T(8,128)(2,1)S(1)}, u32[]{:S(2)}, u32[]{:S(2)}) %all-to-all-start.1) | async-done | bytes 524320 | tf_op jit(solution)/shard_map/all_to_all | solution.py:156
  51.3 3.6 %all-to-all-start = ((bf16[4,128,256]{2,1,0:T(8,128)(2,1)}), bf16[4,128,256]{2,1,0:T(8,128)(2,1)S(1)}, u32[]{:S(2)}, u32[]{:S(2)}) async-start(bf16[4,128,256]{2,1,0:T(8,128)(2,1)} %bitcast.234), calls=%async_computation | async-start | bytes 524288 | tf_op jit(solution)/shard_map/all_to_all | solution.py:159
  55.9 1.4 collective-permute-done.5
  58.1 2.2 %collective-permute-start.7 = (bf16[2,1024,128]{2,1,0:T(8,128)(2,1)}, bf16[2,1024,128]{2,1,0:T(8,128)(2,1)}, u32[]{:S(2)}, u32[]{:S(2)}) collective-permute-start(bf16[2,1024,128]{2,1,0:T(8,128)(2,1)} %pad_maximum_fusion.5), channel_id=1, source_target_pairs={{0,16},{4,20},{8,24},{12,28},{16,0},{20,4},{24,8},{28,12},{1,17},{... | collective-permute-start | bytes 1572872 | tf_op jit(solution)/shard_map/ppermute | solution.py:174
  61.2 2.9 %all-to-all-done = bf16[4,128,256]{2,1,0:T(8,128)(2,1)S(1)} async-done(((bf16[4,128,256]{2,1,0:T(8,128)(2,1)}), bf16[4,128,256]{2,1,0:T(8,128)(2,1)S(1)}, u32[]{:S(2)}, u32[]{:S(2)}) %all-to-all-start) | async-done | bytes 262176 | tf_op jit(solution)/shard_map/all_to_all | solution.py:159
  66.3 9.1 %collective-permute-done.6 = bf16[2,1024,128]{2,1,0:T(8,128)(2,1)} collective-permute-done((bf16[2,1024,128]{2,1,0:T(8,128)(2,1)}, bf16[2,1024,128]{2,1,0:T(8,128)(2,1)}, u32[]{:S(2)}, u32[]{:S(2)}) %collective-permute-start.6) | collective-permute-done | bytes 524320 | tf_op jit(solution)/shard_map/ppermute | solution.py:174
  75.4 1.9 %constant_dynamic-update-slice_fusion.2 = bf16[2,4096,128]{2,1,0:T(8,128)(2,1)} fusion(bf16[2,4096,128]{2,1,0:T(8,128)(2,1)} %constant_dynamic-update-slice_fusion.3, bf16[2,1024,128]{2,1,0:T(8,128)(2,1)} %collective-permute-done.6), kind=kLoop, calls=%fused_computation.196 | loop fusion | bytes 1048576
  77.4 2.0 %constant_dynamic-update-slice_fusion.1 = bf16[2,4096,128]{2,1,0:T(8,128)(2,1)} fusion(bf16[2,4096,128]{2,1,0:T(8,128)(2,1)} %constant_dynamic-update-slice_fusion.2, bf16[2,1024,128]{2,1,0:T(8,128)(2,1)} %collective-permute-done.7), kind=kLoop, calls=%fused_computation.195 | loop fusion | bytes 1048576
  79.3 6.7 %collective-permute-done.8 = bf16[2,1024,128]{2,1,0:T(8,128)(2,1)S(1)} collective-permute-done((bf16[2,1024,128]{2,1,0:T(8,128)(2,1)}, bf16[2,1024,128]{2,1,0:T(8,128)(2,1)S(1)}, u32[]{:S(2)}, u32[]{:S(2)}) %collective-permute-start.8) | collective-permute-done | bytes 524320 | tf_op jit(solution)/shard_map/ppermute | solution.py:174
  86.9 1.7 slice_bitcast_fusion
  88.6 15.1 %shard_map.166 = bf16[1024,128]{1,0:T(8,128)(2,1)S(1)} custom-call(f32[2]{0:T(128)S(1)} %dynamic-slice_multiply_fusion.scale_ref, bf16[1024,128]{1,0:T(8,128)(2,1)S(1)} %pad_maximum_fusion.7.q_ref, bf16[4096,128]{1,0:T(8,128)(2,1)S(1)} %get-tuple-element.21.k_ref, bf16[4096,128]{1,0:T(8,128)(2,1)S(1)} %get-tuple-element.20.v_ref), custom_call_target="tpu_custom_call" | custom-call | flops 2147483648 | bytes 2621440 | tf_op jit(solution)/shard_map/pallas_call | solution.py:87
  106.0 4.9 %all-to-all-start.2 = ((bf16[4,128,256]{1,2,0:T(8,128)(2,1)}), bf16[4,128,256]{1,2,0:T(8,128)(2,1)S(1)}, u32[]{:S(2)}, u32[]{:S(2)}) async-start(bf16[4,128,256]{1,2,0:T(8,128)(2,1)} %maximum_select_fusion), calls=%async_computation.2 | async-start | bytes 524288 | tf_op jit(solution)/shard_map/all_to_all | solution.py:193
  110.9 9.2 %all-to-all-done.2 = bf16[4,128,256]{1,2,0:T(8,128)(2,1)S(1)} async-done(((bf16[4,128,256]{1,2,0:T(8,128)(2,1)}), bf16[4,128,256]{1,2,0:T(8,128)(2,1)S(1)}, u32[]{:S(2)}, u32[]{:S(2)}) %all-to-all-start.2) | async-done | bytes 262176 | tf_op jit(solution)/shard_map/all_to_all | solution.py:193
  120.1 2.1 %fusion.36 = bf16[128,1024]{1,0:T(8,128)(2,1)S(1)} fusion(f32[128,1024]{1,0:T(8,128)S(1)} %bitcast.228, bf16[128,1024]{0,1:T(8,128)(2,1)S(1)} %bitcast.232, bf16[1024,1024]{1,0:T(8,128)(2,1)} %param.26), kind=kOutput, calls=%fused_computation.52 | convolution fusion | flops 268697600 | bytes 3145728 | tf_op jit(solution)/shard_map/dot_general | solution.py:195
  122.2 3.4 %fusion.58 = bf16[128,4,4,32,4]{0,3,4,2,1:T(8,128)(2,1)S(1)} fusion(bf16[4,32,1024,1,1]{2,1,4,3,0:T(8,128)(2,1)S(1)} %bitcast.241, bf16[1024,4,4,128]{3,2,1,0:T(4,128)(2,1)} %param.28), kind=kOutput, calls=%fused_computation.74 | convolution fusion | flops 539230208 | bytes 4980736 | tf_op jit(solution)/shard_map/pqd,dabh->hpaqb/dot_general | solution.py:199
  128.8 3.7 %collective-permute-done.11 = bf16[128,1,128]{2,0,1:T(8,128)(2,1)S(1)} collective-permute-done((bf16[128,1,128]{2,0,1:T(8,128)(2,1)S(1)}, bf16[128,1,128]{2,0,1:T(8,128)(2,1)S(1)}, u32[]{:S(2)}, u32[]{:S(2)}) %collective-permute-start.11) | collective-permute-done | bytes 32800 | tf_op jit(solution)/shard_map/ppermute | solution.py:21
  135.2 1.4 copy.71
  136.6 1.4 collective-permute-start.13
  140.7 2.7 %collective-permute-done.12 = bf16[128,18,1]{0,1,2:T(8,128)(2,1)S(1)} collective-permute-done((bf16[128,18,1]{0,1,2:T(8,128)(2,1)S(1)}, bf16[128,18,1]{0,1,2:T(8,128)(2,1)S(1)}, u32[]{:S(2)}, u32[]{:S(2)}) %collective-permute-start.12) | collective-permute-done | bytes 4640 | tf_op jit(solution)/shard_map/ppermute | solution.py:25
  145.6 2.0 %maximum_maximum_fusion = (bf16[128,18,129]{2,0,1:T(8,128)(2,1)S(1)}, bf16[128,18,129]{2,0,1:T(8,128)(2,1)S(1)}) fusion(bf16[128,1,128]{2,0,1:T(8,128)(2,1)S(1)} %collective-permute-done.11, bf16[128,16,128]{2,0,1:T(8,128)(2,1)S(1)} %copy.65, bf16[128,1,128]{2,0,1:T(8,128)(2,1)S(1)} %collective-permute-done.10, bf16[128,18,1]{2,0,1:T(8,128)(2,1)} %copy.69, ...), kind=kLoop, calls=%fused_computation.54 | loop fusion | flops 4755456 | bytes 1787904 | tf_op jit(solution)/shard_map/concatenate | solution.py:27
  151.8 3.6 %collective-permute-done.14 = f32[64]{0:T(128)S(1)} collective-permute-done((f32[64]{0:T(128)S(1)}, f32[64]{0:T(128)S(1)}, u32[]{:S(2)}, u32[]{:S(2)}) %collective-permute-start.14) | collective-permute-done | bytes 288 | tf_op jit(solution)/shard_map/ppermute | solution.py:34
  155.4 4.4 %collective-permute-done.15 = f32[64]{0:T(128)S(1)} collective-permute-done((f32[64]{0:T(128)S(1)}, f32[64]{0:T(128)S(1)}, u32[]{:S(2)}, u32[]{:S(2)}) %collective-permute-start.15) | collective-permute-done | bytes 288 | tf_op jit(solution)/shard_map/ppermute | solution.py:34
  160.9 2.5 %collective-permute-start.17 = (f32[64]{0:T(128)S(1)}, f32[64]{0:T(128)S(1)}, u32[]{:S(2)}, u32[]{:S(2)}) collective-permute-start(f32[64]{0:T(128)S(1)} %add.243), channel_id=1, source_target_pairs={{0,8},{4,12},{8,0},{12,4},{16,24},{20,28},{24,16},{28,20},{1,9},{5... | collective-permute-start | bytes 776 | tf_op jit(solution)/shard_map/ppermute | solution.py:34
  163.4 1.5 collective-permute-done.17
  165.0 2.1 %collective-permute-start.18 = (f32[64]{0:T(128)S(1)}, f32[64]{0:T(128)S(1)}, u32[]{:S(2)}, u32[]{:S(2)}) collective-permute-start(f32[64]{0:T(128)S(1)} %add.244), channel_id=1, source_target_pairs={{0,16},{4,20},{8,24},{12,28},{16,0},{20,4},{24,8},{28,12},{1,17},{... | collective-permute-start | bytes 776 | tf_op jit(solution)/shard_map/ppermute | solution.py:34
  (124 shorter events, 43.3 us)
Async XLA Ops:
  0.6 25.4 %copy-start = (bf16[1024,1024]{1,0:T(8,128)(2,1)S(1)}, bf16[1024,1024]{1,0:T(8,128)(2,1)}, u32[]{:S(2)}) copy-start(bf16[1024,1024]{1,0:T(8,128)(2,1)} %param.25) | copy-start | bytes 6291460
  0.6 15.0 %copy-start.10 = (bf16[9,128,69]{1,2,0:T(8,128)(2,1)S(1)}, bf16[9,128,69]{1,2,0:T(8,128)(2,1)}, u32[]{:S(2)}) copy-start(bf16[9,128,69]{1,2,0:T(8,128)(2,1)} %param.19) | copy-start | bytes 476932
  2.2 3.7 %collective-permute-start = (bf16[69,2,128]{0,2,1:T(8,128)(2,1)S(1)}, bf16[69,2,128]{0,2,1:T(8,128)(2,1)S(1)}, u32[]{:S(2)}, u32[]{:S(2)}) collective-permute-start(bf16[69,2,128]{0,2,1:T(8,128)(2,1)S(1)} %get-tuple-element.35), channel_id=1, source_target_pairs={{0,4},{4,8},{8,12},{12,16},{16,20},{20,24},{24,28},{1,5},{5,9},{9,... | collective-permute-start | bytes 105992 | tf_op jit(solution)/shard_map/ppermute | solution.py:20
  4.5 5.3 %collective-permute-start.1 = (bf16[69,2,128]{0,2,1:T(8,128)(2,1)S(1)}, bf16[69,2,128]{0,2,1:T(8,128)(2,1)S(1)}, u32[]{:S(2)}, u32[]{:S(2)}) collective-permute-start(bf16[69,2,128]{0,2,1:T(8,128)(2,1)S(1)} %get-tuple-element.36), channel_id=1, source_target_pairs={{4,0},{8,4},{12,8},{16,12},{20,16},{24,20},{28,24},{5,1},{9,5},{13... | collective-permute-start | bytes 105992 | tf_op jit(solution)/shard_map/ppermute | solution.py:21
  9.8 5.5 %collective-permute-start.2 = (bf16[69,20,2]{0,2,1:T(2,128)(2,1)S(1)}, bf16[69,20,2]{0,2,1:T(2,128)(2,1)S(1)}, u32[]{:S(2)}, u32[]{:S(2)}) collective-permute-start(bf16[69,20,2]{0,2,1:T(2,128)(2,1)S(1)} %get-tuple-element.22), channel_id=1, source_target_pairs={{0,1},{1,2},{2,3},{3,0},{4,5},{5,6},{6,7},{7,4},{8,9},{9,10},{10,1... | collective-permute-start | bytes 16568 | tf_op jit(solution)/shard_map/ppermute | solution.py:25
  11.5 3.9 %collective-permute-start.3 = (bf16[69,20,2]{0,2,1:T(2,128)(2,1)S(1)}, bf16[69,20,2]{0,2,1:T(2,128)(2,1)S(1)}, u32[]{:S(2)}, u32[]{:S(2)}) collective-permute-start(bf16[69,20,2]{0,2,1:T(2,128)(2,1)S(1)} %get-tuple-element.23), channel_id=1, source_target_pairs={{1,0},{2,1},{3,2},{0,3},{5,4},{6,5},{7,6},{4,7},{9,8},{10,9},{11,1... | collective-permute-start | bytes 16568 | tf_op jit(solution)/shard_map/ppermute | solution.py:26
  19.4 1.2 copy-start.8
  22.8 2.2 %copy-start.1 = (bf16[4,4,128,1024]{3,2,1,0:T(8,128)(2,1)S(1)}, bf16[4,4,128,1024]{3,2,1,0:T(8,128)(2,1)}, u32[]{:S(2)}) copy-start(bf16[4,4,128,1024]{3,2,1,0:T(8,128)(2,1)} %param.21) | copy-start | bytes 12582916
  26.0 1.6 copy-start.4
  27.6 1.6 copy-start.5
  30.5 20.7 %all-to-all-start.1 = ((bf16[2,4,128,256]{3,2,0,1:T(8,128)(2,1)}), bf16[2,4,128,256]{3,2,0,1:T(8,128)(2,1)S(1)}, u32[]{:S(2)}, u32[]{:S(2)}) async-start(bf16[2,4,128,256]{3,2,0,1:T(8,128)(2,1)} %pad_maximum_fusion.4), calls=%async_computation.1 | async-start | bytes 1048576 | tf_op jit(solution)/shard_map/all_to_all | solution.py:156
  51.3 12.9 %all-to-all-start = ((bf16[4,128,256]{2,1,0:T(8,128)(2,1)}), bf16[4,128,256]{2,1,0:T(8,128)(2,1)S(1)}, u32[]{:S(2)}, u32[]{:S(2)}) async-start(bf16[4,128,256]{2,1,0:T(8,128)(2,1)} %bitcast.234), calls=%async_computation | async-start | bytes 524288 | tf_op jit(solution)/shard_map/all_to_all | solution.py:159
  54.9 9.4 %copy-start.13 = (f32[16]{0:T(128)S(1)}, f32[16]{0:T(128)}, u32[]{:S(2)}) copy-start(f32[16]{0:T(128)} %param.27) | copy-start | bytes 196
  55.8 1.5 collective-permute-start.5
  58.1 19.3 %collective-permute-start.7 = (bf16[2,1024,128]{2,1,0:T(8,128)(2,1)}, bf16[2,1024,128]{2,1,0:T(8,128)(2,1)}, u32[]{:S(2)}, u32[]{:S(2)}) collective-permute-start(bf16[2,1024,128]{2,1,0:T(8,128)(2,1)} %pad_maximum_fusion.5), channel_id=1, source_target_pairs={{0,16},{4,20},{8,24},{12,28},{16,0},{20,4},{24,8},{28,12},{1,17},{... | collective-permute-start | bytes 1572872 | tf_op jit(solution)/shard_map/ppermute | solution.py:174
  60.3 15.1 %collective-permute-start.6 = (bf16[2,1024,128]{2,1,0:T(8,128)(2,1)}, bf16[2,1024,128]{2,1,0:T(8,128)(2,1)}, u32[]{:S(2)}, u32[]{:S(2)}) collective-permute-start(bf16[2,1024,128]{2,1,0:T(8,128)(2,1)} %pad_maximum_fusion.5), channel_id=1, source_target_pairs={{0,8},{4,12},{8,0},{12,4},{16,24},{20,28},{24,16},{28,20},{1,9},{5... | collective-permute-start | bytes 1572872 | tf_op jit(solution)/shard_map/ppermute | solution.py:174
  64.1 1.4 collective-permute-start.4
  64.2 21.8 %collective-permute-start.8 = (bf16[2,1024,128]{2,1,0:T(8,128)(2,1)}, bf16[2,1024,128]{2,1,0:T(8,128)(2,1)S(1)}, u32[]{:S(2)}, u32[]{:S(2)}) collective-permute-start(bf16[2,1024,128]{2,1,0:T(8,128)(2,1)} %pad_maximum_fusion.5), channel_id=1, source_target_pairs={{0,24},{4,28},{8,16},{12,20},{16,8},{20,12},{24,0},{28,4},{1,25},{... | collective-permute-start | bytes 1572872 | tf_op jit(solution)/shard_map/ppermute | solution.py:174
  103.7 1.4 collective-permute-start.9
  106.0 14.1 %all-to-all-start.2 = ((bf16[4,128,256]{1,2,0:T(8,128)(2,1)}), bf16[4,128,256]{1,2,0:T(8,128)(2,1)S(1)}, u32[]{:S(2)}, u32[]{:S(2)}) async-start(bf16[4,128,256]{1,2,0:T(8,128)(2,1)} %maximum_select_fusion), calls=%async_computation.2 | async-start | bytes 524288 | tf_op jit(solution)/shard_map/all_to_all | solution.py:193
  126.2 2.6 %collective-permute-start.10 = (bf16[128,1,128]{2,0,1:T(8,128)(2,1)S(1)}, bf16[128,1,128]{2,0,1:T(8,128)(2,1)S(1)}, u32[]{:S(2)}, u32[]{:S(2)}) collective-permute-start(bf16[128,1,128]{2,0,1:T(8,128)(2,1)S(1)} %get-tuple-element.30), channel_id=1, source_target_pairs={{0,4},{4,8},{8,12},{12,16},{16,20},{20,24},{24,28},{1,5},{5,9},{9,... | collective-permute-start | bytes 98312 | tf_op jit(solution)/shard_map/ppermute | solution.py:20
  127.5 5.0 %collective-permute-start.11 = (bf16[128,1,128]{2,0,1:T(8,128)(2,1)S(1)}, bf16[128,1,128]{2,0,1:T(8,128)(2,1)S(1)}, u32[]{:S(2)}, u32[]{:S(2)}) collective-permute-start(bf16[128,1,128]{2,0,1:T(8,128)(2,1)S(1)} %get-tuple-element.31), channel_id=1, source_target_pairs={{4,0},{8,4},{12,8},{16,12},{20,16},{24,20},{28,24},{5,1},{9,5},{13... | collective-permute-start | bytes 98312 | tf_op jit(solution)/shard_map/ppermute | solution.py:21
  132.6 6.0 %copy-start.9 = (bf16[9,69,128]{2,1,0:T(8,128)(2,1)S(1)}, bf16[9,69,128]{2,1,0:T(8,128)(2,1)}, u32[]{:S(2)}) copy-start(bf16[9,69,128]{2,1,0:T(8,128)(2,1)} %param.29) | copy-start | bytes 476932
  136.6 8.0 %collective-permute-start.13 = (bf16[128,18,1]{0,1,2:T(8,128)(2,1)S(1)}, bf16[128,18,1]{0,1,2:T(8,128)(2,1)S(1)}, u32[]{:S(2)}, u32[]{:S(2)}) collective-permute-start(bf16[128,18,1]{0,1,2:T(8,128)(2,1)S(1)} %copy.71), channel_id=1, source_target_pairs={{1,0},{2,1},{3,2},{0,3},{5,4},{6,5},{7,6},{4,7},{9,8},{10,9},{11,1... | collective-permute-start | bytes 13832 | tf_op jit(solution)/shard_map/ppermute | solution.py:26
  138.0 5.4 %collective-permute-start.12 = (bf16[128,18,1]{0,1,2:T(8,128)(2,1)S(1)}, bf16[128,18,1]{0,1,2:T(8,128)(2,1)S(1)}, u32[]{:S(2)}, u32[]{:S(2)}) collective-permute-start(bf16[128,18,1]{0,1,2:T(8,128)(2,1)S(1)} %copy.68), channel_id=1, source_target_pairs={{0,1},{1,2},{2,3},{3,0},{4,5},{5,6},{6,7},{7,4},{8,9},{9,10},{10,1... | collective-permute-start | bytes 13832 | tf_op jit(solution)/shard_map/ppermute | solution.py:25
  149.6 1.2 copy-start.7
  150.8 17.8 %copy-start.14 = (s32[64]{0:T(128)S(1)}, s32[64]{0:T(128)}, u32[]{:S(2)}) copy-start(s32[64]{0:T(128)} %param.18) | copy-start | bytes 772
  151.8 3.6 %collective-permute-start.14 = (f32[64]{0:T(128)S(1)}, f32[64]{0:T(128)S(1)}, u32[]{:S(2)}, u32[]{:S(2)}) collective-permute-start(f32[64]{0:T(128)S(1)} %fusion.40), channel_id=1, source_target_pairs={{0,1},{1,0},{2,3},{3,2},{4,5},{5,4},{6,7},{7,6},{8,9},{9,8},{10,11... | collective-permute-start | bytes 776 | tf_op jit(solution)/shard_map/ppermute | solution.py:34
  155.3 4.4 %collective-permute-start.15 = (f32[64]{0:T(128)S(1)}, f32[64]{0:T(128)S(1)}, u32[]{:S(2)}, u32[]{:S(2)}) collective-permute-start(f32[64]{0:T(128)S(1)} %add.241), channel_id=1, source_target_pairs={{0,2},{1,3},{2,0},{3,1},{4,6},{5,7},{6,4},{7,5},{8,10},{9,11},{10,... | collective-permute-start | bytes 776 | tf_op jit(solution)/shard_map/ppermute | solution.py:34
  159.8 1.1 collective-permute-start.16
  160.9 4.0 %collective-permute-start.17 = (f32[64]{0:T(128)S(1)}, f32[64]{0:T(128)S(1)}, u32[]{:S(2)}, u32[]{:S(2)}) collective-permute-start(f32[64]{0:T(128)S(1)} %add.243), channel_id=1, source_target_pairs={{0,8},{4,12},{8,0},{12,4},{16,24},{20,28},{24,16},{28,20},{1,9},{5... | collective-permute-start | bytes 776 | tf_op jit(solution)/shard_map/ppermute | solution.py:34
  165.0 3.6 %collective-permute-start.18 = (f32[64]{0:T(128)S(1)}, f32[64]{0:T(128)S(1)}, u32[]{:S(2)}, u32[]{:S(2)}) collective-permute-start(f32[64]{0:T(128)S(1)} %add.244), channel_id=1, source_target_pairs={{0,16},{4,20},{8,24},{12,28},{16,0},{20,4},{24,8},{28,12},{1,17},{... | collective-permute-start | bytes 776 | tf_op jit(solution)/shard_map/ppermute | solution.py:34
  (6 other events, 5.5 us)

commit v5 on v4

--- a/solution.py
+++ b/solution.py
@@ -146,18 +146,18 @@
     ).astype(jnp.bfloat16)
     lon_size = lax.axis_size("lon")
     group_width = model_width // lon_size
-    projections = lax.optimization_barrier(
-        tuple(
-            jnp.dot(normed, weight, preferred_element_type=jnp.float32).astype(jnp.bfloat16)
-            for weight in (query_weight, key_weight, value_weight)
+    normed_band = lax.all_gather(normed, "lon", axis=0, tiled=True)
+    group_first = lax.axis_index("lon") * group_width
+
+    def group_projection(weight):
+        group_weight = lax.dynamic_slice_in_dim(weight, group_first, group_width, axis=1)
+        return jnp.dot(normed_band, group_weight, preferred_element_type=jnp.float32).astype(
+            jnp.bfloat16
         )
-    )
-    by_group = [p.reshape(-1, lon_size, group_width).transpose(1, 0, 2) for p in projections]
-    key_value_spread = lax.all_to_all(
-        jnp.stack(by_group[1:]), "lon", split_axis=1, concat_axis=2, tiled=True
-    )
-    query_spread = lax.all_to_all(by_group[0], "lon", split_axis=0, concat_axis=1, tiled=True)[0]
-    key_spread, value_spread = key_value_spread[0, 0], key_value_spread[1, 0]
+
+    query_spread, key_spread, value_spread = (
+        group_projection(weight) for weight in (query_weight, key_weight, value_weight)
+    )
     lat_size = lax.axis_size("lat")
     core = lax.axis_index("lat") % 2
     half = group_width // 2

time: 170 us -> 188 us (1.11)
  between operations: 1.18 us -> 14.5 us
  waiting for transfers between devices: 70 us -> 78.5 us
  starting transfers between devices: 33.8 us -> 29 us
  matrix products: 20.9 us -> 24.4 us
  local copies, waits for them, and re-layouts: 22.2 us -> 19.1 us
    all_gather x0 -> x1, waiting for transfers between devices: none -> 30.8 us  [on_device(): normed_band = lax.all_gather(normed, 'lon', axis=0, tiled=True)]
    all_to_all x2 -> x0, waiting for transfers between devices: 17.8 us -> none  [the longest x1 14.9 us: on_device(): lax.all_to_all(jnp.stack(by_group[1:]), 'lon', split_axis=1, concat_axis=...]
    all_to_all x2 -> x0, starting transfers between devices: 8.72 us -> none  [the longest x1 5.13 us: on_device(): lax.all_to_all(jnp.stack(by_group[1:]), 'lon', split_axis=1, concat_axis=...]
    dot_general x3, matrix products: 1.33 us -> 4.73 us  [group_projection(): jnp.dot(normed_band, group_weight, preferred_element_type=jnp.float32)]
    ppermute x5, starting transfers between devices: 4.59 us -> 7.89 us  [butterfly_sum(): value = value + lax.ppermute(value, axis, partner)]
    ppermute x2, waiting for transfers between devices: 4.36 us -> 1.64 us  [halo_padded(): from_left = lax.ppermute(array[:, :, -width:], 'lon', right)]
    ppermute x2, starting transfers between devices: 3.69 us -> 6.03 us  [halo_padded(): from_right = lax.ppermute(array[:, :, :width], 'lon', left)]
    unnamed x37 -> x35, local copies, waits for them, and re-layouts: 11.8 us -> 9.52 us
  transfers between devices with their start and end apart: 22 -> 21, of which waited for: 17 -> 14; matrix products, arithmetic and copies ran while one was open for 7% -> 7% of each run, Pallas kernels for 0% -> 0%
where the time goes in v5:
time: 188 us; the launch traced here: 187 us
  waiting for transfers between devices  78.5 us (42%)
  starting transfers between devices  29 us (15%)
  matrix products  24.4 us (13%)
  local copies, waits for them, and re-layouts  19.1 us (10%)
  Pallas kernels  15.3 us (8%)
  between operations  14.5 us (8%)
  other arithmetic  6.62 us (4%)
    all_gather x1, waiting for transfers between devices, on_device(): normed_band = lax.all_gather(normed, 'lon', axis=0, tiled=True)  30.8 us
    ppermute x3, waiting for transfers between devices, on_device(): lax.ppermute(key_value, 'lat', [(i, i ^ 2 * d) for i in range(lat_size)])  17.9 us
    pallas_call x1, Pallas kernels, attend(): pl.pallas_call(functools.partial(attention_kernel, head_size=head_size),...  15.3 us
    dot_general x27, matrix products, convolution_kernel_taps(): jnp.einsum('oc,cyx->oyx', weight[tap_index], window, preferred_element_ty...  12.4 us
    ppermute x5, waiting for transfers between devices, butterfly_sum(): value = value + lax.ppermute(value, axis, partner)  10.7 us
    unnamed x35, local copies, waits for them, and re-layouts  9.52 us
    all_to_all x1, waiting for transfers between devices, on_device(): lax.all_to_all(attended_heads, 'lon', split_axis=0, concat_axis=1, tiled=...  9.42 us
    ppermute x5, starting transfers between devices, butterfly_sum(): value = value + lax.ppermute(value, axis, partner)  7.89 us
  transfers between devices with their start and end apart: 21, of which 14 were waited for; matrix products, arithmetic and copies ran while one was open for 7% of the time, Pallas kernels for 0%

profile of v5, /device:TPU:0, one launch (start us, length us, event | category | flops | bytes accessed | tf_op | source)
XLA Modules:
  0.0 187.3 jit_solution(18343083687427667883)
XLA Ops:
  7.2 1.5 copy.46
  8.8 2.4 %collective-permute-start = (bf16[69,2,128]{0,2,1:T(8,128)(2,1)S(1)}, bf16[69,2,128]{0,2,1:T(8,128)(2,1)S(1)}, u32[]{:S(2)}, u32[]{:S(2)}) collective-permute-start(bf16[69,2,128]{0,2,1:T(8,128)(2,1)S(1)} %get-tuple-element.27), channel_id=1, source_target_pairs={{0,4},{4,8},{8,12},{12,16},{16,20},{20,24},{24,28},{1,5},{5,9},{9,... | collective-permute-start | bytes 105992 | tf_op jit(solution)/shard_map/ppermute | solution.py:20
  12.4 3.9 %collective-permute-done.1 = bf16[69,2,128]{0,2,1:T(8,128)(2,1)S(1)} collective-permute-done((bf16[69,2,128]{0,2,1:T(8,128)(2,1)S(1)}, bf16[69,2,128]{0,2,1:T(8,128)(2,1)S(1)}, u32[]{:S(2)}, u32[]{:S(2)}) %collective-permute-start.1) | collective-permute-done | bytes 35360 | tf_op jit(solution)/shard_map/ppermute | solution.py:21
  16.4 1.6 collective-permute-start.2
  18.0 2.2 %collective-permute-start.3 = (bf16[69,20,2]{0,2,1:T(2,128)(2,1)S(1)}, bf16[69,20,2]{0,2,1:T(2,128)(2,1)S(1)}, u32[]{:S(2)}, u32[]{:S(2)}) collective-permute-start(bf16[69,20,2]{0,2,1:T(2,128)(2,1)S(1)} %get-tuple-element.17), channel_id=1, source_target_pairs={{1,0},{2,1},{3,2},{0,3},{5,4},{6,5},{7,6},{4,7},{9,8},{10,9},{11,1... | collective-permute-start | bytes 16568 | tf_op jit(solution)/shard_map/ppermute | solution.py:26
  20.3 1.6 collective-permute-done.2
  33.3 30.8 %all-gather.2.cloned.1.call-done = bf16[512,1024]{1,0:T(8,128)(2,1)} async-done(((bf16[128,1024]{1,0:T(8,128)(2,1)}), bf16[512,1024]{1,0:T(8,128)(2,1)}) %all-gather.2.cloned.1.call-update) | async-done | bytes 1048592 | tf_op jit(solution)/shard_map/all_gather | solution.py:149
  64.2 1.8 fusion.40
  65.9 1.5 fusion.41
  68.3 1.5 convolution_convert_fusion.2
  69.8 1.5 collective-permute-start.6
  71.4 1.5 collective-permute-start.7
  76.9 7.9 %collective-permute-done.6 = bf16[2,1024,128]{2,1,0:T(8,128)(2,1)} collective-permute-done((bf16[2,1024,128]{2,1,0:T(8,128)(2,1)S(1)}, bf16[2,1024,128]{2,1,0:T(8,128)(2,1)}, u32[]{:S(2)}, u32[]{:S(2)}) %collective-permute-start.6) | collective-permute-done | bytes 524320 | tf_op jit(solution)/shard_map/ppermute | solution.py:174
  84.7 1.9 %constant_dynamic-update-slice_fusion.2 = bf16[2,4096,128]{2,1,0:T(8,128)(2,1)} fusion(bf16[2,4096,128]{2,1,0:T(8,128)(2,1)} %constant_dynamic-update-slice_fusion.3, bf16[2,1024,128]{2,1,0:T(8,128)(2,1)} %collective-permute-done.6), kind=kLoop, calls=%fused_computation.197 | loop fusion | bytes 1048576
  86.7 10.0 %collective-permute-done.7 = bf16[2,1024,128]{2,1,0:T(8,128)(2,1)} collective-permute-done((bf16[2,1024,128]{2,1,0:T(8,128)(2,1)S(1)}, bf16[2,1024,128]{2,1,0:T(8,128)(2,1)}, u32[]{:S(2)}, u32[]{:S(2)}) %collective-permute-start.7) | collective-permute-done | bytes 524320 | tf_op jit(solution)/shard_map/ppermute | solution.py:174
  96.7 1.9 %constant_dynamic-update-slice_fusion.1 = bf16[2,4096,128]{2,1,0:T(8,128)(2,1)} fusion(bf16[2,4096,128]{2,1,0:T(8,128)(2,1)} %constant_dynamic-update-slice_fusion.2, bf16[2,1024,128]{2,1,0:T(8,128)(2,1)} %collective-permute-done.7), kind=kLoop, calls=%fused_computation.196 | loop fusion | bytes 1048576
  99.5 1.7 slice_bitcast_fusion
  101.2 15.3 %shard_map.166 = bf16[1024,128]{1,0:T(8,128)(2,1)S(1)} custom-call(f32[2]{0:T(128)S(1)} %dynamic-slice_multiply_fusion.scale_ref, bf16[1024,128]{1,0:T(8,128)(2,1)S(1)} %pad_maximum_fusion.6.q_ref, bf16[4096,128]{1,0:T(8,128)(2,1)S(1)} %get-tuple-element.15.k_ref, bf16[4096,128]{1,0:T(8,128)(2,1)S(1)} %get-tuple-element.14.v_ref), custom_call_target="tpu_custom_call" | custom-call | flops 2147483648 | bytes 2621440 | tf_op jit(solution)/shard_map/pallas_call | solution.py:87
  118.8 3.4 %all-to-all-start = ((bf16[4,128,256]{1,2,0:T(8,128)(2,1)}), bf16[4,128,256]{1,2,0:T(8,128)(2,1)S(1)}, u32[]{:S(2)}, u32[]{:S(2)}) async-start(bf16[4,128,256]{1,2,0:T(8,128)(2,1)} %maximum_select_fusion), calls=%async_computation | async-start | bytes 524288 | tf_op jit(solution)/shard_map/all_to_all | solution.py:193
  122.2 9.4 %all-to-all-done = bf16[4,128,256]{1,2,0:T(8,128)(2,1)S(1)} async-done(((bf16[4,128,256]{1,2,0:T(8,128)(2,1)}), bf16[4,128,256]{1,2,0:T(8,128)(2,1)S(1)}, u32[]{:S(2)}, u32[]{:S(2)}) %all-to-all-start) | async-done | bytes 262176 | tf_op jit(solution)/shard_map/all_to_all | solution.py:193
  131.6 2.1 %fusion.36 = bf16[128,1024]{1,0:T(8,128)(2,1)S(1)} fusion(f32[128,1024]{1,0:T(8,128)S(1)} %bitcast.205, bf16[128,1024]{0,1:T(8,128)(2,1)S(1)} %bitcast.208, bf16[1024,1024]{1,0:T(8,128)(2,1)} %param.26), kind=kOutput, calls=%fused_computation.52 | convolution fusion | flops 268697600 | bytes 3145728 | tf_op jit(solution)/shard_map/dot_general | solution.py:195
  133.7 3.4 %fusion.60 = bf16[128,4,4,32,4]{0,3,4,2,1:T(8,128)(2,1)S(1)} fusion(bf16[4,32,1024,1,1]{2,1,4,3,0:T(8,128)(2,1)S(1)} %bitcast.211, bf16[1024,4,4,128]{3,2,1,0:T(4,128)(2,1)} %param.28), kind=kOutput, calls=%fused_computation.76 | convolution fusion | flops 539230208 | bytes 4980736 | tf_op jit(solution)/shard_map/pqd,dabh->hpaqb/dot_general | solution.py:199
  140.3 1.7 collective-permute-done.11
  143.4 1.4 copy.59
  144.9 1.4 copy.62
  146.2 3.8 %collective-permute-start.13 = (bf16[128,18,1]{0,1,2:T(8,128)(2,1)S(1)}, bf16[128,18,1]{0,1,2:T(8,128)(2,1)S(1)}, u32[]{:S(2)}, u32[]{:S(2)}) collective-permute-start(bf16[128,18,1]{0,1,2:T(8,128)(2,1)S(1)} %copy.62), channel_id=1, source_target_pairs={{1,0},{2,1},{3,2},{0,3},{5,4},{6,5},{7,6},{4,7},{9,8},{10,9},{11,1... | collective-permute-start | bytes 13832 | tf_op jit(solution)/shard_map/ppermute | solution.py:26
  154.4 2.0 %maximum_maximum_fusion = (bf16[128,18,129]{2,0,1:T(8,128)(2,1)S(1)}, bf16[128,18,129]{2,0,1:T(8,128)(2,1)S(1)}) fusion(bf16[128,1,128]{2,0,1:T(8,128)(2,1)S(1)} %collective-permute-done.11, bf16[128,16,128]{2,0,1:T(8,128)(2,1)S(1)} %copy.56, bf16[128,1,128]{2,0,1:T(8,128)(2,1)S(1)} %collective-permute-done.10, bf16[128,18,1]{2,0,1:T(8,128)(2,1)} %copy.60, ...), kind=kLoop, calls=%fused_computation.54 | loop fusion | flops 4755456 | bytes 1787904 | tf_op jit(solution)/shard_map/concatenate | solution.py:27
  160.5 3.6 %collective-permute-done.14 = f32[64]{0:T(128)S(1)} collective-permute-done((f32[64]{0:T(128)S(1)}, f32[64]{0:T(128)S(1)}, u32[]{:S(2)}, u32[]{:S(2)}) %collective-permute-start.14) | collective-permute-done | bytes 288 | tf_op jit(solution)/shard_map/ppermute | solution.py:34
  164.8 3.7 %collective-permute-done.15 = f32[64]{0:T(128)S(1)} collective-permute-done((f32[64]{0:T(128)S(1)}, f32[64]{0:T(128)S(1)}, u32[]{:S(2)}, u32[]{:S(2)}) %collective-permute-start.15) | collective-permute-done | bytes 288 | tf_op jit(solution)/shard_map/ppermute | solution.py:34
  169.6 3.5 %collective-permute-start.17 = (f32[64]{0:T(128)S(1)}, f32[64]{0:T(128)S(1)}, u32[]{:S(2)}, u32[]{:S(2)}) collective-permute-start(f32[64]{0:T(128)S(1)} %add.249), channel_id=1, source_target_pairs={{0,8},{4,12},{8,0},{12,4},{16,24},{20,28},{24,16},{28,20},{1,9},{5... | collective-permute-start | bytes 776 | tf_op jit(solution)/shard_map/ppermute | solution.py:34
  173.2 1.5 collective-permute-done.17
  174.7 3.6 %collective-permute-start.18 = (f32[64]{0:T(128)S(1)}, f32[64]{0:T(128)S(1)}, u32[]{:S(2)}, u32[]{:S(2)}) collective-permute-start(f32[64]{0:T(128)S(1)} %add.250), channel_id=1, source_target_pairs={{0,16},{4,20},{8,24},{12,28},{16,0},{20,4},{24,8},{28,12},{1,17},{... | collective-permute-start | bytes 776 | tf_op jit(solution)/shard_map/ppermute | solution.py:34
  (117 shorter events, 37.8 us)
Async XLA Ops:
  7.2 57.0 %copy-start = (bf16[1024,1024]{1,0:T(8,128)(2,1)S(1)}, bf16[1024,1024]{1,0:T(8,128)(2,1)}, u32[]{:S(2)}) copy-start(bf16[1024,1024]{1,0:T(8,128)(2,1)} %param.24) | copy-start | bytes 6291460
  7.2 15.0 %copy-start.8 = (bf16[9,128,69]{1,2,0:T(8,128)(2,1)S(1)}, bf16[9,128,69]{1,2,0:T(8,128)(2,1)}, u32[]{:S(2)}) copy-start(bf16[9,128,69]{1,2,0:T(8,128)(2,1)} %param.19) | copy-start | bytes 476932
  7.2 57.0 %all-gather.2.cloned.1.call-start = ((), (), s32[]{:S(2)}) async-start(), calls=%async_computation.1 | async-start | bytes 1310720 | tf_op jit(solution)/shard_map/all_gather | solution.py:149
  8.8 3.7 %collective-permute-start = (bf16[69,2,128]{0,2,1:T(8,128)(2,1)S(1)}, bf16[69,2,128]{0,2,1:T(8,128)(2,1)S(1)}, u32[]{:S(2)}, u32[]{:S(2)}) collective-permute-start(bf16[69,2,128]{0,2,1:T(8,128)(2,1)S(1)} %get-tuple-element.27), channel_id=1, source_target_pairs={{0,4},{4,8},{8,12},{12,16},{16,20},{20,24},{24,28},{1,5},{5,9},{9,... | collective-permute-start | bytes 105992 | tf_op jit(solution)/shard_map/ppermute | solution.py:20
  11.1 5.3 %collective-permute-start.1 = (bf16[69,2,128]{0,2,1:T(8,128)(2,1)S(1)}, bf16[69,2,128]{0,2,1:T(8,128)(2,1)S(1)}, u32[]{:S(2)}, u32[]{:S(2)}) collective-permute-start(bf16[69,2,128]{0,2,1:T(8,128)(2,1)S(1)} %get-tuple-element.28), channel_id=1, source_target_pairs={{4,0},{8,4},{12,8},{16,12},{20,16},{24,20},{28,24},{5,1},{9,5},{13... | collective-permute-start | bytes 105992 | tf_op jit(solution)/shard_map/ppermute | solution.py:21
  16.4 5.5 %collective-permute-start.2 = (bf16[69,20,2]{0,2,1:T(2,128)(2,1)S(1)}, bf16[69,20,2]{0,2,1:T(2,128)(2,1)S(1)}, u32[]{:S(2)}, u32[]{:S(2)}) collective-permute-start(bf16[69,20,2]{0,2,1:T(2,128)(2,1)S(1)} %get-tuple-element.16), channel_id=1, source_target_pairs={{0,1},{1,2},{2,3},{3,0},{4,5},{5,6},{6,7},{7,4},{8,9},{9,10},{10,1... | collective-permute-start | bytes 16568 | tf_op jit(solution)/shard_map/ppermute | solution.py:25
  18.0 3.9 %collective-permute-start.3 = (bf16[69,20,2]{0,2,1:T(2,128)(2,1)S(1)}, bf16[69,20,2]{0,2,1:T(2,128)(2,1)S(1)}, u32[]{:S(2)}, u32[]{:S(2)}) collective-permute-start(bf16[69,20,2]{0,2,1:T(2,128)(2,1)S(1)} %get-tuple-element.17), channel_id=1, source_target_pairs={{1,0},{2,1},{3,2},{0,3},{5,4},{6,5},{7,6},{4,7},{9,8},{10,9},{11,1... | collective-permute-start | bytes 16568 | tf_op jit(solution)/shard_map/ppermute | solution.py:26
  26.0 1.2 copy-start.6
  29.3 2.2 %copy-start.1 = (bf16[4,4,128,1024]{3,2,1,0:T(8,128)(2,1)S(1)}, bf16[4,4,128,1024]{3,2,1,0:T(8,128)(2,1)}, u32[]{:S(2)}) copy-start(bf16[4,4,128,1024]{3,2,1,0:T(8,128)(2,1)} %param.21) | copy-start | bytes 12582916
  64.2 1.8 copy-start.10
  68.3 5.8 %copy-start.12 = (f32[16]{0:T(128)S(1)}, f32[16]{0:T(128)}, u32[]{:S(2)}) copy-start(f32[16]{0:T(128)} %param.27) | copy-start | bytes 196
  68.3 1.5 collective-permute-start.5
  69.8 14.9 %collective-permute-start.6 = (bf16[2,1024,128]{2,1,0:T(8,128)(2,1)S(1)}, bf16[2,1024,128]{2,1,0:T(8,128)(2,1)}, u32[]{:S(2)}, u32[]{:S(2)}) collective-permute-start(bf16[2,1024,128]{2,1,0:T(8,128)(2,1)S(1)} %pad_maximum_fusion.4), channel_id=1, source_target_pairs={{0,8},{4,12},{8,0},{12,4},{16,24},{20,28},{24,16},{28,20},{1,9},{5... | collective-permute-start | bytes 1572872 | tf_op jit(solution)/shard_map/ppermute | solution.py:174
  71.4 25.4 %collective-permute-start.7 = (bf16[2,1024,128]{2,1,0:T(8,128)(2,1)S(1)}, bf16[2,1024,128]{2,1,0:T(8,128)(2,1)}, u32[]{:S(2)}, u32[]{:S(2)}) collective-permute-start(bf16[2,1024,128]{2,1,0:T(8,128)(2,1)S(1)} %pad_maximum_fusion.4), channel_id=1, source_target_pairs={{0,16},{4,20},{8,24},{12,28},{16,0},{20,4},{24,8},{28,12},{1,17},{... | collective-permute-start | bytes 1572872 | tf_op jit(solution)/shard_map/ppermute | solution.py:174
  73.5 1.7 collective-permute-start.4
  73.5 25.2 %collective-permute-start.8 = (bf16[2,1024,128]{2,1,0:T(8,128)(2,1)S(1)}, bf16[2,1024,128]{2,1,0:T(8,128)(2,1)S(1)}, u32[]{:S(2)}, u32[]{:S(2)}) collective-permute-start(bf16[2,1024,128]{2,1,0:T(8,128)(2,1)S(1)} %pad_maximum_fusion.4), channel_id=1, source_target_pairs={{0,24},{4,28},{8,16},{12,20},{16,8},{20,12},{24,0},{28,4},{1,25},{... | collective-permute-start | bytes 1572872 | tf_op jit(solution)/shard_map/ppermute | solution.py:174
  116.5 1.4 collective-permute-start.9
  118.8 12.8 %all-to-all-start = ((bf16[4,128,256]{1,2,0:T(8,128)(2,1)}), bf16[4,128,256]{1,2,0:T(8,128)(2,1)S(1)}, u32[]{:S(2)}, u32[]{:S(2)}) async-start(bf16[4,128,256]{1,2,0:T(8,128)(2,1)} %maximum_select_fusion), calls=%async_computation | async-start | bytes 524288 | tf_op jit(solution)/shard_map/all_to_all | solution.py:193
  137.7 2.6 %collective-permute-start.10 = (bf16[128,1,128]{2,0,1:T(8,128)(2,1)S(1)}, bf16[128,1,128]{2,0,1:T(8,128)(2,1)S(1)}, u32[]{:S(2)}, u32[]{:S(2)}) collective-permute-start(bf16[128,1,128]{2,0,1:T(8,128)(2,1)S(1)} %get-tuple-element.24), channel_id=1, source_target_pairs={{0,4},{4,8},{8,12},{12,16},{16,20},{20,24},{24,28},{1,5},{5,9},{9,... | collective-permute-start | bytes 98312 | tf_op jit(solution)/shard_map/ppermute | solution.py:20
  139.0 3.1 %collective-permute-start.11 = (bf16[128,1,128]{2,0,1:T(8,128)(2,1)S(1)}, bf16[128,1,128]{2,0,1:T(8,128)(2,1)S(1)}, u32[]{:S(2)}, u32[]{:S(2)}) collective-permute-start(bf16[128,1,128]{2,0,1:T(8,128)(2,1)S(1)} %get-tuple-element.25), channel_id=1, source_target_pairs={{4,0},{8,4},{12,8},{16,12},{20,16},{24,20},{28,24},{5,1},{9,5},{13... | collective-permute-start | bytes 98312 | tf_op jit(solution)/shard_map/ppermute | solution.py:21
  142.2 7.9 %copy-start.7 = (bf16[9,69,128]{2,1,0:T(8,128)(2,1)S(1)}, bf16[9,69,128]{2,1,0:T(8,128)(2,1)}, u32[]{:S(2)}) copy-start(bf16[9,69,128]{2,1,0:T(8,128)(2,1)} %param.29) | copy-start | bytes 476932
  144.8 7.4 %collective-permute-start.12 = (bf16[128,18,1]{0,1,2:T(8,128)(2,1)S(1)}, bf16[128,18,1]{0,1,2:T(8,128)(2,1)S(1)}, u32[]{:S(2)}, u32[]{:S(2)}) collective-permute-start(bf16[128,18,1]{0,1,2:T(8,128)(2,1)S(1)} %copy.59), channel_id=1, source_target_pairs={{0,1},{1,2},{2,3},{3,0},{4,5},{5,6},{6,7},{7,4},{8,9},{9,10},{10,1... | collective-permute-start | bytes 13832 | tf_op jit(solution)/shard_map/ppermute | solution.py:25
  146.2 7.0 %collective-permute-start.13 = (bf16[128,18,1]{0,1,2:T(8,128)(2,1)S(1)}, bf16[128,18,1]{0,1,2:T(8,128)(2,1)S(1)}, u32[]{:S(2)}, u32[]{:S(2)}) collective-permute-start(bf16[128,18,1]{0,1,2:T(8,128)(2,1)S(1)} %copy.62), channel_id=1, source_target_pairs={{1,0},{2,1},{3,2},{0,3},{5,4},{6,5},{7,6},{4,7},{9,8},{10,9},{11,1... | collective-permute-start | bytes 13832 | tf_op jit(solution)/shard_map/ppermute | solution.py:26
  156.3 1.1 copy-start.3
  158.3 1.1 copy-start.4
  158.3 1.2 copy-start.5
  159.5 20.4 %copy-start.13 = (s32[64]{0:T(128)S(1)}, s32[64]{0:T(128)}, u32[]{:S(2)}) copy-start(s32[64]{0:T(128)} %param.18) | copy-start | bytes 772
  160.5 3.6 %collective-permute-start.14 = (f32[64]{0:T(128)S(1)}, f32[64]{0:T(128)S(1)}, u32[]{:S(2)}, u32[]{:S(2)}) collective-permute-start(f32[64]{0:T(128)S(1)} %fusion.42), channel_id=1, source_target_pairs={{0,1},{1,0},{2,3},{3,2},{4,5},{5,4},{6,7},{7,6},{8,9},{9,8},{10,11... | collective-permute-start | bytes 776 | tf_op jit(solution)/shard_map/ppermute | solution.py:34
  164.1 4.4 %collective-permute-start.15 = (f32[64]{0:T(128)S(1)}, f32[64]{0:T(128)S(1)}, u32[]{:S(2)}, u32[]{:S(2)}) collective-permute-start(f32[64]{0:T(128)S(1)} %add.247), channel_id=1, source_target_pairs={{0,2},{1,3},{2,0},{3,1},{4,6},{5,7},{6,4},{7,5},{8,10},{9,11},{10,... | collective-permute-start | bytes 776 | tf_op jit(solution)/shard_map/ppermute | solution.py:34
  168.5 1.1 collective-permute-start.16
  169.6 5.1 %collective-permute-start.17 = (f32[64]{0:T(128)S(1)}, f32[64]{0:T(128)S(1)}, u32[]{:S(2)}, u32[]{:S(2)}) collective-permute-start(f32[64]{0:T(128)S(1)} %add.249), channel_id=1, source_target_pairs={{0,8},{4,12},{8,0},{12,4},{16,24},{20,28},{24,16},{28,20},{1,9},{5... | collective-permute-start | bytes 776 | tf_op jit(solution)/shard_map/ppermute | solution.py:34
  174.7 5.1 %collective-permute-start.18 = (f32[64]{0:T(128)S(1)}, f32[64]{0:T(128)S(1)}, u32[]{:S(2)}, u32[]{:S(2)}) collective-permute-start(f32[64]{0:T(128)S(1)} %add.250), channel_id=1, source_target_pairs={{0,16},{4,20},{8,24},{12,28},{16,0},{20,4},{24,8},{28,12},{1,17},{... | collective-permute-start | bytes 776 | tf_op jit(solution)/shard_map/ppermute | solution.py:34
  (4 other events, 3.3 us)
Sparse Core Ops, SparseCore 0:
  33.4 30.6 all-gather.1

commit v6 on v4

--- a/solution.py
+++ b/solution.py
@@ -102,6 +102,27 @@
             bytes_accessed=2 * (2 * query_count * width + 2 * key_count * width),
         ),
     )(scales, queries, keys, values)
+
+
+def exchange_blocks(blocks, axis):
+    size, index = lax.axis_size(axis), lax.axis_index(axis)
+    received = [lax.dynamic_index_in_dim(blocks, index, 0, keepdims=False)]
+    for shift in range(1, size):
+        outgoing = lax.dynamic_index_in_dim(blocks, (index + shift) % size, 0, keepdims=False)
+        received.append(
+            lax.ppermute(outgoing, axis, [(i, (i + shift) % size) for i in range(size)])
+        )
+    return received
+
+
+def return_blocks(blocks, axis):
+    size, index = lax.axis_size(axis), lax.axis_index(axis)
+    received = [blocks[0]] + [
+        lax.ppermute(blocks[shift], axis, [((i + shift) % size, i) for i in range(size)])
+        for shift in range(1, size)
+    ]
+    rotated = jnp.stack(received + received)
+    return lax.dynamic_slice_in_dim(rotated, size - index, size, axis=0)
 
 
 def on_device(
@@ -153,11 +174,11 @@
         )
     )
     by_group = [p.reshape(-1, lon_size, group_width).transpose(1, 0, 2) for p in projections]
-    key_value_spread = lax.all_to_all(
-        jnp.stack(by_group[1:]), "lon", split_axis=1, concat_axis=2, tiled=True
-    )
-    query_spread = lax.all_to_all(by_group[0], "lon", split_axis=0, concat_axis=1, tiled=True)[0]
-    key_spread, value_spread = key_value_spread[0, 0], key_value_spread[1, 0]
+    key_value_spread = jnp.concatenate(
+        exchange_blocks(jnp.stack(by_group[1:], axis=1), "lon"), axis=1
+    )
+    query_spread = jnp.concatenate(exchange_blocks(by_group[0], "lon"), axis=0)
+    key_spread, value_spread = key_value_spread[0], key_value_spread[1]
     lat_size = lax.axis_size("lat")
     core = lax.axis_index("lat") % 2
     half = group_width // 2
@@ -190,7 +211,11 @@
         jnp.concatenate([own_part, returned], axis=1),
         jnp.concatenate([returned, own_part], axis=1),
     )
-    attended = lax.all_to_all(attended_heads, "lon", split_axis=0, concat_axis=1, tiled=True)
+    token_block = attended_heads.shape[0] // lon_size
+    attended = return_blocks(
+        [attended_heads[d * token_block : (d + 1) * token_block] for d in range(lon_size)], "lon"
+    )
+    attended = attended.transpose(1, 0, 2).reshape(token_block, model_width)
     latent_two = (
         latent_wide + jnp.dot(attended, output_weight, preferred_element_type=jnp.float32)
     ).astype(jnp.bfloat16)

time: 170 us -> 167 us (0.982)
  waiting for transfers between devices: 70 us -> 61.9 us
  starting transfers between devices: 33.8 us -> 38.3 us
    all_to_all x3 -> x0, waiting for transfers between devices: 27 us -> none  [the longest x1 14.9 us: on_device(): lax.all_to_all(jnp.stack(by_group[1:]), 'lon', split_axis=1, concat_axis=...]
    ppermute x0 -> x9, waiting for transfers between devices: none -> 22.4 us  [the longest x6 16.4 us: exchange_blocks(): lax.ppermute(outgoing, axis, [(i, (i + shift) % size) for i in range(size)])]
    all_to_all x3 -> x0, starting transfers between devices: 13.6 us -> none  [the longest x1 5.13 us: on_device(): lax.all_to_all(jnp.stack(by_group[1:]), 'lon', split_axis=1, concat_axis=...]
    ppermute x0 -> x9, starting transfers between devices: none -> 12.9 us  [the longest x6 8.64 us: exchange_blocks(): lax.ppermute(outgoing, axis, [(i, (i + shift) % size) for i in range(size)])]
    ppermute x3, waiting for transfers between devices: 15.9 us -> 19.7 us  [on_device(): lax.ppermute(key_value, 'lat', [(i, i ^ 2 * d) for i in range(lat_size)])]
    ppermute x2, waiting for transfers between devices: 4.36 us -> 1.64 us  [halo_padded(): from_left = lax.ppermute(array[:, :, -width:], 'lon', right)]
    ppermute x2, waiting for transfers between devices: 2.54 us -> 0.01 us  [with_partner(): lax.ppermute(theirs, 'lat', partner)]
    ppermute x2, starting transfers between devices: 3.69 us -> 5.98 us  [halo_padded(): from_right = lax.ppermute(array[:, :, :width], 'lon', left)]
  transfers between devices with their start and end apart: 22 -> 28, of which waited for: 17 -> 18; matrix products, arithmetic and copies ran while one was open for 7% -> 7% of each run, Pallas kernels for 0% -> 0%
where the time goes in v6:
time: 167 us; the launch traced here: 166 us
  waiting for transfers between devices  61.9 us (37%)
  starting transfers between devices  38.3 us (23%)
  local copies, waits for them, and re-layouts  22.2 us (13%)
  matrix products  21 us (13%)
  Pallas kernels  15.1 us (9%)
  other arithmetic  6.21 us (4%)
    ppermute x3, waiting for transfers between devices, on_device(): lax.ppermute(key_value, 'lat', [(i, i ^ 2 * d) for i in range(lat_size)])  19.7 us
    ppermute x6, waiting for transfers between devices, exchange_blocks(): lax.ppermute(outgoing, axis, [(i, (i + shift) % size) for i in range(size)])  16.4 us
    pallas_call x1, Pallas kernels, attend(): pl.pallas_call(functools.partial(attention_kernel, head_size=head_size),...  15.1 us
    dot_general x27, matrix products, convolution_kernel_taps(): jnp.einsum('oc,cyx->oyx', weight[tap_index], window, preferred_element_ty...  12.4 us
    unnamed x48, local copies, waits for them, and re-layouts  11.8 us
    ppermute x5, waiting for transfers between devices, butterfly_sum(): value = value + lax.ppermute(value, axis, partner)  10.7 us
    ppermute x6, starting transfers between devices, exchange_blocks(): lax.ppermute(outgoing, axis, [(i, (i + shift) % size) for i in range(size)])  8.64 us
    ppermute x5, starting transfers between devices, butterfly_sum(): value = value + lax.ppermute(value, axis, partner)  6.22 us
  transfers between devices with their start and end apart: 28, of which 18 were waited for; matrix products, arithmetic and copies ran while one was open for 7% of the time, Pallas kernels for 0%

profile of v6, /device:TPU:0, one launch (start us, length us, event | category | flops | bytes accessed | tf_op | source)
XLA Modules:
  0.0 165.9 jit_solution(1862480464362037879)
XLA Ops:
  2.2 2.5 %collective-permute-start = (bf16[69,2,128]{0,2,1:T(8,128)(2,1)S(1)}, bf16[69,2,128]{0,2,1:T(8,128)(2,1)S(1)}, u32[]{:S(2)}, u32[]{:S(2)}) collective-permute-start(bf16[69,2,128]{0,2,1:T(8,128)(2,1)S(1)} %get-tuple-element.37), channel_id=1, source_target_pairs={{0,4},{4,8},{8,12},{12,16},{16,20},{20,24},{24,28},{1,5},{5,9},{9,... | collective-permute-start | bytes 105992 | tf_op jit(solution)/shard_map/ppermute | solution.py:20
  6.0 3.9 %collective-permute-done.1 = bf16[69,2,128]{0,2,1:T(8,128)(2,1)S(1)} collective-permute-done((bf16[69,2,128]{0,2,1:T(8,128)(2,1)S(1)}, bf16[69,2,128]{0,2,1:T(8,128)(2,1)S(1)}, u32[]{:S(2)}, u32[]{:S(2)}) %collective-permute-start.1) | collective-permute-done | bytes 35360 | tf_op jit(solution)/shard_map/ppermute | solution.py:21
  9.9 1.6 collective-permute-start.2
  11.6 2.2 %collective-permute-start.3 = (bf16[69,20,2]{0,2,1:T(2,128)(2,1)S(1)}, bf16[69,20,2]{0,2,1:T(2,128)(2,1)S(1)}, u32[]{:S(2)}, u32[]{:S(2)}) collective-permute-start(bf16[69,20,2]{0,2,1:T(2,128)(2,1)S(1)} %get-tuple-element.23), channel_id=1, source_target_pairs={{1,0},{2,1},{3,2},{0,3},{5,4},{6,5},{7,6},{4,7},{9,8},{10,9},{11,1... | collective-permute-start | bytes 16568 | tf_op jit(solution)/shard_map/ppermute | solution.py:26
  13.8 1.6 collective-permute-done.2
  30.6 3.9 %collective-permute-start.10 = (bf16[2,128,256]{2,1,0:T(8,128)(2,1)}, bf16[2,128,256]{2,1,0:T(8,128)(2,1)S(1)}, u32[]{:S(2)}, u32[]{:S(2)}) collective-permute-start(bf16[2,128,256]{2,1,0:T(8,128)(2,1)} %get-tuple-element.36), channel_id=1, source_target_pairs={{0,3},{1,0},{2,1},{3,2},{4,7},{5,4},{6,5},{7,6},{8,11},{9,8},{10,9... | collective-permute-start | bytes 393224 | tf_op jit(solution)/shard_map/ppermute | solution.py:113
  35.2 3.0 %collective-permute-done.10 = bf16[2,128,256]{2,1,0:T(8,128)(2,1)S(1)} collective-permute-done((bf16[2,128,256]{2,1,0:T(8,128)(2,1)}, bf16[2,128,256]{2,1,0:T(8,128)(2,1)S(1)}, u32[]{:S(2)}, u32[]{:S(2)}) %collective-permute-start.10) | collective-permute-done | bytes 131104 | tf_op jit(solution)/shard_map/ppermute | solution.py:113
  38.2 4.6 %collective-permute-done.8 = bf16[2,128,256]{2,1,0:T(8,128)(2,1)} collective-permute-done((bf16[2,128,256]{2,1,0:T(8,128)(2,1)}, bf16[2,128,256]{2,1,0:T(8,128)(2,1)}, u32[]{:S(2)}, u32[]{:S(2)}) %collective-permute-start.8) | collective-permute-done | bytes 131104 | tf_op jit(solution)/shard_map/ppermute | solution.py:113
  42.7 4.4 %collective-permute-done.9 = bf16[2,128,256]{2,1,0:T(8,128)(2,1)} collective-permute-done((bf16[2,128,256]{2,1,0:T(8,128)(2,1)S(1)}, bf16[2,128,256]{2,1,0:T(8,128)(2,1)}, u32[]{:S(2)}, u32[]{:S(2)}) %collective-permute-start.9) | collective-permute-done | bytes 131104 | tf_op jit(solution)/shard_map/ppermute | solution.py:113
  49.7 2.6 %collective-permute-start.5 = (bf16[128,256]{1,0:T(8,128)(2,1)S(1)}, bf16[128,256]{1,0:T(8,128)(2,1)S(1)}, u32[]{:S(2)}, u32[]{:S(2)}) collective-permute-start(bf16[128,256]{1,0:T(8,128)(2,1)S(1)} %bitcast.261), channel_id=1, source_target_pairs={{0,2},{1,3},{2,0},{3,1},{4,6},{5,7},{6,4},{7,5},{8,10},{9,11},{10,... | collective-permute-start | bytes 196616 | tf_op jit(solution)/shard_map/ppermute | solution.py:113
  53.9 2.6 %collective-permute-done.4 = bf16[128,256]{1,0:T(8,128)(2,1)S(1)} collective-permute-done((bf16[128,256]{1,0:T(8,128)(2,1)S(1)}, bf16[128,256]{1,0:T(8,128)(2,1)S(1)}, u32[]{:S(2)}, u32[]{:S(2)}) %collective-permute-start.4) | collective-permute-done | bytes 65568 | tf_op jit(solution)/shard_map/ppermute | solution.py:113
  56.5 1.8 %collective-permute-done.5 = bf16[128,256]{1,0:T(8,128)(2,1)S(1)} collective-permute-done((bf16[128,256]{1,0:T(8,128)(2,1)S(1)}, bf16[128,256]{1,0:T(8,128)(2,1)S(1)}, u32[]{:S(2)}, u32[]{:S(2)}) %collective-permute-start.5) | collective-permute-done | bytes 65568 | tf_op jit(solution)/shard_map/ppermute | solution.py:113
  59.2 3.0 %collective-permute-start.12 = (bf16[2,1024,128]{2,1,0:T(8,128)(2,1)}, bf16[2,1024,128]{2,1,0:T(8,128)(2,1)}, u32[]{:S(2)}, u32[]{:S(2)}) collective-permute-start(bf16[2,1024,128]{2,1,0:T(8,128)(2,1)} %pad_maximum_fusion.5), channel_id=1, source_target_pairs={{0,8},{4,12},{8,0},{12,4},{16,24},{20,28},{24,16},{28,20},{1,9},{5... | collective-permute-start | bytes 1572872 | tf_op jit(solution)/shard_map/ppermute | solution.py:195
  62.4 1.5 collective-permute-start.14
  64.7 10.7 %collective-permute-done.12 = bf16[2,1024,128]{2,1,0:T(8,128)(2,1)} collective-permute-done((bf16[2,1024,128]{2,1,0:T(8,128)(2,1)}, bf16[2,1024,128]{2,1,0:T(8,128)(2,1)}, u32[]{:S(2)}, u32[]{:S(2)}) %collective-permute-start.12) | collective-permute-done | bytes 524320 | tf_op jit(solution)/shard_map/ppermute | solution.py:195
  75.4 1.9 %constant_dynamic-update-slice_fusion.2 = bf16[2,4096,128]{2,1,0:T(8,128)(2,1)} fusion(bf16[2,4096,128]{2,1,0:T(8,128)(2,1)} %constant_dynamic-update-slice_fusion.3, bf16[2,1024,128]{2,1,0:T(8,128)(2,1)} %collective-permute-done.12), kind=kLoop, calls=%fused_computation.181 | loop fusion | bytes 1048576
  77.4 9.0 %collective-permute-done.13 = bf16[2,1024,128]{2,1,0:T(8,128)(2,1)} collective-permute-done((bf16[2,1024,128]{2,1,0:T(8,128)(2,1)}, bf16[2,1024,128]{2,1,0:T(8,128)(2,1)}, u32[]{:S(2)}, u32[]{:S(2)}) %collective-permute-start.13) | collective-permute-done | bytes 524320 | tf_op jit(solution)/shard_map/ppermute | solution.py:195
  86.4 1.9 %constant_dynamic-update-slice_fusion.1 = bf16[2,4096,128]{2,1,0:T(8,128)(2,1)} fusion(bf16[2,4096,128]{2,1,0:T(8,128)(2,1)} %constant_dynamic-update-slice_fusion.2, bf16[2,1024,128]{2,1,0:T(8,128)(2,1)} %collective-permute-done.13), kind=kLoop, calls=%fused_computation.180 | loop fusion | bytes 1048576
  89.2 1.7 %slice_bitcast_fusion = (bf16[4096,128]{1,0:T(8,128)(2,1)S(1)}, bf16[4096,128]{1,0:T(8,128)(2,1)S(1)}) fusion(bf16[2,4096,128]{2,1,0:T(8,128)(2,1)} %constant_dynamic-update-slice_fusion), kind=kLoop, calls=%fused_computation.75 | loop fusion | bytes 4194304 | tf_op jit(solution)/shard_map/squeeze | solution.py:204
  90.9 15.1 %shard_map.166 = bf16[1024,128]{1,0:T(8,128)(2,1)S(1)} custom-call(f32[2]{0:T(128)S(1)} %dynamic-slice_multiply_fusion.scale_ref, bf16[1024,128]{1,0:T(8,128)(2,1)S(1)} %pad_maximum_fusion.7.q_ref, bf16[4096,128]{1,0:T(8,128)(2,1)S(1)} %get-tuple-element.21.k_ref, bf16[4096,128]{1,0:T(8,128)(2,1)S(1)} %get-tuple-element.20.v_ref), custom_call_target="tpu_custom_call" | custom-call | flops 2147483648 | bytes 2621440 | tf_op jit(solution)/shard_map/pallas_call | solution.py:87
  107.5 3.6 %collective-permute-start.16 = (bf16[128,256]{1,0:T(8,128)(2,1)S(1)}, bf16[128,256]{1,0:T(8,128)(2,1)S(1)}, u32[]{:S(2)}, u32[]{:S(2)}) collective-permute-start(bf16[128,256]{1,0:T(8,128)(2,1)S(1)} %get-tuple-element.41), channel_id=1, source_target_pairs={{1,0},{2,1},{3,2},{0,3},{5,4},{6,5},{7,6},{4,7},{9,8},{10,9},{11,1... | collective-permute-start | bytes 196616 | tf_op jit(solution)/shard_map/ppermute | solution.py:121
  111.8 1.8 %collective-permute-done.16 = bf16[128,256]{1,0:T(8,128)(2,1)S(1)} collective-permute-done((bf16[128,256]{1,0:T(8,128)(2,1)S(1)}, bf16[128,256]{1,0:T(8,128)(2,1)S(1)}, u32[]{:S(2)}, u32[]{:S(2)}) %collective-permute-start.16) | collective-permute-done | bytes 65568 | tf_op jit(solution)/shard_map/ppermute | solution.py:121
  113.6 4.1 %collective-permute-done.17 = bf16[128,256]{1,0:T(8,128)(2,1)S(1)} collective-permute-done((bf16[128,256]{1,0:T(8,128)(2,1)S(1)}, bf16[128,256]{1,0:T(8,128)(2,1)S(1)}, u32[]{:S(2)}, u32[]{:S(2)}) %collective-permute-start.17) | collective-permute-done | bytes 65568 | tf_op jit(solution)/shard_map/ppermute | solution.py:121
  118.0 2.1 %fusion.36 = bf16[128,1024]{1,0:T(8,128)(2,1)S(1)} fusion(f32[128,1024]{1,0:T(8,128)S(1)} %bitcast.251, bf16[128,1024]{0,1:T(8,128)(2,1)S(1)} %bitcast.254, bf16[1024,1024]{1,0:T(8,128)(2,1)} %param.26), kind=kOutput, calls=%fused_computation.52 | convolution fusion | flops 268697600 | bytes 3145728 | tf_op jit(solution)/shard_map/dot_general | solution.py:220
  120.1 3.4 %fusion.58 = bf16[128,4,4,32,4]{0,3,4,2,1:T(8,128)(2,1)S(1)} fusion(bf16[4,32,1024,1,1]{2,1,4,3,0:T(8,128)(2,1)S(1)} %bitcast.258, bf16[1024,4,4,128]{3,2,1,0:T(4,128)(2,1)} %param.28), kind=kOutput, calls=%fused_computation.74 | convolution fusion | flops 539230208 | bytes 4980736 | tf_op jit(solution)/shard_map/pqd,dabh->hpaqb/dot_general | solution.py:224
  126.7 2.3 %collective-permute-done.20 = bf16[128,1,128]{2,0,1:T(8,128)(2,1)S(1)} collective-permute-done((bf16[128,1,128]{2,0,1:T(8,128)(2,1)S(1)}, bf16[128,1,128]{2,0,1:T(8,128)(2,1)S(1)}, u32[]{:S(2)}, u32[]{:S(2)}) %collective-permute-start.20) | collective-permute-done | bytes 32800 | tf_op jit(solution)/shard_map/ppermute | solution.py:21
  133.4 3.7 %collective-permute-start.22 = (bf16[128,18,1]{0,1,2:T(8,128)(2,1)S(1)}, bf16[128,18,1]{0,1,2:T(8,128)(2,1)S(1)}, u32[]{:S(2)}, u32[]{:S(2)}) collective-permute-start(bf16[128,18,1]{0,1,2:T(8,128)(2,1)S(1)} %copy.74), channel_id=1, source_target_pairs={{1,0},{2,1},{3,2},{0,3},{5,4},{6,5},{7,6},{4,7},{9,8},{10,9},{11,1... | collective-permute-start | bytes 13832 | tf_op jit(solution)/shard_map/ppermute | solution.py:26
  141.5 2.0 %maximum_maximum_fusion = (bf16[128,18,129]{2,0,1:T(8,128)(2,1)S(1)}, bf16[128,18,129]{2,0,1:T(8,128)(2,1)S(1)}) fusion(bf16[128,1,128]{2,0,1:T(8,128)(2,1)S(1)} %collective-permute-done.20, bf16[128,16,128]{2,0,1:T(8,128)(2,1)S(1)} %copy.68, bf16[128,1,128]{2,0,1:T(8,128)(2,1)S(1)} %collective-permute-done.19, bf16[128,18,1]{2,0,1:T(8,128)(2,1)} %copy.72, ...), kind=kLoop, calls=%fused_computation.54 | loop fusion | flops 4755456 | bytes 1787904 | tf_op jit(solution)/shard_map/concatenate | solution.py:27
  147.6 3.6 %collective-permute-done.23 = f32[64]{0:T(128)S(1)} collective-permute-done((f32[64]{0:T(128)S(1)}, f32[64]{0:T(128)S(1)}, u32[]{:S(2)}, u32[]{:S(2)}) %collective-permute-start.23) | collective-permute-done | bytes 288 | tf_op jit(solution)/shard_map/ppermute | solution.py:34
  151.9 3.7 %collective-permute-done.24 = f32[64]{0:T(128)S(1)} collective-permute-done((f32[64]{0:T(128)S(1)}, f32[64]{0:T(128)S(1)}, u32[]{:S(2)}, u32[]{:S(2)}) %collective-permute-start.24) | collective-permute-done | bytes 288 | tf_op jit(solution)/shard_map/ppermute | solution.py:34
  156.8 2.5 %collective-permute-start.26 = (f32[64]{0:T(128)S(1)}, f32[64]{0:T(128)S(1)}, u32[]{:S(2)}, u32[]{:S(2)}) collective-permute-start(f32[64]{0:T(128)S(1)} %add.300), channel_id=1, source_target_pairs={{0,8},{4,12},{8,0},{12,4},{16,24},{20,28},{24,16},{28,20},{1,9},{5... | collective-permute-start | bytes 776 | tf_op jit(solution)/shard_map/ppermute | solution.py:34
  160.8 2.9 %collective-permute-start.27 = (f32[64]{0:T(128)S(1)}, f32[64]{0:T(128)S(1)}, u32[]{:S(2)}, u32[]{:S(2)}) collective-permute-start(f32[64]{0:T(128)S(1)} %add.301), channel_id=1, source_target_pairs={{0,16},{4,20},{8,24},{12,28},{16,0},{20,4},{24,8},{28,12},{1,17},{... | collective-permute-start | bytes 776 | tf_op jit(solution)/shard_map/ppermute | solution.py:34
  (151 shorter events, 49.2 us)
Async XLA Ops:
  0.6 25.5 %copy-start = (bf16[1024,1024]{1,0:T(8,128)(2,1)S(1)}, bf16[1024,1024]{1,0:T(8,128)(2,1)}, u32[]{:S(2)}) copy-start(bf16[1024,1024]{1,0:T(8,128)(2,1)} %param.25) | copy-start | bytes 6291460
  2.1 13.6 %copy-start.10 = (bf16[9,128,69]{1,2,0:T(8,128)(2,1)S(1)}, bf16[9,128,69]{1,2,0:T(8,128)(2,1)}, u32[]{:S(2)}) copy-start(bf16[9,128,69]{1,2,0:T(8,128)(2,1)} %param.19) | copy-start | bytes 476932
  2.2 3.8 %collective-permute-start = (bf16[69,2,128]{0,2,1:T(8,128)(2,1)S(1)}, bf16[69,2,128]{0,2,1:T(8,128)(2,1)S(1)}, u32[]{:S(2)}, u32[]{:S(2)}) collective-permute-start(bf16[69,2,128]{0,2,1:T(8,128)(2,1)S(1)} %get-tuple-element.37), channel_id=1, source_target_pairs={{0,4},{4,8},{8,12},{12,16},{16,20},{20,24},{24,28},{1,5},{5,9},{9,... | collective-permute-start | bytes 105992 | tf_op jit(solution)/shard_map/ppermute | solution.py:20
  4.7 5.3 %collective-permute-start.1 = (bf16[69,2,128]{0,2,1:T(8,128)(2,1)S(1)}, bf16[69,2,128]{0,2,1:T(8,128)(2,1)S(1)}, u32[]{:S(2)}, u32[]{:S(2)}) collective-permute-start(bf16[69,2,128]{0,2,1:T(8,128)(2,1)S(1)} %get-tuple-element.38), channel_id=1, source_target_pairs={{4,0},{8,4},{12,8},{16,12},{20,16},{24,20},{28,24},{5,1},{9,5},{13... | collective-permute-start | bytes 105992 | tf_op jit(solution)/shard_map/ppermute | solution.py:21
  9.9 5.5 %collective-permute-start.2 = (bf16[69,20,2]{0,2,1:T(2,128)(2,1)S(1)}, bf16[69,20,2]{0,2,1:T(2,128)(2,1)S(1)}, u32[]{:S(2)}, u32[]{:S(2)}) collective-permute-start(bf16[69,20,2]{0,2,1:T(2,128)(2,1)S(1)} %get-tuple-element.22), channel_id=1, source_target_pairs={{0,1},{1,2},{2,3},{3,0},{4,5},{5,6},{6,7},{7,4},{8,9},{9,10},{10,1... | collective-permute-start | bytes 16568 | tf_op jit(solution)/shard_map/ppermute | solution.py:25
  11.6 3.9 %collective-permute-start.3 = (bf16[69,20,2]{0,2,1:T(2,128)(2,1)S(1)}, bf16[69,20,2]{0,2,1:T(2,128)(2,1)S(1)}, u32[]{:S(2)}, u32[]{:S(2)}) collective-permute-start(bf16[69,20,2]{0,2,1:T(2,128)(2,1)S(1)} %get-tuple-element.23), channel_id=1, source_target_pairs={{1,0},{2,1},{3,2},{0,3},{5,4},{6,5},{7,6},{4,7},{9,8},{10,9},{11,1... | collective-permute-start | bytes 16568 | tf_op jit(solution)/shard_map/ppermute | solution.py:26
  30.6 7.6 %collective-permute-start.10 = (bf16[2,128,256]{2,1,0:T(8,128)(2,1)}, bf16[2,128,256]{2,1,0:T(8,128)(2,1)S(1)}, u32[]{:S(2)}, u32[]{:S(2)}) collective-permute-start(bf16[2,128,256]{2,1,0:T(8,128)(2,1)} %get-tuple-element.36), channel_id=1, source_target_pairs={{0,3},{1,0},{2,1},{3,2},{4,7},{5,4},{6,5},{7,6},{8,11},{9,8},{10,9... | collective-permute-start | bytes 393224 | tf_op jit(solution)/shard_map/ppermute | solution.py:113
  34.4 8.3 %collective-permute-start.8 = (bf16[2,128,256]{2,1,0:T(8,128)(2,1)}, bf16[2,128,256]{2,1,0:T(8,128)(2,1)}, u32[]{:S(2)}, u32[]{:S(2)}) collective-permute-start(bf16[2,128,256]{2,1,0:T(8,128)(2,1)} %get-tuple-element.34), channel_id=1, source_target_pairs={{0,1},{1,2},{2,3},{3,0},{4,5},{5,6},{6,7},{7,4},{8,9},{9,10},{10,1... | collective-permute-start | bytes 393224 | tf_op jit(solution)/shard_map/ppermute | solution.py:113
  34.4 12.7 %collective-permute-start.9 = (bf16[2,128,256]{2,1,0:T(8,128)(2,1)S(1)}, bf16[2,128,256]{2,1,0:T(8,128)(2,1)}, u32[]{:S(2)}, u32[]{:S(2)}) collective-permute-start(bf16[2,128,256]{2,1,0:T(8,128)(2,1)S(1)} %get-tuple-element.35), channel_id=1, source_target_pairs={{0,2},{1,3},{2,0},{3,1},{4,6},{5,7},{6,4},{7,5},{8,10},{9,11},{10,... | collective-permute-start | bytes 393224 | tf_op jit(solution)/shard_map/ppermute | solution.py:113
  48.9 9.5 %collective-permute-start.11 = (bf16[2,512,128]{2,1,0:T(8,128)(2,1)S(1)}, bf16[2,512,128]{2,1,0:T(8,128)(2,1)S(1)}, u32[]{:S(2)}, u32[]{:S(2)}) collective-permute-start(bf16[2,512,128]{2,1,0:T(8,128)(2,1)S(1)} %get-tuple-element.32), channel_id=1, source_target_pairs={{0,4},{4,0},{8,12},{12,8},{16,20},{20,16},{24,28},{28,24},{1,5},{5... | collective-permute-start | bytes 786440 | tf_op jit(solution)/shard_map/ppermute | solution.py:191
  49.6 14.3 %copy-start.13 = (f32[16]{0:T(128)S(1)}, f32[16]{0:T(128)}, u32[]{:S(2)}) copy-start(f32[16]{0:T(128)} %param.27) | copy-start | bytes 196
  49.7 6.9 %collective-permute-start.4 = (bf16[128,256]{1,0:T(8,128)(2,1)S(1)}, bf16[128,256]{1,0:T(8,128)(2,1)S(1)}, u32[]{:S(2)}, u32[]{:S(2)}) collective-permute-start(bf16[128,256]{1,0:T(8,128)(2,1)S(1)} %bitcast.260), channel_id=1, source_target_pairs={{0,1},{1,2},{2,3},{3,0},{4,5},{5,6},{6,7},{7,4},{8,9},{9,10},{10,1... | collective-permute-start | bytes 196616 | tf_op jit(solution)/shard_map/ppermute | solution.py:113
  49.7 8.6 %collective-permute-start.5 = (bf16[128,256]{1,0:T(8,128)(2,1)S(1)}, bf16[128,256]{1,0:T(8,128)(2,1)S(1)}, u32[]{:S(2)}, u32[]{:S(2)}) collective-permute-start(bf16[128,256]{1,0:T(8,128)(2,1)S(1)} %bitcast.261), channel_id=1, source_target_pairs={{0,2},{1,3},{2,0},{3,1},{4,6},{5,7},{6,4},{7,5},{8,10},{9,11},{10,... | collective-permute-start | bytes 196616 | tf_op jit(solution)/shard_map/ppermute | solution.py:113
  52.4 6.0 %collective-permute-start.6 = (bf16[128,256]{1,0:T(8,128)(2,1)S(1)}, bf16[128,256]{1,0:T(8,128)(2,1)S(1)}, u32[]{:S(2)}, u32[]{:S(2)}) collective-permute-start(bf16[128,256]{1,0:T(8,128)(2,1)S(1)} %bitcast.262), channel_id=1, source_target_pairs={{0,3},{1,0},{2,1},{3,2},{4,7},{5,4},{6,5},{7,6},{8,11},{9,8},{10,9... | collective-permute-start | bytes 196616 | tf_op jit(solution)/shard_map/ppermute | solution.py:113
  59.2 16.2 %collective-permute-start.12 = (bf16[2,1024,128]{2,1,0:T(8,128)(2,1)}, bf16[2,1024,128]{2,1,0:T(8,128)(2,1)}, u32[]{:S(2)}, u32[]{:S(2)}) collective-permute-start(bf16[2,1024,128]{2,1,0:T(8,128)(2,1)} %pad_maximum_fusion.5), channel_id=1, source_target_pairs={{0,8},{4,12},{8,0},{12,4},{16,24},{20,28},{24,16},{28,20},{1,9},{5... | collective-permute-start | bytes 1572872 | tf_op jit(solution)/shard_map/ppermute | solution.py:195
  62.3 24.1 %collective-permute-start.13 = (bf16[2,1024,128]{2,1,0:T(8,128)(2,1)}, bf16[2,1024,128]{2,1,0:T(8,128)(2,1)}, u32[]{:S(2)}, u32[]{:S(2)}) collective-permute-start(bf16[2,1024,128]{2,1,0:T(8,128)(2,1)} %pad_maximum_fusion.5), channel_id=1, source_target_pairs={{0,16},{4,20},{8,24},{12,28},{16,0},{20,4},{24,8},{28,12},{1,17},{... | collective-permute-start | bytes 1572872 | tf_op jit(solution)/shard_map/ppermute | solution.py:195
  62.3 1.7 %collective-permute-start.7 = (bf16[512,128]{1,0:T(8,128)(2,1)S(1)}, bf16[512,128]{1,0:T(8,128)(2,1)S(1)}, u32[]{:S(2)}, u32[]{:S(2)}) collective-permute-start(bf16[512,128]{1,0:T(8,128)(2,1)S(1)} %get-tuple-element.45), channel_id=1, source_target_pairs={{0,4},{4,0},{8,12},{12,8},{16,20},{20,16},{24,28},{28,24},{1,5},{5... | collective-permute-start | bytes 393224 | tf_op jit(solution)/shard_map/ppermute | solution.py:191
  62.4 25.9 %collective-permute-start.14 = (bf16[2,1024,128]{2,1,0:T(8,128)(2,1)}, bf16[2,1024,128]{2,1,0:T(8,128)(2,1)S(1)}, u32[]{:S(2)}, u32[]{:S(2)}) collective-permute-start(bf16[2,1024,128]{2,1,0:T(8,128)(2,1)} %pad_maximum_fusion.5), channel_id=1, source_target_pairs={{0,24},{4,28},{8,16},{12,20},{16,8},{20,12},{24,0},{28,4},{1,25},{... | collective-permute-start | bytes 1572872 | tf_op jit(solution)/shard_map/ppermute | solution.py:195
  106.0 1.4 collective-permute-start.15
  107.5 6.1 %collective-permute-start.16 = (bf16[128,256]{1,0:T(8,128)(2,1)S(1)}, bf16[128,256]{1,0:T(8,128)(2,1)S(1)}, u32[]{:S(2)}, u32[]{:S(2)}) collective-permute-start(bf16[128,256]{1,0:T(8,128)(2,1)S(1)} %get-tuple-element.41), channel_id=1, source_target_pairs={{1,0},{2,1},{3,2},{0,3},{5,4},{6,5},{7,6},{4,7},{9,8},{10,9},{11,1... | collective-permute-start | bytes 196616 | tf_op jit(solution)/shard_map/ppermute | solution.py:121
  111.1 6.6 %collective-permute-start.17 = (bf16[128,256]{1,0:T(8,128)(2,1)S(1)}, bf16[128,256]{1,0:T(8,128)(2,1)S(1)}, u32[]{:S(2)}, u32[]{:S(2)}) collective-permute-start(bf16[128,256]{1,0:T(8,128)(2,1)S(1)} %get-tuple-element.40), channel_id=1, source_target_pairs={{2,0},{3,1},{0,2},{1,3},{6,4},{7,5},{4,6},{5,7},{10,8},{11,9},{8,1... | collective-permute-start | bytes 196616 | tf_op jit(solution)/shard_map/ppermute | solution.py:121
  111.1 6.6 %collective-permute-start.18 = (bf16[128,256]{1,0:T(8,128)(2,1)S(1)}, bf16[128,256]{1,0:T(8,128)(2,1)S(1)}, u32[]{:S(2)}, u32[]{:S(2)}) collective-permute-start(bf16[128,256]{1,0:T(8,128)(2,1)S(1)} %get-tuple-element.39), channel_id=1, source_target_pairs={{3,0},{0,1},{1,2},{2,3},{7,4},{4,5},{5,6},{6,7},{11,8},{8,9},{9,10... | collective-permute-start | bytes 196616 | tf_op jit(solution)/shard_map/ppermute | solution.py:121
  124.1 2.6 %collective-permute-start.19 = (bf16[128,1,128]{2,0,1:T(8,128)(2,1)S(1)}, bf16[128,1,128]{2,0,1:T(8,128)(2,1)S(1)}, u32[]{:S(2)}, u32[]{:S(2)}) collective-permute-start(bf16[128,1,128]{2,0,1:T(8,128)(2,1)S(1)} %get-tuple-element.30), channel_id=1, source_target_pairs={{0,4},{4,8},{8,12},{12,16},{16,20},{20,24},{24,28},{1,5},{5,9},{9,... | collective-permute-start | bytes 98312 | tf_op jit(solution)/shard_map/ppermute | solution.py:20
  125.4 3.6 %collective-permute-start.20 = (bf16[128,1,128]{2,0,1:T(8,128)(2,1)S(1)}, bf16[128,1,128]{2,0,1:T(8,128)(2,1)S(1)}, u32[]{:S(2)}, u32[]{:S(2)}) collective-permute-start(bf16[128,1,128]{2,0,1:T(8,128)(2,1)S(1)} %get-tuple-element.31), channel_id=1, source_target_pairs={{4,0},{8,4},{12,8},{16,12},{20,16},{24,20},{28,24},{5,1},{9,5},{13... | collective-permute-start | bytes 98312 | tf_op jit(solution)/shard_map/ppermute | solution.py:21
  131.7 7.6 %collective-permute-start.21 = (bf16[128,18,1]{0,1,2:T(8,128)(2,1)S(1)}, bf16[128,18,1]{0,1,2:T(8,128)(2,1)S(1)}, u32[]{:S(2)}, u32[]{:S(2)}) collective-permute-start(bf16[128,18,1]{0,1,2:T(8,128)(2,1)S(1)} %copy.71), channel_id=1, source_target_pairs={{0,1},{1,2},{2,3},{3,0},{4,5},{5,6},{6,7},{7,4},{8,9},{9,10},{10,1... | collective-permute-start | bytes 13832 | tf_op jit(solution)/shard_map/ppermute | solution.py:25
  133.4 7.0 %collective-permute-start.22 = (bf16[128,18,1]{0,1,2:T(8,128)(2,1)S(1)}, bf16[128,18,1]{0,1,2:T(8,128)(2,1)S(1)}, u32[]{:S(2)}, u32[]{:S(2)}) collective-permute-start(bf16[128,18,1]{0,1,2:T(8,128)(2,1)S(1)} %copy.74), channel_id=1, source_target_pairs={{1,0},{2,1},{3,2},{0,3},{5,4},{6,5},{7,6},{4,7},{9,8},{10,9},{11,1... | collective-permute-start | bytes 13832 | tf_op jit(solution)/shard_map/ppermute | solution.py:26
  146.6 18.7 %copy-start.14 = (s32[64]{0:T(128)S(1)}, s32[64]{0:T(128)}, u32[]{:S(2)}) copy-start(s32[64]{0:T(128)} %param.18) | copy-start | bytes 772
  147.6 3.6 %collective-permute-start.23 = (f32[64]{0:T(128)S(1)}, f32[64]{0:T(128)S(1)}, u32[]{:S(2)}, u32[]{:S(2)}) collective-permute-start(f32[64]{0:T(128)S(1)} %fusion.40), channel_id=1, source_target_pairs={{0,1},{1,0},{2,3},{3,2},{4,5},{5,4},{6,7},{7,6},{8,9},{9,8},{10,11... | collective-permute-start | bytes 776 | tf_op jit(solution)/shard_map/ppermute | solution.py:34
  151.2 4.4 %collective-permute-start.24 = (f32[64]{0:T(128)S(1)}, f32[64]{0:T(128)S(1)}, u32[]{:S(2)}, u32[]{:S(2)}) collective-permute-start(f32[64]{0:T(128)S(1)} %add.298), channel_id=1, source_target_pairs={{0,2},{1,3},{2,0},{3,1},{4,6},{5,7},{6,4},{7,5},{8,10},{9,11},{10,... | collective-permute-start | bytes 776 | tf_op jit(solution)/shard_map/ppermute | solution.py:34
  155.6 1.1 collective-permute-start.25
  156.8 4.0 %collective-permute-start.26 = (f32[64]{0:T(128)S(1)}, f32[64]{0:T(128)S(1)}, u32[]{:S(2)}, u32[]{:S(2)}) collective-permute-start(f32[64]{0:T(128)S(1)} %add.300), channel_id=1, source_target_pairs={{0,8},{4,12},{8,0},{12,4},{16,24},{20,28},{24,16},{28,20},{1,9},{5... | collective-permute-start | bytes 776 | tf_op jit(solution)/shard_map/ppermute | solution.py:34
  160.8 4.5 %collective-permute-start.27 = (f32[64]{0:T(128)S(1)}, f32[64]{0:T(128)S(1)}, u32[]{:S(2)}, u32[]{:S(2)}) collective-permute-start(f32[64]{0:T(128)S(1)} %add.301), channel_id=1, source_target_pairs={{0,16},{4,20},{8,24},{12,28},{16,0},{20,4},{24,8},{28,12},{1,17},{... | collective-permute-start | bytes 776 | tf_op jit(solution)/shard_map/ppermute | solution.py:34
  (12 other events, 21.4 us)

commit v7 on v6

--- a/solution.py
+++ b/solution.py
@@ -57,51 +57,84 @@
     return jnp.cos(math.pi * ((row_index + 0.5) / rows_total - 0.5))
 
 
-def attention_kernel(scale_ref, q_ref, k_ref, v_ref, o_ref, *, head_size):
+def attention_kernel(scale_ref, q_ref, *refs, head_size, chunk_count):
+    key_refs, value_refs = refs[:chunk_count], refs[chunk_count : 2 * chunk_count]
+    o_ref, m_ref, l_ref = refs[2 * chunk_count :]
     queries = q_ref[...]
-    keys = k_ref[...]
-    values = v_ref[...]
     column_head = lax.broadcasted_iota(jnp.int32, queries.shape, 1) // head_size
     total = jnp.zeros(queries.shape, jnp.float32)
+    maxima = jnp.zeros(queries.shape, jnp.float32)
+    sums = jnp.zeros(queries.shape, jnp.float32)
     for head in range(queries.shape[1] // head_size):
         in_head = column_head == head
         masked = jnp.where(in_head, queries, jnp.zeros_like(queries))
-        scores = lax.dot_general(
-            masked, keys, (((1,), (1,)), ((), ())), preferred_element_type=jnp.float32
-        ) * scale_ref[head]
-        row_max = jnp.max(scores, axis=1, keepdims=True)
-        weights = jnp.exp(scores - row_max)
-        weight_sum = jnp.sum(weights, axis=1, keepdims=True)
-        weighted = jnp.dot(
-            weights.astype(jnp.bfloat16), values, preferred_element_type=jnp.float32
+        scores = [
+            lax.dot_general(
+                masked, key_ref[...], (((1,), (1,)), ((), ())), preferred_element_type=jnp.float32
+            )
+            * scale_ref[head]
+            for key_ref in key_refs
+        ]
+        row_max = functools.reduce(
+            jnp.maximum, [jnp.max(score, axis=1, keepdims=True) for score in scores]
         )
-        total = jnp.where(in_head, weighted / weight_sum, total)
-    o_ref[...] = total.astype(o_ref.dtype)
-
-
-def attend(queries, keys, values, scales, head_size):
+        weighted = None
+        weight_sum = None
+        for score, value_ref in zip(scores, value_refs):
+            weights = jnp.exp(score - row_max)
+            chunk_sum = jnp.sum(weights, axis=1, keepdims=True)
+            chunk_weighted = jnp.dot(
+                weights.astype(jnp.bfloat16), value_ref[...], preferred_element_type=jnp.float32
+            )
+            weight_sum = chunk_sum if weight_sum is None else weight_sum + chunk_sum
+            weighted = chunk_weighted if weighted is None else weighted + chunk_weighted
+        total = jnp.where(in_head, weighted, total)
+        maxima = jnp.where(in_head, row_max, maxima)
+        sums = jnp.where(in_head, weight_sum, sums)
+    o_ref[...] = total
+    m_ref[...] = maxima
+    l_ref[...] = sums
+
+
+def attend_part(queries, key_chunks, value_chunks, scales, head_size):
     query_count, width = queries.shape
-    key_count = keys.shape[0]
-    block = math.gcd(query_count, max(8, (1 << 20) // key_count))
+    key_count = sum(chunk.shape[0] for chunk in key_chunks)
+    cap = 1 << (max(8, (1 << 20) // key_count).bit_length() - 1)
+    block = math.gcd(query_count, cap)
     heads = width // head_size
+    part = jax.ShapeDtypeStruct((query_count, width), jnp.float32)
+    part_spec = pl.BlockSpec((block, width), lambda i: (i, 0))
+    chunk_specs = [
+        pl.BlockSpec((chunk.shape[0], width), lambda i: (0, 0))
+        for chunk in list(key_chunks) + list(value_chunks)
+    ]
     return pl.pallas_call(
-        functools.partial(attention_kernel, head_size=head_size),
-        out_shape=jax.ShapeDtypeStruct((query_count, width), jnp.bfloat16),
+        functools.partial(attention_kernel, head_size=head_size, chunk_count=len(key_chunks)),
+        out_shape=(part, part, part),
         grid=(query_count // block,),
         in_specs=[
             pl.BlockSpec(memory_space=pltpu.SMEM),
             pl.BlockSpec((block, width), lambda i: (i, 0)),
-            pl.BlockSpec((key_count, width), lambda i: (0, 0)),
-            pl.BlockSpec((key_count, width), lambda i: (0, 0)),
-        ],
-        out_specs=pl.BlockSpec((block, width), lambda i: (i, 0)),
+        ]
+        + chunk_specs,
+        out_specs=(part_spec, part_spec, part_spec),
         compiler_params=pltpu.CompilerParams(vmem_limit_bytes=48 * 1024 * 1024),
         cost_estimate=pl.CostEstimate(
             flops=4 * query_count * key_count * width,
             transcendentals=query_count * key_count * heads,
-            bytes_accessed=2 * (2 * query_count * width + 2 * key_count * width),
+            bytes_accessed=2 * (query_count * width + 2 * key_count * width)
+            + 12 * query_count * width,
         ),
-    )(scales, queries, keys, values)
+    )(scales, queries, *key_chunks, *value_chunks)
+
+
+def merge_parts(first, second):
+    total_a, max_a, sum_a = first
+    total_b, max_b, sum_b = second
+    joint = jnp.maximum(max_a, max_b)
+    rescale_a, rescale_b = jnp.exp(max_a - joint), jnp.exp(max_b - joint)
+    total = total_a * rescale_a + total_b * rescale_b
+    return (total / (sum_a * rescale_a + sum_b * rescale_b)).astype(jnp.bfloat16)
 
 
 def exchange_blocks(blocks, axis):
@@ -191,17 +224,23 @@
         return jnp.concatenate([mine, lax.ppermute(theirs, "lat", partner)], axis=-2)
 
     key_value = with_partner(jnp.stack([key_spread, value_spread]))
-    chunks = [key_value] + [
+    remote_chunks = [
         lax.ppermute(key_value, "lat", [(i, i ^ (2 * d)) for i in range(lat_size)])
         for d in range(1, lat_size // 2)
     ]
-    all_key_value = jnp.concatenate(chunks, axis=1)
     pair_queries = with_partner(query_spread)
     local_heads = half // head_size
     head_first = (lax.axis_index("lon") * 2 + core) * local_heads
     scales = lax.dynamic_slice_in_dim(head_scale, head_first, local_heads) / math.sqrt(head_size)
-    pair_attended = attend(
-        pair_queries, all_key_value[0], all_key_value[1], scales, head_size
+    pair_attended = merge_parts(
+        attend_part(pair_queries, [key_value[0]], [key_value[1]], scales, head_size),
+        attend_part(
+            pair_queries,
+            [chunk[0] for chunk in remote_chunks],
+            [chunk[1] for chunk in remote_chunks],
+            scales,
+            head_size,
+        ),
     )
     token_count = query_spread.shape[0]
     own_part = pair_attended[:token_count]

time: 167 us -> 148 us (0.89)
  local copies, waits for them, and re-layouts: 22.2 us -> 11.6 us
  waiting for transfers between devices: 61.9 us -> 56.5 us
  matrix products: 21 us -> 17.7 us
  starting transfers between devices: 38.3 us -> 41.4 us
  other arithmetic: 6.21 us -> 3.16 us
    unnamed x48 -> x45, local copies, waits for them, and re-layouts: 11.8 us -> 6.44 us
    ppermute x3, waiting for transfers between devices: 19.7 us -> 14.9 us  [on_device(): lax.ppermute(key_value, 'lat', [(i, i ^ 2 * d) for i in range(lat_size)])]
    ppermute x5, waiting for transfers between devices: 10.7 us -> 8.07 us  [butterfly_sum(): value = value + lax.ppermute(value, axis, partner)]
    ppermute x5, starting transfers between devices: 6.22 us -> 8.38 us  [butterfly_sum(): value = value + lax.ppermute(value, axis, partner)]
    slice x2, local copies, waits for them, and re-layouts: 2.62 us -> 0.57 us  [halo_padded(): from_left = lax.ppermute(array[:, :, -width:], 'lon', right)]
    pallas_call x1 -> x2, Pallas kernels: 15.1 us -> 16.2 us  [attend_part(): pl.pallas_call(functools.partial(attention_kernel, head_size=head_size, c...]
  transfers between devices with their start and end apart: 28 -> 28, of which waited for: 18 -> 20; matrix products, arithmetic and copies ran while one was open for 7% -> 3% of each run, Pallas kernels for 0% -> 3%
where the time goes in v7:
time: 148 us
  waiting for transfers between devices  56.5 us (38%)
  starting transfers between devices  41.4 us (28%)
  matrix products  17.7 us (12%)
  Pallas kernels  16.2 us (11%)
  local copies, waits for them, and re-layouts  11.6 us (8%)
  other arithmetic  3.16 us (2%)
    ppermute x6, waiting for transfers between devices, exchange_blocks(): lax.ppermute(outgoing, axis, [(i, (i + shift) % size) for i in range(size)])  16.2 us
    pallas_call x2, Pallas kernels, attend_part(): pl.pallas_call(functools.partial(attention_kernel, head_size=head_size, c...  16.2 us
    ppermute x3, waiting for transfers between devices, on_device(): lax.ppermute(key_value, 'lat', [(i, i ^ 2 * d) for i in range(lat_size)])  14.9 us
    dot_general x27, matrix products, convolution_kernel_taps(): jnp.einsum('oc,cyx->oyx', weight[tap_index], window, preferred_element_ty...  10.8 us
    ppermute x6, starting transfers between devices, exchange_blocks(): lax.ppermute(outgoing, axis, [(i, (i + shift) % size) for i in range(size)])  8.74 us
    ppermute x5, starting transfers between devices, butterfly_sum(): value = value + lax.ppermute(value, axis, partner)  8.38 us
    ppermute x5, waiting for transfers between devices, butterfly_sum(): value = value + lax.ppermute(value, axis, partner)  8.07 us
    ppermute x2, waiting for transfers between devices, halo_padded(): from_below = lax.ppermute(array[:, :width], 'lat', up)  7.78 us
  transfers between devices with their start and end apart: 28, of which 20 were waited for; matrix products, arithmetic and copies ran while one was open for 3% of the time, Pallas kernels for 3%

profile of v7, /device:TPU:0, one launch (start us, length us, event | category | flops | bytes accessed | tf_op | source)
XLA Modules:
  0.0 147.8 jit_solution(14770764563338774719)
XLA Ops:
  0.6 1.5 %copy.55 = bf16[69,16,128]{0,2,1:T(8,128)(2,1)S(1)} copy(bf16[69,16,128]{2,1,0:T(8,128)(2,1)} %param.15) | data formatting | bytes 565248 | tf_op args[0]
  2.2 2.5 %collective-permute-start = (bf16[69,2,128]{0,2,1:T(8,128)(2,1)S(1)}, bf16[69,2,128]{0,2,1:T(8,128)(2,1)S(1)}, u32[]{:S(2)}, u32[]{:S(2)}) collective-permute-start(bf16[69,2,128]{0,2,1:T(8,128)(2,1)S(1)} %get-tuple-element.54), channel_id=1, source_target_pairs={{0,4},{4,8},{8,12},{12,16},{16,20},{20,24},{24,28},{1,5},{5,9},{9,... | collective-permute-start | bytes 105992 | tf_op jit(solution)/shard_map/ppermute | solution.py:20
  6.0 3.9 %collective-permute-done.1 = bf16[69,2,128]{0,2,1:T(8,128)(2,1)S(1)} collective-permute-done((bf16[69,2,128]{0,2,1:T(8,128)(2,1)S(1)}, bf16[69,2,128]{0,2,1:T(8,128)(2,1)S(1)}, u32[]{:S(2)}, u32[]{:S(2)}) %collective-permute-start.1) | collective-permute-done | bytes 35360 | tf_op jit(solution)/shard_map/ppermute | solution.py:21
  9.9 1.6 %collective-permute-start.2 = (bf16[69,20,2]{0,2,1:T(2,128)(2,1)S(1)}, bf16[69,20,2]{0,2,1:T(2,128)(2,1)S(1)}, u32[]{:S(2)}, u32[]{:S(2)}) collective-permute-start(bf16[69,20,2]{0,2,1:T(2,128)(2,1)S(1)} %get-tuple-element.30), channel_id=1, source_target_pairs={{0,1},{1,2},{2,3},{3,0},{4,5},{5,6},{6,7},{7,4},{8,9},{9,10},{10,1... | collective-permute-start | bytes 16568 | tf_op jit(solution)/shard_map/ppermute | solution.py:25
  11.6 2.2 %collective-permute-start.3 = (bf16[69,20,2]{0,2,1:T(2,128)(2,1)S(1)}, bf16[69,20,2]{0,2,1:T(2,128)(2,1)S(1)}, u32[]{:S(2)}, u32[]{:S(2)}) collective-permute-start(bf16[69,20,2]{0,2,1:T(2,128)(2,1)S(1)} %get-tuple-element.31), channel_id=1, source_target_pairs={{1,0},{2,1},{3,2},{0,3},{5,4},{6,5},{7,6},{4,7},{9,8},{10,9},{11,1... | collective-permute-start | bytes 16568 | tf_op jit(solution)/shard_map/ppermute | solution.py:26
  13.8 1.6 %collective-permute-done.2 = bf16[69,20,2]{0,2,1:T(2,128)(2,1)S(1)} collective-permute-done((bf16[69,20,2]{0,2,1:T(2,128)(2,1)S(1)}, bf16[69,20,2]{0,2,1:T(2,128)(2,1)S(1)}, u32[]{:S(2)}, u32[]{:S(2)}) %collective-permute-start.2) | collective-permute-done | bytes 5552 | tf_op jit(solution)/shard_map/ppermute | solution.py:25
  29.9 3.9 %collective-permute-start.10 = (bf16[2,128,256]{2,1,0:T(8,128)(2,1)S(1)}, bf16[2,128,256]{2,1,0:T(8,128)(2,1)S(1)}, u32[]{:S(2)}, u32[]{:S(2)}) collective-permute-start(bf16[2,128,256]{2,1,0:T(8,128)(2,1)S(1)} %get-tuple-element.53), channel_id=1, source_target_pairs={{0,3},{1,0},{2,1},{3,2},{4,7},{5,4},{6,5},{7,6},{8,11},{9,8},{10,9... | collective-permute-start | bytes 393224 | tf_op jit(solution)/shard_map/ppermute | solution.py:146
  34.6 2.6 %collective-permute-done.10 = bf16[2,128,256]{2,1,0:T(8,128)(2,1)S(1)} collective-permute-done((bf16[2,128,256]{2,1,0:T(8,128)(2,1)S(1)}, bf16[2,128,256]{2,1,0:T(8,128)(2,1)S(1)}, u32[]{:S(2)}, u32[]{:S(2)}) %collective-permute-start.10) | collective-permute-done | bytes 131104 | tf_op jit(solution)/shard_map/ppermute | solution.py:146
  37.2 4.6 %collective-permute-done.8 = bf16[2,128,256]{2,1,0:T(8,128)(2,1)S(1)} collective-permute-done((bf16[2,128,256]{2,1,0:T(8,128)(2,1)S(1)}, bf16[2,128,256]{2,1,0:T(8,128)(2,1)S(1)}, u32[]{:S(2)}, u32[]{:S(2)}) %collective-permute-start.8) | collective-permute-done | bytes 131104 | tf_op jit(solution)/shard_map/ppermute | solution.py:146
  41.7 4.6 %collective-permute-done.9 = bf16[2,128,256]{2,1,0:T(8,128)(2,1)S(1)} collective-permute-done((bf16[2,128,256]{2,1,0:T(8,128)(2,1)S(1)}, bf16[2,128,256]{2,1,0:T(8,128)(2,1)S(1)}, u32[]{:S(2)}, u32[]{:S(2)}) %collective-permute-start.9) | collective-permute-done | bytes 131104 | tf_op jit(solution)/shard_map/ppermute | solution.py:146
  47.3 2.4 %collective-permute-start.5 = (bf16[128,256]{1,0:T(8,128)(2,1)S(1)}, bf16[128,256]{1,0:T(8,128)(2,1)S(1)}, u32[]{:S(2)}, u32[]{:S(2)}) collective-permute-start(bf16[128,256]{1,0:T(8,128)(2,1)S(1)} %bitcast.273), channel_id=1, source_target_pairs={{0,2},{1,3},{2,0},{3,1},{4,6},{5,7},{6,4},{7,5},{8,10},{9,11},{10,... | collective-permute-start | bytes 196616 | tf_op jit(solution)/shard_map/ppermute | solution.py:146
  49.8 1.7 %collective-permute-start.6 = (bf16[128,256]{1,0:T(8,128)(2,1)S(1)}, bf16[128,256]{1,0:T(8,128)(2,1)S(1)}, u32[]{:S(2)}, u32[]{:S(2)}) collective-permute-start(bf16[128,256]{1,0:T(8,128)(2,1)S(1)} %bitcast.274), channel_id=1, source_target_pairs={{0,3},{1,0},{2,1},{3,2},{4,7},{5,4},{6,5},{7,6},{8,11},{9,8},{10,9... | collective-permute-start | bytes 196616 | tf_op jit(solution)/shard_map/ppermute | solution.py:146
  51.5 2.6 %collective-permute-done.4 = bf16[128,256]{1,0:T(8,128)(2,1)S(1)} collective-permute-done((bf16[128,256]{1,0:T(8,128)(2,1)S(1)}, bf16[128,256]{1,0:T(8,128)(2,1)S(1)}, u32[]{:S(2)}, u32[]{:S(2)}) %collective-permute-start.4) | collective-permute-done | bytes 65568 | tf_op jit(solution)/shard_map/ppermute | solution.py:146
  54.1 1.8 %collective-permute-done.5 = bf16[128,256]{1,0:T(8,128)(2,1)S(1)} collective-permute-done((bf16[128,256]{1,0:T(8,128)(2,1)S(1)}, bf16[128,256]{1,0:T(8,128)(2,1)S(1)}, u32[]{:S(2)}, u32[]{:S(2)}) %collective-permute-start.5) | collective-permute-done | bytes 65568 | tf_op jit(solution)/shard_map/ppermute | solution.py:146
  56.9 4.0 %collective-permute-start.13 = (bf16[2,1024,128]{2,1,0:T(8,128)(2,1)S(1)}, bf16[2,1024,128]{2,1,0:T(8,128)(2,1)S(1)}, u32[]{:S(2)}, u32[]{:S(2)}) collective-permute-start(bf16[2,1024,128]{2,1,0:T(8,128)(2,1)S(1)} %pad_maximum_fusion.3), channel_id=1, source_target_pairs={{0,16},{4,20},{8,24},{12,28},{16,0},{20,4},{24,8},{28,12},{1,17},{... | collective-permute-start | bytes 1572872 | tf_op jit(solution)/shard_map/ppermute | solution.py:228
  61.2 4.5 %shard_map.166 = (f32[1024,128]{1,0:T(8,128)S(1)}, f32[1024,128]{1,0:T(8,128)S(1)}, f32[1024,128]{1,0:T(8,128)S(1)}) custom-call(f32[2]{0:T(128)S(1)} %dynamic-slice_multiply_fusion.scale_ref, bf16[1024,128]{1,0:T(8,128)(2,1)S(1)} %pad_maximum_fusion.7.q_ref, bf16[1024,128]{1,0:T(8,128)(2,1)S(1)} %get-tuple-element.41.refs_0_, ...), custom_call_target="tpu_custom_call" | custom-call | flops 536870912 | bytes 2359296 | tf_op jit(solution)/shard_map/pallas_call | solution.py:111
  65.7 6.3 %collective-permute-done.14 = bf16[2,1024,128]{2,1,0:T(8,128)(2,1)} collective-permute-done((bf16[2,1024,128]{2,1,0:T(8,128)(2,1)S(1)}, bf16[2,1024,128]{2,1,0:T(8,128)(2,1)}, u32[]{:S(2)}, u32[]{:S(2)}) %collective-permute-start.14) | collective-permute-done | bytes 524320 | tf_op jit(solution)/shard_map/ppermute | solution.py:228
  73.1 7.9 %collective-permute-done.13 = bf16[2,1024,128]{2,1,0:T(8,128)(2,1)S(1)} collective-permute-done((bf16[2,1024,128]{2,1,0:T(8,128)(2,1)S(1)}, bf16[2,1024,128]{2,1,0:T(8,128)(2,1)S(1)}, u32[]{:S(2)}, u32[]{:S(2)}) %collective-permute-start.13) | collective-permute-done | bytes 524320 | tf_op jit(solution)/shard_map/ppermute | solution.py:228
  81.8 11.6 %shard_map.167 = (f32[1024,128]{1,0:T(8,128)S(1)}, f32[1024,128]{1,0:T(8,128)S(1)}, f32[1024,128]{1,0:T(8,128)S(1)}) custom-call(f32[2]{0:T(128)S(1)} %dynamic-slice_multiply_fusion.scale_ref, bf16[1024,128]{1,0:T(8,128)(2,1)S(1)} %pad_maximum_fusion.7.q_ref, bf16[1024,128]{1,0:T(8,128)(2,1)S(1)} %get-tuple-element.47.refs_0_, ...), custom_call_target="tpu_custom_call" | custom-call | flops 1610612736 | bytes 3407872 | tf_op jit(solution)/shard_map/pallas_call | solution.py:111
  95.3 4.0 %collective-permute-start.16 = (bf16[128,256]{1,0:T(8,128)(2,1)S(1)}, bf16[128,256]{1,0:T(8,128)(2,1)S(1)}, u32[]{:S(2)}, u32[]{:S(2)}) collective-permute-start(bf16[128,256]{1,0:T(8,128)(2,1)S(1)} %get-tuple-element.58), channel_id=1, source_target_pairs={{1,0},{2,1},{3,2},{0,3},{5,4},{6,5},{7,6},{4,7},{9,8},{10,9},{11,1... | collective-permute-start | bytes 196616 | tf_op jit(solution)/shard_map/ppermute | solution.py:154
  100.0 1.8 %collective-permute-done.16 = bf16[128,256]{1,0:T(8,128)(2,1)S(1)} collective-permute-done((bf16[128,256]{1,0:T(8,128)(2,1)S(1)}, bf16[128,256]{1,0:T(8,128)(2,1)S(1)}, u32[]{:S(2)}, u32[]{:S(2)}) %collective-permute-start.16) | collective-permute-done | bytes 65568 | tf_op jit(solution)/shard_map/ppermute | solution.py:154
  101.8 4.1 %collective-permute-done.17 = bf16[128,256]{1,0:T(8,128)(2,1)S(1)} collective-permute-done((bf16[128,256]{1,0:T(8,128)(2,1)S(1)}, bf16[128,256]{1,0:T(8,128)(2,1)S(1)}, u32[]{:S(2)}, u32[]{:S(2)}) %collective-permute-start.17) | collective-permute-done | bytes 65568 | tf_op jit(solution)/shard_map/ppermute | solution.py:154
  106.7 3.4 %fusion.58 = bf16[128,4,4,32,4]{0,3,4,2,1:T(8,128)(2,1)S(1)} fusion(bf16[4,32,1024,1,1]{2,1,4,3,0:T(8,128)(2,1)S(1)} %bitcast.270, bf16[1024,4,4,128]{3,2,1,0:T(4,128)(2,1)} %param.28), kind=kOutput, calls=%fused_computation.74 | convolution fusion | flops 539230208 | bytes 4980736 | tf_op jit(solution)/shard_map/pqd,dabh->hpaqb/dot_general | solution.py:263
  113.4 3.8 %collective-permute-done.20 = bf16[128,1,128]{2,0,1:T(8,128)(2,1)S(1)} collective-permute-done((bf16[128,1,128]{2,0,1:T(8,128)(2,1)S(1)}, bf16[128,1,128]{2,0,1:T(8,128)(2,1)S(1)}, u32[]{:S(2)}, u32[]{:S(2)}) %collective-permute-start.20) | collective-permute-done | bytes 32800 | tf_op jit(solution)/shard_map/ppermute | solution.py:21
  118.4 3.8 %collective-permute-start.22 = (bf16[128,18,1]{0,1,2:T(8,128)(2,1)S(1)}, bf16[128,18,1]{0,1,2:T(8,128)(2,1)S(1)}, u32[]{:S(2)}, u32[]{:S(2)}) collective-permute-start(bf16[128,18,1]{0,1,2:T(8,128)(2,1)S(1)} %copy.74), channel_id=1, source_target_pairs={{1,0},{2,1},{3,2},{0,3},{5,4},{6,5},{7,6},{4,7},{9,8},{10,9},{11,1... | collective-permute-start | bytes 13832 | tf_op jit(solution)/shard_map/ppermute | solution.py:26
  124.8 1.8 %maximum_maximum_fusion = (bf16[128,18,129]{2,0,1:T(8,128)(2,1)S(1)}, bf16[128,18,129]{2,0,1:T(8,128)(2,1)S(1)}) fusion(bf16[128,1,128]{2,0,1:T(8,128)(2,1)S(1)} %collective-permute-done.20, bf16[128,16,128]{2,0,1:T(8,128)(2,1)S(1)} %copy.68, bf16[128,1,128]{2,0,1:T(8,128)(2,1)S(1)} %collective-permute-done.19, bf16[128,18,1]{2,0,1:T(8,128)(2,1)S(1)} %copy.72, ...), kind=kLoop, calls=%fused_computation.54 | loop fusion | flops 4755456 | bytes 1787904 | tf_op jit(solution)/shard_map/concatenate | solution.py:27
  130.7 2.8 %collective-permute-done.23 = f32[64]{0:T(128)S(1)} collective-permute-done((f32[64]{0:T(128)S(1)}, f32[64]{0:T(128)S(1)}, u32[]{:S(2)}, u32[]{:S(2)}) %collective-permute-start.23) | collective-permute-done | bytes 288 | tf_op jit(solution)/shard_map/ppermute | solution.py:34
  133.5 2.6 %collective-permute-start.24 = (f32[64]{0:T(128)S(1)}, f32[64]{0:T(128)S(1)}, u32[]{:S(2)}, u32[]{:S(2)}) collective-permute-start(f32[64]{0:T(128)S(1)} %add.306), channel_id=1, source_target_pairs={{0,2},{1,3},{2,0},{3,1},{4,6},{5,7},{6,4},{7,5},{8,10},{9,11},{10,... | collective-permute-start | bytes 776 | tf_op jit(solution)/shard_map/ppermute | solution.py:34
  136.1 1.9 %collective-permute-done.24 = f32[64]{0:T(128)S(1)} collective-permute-done((f32[64]{0:T(128)S(1)}, f32[64]{0:T(128)S(1)}, u32[]{:S(2)}, u32[]{:S(2)}) %collective-permute-start.24) | collective-permute-done | bytes 288 | tf_op jit(solution)/shard_map/ppermute | solution.py:34
  139.1 2.5 %collective-permute-start.26 = (f32[64]{0:T(128)S(1)}, f32[64]{0:T(128)S(1)}, u32[]{:S(2)}, u32[]{:S(2)}) collective-permute-start(f32[64]{0:T(128)S(1)} %add.308), channel_id=1, source_target_pairs={{0,8},{4,12},{8,0},{12,4},{16,24},{20,28},{24,16},{28,20},{1,9},{5... | collective-permute-start | bytes 776 | tf_op jit(solution)/shard_map/ppermute | solution.py:34
  141.6 1.5 %collective-permute-done.26 = f32[64]{0:T(128)S(1)} collective-permute-done((f32[64]{0:T(128)S(1)}, f32[64]{0:T(128)S(1)}, u32[]{:S(2)}, u32[]{:S(2)}) %collective-permute-start.26) | collective-permute-done | bytes 288 | tf_op jit(solution)/shard_map/ppermute | solution.py:34
  143.1 2.5 %collective-permute-start.27 = (f32[64]{0:T(128)S(1)}, f32[64]{0:T(128)S(1)}, u32[]{:S(2)}, u32[]{:S(2)}) collective-permute-start(f32[64]{0:T(128)S(1)} %add.309), channel_id=1, source_target_pairs={{0,16},{4,20},{8,24},{12,28},{16,0},{20,4},{24,8},{28,12},{1,17},{... | collective-permute-start | bytes 776 | tf_op jit(solution)/shard_map/ppermute | solution.py:34
  (152 shorter events, 37.9 us)
Async XLA Ops:
  0.6 25.5 %copy-start = (bf16[1024,1024]{1,0:T(8,128)(2,1)S(1)}, bf16[1024,1024]{1,0:T(8,128)(2,1)}, u32[]{:S(2)}) copy-start(bf16[1024,1024]{1,0:T(8,128)(2,1)} %param.25) | copy-start | bytes 6291460
  2.1 13.6 %copy-start.10 = (bf16[9,128,69]{1,2,0:T(8,128)(2,1)S(1)}, bf16[9,128,69]{1,2,0:T(8,128)(2,1)}, u32[]{:S(2)}) copy-start(bf16[9,128,69]{1,2,0:T(8,128)(2,1)} %param.19) | copy-start | bytes 476932
  2.2 3.8 %collective-permute-start = (bf16[69,2,128]{0,2,1:T(8,128)(2,1)S(1)}, bf16[69,2,128]{0,2,1:T(8,128)(2,1)S(1)}, u32[]{:S(2)}, u32[]{:S(2)}) collective-permute-start(bf16[69,2,128]{0,2,1:T(8,128)(2,1)S(1)} %get-tuple-element.54), channel_id=1, source_target_pairs={{0,4},{4,8},{8,12},{12,16},{16,20},{20,24},{24,28},{1,5},{5,9},{9,... | collective-permute-start | bytes 105992 | tf_op jit(solution)/shard_map/ppermute | solution.py:20
  4.7 5.3 %collective-permute-start.1 = (bf16[69,2,128]{0,2,1:T(8,128)(2,1)S(1)}, bf16[69,2,128]{0,2,1:T(8,128)(2,1)S(1)}, u32[]{:S(2)}, u32[]{:S(2)}) collective-permute-start(bf16[69,2,128]{0,2,1:T(8,128)(2,1)S(1)} %get-tuple-element.55), channel_id=1, source_target_pairs={{4,0},{8,4},{12,8},{16,12},{20,16},{24,20},{28,24},{5,1},{9,5},{13... | collective-permute-start | bytes 105992 | tf_op jit(solution)/shard_map/ppermute | solution.py:21
  9.9 5.5 %collective-permute-start.2 = (bf16[69,20,2]{0,2,1:T(2,128)(2,1)S(1)}, bf16[69,20,2]{0,2,1:T(2,128)(2,1)S(1)}, u32[]{:S(2)}, u32[]{:S(2)}) collective-permute-start(bf16[69,20,2]{0,2,1:T(2,128)(2,1)S(1)} %get-tuple-element.30), channel_id=1, source_target_pairs={{0,1},{1,2},{2,3},{3,0},{4,5},{5,6},{6,7},{7,4},{8,9},{9,10},{10,1... | collective-permute-start | bytes 16568 | tf_op jit(solution)/shard_map/ppermute | solution.py:25
  11.6 3.9 %collective-permute-start.3 = (bf16[69,20,2]{0,2,1:T(2,128)(2,1)S(1)}, bf16[69,20,2]{0,2,1:T(2,128)(2,1)S(1)}, u32[]{:S(2)}, u32[]{:S(2)}) collective-permute-start(bf16[69,20,2]{0,2,1:T(2,128)(2,1)S(1)} %get-tuple-element.31), channel_id=1, source_target_pairs={{1,0},{2,1},{3,2},{0,3},{5,4},{6,5},{7,6},{4,7},{9,8},{10,9},{11,1... | collective-permute-start | bytes 16568 | tf_op jit(solution)/shard_map/ppermute | solution.py:26
  29.9 7.3 %collective-permute-start.10 = (bf16[2,128,256]{2,1,0:T(8,128)(2,1)S(1)}, bf16[2,128,256]{2,1,0:T(8,128)(2,1)S(1)}, u32[]{:S(2)}, u32[]{:S(2)}) collective-permute-start(bf16[2,128,256]{2,1,0:T(8,128)(2,1)S(1)} %get-tuple-element.53), channel_id=1, source_target_pairs={{0,3},{1,0},{2,1},{3,2},{4,7},{5,4},{6,5},{7,6},{8,11},{9,8},{10,9... | collective-permute-start | bytes 393224 | tf_op jit(solution)/shard_map/ppermute | solution.py:146
  33.8 7.9 %collective-permute-start.8 = (bf16[2,128,256]{2,1,0:T(8,128)(2,1)S(1)}, bf16[2,128,256]{2,1,0:T(8,128)(2,1)S(1)}, u32[]{:S(2)}, u32[]{:S(2)}) collective-permute-start(bf16[2,128,256]{2,1,0:T(8,128)(2,1)S(1)} %get-tuple-element.51), channel_id=1, source_target_pairs={{0,1},{1,2},{2,3},{3,0},{4,5},{5,6},{6,7},{7,4},{8,9},{9,10},{10,1... | collective-permute-start | bytes 393224 | tf_op jit(solution)/shard_map/ppermute | solution.py:146
  33.8 12.6 %collective-permute-start.9 = (bf16[2,128,256]{2,1,0:T(8,128)(2,1)S(1)}, bf16[2,128,256]{2,1,0:T(8,128)(2,1)S(1)}, u32[]{:S(2)}, u32[]{:S(2)}) collective-permute-start(bf16[2,128,256]{2,1,0:T(8,128)(2,1)S(1)} %get-tuple-element.52), channel_id=1, source_target_pairs={{0,2},{1,3},{2,0},{3,1},{4,6},{5,7},{6,4},{7,5},{8,10},{9,11},{10,... | collective-permute-start | bytes 393224 | tf_op jit(solution)/shard_map/ppermute | solution.py:146
  46.4 9.5 %collective-permute-start.11 = (bf16[2,512,128]{2,1,0:T(8,128)(2,1)S(1)}, bf16[2,512,128]{2,1,0:T(8,128)(2,1)S(1)}, u32[]{:S(2)}, u32[]{:S(2)}) collective-permute-start(bf16[2,512,128]{2,1,0:T(8,128)(2,1)S(1)} %get-tuple-element.49), channel_id=1, source_target_pairs={{0,4},{4,0},{8,12},{12,8},{16,20},{20,16},{24,28},{28,24},{1,5},{5... | collective-permute-start | bytes 786440 | tf_op jit(solution)/shard_map/ppermute | solution.py:224
  47.2 6.9 %collective-permute-start.4 = (bf16[128,256]{1,0:T(8,128)(2,1)S(1)}, bf16[128,256]{1,0:T(8,128)(2,1)S(1)}, u32[]{:S(2)}, u32[]{:S(2)}) collective-permute-start(bf16[128,256]{1,0:T(8,128)(2,1)S(1)} %bitcast.272), channel_id=1, source_target_pairs={{0,1},{1,2},{2,3},{3,0},{4,5},{5,6},{6,7},{7,4},{8,9},{9,10},{10,1... | collective-permute-start | bytes 196616 | tf_op jit(solution)/shard_map/ppermute | solution.py:146
  47.3 8.6 %collective-permute-start.5 = (bf16[128,256]{1,0:T(8,128)(2,1)S(1)}, bf16[128,256]{1,0:T(8,128)(2,1)S(1)}, u32[]{:S(2)}, u32[]{:S(2)}) collective-permute-start(bf16[128,256]{1,0:T(8,128)(2,1)S(1)} %bitcast.273), channel_id=1, source_target_pairs={{0,2},{1,3},{2,0},{3,1},{4,6},{5,7},{6,4},{7,5},{8,10},{9,11},{10,... | collective-permute-start | bytes 196616 | tf_op jit(solution)/shard_map/ppermute | solution.py:146
  49.8 6.2 %collective-permute-start.6 = (bf16[128,256]{1,0:T(8,128)(2,1)S(1)}, bf16[128,256]{1,0:T(8,128)(2,1)S(1)}, u32[]{:S(2)}, u32[]{:S(2)}) collective-permute-start(bf16[128,256]{1,0:T(8,128)(2,1)S(1)} %bitcast.274), channel_id=1, source_target_pairs={{0,3},{1,0},{2,1},{3,2},{4,7},{5,4},{6,5},{7,6},{8,11},{9,8},{10,9... | collective-permute-start | bytes 196616 | tf_op jit(solution)/shard_map/ppermute | solution.py:146
  56.0 16.0 %collective-permute-start.14 = (bf16[2,1024,128]{2,1,0:T(8,128)(2,1)S(1)}, bf16[2,1024,128]{2,1,0:T(8,128)(2,1)}, u32[]{:S(2)}, u32[]{:S(2)}) collective-permute-start(bf16[2,1024,128]{2,1,0:T(8,128)(2,1)S(1)} %pad_maximum_fusion.3), channel_id=1, source_target_pairs={{0,24},{4,28},{8,16},{12,20},{16,8},{20,12},{24,0},{28,4},{1,25},{... | collective-permute-start | bytes 1572872 | tf_op jit(solution)/shard_map/ppermute | solution.py:228
  56.7 4.2 %collective-permute-start.7 = (bf16[512,128]{1,0:T(8,128)(2,1)S(1)}, bf16[512,128]{1,0:T(8,128)(2,1)S(1)}, u32[]{:S(2)}, u32[]{:S(2)}) collective-permute-start(bf16[512,128]{1,0:T(8,128)(2,1)S(1)} %get-tuple-element.62), channel_id=1, source_target_pairs={{0,4},{4,0},{8,12},{12,8},{16,20},{20,16},{24,28},{28,24},{1,5},{5... | collective-permute-start | bytes 393224 | tf_op jit(solution)/shard_map/ppermute | solution.py:224
  56.9 24.1 %collective-permute-start.13 = (bf16[2,1024,128]{2,1,0:T(8,128)(2,1)S(1)}, bf16[2,1024,128]{2,1,0:T(8,128)(2,1)S(1)}, u32[]{:S(2)}, u32[]{:S(2)}) collective-permute-start(bf16[2,1024,128]{2,1,0:T(8,128)(2,1)S(1)} %pad_maximum_fusion.3), channel_id=1, source_target_pairs={{0,16},{4,20},{8,24},{12,28},{16,0},{20,4},{24,8},{28,12},{1,17},{... | collective-permute-start | bytes 1572872 | tf_op jit(solution)/shard_map/ppermute | solution.py:228
  60.9 20.9 %collective-permute-start.12 = (bf16[2,1024,128]{2,1,0:T(8,128)(2,1)S(1)}, bf16[2,1024,128]{2,1,0:T(8,128)(2,1)S(1)}, u32[]{:S(2)}, u32[]{:S(2)}) collective-permute-start(bf16[2,1024,128]{2,1,0:T(8,128)(2,1)S(1)} %pad_maximum_fusion.3), channel_id=1, source_target_pairs={{0,8},{4,12},{8,0},{12,4},{16,24},{20,28},{24,16},{28,20},{1,9},{5... | collective-permute-start | bytes 1572872 | tf_op jit(solution)/shard_map/ppermute | solution.py:228
  93.8 1.4 collective-permute-start.15
  95.3 6.5 %collective-permute-start.16 = (bf16[128,256]{1,0:T(8,128)(2,1)S(1)}, bf16[128,256]{1,0:T(8,128)(2,1)S(1)}, u32[]{:S(2)}, u32[]{:S(2)}) collective-permute-start(bf16[128,256]{1,0:T(8,128)(2,1)S(1)} %get-tuple-element.58), channel_id=1, source_target_pairs={{1,0},{2,1},{3,2},{0,3},{5,4},{6,5},{7,6},{4,7},{9,8},{10,9},{11,1... | collective-permute-start | bytes 196616 | tf_op jit(solution)/shard_map/ppermute | solution.py:154
  99.3 6.6 %collective-permute-start.17 = (bf16[128,256]{1,0:T(8,128)(2,1)S(1)}, bf16[128,256]{1,0:T(8,128)(2,1)S(1)}, u32[]{:S(2)}, u32[]{:S(2)}) collective-permute-start(bf16[128,256]{1,0:T(8,128)(2,1)S(1)} %get-tuple-element.57), channel_id=1, source_target_pairs={{2,0},{3,1},{0,2},{1,3},{6,4},{7,5},{4,6},{5,7},{10,8},{11,9},{8,1... | collective-permute-start | bytes 196616 | tf_op jit(solution)/shard_map/ppermute | solution.py:154
  99.3 6.6 %collective-permute-start.18 = (bf16[128,256]{1,0:T(8,128)(2,1)S(1)}, bf16[128,256]{1,0:T(8,128)(2,1)S(1)}, u32[]{:S(2)}, u32[]{:S(2)}) collective-permute-start(bf16[128,256]{1,0:T(8,128)(2,1)S(1)} %get-tuple-element.56), channel_id=1, source_target_pairs={{3,0},{0,1},{1,2},{2,3},{7,4},{4,5},{5,6},{6,7},{11,8},{8,9},{9,10... | collective-permute-start | bytes 196616 | tf_op jit(solution)/shard_map/ppermute | solution.py:154
  110.7 2.6 %collective-permute-start.19 = (bf16[128,1,128]{2,0,1:T(8,128)(2,1)S(1)}, bf16[128,1,128]{2,0,1:T(8,128)(2,1)S(1)}, u32[]{:S(2)}, u32[]{:S(2)}) collective-permute-start(bf16[128,1,128]{2,0,1:T(8,128)(2,1)S(1)} %get-tuple-element.38), channel_id=1, source_target_pairs={{0,4},{4,8},{8,12},{12,16},{16,20},{20,24},{24,28},{1,5},{5,9},{9,... | collective-permute-start | bytes 98312 | tf_op jit(solution)/shard_map/ppermute | solution.py:20
  112.0 5.2 %collective-permute-start.20 = (bf16[128,1,128]{2,0,1:T(8,128)(2,1)S(1)}, bf16[128,1,128]{2,0,1:T(8,128)(2,1)S(1)}, u32[]{:S(2)}, u32[]{:S(2)}) collective-permute-start(bf16[128,1,128]{2,0,1:T(8,128)(2,1)S(1)} %get-tuple-element.39), channel_id=1, source_target_pairs={{4,0},{8,4},{12,8},{16,12},{20,16},{24,20},{28,24},{5,1},{9,5},{13... | collective-permute-start | bytes 98312 | tf_op jit(solution)/shard_map/ppermute | solution.py:21
  117.9 5.5 %collective-permute-start.21 = (bf16[128,18,1]{0,1,2:T(8,128)(2,1)S(1)}, bf16[128,18,1]{0,1,2:T(8,128)(2,1)S(1)}, u32[]{:S(2)}, u32[]{:S(2)}) collective-permute-start(bf16[128,18,1]{0,1,2:T(8,128)(2,1)S(1)} %copy.71), channel_id=1, source_target_pairs={{0,1},{1,2},{2,3},{3,0},{4,5},{5,6},{6,7},{7,4},{8,9},{9,10},{10,1... | collective-permute-start | bytes 13832 | tf_op jit(solution)/shard_map/ppermute | solution.py:25
  118.4 5.2 %collective-permute-start.22 = (bf16[128,18,1]{0,1,2:T(8,128)(2,1)S(1)}, bf16[128,18,1]{0,1,2:T(8,128)(2,1)S(1)}, u32[]{:S(2)}, u32[]{:S(2)}) collective-permute-start(bf16[128,18,1]{0,1,2:T(8,128)(2,1)S(1)} %copy.74), channel_id=1, source_target_pairs={{1,0},{2,1},{3,2},{0,3},{5,4},{6,5},{7,6},{4,7},{9,8},{10,9},{11,1... | collective-permute-start | bytes 13832 | tf_op jit(solution)/shard_map/ppermute | solution.py:26
  128.3 19.5 %copy-start.1 = (bf16[1024,1024]{1,0:T(8,128)(2,1)S(1)}, bf16[1024,1024]{1,0:T(8,128)(2,1)}, u32[]{:S(2)}) copy-start(bf16[1024,1024]{1,0:T(8,128)(2,1)} %param.25) | copy-start | bytes 6291460
  128.9 18.3 %copy-start.14 = (s32[64]{0:T(128)S(1)}, s32[64]{0:T(128)}, u32[]{:S(2)}) copy-start(s32[64]{0:T(128)} %param.18) | copy-start | bytes 772
  130.0 3.6 %collective-permute-start.23 = (f32[64]{0:T(128)S(1)}, f32[64]{0:T(128)S(1)}, u32[]{:S(2)}, u32[]{:S(2)}) collective-permute-start(f32[64]{0:T(128)S(1)} %fusion.40), channel_id=1, source_target_pairs={{0,1},{1,0},{2,3},{3,2},{4,5},{5,4},{6,7},{7,6},{8,9},{9,8},{10,11... | collective-permute-start | bytes 776 | tf_op jit(solution)/shard_map/ppermute | solution.py:34
  133.5 4.4 %collective-permute-start.24 = (f32[64]{0:T(128)S(1)}, f32[64]{0:T(128)S(1)}, u32[]{:S(2)}, u32[]{:S(2)}) collective-permute-start(f32[64]{0:T(128)S(1)} %add.306), channel_id=1, source_target_pairs={{0,2},{1,3},{2,0},{3,1},{4,6},{5,7},{6,4},{7,5},{8,10},{9,11},{10,... | collective-permute-start | bytes 776 | tf_op jit(solution)/shard_map/ppermute | solution.py:34
  138.0 1.1 collective-permute-start.25
  139.1 4.0 %collective-permute-start.26 = (f32[64]{0:T(128)S(1)}, f32[64]{0:T(128)S(1)}, u32[]{:S(2)}, u32[]{:S(2)}) collective-permute-start(f32[64]{0:T(128)S(1)} %add.308), channel_id=1, source_target_pairs={{0,8},{4,12},{8,0},{12,4},{16,24},{20,28},{24,16},{28,20},{1,9},{5... | collective-permute-start | bytes 776 | tf_op jit(solution)/shard_map/ppermute | solution.py:34
  143.1 4.0 %collective-permute-start.27 = (f32[64]{0:T(128)S(1)}, f32[64]{0:T(128)S(1)}, u32[]{:S(2)}, u32[]{:S(2)}) collective-permute-start(f32[64]{0:T(128)S(1)} %add.309), channel_id=1, source_target_pairs={{0,16},{4,20},{8,24},{12,28},{16,0},{20,4},{24,8},{28,12},{1,17},{... | collective-permute-start | bytes 776 | tf_op jit(solution)/shard_map/ppermute | solution.py:34
  (12 other events, 36.4 us)

commit v8 on v7

--- a/solution.py
+++ b/solution.py
@@ -128,13 +128,12 @@
     )(scales, queries, *key_chunks, *value_chunks)
 
 
-def merge_parts(first, second):
-    total_a, max_a, sum_a = first
-    total_b, max_b, sum_b = second
-    joint = jnp.maximum(max_a, max_b)
-    rescale_a, rescale_b = jnp.exp(max_a - joint), jnp.exp(max_b - joint)
-    total = total_a * rescale_a + total_b * rescale_b
-    return (total / (sum_a * rescale_a + sum_b * rescale_b)).astype(jnp.bfloat16)
+def merge_parts(parts):
+    joint = functools.reduce(jnp.maximum, [maxima for total, maxima, sums in parts])
+    rescales = [jnp.exp(maxima - joint) for total, maxima, sums in parts]
+    total = sum(part[0] * rescale for part, rescale in zip(parts, rescales))
+    weight_sum = sum(part[2] * rescale for part, rescale in zip(parts, rescales))
+    return (total / weight_sum).astype(jnp.bfloat16)
 
 
 def exchange_blocks(blocks, axis):
@@ -207,11 +206,7 @@
         )
     )
     by_group = [p.reshape(-1, lon_size, group_width).transpose(1, 0, 2) for p in projections]
-    key_value_spread = jnp.concatenate(
-        exchange_blocks(jnp.stack(by_group[1:], axis=1), "lon"), axis=1
-    )
-    query_spread = jnp.concatenate(exchange_blocks(by_group[0], "lon"), axis=0)
-    key_spread, value_spread = key_value_spread[0], key_value_spread[1]
+    spread = jnp.concatenate(exchange_blocks(jnp.stack(by_group, axis=1), "lon"), axis=1)
     lat_size = lax.axis_size("lat")
     core = lax.axis_index("lat") % 2
     half = group_width // 2
@@ -223,26 +218,29 @@
         theirs = jnp.where(core == 0, high, low)
         return jnp.concatenate([mine, lax.ppermute(theirs, "lat", partner)], axis=-2)
 
-    key_value = with_partner(jnp.stack([key_spread, value_spread]))
+    pair_spread = with_partner(spread)
+    pair_queries, key_value = pair_spread[0], pair_spread[1:]
     remote_chunks = [
         lax.ppermute(key_value, "lat", [(i, i ^ (2 * d)) for i in range(lat_size)])
         for d in range(1, lat_size // 2)
     ]
-    pair_queries = with_partner(query_spread)
     local_heads = half // head_size
     head_first = (lax.axis_index("lon") * 2 + core) * local_heads
     scales = lax.dynamic_slice_in_dim(head_scale, head_first, local_heads) / math.sqrt(head_size)
-    pair_attended = merge_parts(
-        attend_part(pair_queries, [key_value[0]], [key_value[1]], scales, head_size),
+    key_groups = [[key_value], remote_chunks[:1], remote_chunks[1:]]
+    parts = [
         attend_part(
             pair_queries,
-            [chunk[0] for chunk in remote_chunks],
-            [chunk[1] for chunk in remote_chunks],
+            [chunk[0] for chunk in group],
+            [chunk[1] for chunk in group],
             scales,
             head_size,
-        ),
-    )
-    token_count = query_spread.shape[0]
+        )
+        for group in key_groups
+        if group
+    ]
+    pair_attended = merge_parts(parts)
+    token_count = spread.shape[1]
     own_part = pair_attended[:token_count]
     returned = lax.ppermute(pair_attended[token_count:], "lat", partner)
     attended_heads = jnp.where(

time: 148 us -> 144 us (0.973)
  waiting for transfers between devices: 56.5 us -> 53.3 us
  starting transfers between devices: 41.4 us -> 39.1 us
  Pallas kernels: 16.2 us -> 18.3 us
    ppermute x6 -> x3, waiting for transfers between devices: 16.2 us -> 12.7 us  [exchange_blocks(): lax.ppermute(outgoing, axis, [(i, (i + shift) % size) for i in range(size)])]
    ppermute x6 -> x3, starting transfers between devices: 8.74 us -> 5.34 us  [exchange_blocks(): lax.ppermute(outgoing, axis, [(i, (i + shift) % size) for i in range(size)])]
    pallas_call x2 -> x3, Pallas kernels: 16.2 us -> 18.3 us  [attend_part(): pl.pallas_call(functools.partial(attention_kernel, head_size=head_size, c...]
    ppermute x2 -> x1, waiting for transfers between devices: 0.01 us -> 1.61 us  [with_partner(): lax.ppermute(theirs, 'lat', partner)]
    ppermute x3, starting transfers between devices: 4.65 us -> 6.2 us  [return_blocks(): lax.ppermute(blocks[shift], axis, [((i + shift) % size, i) for i in range...]
    unnamed x45 -> x41, local copies, waits for them, and re-layouts: 6.44 us -> 6.4 us
  transfers between devices with their start and end apart: 28 -> 24, of which waited for: 20 -> 18; matrix products, arithmetic and copies ran while one was open for 3% -> 2% of each run, Pallas kernels for 3% -> 6%
where the time goes in v8:
time: 144 us
  waiting for transfers between devices  53.3 us (37%)
  starting transfers between devices  39.1 us (27%)
  Pallas kernels  18.3 us (13%)
  matrix products  17.7 us (12%)
  local copies, waits for them, and re-layouts  10.9 us (8%)
  other arithmetic  3.29 us (2%)
    pallas_call x3, Pallas kernels, attend_part(): pl.pallas_call(functools.partial(attention_kernel, head_size=head_size, c...  18.3 us
    ppermute x3, waiting for transfers between devices, on_device(): lax.ppermute(key_value, 'lat', [(i, i ^ 2 * d) for i in range(lat_size)])  14.1 us
    ppermute x3, waiting for transfers between devices, exchange_blocks(): lax.ppermute(outgoing, axis, [(i, (i + shift) % size) for i in range(size)])  12.7 us
    dot_general x27, matrix products, convolution_kernel_taps(): jnp.einsum('oc,cyx->oyx', weight[tap_index], window, preferred_element_ty...  10.8 us
    ppermute x5, starting transfers between devices, butterfly_sum(): value = value + lax.ppermute(value, axis, partner)  8.54 us
    ppermute x5, waiting for transfers between devices, butterfly_sum(): value = value + lax.ppermute(value, axis, partner)  8.39 us
    ppermute x2, waiting for transfers between devices, halo_padded(): from_below = lax.ppermute(array[:, :width], 'lat', up)  6.5 us
    ppermute x3, waiting for transfers between devices, return_blocks(): lax.ppermute(blocks[shift], axis, [((i + shift) % size, i) for i in range...  6.44 us
  transfers between devices with their start and end apart: 24, of which 18 were waited for; matrix products, arithmetic and copies ran while one was open for 2% of the time, Pallas kernels for 6%

profile of v8, /device:TPU:0, one launch (start us, length us, event | category | flops | bytes accessed | tf_op | source)
XLA Modules:
  0.0 143.8 jit_solution(12532913937730530508)
XLA Ops:
  0.6 1.5 %copy.49 = bf16[69,16,128]{0,2,1:T(8,128)(2,1)S(1)} copy(bf16[69,16,128]{2,1,0:T(8,128)(2,1)} %param.15) | data formatting | bytes 565248 | tf_op args[0]
  2.2 2.5 %collective-permute-start = (bf16[69,2,128]{0,2,1:T(8,128)(2,1)S(1)}, bf16[69,2,128]{0,2,1:T(8,128)(2,1)S(1)}, u32[]{:S(2)}, u32[]{:S(2)}) collective-permute-start(bf16[69,2,128]{0,2,1:T(8,128)(2,1)S(1)} %get-tuple-element.61), channel_id=1, source_target_pairs={{0,4},{4,8},{8,12},{12,16},{16,20},{20,24},{24,28},{1,5},{5,9},{9,... | collective-permute-start | bytes 105992 | tf_op jit(solution)/shard_map/ppermute | solution.py:20
  6.0 3.9 %collective-permute-done.1 = bf16[69,2,128]{0,2,1:T(8,128)(2,1)S(1)} collective-permute-done((bf16[69,2,128]{0,2,1:T(8,128)(2,1)S(1)}, bf16[69,2,128]{0,2,1:T(8,128)(2,1)S(1)}, u32[]{:S(2)}, u32[]{:S(2)}) %collective-permute-start.1) | collective-permute-done | bytes 35360 | tf_op jit(solution)/shard_map/ppermute | solution.py:21
  9.9 1.6 %collective-permute-start.2 = (bf16[69,20,2]{0,2,1:T(2,128)(2,1)S(1)}, bf16[69,20,2]{0,2,1:T(2,128)(2,1)S(1)}, u32[]{:S(2)}, u32[]{:S(2)}) collective-permute-start(bf16[69,20,2]{0,2,1:T(2,128)(2,1)S(1)} %get-tuple-element.45), channel_id=1, source_target_pairs={{0,1},{1,2},{2,3},{3,0},{4,5},{5,6},{6,7},{7,4},{8,9},{9,10},{10,1... | collective-permute-start | bytes 16568 | tf_op jit(solution)/shard_map/ppermute | solution.py:25
  11.6 2.2 %collective-permute-start.3 = (bf16[69,20,2]{0,2,1:T(2,128)(2,1)S(1)}, bf16[69,20,2]{0,2,1:T(2,128)(2,1)S(1)}, u32[]{:S(2)}, u32[]{:S(2)}) collective-permute-start(bf16[69,20,2]{0,2,1:T(2,128)(2,1)S(1)} %get-tuple-element.46), channel_id=1, source_target_pairs={{1,0},{2,1},{3,2},{0,3},{5,4},{6,5},{7,6},{4,7},{9,8},{10,9},{11,1... | collective-permute-start | bytes 16568 | tf_op jit(solution)/shard_map/ppermute | solution.py:26
  13.8 1.6 %collective-permute-done.2 = bf16[69,20,2]{0,2,1:T(2,128)(2,1)S(1)} collective-permute-done((bf16[69,20,2]{0,2,1:T(2,128)(2,1)S(1)}, bf16[69,20,2]{0,2,1:T(2,128)(2,1)S(1)}, u32[]{:S(2)}, u32[]{:S(2)}) %collective-permute-start.2) | collective-permute-done | bytes 5552 | tf_op jit(solution)/shard_map/ppermute | solution.py:25
  30.0 1.4 collective-permute-start.4
  31.4 3.1 %collective-permute-start.5 = (bf16[3,128,256]{2,1,0:T(8,128)(2,1)S(1)}, bf16[3,128,256]{2,1,0:T(8,128)(2,1)S(1)}, u32[]{:S(2)}, u32[]{:S(2)}) collective-permute-start(bf16[3,128,256]{2,1,0:T(8,128)(2,1)S(1)} %get-tuple-element.43), channel_id=1, source_target_pairs={{0,2},{1,3},{2,0},{3,1},{4,6},{5,7},{6,4},{7,5},{8,10},{9,11},{10,... | collective-permute-start | bytes 589832 | tf_op jit(solution)/shard_map/ppermute | solution.py:145
  35.3 3.6 %collective-permute-done.4 = bf16[3,128,256]{2,1,0:T(8,128)(2,1)S(1)} collective-permute-done((bf16[3,128,256]{2,1,0:T(8,128)(2,1)S(1)}, bf16[3,128,256]{2,1,0:T(8,128)(2,1)S(1)}, u32[]{:S(2)}, u32[]{:S(2)}) %collective-permute-start.4) | collective-permute-done | bytes 196640 | tf_op jit(solution)/shard_map/ppermute | solution.py:145
  39.0 9.1 %collective-permute-done.5 = bf16[3,128,256]{2,1,0:T(8,128)(2,1)S(1)} collective-permute-done((bf16[3,128,256]{2,1,0:T(8,128)(2,1)S(1)}, bf16[3,128,256]{2,1,0:T(8,128)(2,1)S(1)}, u32[]{:S(2)}, u32[]{:S(2)}) %collective-permute-start.5) | collective-permute-done | bytes 196640 | tf_op jit(solution)/shard_map/ppermute | solution.py:145
  48.4 1.6 %collective-permute-done.7 = bf16[3,512,128]{2,1,0:T(8,128)(2,1)S(1)} collective-permute-done((bf16[3,512,128]{2,1,0:T(8,128)(2,1)S(1)}, bf16[3,512,128]{2,1,0:T(8,128)(2,1)S(1)}, u32[]{:S(2)}, u32[]{:S(2)}) %collective-permute-start.7) | collective-permute-done | bytes 393248 | tf_op jit(solution)/shard_map/ppermute | solution.py:219
  50.0 2.8 %collective-permute-start.8 = (bf16[2,1024,128]{2,1,0:T(8,128)(2,1)S(1)}, bf16[2,1024,128]{2,1,0:T(8,128)(2,1)}, u32[]{:S(2)}, u32[]{:S(2)}) collective-permute-start(bf16[2,1024,128]{2,1,0:T(8,128)(2,1)S(1)} %pad_maximum_fusion.6), channel_id=1, source_target_pairs={{0,8},{4,12},{8,0},{12,4},{16,24},{20,28},{24,16},{28,20},{1,9},{5... | collective-permute-start | bytes 1572872 | tf_op jit(solution)/shard_map/ppermute | solution.py:224
  54.5 4.5 %shard_map.166 = (f32[1024,128]{1,0:T(8,128)S(1)}, f32[1024,128]{1,0:T(8,128)S(1)}, f32[1024,128]{1,0:T(8,128)S(1)}) custom-call(f32[2]{0:T(128)S(1)} %dynamic-slice_multiply_fusion.scale_ref, bf16[1024,128]{1,0:T(8,128)(2,1)S(1)} %get-tuple-element.37.q_ref, bf16[1024,128]{1,0:T(8,128)(2,1)S(1)} %get-tuple-element.38.refs_0_, ...), custom_call_target="tpu_custom_call" | custom-call | flops 536870912 | bytes 2359296 | tf_op jit(solution)/shard_map/pallas_call | solution.py:111
  59.1 6.6 %collective-permute-done.8 = bf16[2,1024,128]{2,1,0:T(8,128)(2,1)} collective-permute-done((bf16[2,1024,128]{2,1,0:T(8,128)(2,1)S(1)}, bf16[2,1024,128]{2,1,0:T(8,128)(2,1)}, u32[]{:S(2)}, u32[]{:S(2)}) %collective-permute-start.8) | collective-permute-done | bytes 524320 | tf_op jit(solution)/shard_map/ppermute | solution.py:224
  66.7 4.5 %shard_map.167 = (f32[1024,128]{1,0:T(8,128)S(1)}, f32[1024,128]{1,0:T(8,128)S(1)}, f32[1024,128]{1,0:T(8,128)S(1)}) custom-call(f32[2]{0:T(128)S(1)} %dynamic-slice_multiply_fusion.scale_ref, bf16[1024,128]{1,0:T(8,128)(2,1)S(1)} %get-tuple-element.37.q_ref, bf16[1024,128]{1,0:T(8,128)(2,1)S(1)} %get-tuple-element.56.refs_0_, ...), custom_call_target="tpu_custom_call" | custom-call | flops 536870912 | bytes 2359296 | tf_op jit(solution)/shard_map/pallas_call | solution.py:111
  71.3 6.1 %collective-permute-done.10 = bf16[2,1024,128]{2,1,0:T(8,128)(2,1)S(1)} collective-permute-done((bf16[2,1024,128]{2,1,0:T(8,128)(2,1)S(1)}, bf16[2,1024,128]{2,1,0:T(8,128)(2,1)S(1)}, u32[]{:S(2)}, u32[]{:S(2)}) %collective-permute-start.10) | collective-permute-done | bytes 524320 | tf_op jit(solution)/shard_map/ppermute | solution.py:224
  77.4 1.4 collective-permute-done.9
  78.9 9.2 %shard_map.168 = (f32[1024,128]{1,0:T(8,128)S(1)}, f32[1024,128]{1,0:T(8,128)S(1)}, f32[1024,128]{1,0:T(8,128)S(1)}) custom-call(f32[2]{0:T(128)S(1)} %dynamic-slice_multiply_fusion.scale_ref, bf16[1024,128]{1,0:T(8,128)(2,1)S(1)} %get-tuple-element.37.q_ref, bf16[1024,128]{1,0:T(8,128)(2,1)S(1)} %get-tuple-element.60.refs_0_, ...), custom_call_target="tpu_custom_call" | custom-call | flops 1073741824 | bytes 2883584 | tf_op jit(solution)/shard_map/pallas_call | solution.py:111
  88.6 1.3 collective-permute-done.11
  90.1 5.2 %collective-permute-start.12 = (bf16[128,256]{1,0:T(8,128)(2,1)S(1)}, bf16[128,256]{1,0:T(8,128)(2,1)S(1)}, u32[]{:S(2)}, u32[]{:S(2)}) collective-permute-start(bf16[128,256]{1,0:T(8,128)(2,1)S(1)} %get-tuple-element.65), channel_id=1, source_target_pairs={{1,0},{2,1},{3,2},{0,3},{5,4},{6,5},{7,6},{4,7},{9,8},{10,9},{11,1... | collective-permute-start | bytes 196616 | tf_op jit(solution)/shard_map/ppermute | solution.py:153
  96.3 1.5 %collective-permute-done.12 = bf16[128,256]{1,0:T(8,128)(2,1)S(1)} collective-permute-done((bf16[128,256]{1,0:T(8,128)(2,1)S(1)}, bf16[128,256]{1,0:T(8,128)(2,1)S(1)}, u32[]{:S(2)}, u32[]{:S(2)}) %collective-permute-start.12) | collective-permute-done | bytes 65568 | tf_op jit(solution)/shard_map/ppermute | solution.py:153
  97.8 4.9 %collective-permute-done.13 = bf16[128,256]{1,0:T(8,128)(2,1)S(1)} collective-permute-done((bf16[128,256]{1,0:T(8,128)(2,1)S(1)}, bf16[128,256]{1,0:T(8,128)(2,1)S(1)}, u32[]{:S(2)}, u32[]{:S(2)}) %collective-permute-start.13) | collective-permute-done | bytes 65568 | tf_op jit(solution)/shard_map/ppermute | solution.py:153
  103.5 3.4 %fusion.58 = bf16[128,4,4,32,4]{0,3,4,2,1:T(8,128)(2,1)S(1)} fusion(bf16[4,32,1024,1,1]{2,1,4,3,0:T(8,128)(2,1)S(1)} %bitcast.271, bf16[1024,4,4,128]{3,2,1,0:T(4,128)(2,1)} %param.28), kind=kOutput, calls=%fused_computation.74 | convolution fusion | flops 539230208 | bytes 4980736 | tf_op jit(solution)/shard_map/pqd,dabh->hpaqb/dot_general | solution.py:261
  110.1 2.6 %collective-permute-done.16 = bf16[128,1,128]{2,0,1:T(8,128)(2,1)S(1)} collective-permute-done((bf16[128,1,128]{2,0,1:T(8,128)(2,1)S(1)}, bf16[128,1,128]{2,0,1:T(8,128)(2,1)S(1)}, u32[]{:S(2)}, u32[]{:S(2)}) %collective-permute-start.16) | collective-permute-done | bytes 32800 | tf_op jit(solution)/shard_map/ppermute | solution.py:21
  113.7 4.1 %collective-permute-start.18 = (bf16[128,18,1]{0,1,2:T(8,128)(2,1)S(1)}, bf16[128,18,1]{0,1,2:T(8,128)(2,1)S(1)}, u32[]{:S(2)}, u32[]{:S(2)}) collective-permute-start(bf16[128,18,1]{0,1,2:T(8,128)(2,1)S(1)} %copy.65), channel_id=1, source_target_pairs={{1,0},{2,1},{3,2},{0,3},{5,4},{6,5},{7,6},{4,7},{9,8},{10,9},{11,1... | collective-permute-start | bytes 13832 | tf_op jit(solution)/shard_map/ppermute | solution.py:26
  120.3 1.8 %maximum_maximum_fusion = (bf16[128,18,129]{2,0,1:T(8,128)(2,1)S(1)}, bf16[128,18,129]{2,0,1:T(8,128)(2,1)S(1)}) fusion(bf16[128,1,128]{2,0,1:T(8,128)(2,1)S(1)} %collective-permute-done.16, bf16[128,16,128]{2,0,1:T(8,128)(2,1)S(1)} %copy.59, bf16[128,1,128]{2,0,1:T(8,128)(2,1)S(1)} %collective-permute-done.15, bf16[128,18,1]{2,0,1:T(8,128)(2,1)S(1)} %copy.63, ...), kind=kLoop, calls=%fused_computation.54 | loop fusion | flops 4755456 | bytes 1787904 | tf_op jit(solution)/shard_map/concatenate | solution.py:27
  125.9 3.1 %collective-permute-done.19 = f32[64]{0:T(128)S(1)} collective-permute-done((f32[64]{0:T(128)S(1)}, f32[64]{0:T(128)S(1)}, u32[]{:S(2)}, u32[]{:S(2)}) %collective-permute-start.19) | collective-permute-done | bytes 288 | tf_op jit(solution)/shard_map/ppermute | solution.py:34
  129.0 2.6 %collective-permute-start.20 = (f32[64]{0:T(128)S(1)}, f32[64]{0:T(128)S(1)}, u32[]{:S(2)}, u32[]{:S(2)}) collective-permute-start(f32[64]{0:T(128)S(1)} %add.303), channel_id=1, source_target_pairs={{0,2},{1,3},{2,0},{3,1},{4,6},{5,7},{6,4},{7,5},{8,10},{9,11},{10,... | collective-permute-start | bytes 776 | tf_op jit(solution)/shard_map/ppermute | solution.py:34
  131.6 1.8 %collective-permute-done.20 = f32[64]{0:T(128)S(1)} collective-permute-done((f32[64]{0:T(128)S(1)}, f32[64]{0:T(128)S(1)}, u32[]{:S(2)}, u32[]{:S(2)}) %collective-permute-start.20) | collective-permute-done | bytes 288 | tf_op jit(solution)/shard_map/ppermute | solution.py:34
  134.6 2.5 %collective-permute-start.22 = (f32[64]{0:T(128)S(1)}, f32[64]{0:T(128)S(1)}, u32[]{:S(2)}, u32[]{:S(2)}) collective-permute-start(f32[64]{0:T(128)S(1)} %add.305), channel_id=1, source_target_pairs={{0,8},{4,12},{8,0},{12,4},{16,24},{20,28},{24,16},{28,20},{1,9},{5... | collective-permute-start | bytes 776 | tf_op jit(solution)/shard_map/ppermute | solution.py:34
  137.1 1.5 %collective-permute-done.22 = f32[64]{0:T(128)S(1)} collective-permute-done((f32[64]{0:T(128)S(1)}, f32[64]{0:T(128)S(1)}, u32[]{:S(2)}, u32[]{:S(2)}) %collective-permute-start.22) | collective-permute-done | bytes 288 | tf_op jit(solution)/shard_map/ppermute | solution.py:34
  138.6 3.0 %collective-permute-start.23 = (f32[64]{0:T(128)S(1)}, f32[64]{0:T(128)S(1)}, u32[]{:S(2)}, u32[]{:S(2)}) collective-permute-start(f32[64]{0:T(128)S(1)} %add.306), channel_id=1, source_target_pairs={{0,16},{4,20},{8,24},{12,28},{16,0},{20,4},{24,8},{28,12},{1,17},{... | collective-permute-start | bytes 776 | tf_op jit(solution)/shard_map/ppermute | solution.py:34
  (138 shorter events, 35.6 us)
Async XLA Ops:
  0.6 25.5 %copy-start = (bf16[1024,1024]{1,0:T(8,128)(2,1)S(1)}, bf16[1024,1024]{1,0:T(8,128)(2,1)}, u32[]{:S(2)}) copy-start(bf16[1024,1024]{1,0:T(8,128)(2,1)} %param.25) | copy-start | bytes 6291460
  2.1 13.6 %copy-start.10 = (bf16[9,128,69]{1,2,0:T(8,128)(2,1)S(1)}, bf16[9,128,69]{1,2,0:T(8,128)(2,1)}, u32[]{:S(2)}) copy-start(bf16[9,128,69]{1,2,0:T(8,128)(2,1)} %param.19) | copy-start | bytes 476932
  2.2 3.8 %collective-permute-start = (bf16[69,2,128]{0,2,1:T(8,128)(2,1)S(1)}, bf16[69,2,128]{0,2,1:T(8,128)(2,1)S(1)}, u32[]{:S(2)}, u32[]{:S(2)}) collective-permute-start(bf16[69,2,128]{0,2,1:T(8,128)(2,1)S(1)} %get-tuple-element.61), channel_id=1, source_target_pairs={{0,4},{4,8},{8,12},{12,16},{16,20},{20,24},{24,28},{1,5},{5,9},{9,... | collective-permute-start | bytes 105992 | tf_op jit(solution)/shard_map/ppermute | solution.py:20
  4.7 5.3 %collective-permute-start.1 = (bf16[69,2,128]{0,2,1:T(8,128)(2,1)S(1)}, bf16[69,2,128]{0,2,1:T(8,128)(2,1)S(1)}, u32[]{:S(2)}, u32[]{:S(2)}) collective-permute-start(bf16[69,2,128]{0,2,1:T(8,128)(2,1)S(1)} %get-tuple-element.62), channel_id=1, source_target_pairs={{4,0},{8,4},{12,8},{16,12},{20,16},{24,20},{28,24},{5,1},{9,5},{13... | collective-permute-start | bytes 105992 | tf_op jit(solution)/shard_map/ppermute | solution.py:21
  9.9 5.5 %collective-permute-start.2 = (bf16[69,20,2]{0,2,1:T(2,128)(2,1)S(1)}, bf16[69,20,2]{0,2,1:T(2,128)(2,1)S(1)}, u32[]{:S(2)}, u32[]{:S(2)}) collective-permute-start(bf16[69,20,2]{0,2,1:T(2,128)(2,1)S(1)} %get-tuple-element.45), channel_id=1, source_target_pairs={{0,1},{1,2},{2,3},{3,0},{4,5},{5,6},{6,7},{7,4},{8,9},{9,10},{10,1... | collective-permute-start | bytes 16568 | tf_op jit(solution)/shard_map/ppermute | solution.py:25
  11.6 3.9 %collective-permute-start.3 = (bf16[69,20,2]{0,2,1:T(2,128)(2,1)S(1)}, bf16[69,20,2]{0,2,1:T(2,128)(2,1)S(1)}, u32[]{:S(2)}, u32[]{:S(2)}) collective-permute-start(bf16[69,20,2]{0,2,1:T(2,128)(2,1)S(1)} %get-tuple-element.46), channel_id=1, source_target_pairs={{1,0},{2,1},{3,2},{0,3},{5,4},{6,5},{7,6},{4,7},{9,8},{10,9},{11,1... | collective-permute-start | bytes 16568 | tf_op jit(solution)/shard_map/ppermute | solution.py:26
  22.9 2.2 %copy-start.2 = (bf16[4,4,128,1024]{3,2,1,0:T(8,128)(2,1)S(1)}, bf16[4,4,128,1024]{3,2,1,0:T(8,128)(2,1)}, u32[]{:S(2)}) copy-start(bf16[4,4,128,1024]{3,2,1,0:T(8,128)(2,1)} %param.21) | copy-start | bytes 12582916
  30.0 9.0 %collective-permute-start.4 = (bf16[3,128,256]{2,1,0:T(8,128)(2,1)S(1)}, bf16[3,128,256]{2,1,0:T(8,128)(2,1)S(1)}, u32[]{:S(2)}, u32[]{:S(2)}) collective-permute-start(bf16[3,128,256]{2,1,0:T(8,128)(2,1)S(1)} %get-tuple-element.44), channel_id=1, source_target_pairs={{0,1},{1,2},{2,3},{3,0},{4,5},{5,6},{6,7},{7,4},{8,9},{9,10},{10,1... | collective-permute-start | bytes 589832 | tf_op jit(solution)/shard_map/ppermute | solution.py:145
  31.4 16.6 %collective-permute-start.5 = (bf16[3,128,256]{2,1,0:T(8,128)(2,1)S(1)}, bf16[3,128,256]{2,1,0:T(8,128)(2,1)S(1)}, u32[]{:S(2)}, u32[]{:S(2)}) collective-permute-start(bf16[3,128,256]{2,1,0:T(8,128)(2,1)S(1)} %get-tuple-element.43), channel_id=1, source_target_pairs={{0,2},{1,3},{2,0},{3,1},{4,6},{5,7},{6,4},{7,5},{8,10},{9,11},{10,... | collective-permute-start | bytes 589832 | tf_op jit(solution)/shard_map/ppermute | solution.py:145
  34.5 13.6 %collective-permute-start.6 = (bf16[3,128,256]{2,1,0:T(8,128)(2,1)S(1)}, bf16[3,128,256]{2,1,0:T(8,128)(2,1)S(1)}, u32[]{:S(2)}, u32[]{:S(2)}) collective-permute-start(bf16[3,128,256]{2,1,0:T(8,128)(2,1)S(1)} %get-tuple-element.42), channel_id=1, source_target_pairs={{0,3},{1,0},{2,1},{3,2},{4,7},{5,4},{6,5},{7,6},{8,11},{9,8},{10,9... | collective-permute-start | bytes 589832 | tf_op jit(solution)/shard_map/ppermute | solution.py:145
  48.1 6.0 %copy-start.13 = (f32[16]{0:T(128)S(1)}, f32[16]{0:T(128)}, u32[]{:S(2)}) copy-start(f32[16]{0:T(128)} %param.27) | copy-start | bytes 196
  48.2 1.8 %collective-permute-start.7 = (bf16[3,512,128]{2,1,0:T(8,128)(2,1)S(1)}, bf16[3,512,128]{2,1,0:T(8,128)(2,1)S(1)}, u32[]{:S(2)}, u32[]{:S(2)}) collective-permute-start(bf16[3,512,128]{2,1,0:T(8,128)(2,1)S(1)} %get-tuple-element.39), channel_id=1, source_target_pairs={{0,4},{4,0},{8,12},{12,8},{16,20},{20,16},{24,28},{28,24},{1,5},{5... | collective-permute-start | bytes 1179656 | tf_op jit(solution)/shard_map/ppermute | solution.py:219
  50.0 15.7 %collective-permute-start.8 = (bf16[2,1024,128]{2,1,0:T(8,128)(2,1)S(1)}, bf16[2,1024,128]{2,1,0:T(8,128)(2,1)}, u32[]{:S(2)}, u32[]{:S(2)}) collective-permute-start(bf16[2,1024,128]{2,1,0:T(8,128)(2,1)S(1)} %pad_maximum_fusion.6), channel_id=1, source_target_pairs={{0,8},{4,12},{8,0},{12,4},{16,24},{20,28},{24,16},{28,20},{1,9},{5... | collective-permute-start | bytes 1572872 | tf_op jit(solution)/shard_map/ppermute | solution.py:224
  52.9 24.5 %collective-permute-start.10 = (bf16[2,1024,128]{2,1,0:T(8,128)(2,1)S(1)}, bf16[2,1024,128]{2,1,0:T(8,128)(2,1)S(1)}, u32[]{:S(2)}, u32[]{:S(2)}) collective-permute-start(bf16[2,1024,128]{2,1,0:T(8,128)(2,1)S(1)} %pad_maximum_fusion.6), channel_id=1, source_target_pairs={{0,24},{4,28},{8,16},{12,20},{16,8},{20,12},{24,0},{28,4},{1,25},{... | collective-permute-start | bytes 1572872 | tf_op jit(solution)/shard_map/ppermute | solution.py:224
  54.2 24.6 %collective-permute-start.9 = (bf16[2,1024,128]{2,1,0:T(8,128)(2,1)S(1)}, bf16[2,1024,128]{2,1,0:T(8,128)(2,1)S(1)}, u32[]{:S(2)}, u32[]{:S(2)}) collective-permute-start(bf16[2,1024,128]{2,1,0:T(8,128)(2,1)S(1)} %pad_maximum_fusion.6), channel_id=1, source_target_pairs={{0,16},{4,20},{8,24},{12,28},{16,0},{20,4},{24,8},{28,12},{1,17},{... | collective-permute-start | bytes 1572872 | tf_op jit(solution)/shard_map/ppermute | solution.py:224
  88.6 1.4 collective-permute-start.11
  90.0 13.1 %copy-start.5 = (bf16[1024,1024]{1,0:T(8,128)(2,1)S(1)}, bf16[1024,1024]{1,0:T(8,128)(2,1)}, u32[]{:S(2)}) copy-start(bf16[1024,1024]{1,0:T(8,128)(2,1)} %param.26) | copy-start | bytes 6291460
  90.1 7.7 %collective-permute-start.12 = (bf16[128,256]{1,0:T(8,128)(2,1)S(1)}, bf16[128,256]{1,0:T(8,128)(2,1)S(1)}, u32[]{:S(2)}, u32[]{:S(2)}) collective-permute-start(bf16[128,256]{1,0:T(8,128)(2,1)S(1)} %get-tuple-element.65), channel_id=1, source_target_pairs={{1,0},{2,1},{3,2},{0,3},{5,4},{6,5},{7,6},{4,7},{9,8},{10,9},{11,1... | collective-permute-start | bytes 196616 | tf_op jit(solution)/shard_map/ppermute | solution.py:153
  95.3 7.4 %collective-permute-start.13 = (bf16[128,256]{1,0:T(8,128)(2,1)S(1)}, bf16[128,256]{1,0:T(8,128)(2,1)S(1)}, u32[]{:S(2)}, u32[]{:S(2)}) collective-permute-start(bf16[128,256]{1,0:T(8,128)(2,1)S(1)} %get-tuple-element.64), channel_id=1, source_target_pairs={{2,0},{3,1},{0,2},{1,3},{6,4},{7,5},{4,6},{5,7},{10,8},{11,9},{8,1... | collective-permute-start | bytes 196616 | tf_op jit(solution)/shard_map/ppermute | solution.py:153
  96.3 6.5 %collective-permute-start.14 = (bf16[128,256]{1,0:T(8,128)(2,1)S(1)}, bf16[128,256]{1,0:T(8,128)(2,1)S(1)}, u32[]{:S(2)}, u32[]{:S(2)}) collective-permute-start(bf16[128,256]{1,0:T(8,128)(2,1)S(1)} %get-tuple-element.63), channel_id=1, source_target_pairs={{3,0},{0,1},{1,2},{2,3},{7,4},{4,5},{5,6},{6,7},{11,8},{8,9},{9,10... | collective-permute-start | bytes 196616 | tf_op jit(solution)/shard_map/ppermute | solution.py:153
  107.5 2.6 %collective-permute-start.15 = (bf16[128,1,128]{2,0,1:T(8,128)(2,1)S(1)}, bf16[128,1,128]{2,0,1:T(8,128)(2,1)S(1)}, u32[]{:S(2)}, u32[]{:S(2)}) collective-permute-start(bf16[128,1,128]{2,0,1:T(8,128)(2,1)S(1)} %get-tuple-element.53), channel_id=1, source_target_pairs={{0,4},{4,8},{8,12},{12,16},{16,20},{20,24},{24,28},{1,5},{5,9},{9,... | collective-permute-start | bytes 98312 | tf_op jit(solution)/shard_map/ppermute | solution.py:20
  108.8 3.9 %collective-permute-start.16 = (bf16[128,1,128]{2,0,1:T(8,128)(2,1)S(1)}, bf16[128,1,128]{2,0,1:T(8,128)(2,1)S(1)}, u32[]{:S(2)}, u32[]{:S(2)}) collective-permute-start(bf16[128,1,128]{2,0,1:T(8,128)(2,1)S(1)} %get-tuple-element.54), channel_id=1, source_target_pairs={{4,0},{8,4},{12,8},{16,12},{20,16},{24,20},{28,24},{5,1},{9,5},{13... | collective-permute-start | bytes 98312 | tf_op jit(solution)/shard_map/ppermute | solution.py:21
  112.8 5.0 %copy-start.9 = (bf16[9,69,128]{2,1,0:T(8,128)(2,1)S(1)}, bf16[9,69,128]{2,1,0:T(8,128)(2,1)}, u32[]{:S(2)}) copy-start(bf16[9,69,128]{2,1,0:T(8,128)(2,1)} %param.29) | copy-start | bytes 476932
  113.4 5.5 %collective-permute-start.17 = (bf16[128,18,1]{0,1,2:T(8,128)(2,1)S(1)}, bf16[128,18,1]{0,1,2:T(8,128)(2,1)S(1)}, u32[]{:S(2)}, u32[]{:S(2)}) collective-permute-start(bf16[128,18,1]{0,1,2:T(8,128)(2,1)S(1)} %copy.62), channel_id=1, source_target_pairs={{0,1},{1,2},{2,3},{3,0},{4,5},{5,6},{6,7},{7,4},{8,9},{9,10},{10,1... | collective-permute-start | bytes 13832 | tf_op jit(solution)/shard_map/ppermute | solution.py:25
  113.7 5.5 %collective-permute-start.18 = (bf16[128,18,1]{0,1,2:T(8,128)(2,1)S(1)}, bf16[128,18,1]{0,1,2:T(8,128)(2,1)S(1)}, u32[]{:S(2)}, u32[]{:S(2)}) collective-permute-start(bf16[128,18,1]{0,1,2:T(8,128)(2,1)S(1)} %copy.65), channel_id=1, source_target_pairs={{1,0},{2,1},{3,2},{0,3},{5,4},{6,5},{7,6},{4,7},{9,8},{10,9},{11,1... | collective-permute-start | bytes 13832 | tf_op jit(solution)/shard_map/ppermute | solution.py:26
  123.8 20.0 %copy-start.1 = (bf16[1024,1024]{1,0:T(8,128)(2,1)S(1)}, bf16[1024,1024]{1,0:T(8,128)(2,1)}, u32[]{:S(2)}) copy-start(bf16[1024,1024]{1,0:T(8,128)(2,1)} %param.25) | copy-start | bytes 6291460
  124.4 18.8 %copy-start.14 = (s32[64]{0:T(128)S(1)}, s32[64]{0:T(128)}, u32[]{:S(2)}) copy-start(s32[64]{0:T(128)} %param.18) | copy-start | bytes 772
  125.5 3.6 %collective-permute-start.19 = (f32[64]{0:T(128)S(1)}, f32[64]{0:T(128)S(1)}, u32[]{:S(2)}, u32[]{:S(2)}) collective-permute-start(f32[64]{0:T(128)S(1)} %fusion.40), channel_id=1, source_target_pairs={{0,1},{1,0},{2,3},{3,2},{4,5},{5,4},{6,7},{7,6},{8,9},{9,8},{10,11... | collective-permute-start | bytes 776 | tf_op jit(solution)/shard_map/ppermute | solution.py:34
  129.0 4.4 %collective-permute-start.20 = (f32[64]{0:T(128)S(1)}, f32[64]{0:T(128)S(1)}, u32[]{:S(2)}, u32[]{:S(2)}) collective-permute-start(f32[64]{0:T(128)S(1)} %add.303), channel_id=1, source_target_pairs={{0,2},{1,3},{2,0},{3,1},{4,6},{5,7},{6,4},{7,5},{8,10},{9,11},{10,... | collective-permute-start | bytes 776 | tf_op jit(solution)/shard_map/ppermute | solution.py:34
  133.5 1.1 collective-permute-start.21
  134.6 4.0 %collective-permute-start.22 = (f32[64]{0:T(128)S(1)}, f32[64]{0:T(128)S(1)}, u32[]{:S(2)}, u32[]{:S(2)}) collective-permute-start(f32[64]{0:T(128)S(1)} %add.305), channel_id=1, source_target_pairs={{0,8},{4,12},{8,0},{12,4},{16,24},{20,28},{24,16},{28,20},{1,9},{5... | collective-permute-start | bytes 776 | tf_op jit(solution)/shard_map/ppermute | solution.py:34
  138.6 4.5 %collective-permute-start.23 = (f32[64]{0:T(128)S(1)}, f32[64]{0:T(128)S(1)}, u32[]{:S(2)}, u32[]{:S(2)}) collective-permute-start(f32[64]{0:T(128)S(1)} %add.306), channel_id=1, source_target_pairs={{0,16},{4,20},{8,24},{12,28},{16,0},{20,4},{24,8},{28,12},{1,17},{... | collective-permute-start | bytes 776 | tf_op jit(solution)/shard_map/ppermute | solution.py:34
  (8 other events, 8.7 us)

commit v9 on v8

--- a/solution.py
+++ b/solution.py
@@ -227,7 +227,7 @@
     local_heads = half // head_size
     head_first = (lax.axis_index("lon") * 2 + core) * local_heads
     scales = lax.dynamic_slice_in_dim(head_scale, head_first, local_heads) / math.sqrt(head_size)
-    key_groups = [[key_value], remote_chunks[:1], remote_chunks[1:]]
+    key_groups = [[key_value]] + [[chunk] for chunk in remote_chunks]
     parts = [
         attend_part(
             pair_queries,

time: 144 us -> 143 us (level)
    pallas_call x3 -> x4, Pallas kernels: 18.3 us -> 18.4 us  [attend_part(): pl.pallas_call(functools.partial(attention_kernel, head_size=head_size, c...]
  transfers between devices with their start and end apart: 24 -> 24, of which waited for: 18 -> 17; matrix products, arithmetic and copies ran while one was open for 2% -> 2% of each run, Pallas kernels for 6% -> 10%
where the time goes in v9:
time: 143 us
  waiting for transfers between devices  52.8 us (37%)
  starting transfers between devices  38.3 us (27%)
  Pallas kernels  18.4 us (13%)
  matrix products  17.7 us (12%)
  local copies, waits for them, and re-layouts  10.9 us (8%)
  other arithmetic  3.6 us (3%)
    pallas_call x4, Pallas kernels, attend_part(): pl.pallas_call(functools.partial(attention_kernel, head_size=head_size, c...  18.4 us
    ppermute x3, waiting for transfers between devices, on_device(): lax.ppermute(key_value, 'lat', [(i, i ^ 2 * d) for i in range(lat_size)])  13.1 us
    ppermute x3, waiting for transfers between devices, exchange_blocks(): lax.ppermute(outgoing, axis, [(i, (i + shift) % size) for i in range(size)])  12.7 us
    dot_general x27, matrix products, convolution_kernel_taps(): jnp.einsum('oc,cyx->oyx', weight[tap_index], window, preferred_element_ty...  10.7 us
    ppermute x5, waiting for transfers between devices, butterfly_sum(): value = value + lax.ppermute(value, axis, partner)  8.91 us
    ppermute x5, starting transfers between devices, butterfly_sum(): value = value + lax.ppermute(value, axis, partner)  7.86 us
    ppermute x3, waiting for transfers between devices, return_blocks(): lax.ppermute(blocks[shift], axis, [((i + shift) % size, i) for i in range...  6.44 us
    unnamed x41, local copies, waits for them, and re-layouts  6.4 us
  transfers between devices with their start and end apart: 24, of which 17 were waited for; matrix products, arithmetic and copies ran while one was open for 2% of the time, Pallas kernels for 10%

profile of v9, /device:TPU:0, one launch (start us, length us, event | category | flops | bytes accessed | tf_op | source)
XLA Modules:
  0.0 142.9 jit_solution(515854842267351222)
XLA Ops:
  0.6 1.5 %copy.49 = bf16[69,16,128]{0,2,1:T(8,128)(2,1)S(1)} copy(bf16[69,16,128]{2,1,0:T(8,128)(2,1)} %param.15) | data formatting | bytes 565248 | tf_op args[0]
  2.2 2.5 %collective-permute-start = (bf16[69,2,128]{0,2,1:T(8,128)(2,1)S(1)}, bf16[69,2,128]{0,2,1:T(8,128)(2,1)S(1)}, u32[]{:S(2)}, u32[]{:S(2)}) collective-permute-start(bf16[69,2,128]{0,2,1:T(8,128)(2,1)S(1)} %get-tuple-element.67), channel_id=1, source_target_pairs={{0,4},{4,8},{8,12},{12,16},{16,20},{20,24},{24,28},{1,5},{5,9},{9,... | collective-permute-start | bytes 105992 | tf_op jit(solution)/shard_map/ppermute | solution.py:20
  6.0 3.9 %collective-permute-done.1 = bf16[69,2,128]{0,2,1:T(8,128)(2,1)S(1)} collective-permute-done((bf16[69,2,128]{0,2,1:T(8,128)(2,1)S(1)}, bf16[69,2,128]{0,2,1:T(8,128)(2,1)S(1)}, u32[]{:S(2)}, u32[]{:S(2)}) %collective-permute-start.1) | collective-permute-done | bytes 35360 | tf_op jit(solution)/shard_map/ppermute | solution.py:21
  9.9 1.6 %collective-permute-start.2 = (bf16[69,20,2]{0,2,1:T(2,128)(2,1)S(1)}, bf16[69,20,2]{0,2,1:T(2,128)(2,1)S(1)}, u32[]{:S(2)}, u32[]{:S(2)}) collective-permute-start(bf16[69,20,2]{0,2,1:T(2,128)(2,1)S(1)} %get-tuple-element.51), channel_id=1, source_target_pairs={{0,1},{1,2},{2,3},{3,0},{4,5},{5,6},{6,7},{7,4},{8,9},{9,10},{10,1... | collective-permute-start | bytes 16568 | tf_op jit(solution)/shard_map/ppermute | solution.py:25
  11.6 2.2 %collective-permute-start.3 = (bf16[69,20,2]{0,2,1:T(2,128)(2,1)S(1)}, bf16[69,20,2]{0,2,1:T(2,128)(2,1)S(1)}, u32[]{:S(2)}, u32[]{:S(2)}) collective-permute-start(bf16[69,20,2]{0,2,1:T(2,128)(2,1)S(1)} %get-tuple-element.52), channel_id=1, source_target_pairs={{1,0},{2,1},{3,2},{0,3},{5,4},{6,5},{7,6},{4,7},{9,8},{10,9},{11,1... | collective-permute-start | bytes 16568 | tf_op jit(solution)/shard_map/ppermute | solution.py:26
  13.8 1.6 %collective-permute-done.2 = bf16[69,20,2]{0,2,1:T(2,128)(2,1)S(1)} collective-permute-done((bf16[69,20,2]{0,2,1:T(2,128)(2,1)S(1)}, bf16[69,20,2]{0,2,1:T(2,128)(2,1)S(1)}, u32[]{:S(2)}, u32[]{:S(2)}) %collective-permute-start.2) | collective-permute-done | bytes 5552 | tf_op jit(solution)/shard_map/ppermute | solution.py:25
  30.0 1.4 collective-permute-start.4
  31.4 3.1 %collective-permute-start.5 = (bf16[3,128,256]{2,1,0:T(8,128)(2,1)S(1)}, bf16[3,128,256]{2,1,0:T(8,128)(2,1)S(1)}, u32[]{:S(2)}, u32[]{:S(2)}) collective-permute-start(bf16[3,128,256]{2,1,0:T(8,128)(2,1)S(1)} %get-tuple-element.49), channel_id=1, source_target_pairs={{0,2},{1,3},{2,0},{3,1},{4,6},{5,7},{6,4},{7,5},{8,10},{9,11},{10,... | collective-permute-start | bytes 589832 | tf_op jit(solution)/shard_map/ppermute | solution.py:145
  35.3 3.6 %collective-permute-done.4 = bf16[3,128,256]{2,1,0:T(8,128)(2,1)S(1)} collective-permute-done((bf16[3,128,256]{2,1,0:T(8,128)(2,1)S(1)}, bf16[3,128,256]{2,1,0:T(8,128)(2,1)S(1)}, u32[]{:S(2)}, u32[]{:S(2)}) %collective-permute-start.4) | collective-permute-done | bytes 196640 | tf_op jit(solution)/shard_map/ppermute | solution.py:145
  39.0 9.1 %collective-permute-done.5 = bf16[3,128,256]{2,1,0:T(8,128)(2,1)S(1)} collective-permute-done((bf16[3,128,256]{2,1,0:T(8,128)(2,1)S(1)}, bf16[3,128,256]{2,1,0:T(8,128)(2,1)S(1)}, u32[]{:S(2)}, u32[]{:S(2)}) %collective-permute-start.5) | collective-permute-done | bytes 196640 | tf_op jit(solution)/shard_map/ppermute | solution.py:145
  48.4 1.6 %collective-permute-done.7 = bf16[3,512,128]{2,1,0:T(8,128)(2,1)S(1)} collective-permute-done((bf16[3,512,128]{2,1,0:T(8,128)(2,1)S(1)}, bf16[3,512,128]{2,1,0:T(8,128)(2,1)S(1)}, u32[]{:S(2)}, u32[]{:S(2)}) %collective-permute-start.7) | collective-permute-done | bytes 393248 | tf_op jit(solution)/shard_map/ppermute | solution.py:219
  50.0 2.8 %collective-permute-start.8 = (bf16[2,1024,128]{2,1,0:T(8,128)(2,1)S(1)}, bf16[2,1024,128]{2,1,0:T(8,128)(2,1)}, u32[]{:S(2)}, u32[]{:S(2)}) collective-permute-start(bf16[2,1024,128]{2,1,0:T(8,128)(2,1)S(1)} %pad_maximum_fusion.6), channel_id=1, source_target_pairs={{0,8},{4,12},{8,0},{12,4},{16,24},{20,28},{24,16},{28,20},{1,9},{5... | collective-permute-start | bytes 1572872 | tf_op jit(solution)/shard_map/ppermute | solution.py:224
  52.9 1.6 %collective-permute-start.10 = (bf16[2,1024,128]{2,1,0:T(8,128)(2,1)S(1)}, bf16[2,1024,128]{2,1,0:T(8,128)(2,1)S(1)}, u32[]{:S(2)}, u32[]{:S(2)}) collective-permute-start(bf16[2,1024,128]{2,1,0:T(8,128)(2,1)S(1)} %pad_maximum_fusion.6), channel_id=1, source_target_pairs={{0,24},{4,28},{8,16},{12,20},{16,8},{20,12},{24,0},{28,4},{1,25},{... | collective-permute-start | bytes 1572872 | tf_op jit(solution)/shard_map/ppermute | solution.py:224
  54.5 4.5 %shard_map.166 = (f32[1024,128]{1,0:T(8,128)S(1)}, f32[1024,128]{1,0:T(8,128)S(1)}, f32[1024,128]{1,0:T(8,128)S(1)}) custom-call(f32[2]{0:T(128)S(1)} %dynamic-slice_multiply_fusion.scale_ref, bf16[1024,128]{1,0:T(8,128)(2,1)S(1)} %get-tuple-element.43.q_ref, bf16[1024,128]{1,0:T(8,128)(2,1)S(1)} %get-tuple-element.44.refs_0_, ...), custom_call_target="tpu_custom_call" | custom-call | flops 536870912 | bytes 2359296 | tf_op jit(solution)/shard_map/pallas_call | solution.py:111
  59.1 6.6 %collective-permute-done.8 = bf16[2,1024,128]{2,1,0:T(8,128)(2,1)} collective-permute-done((bf16[2,1024,128]{2,1,0:T(8,128)(2,1)S(1)}, bf16[2,1024,128]{2,1,0:T(8,128)(2,1)}, u32[]{:S(2)}, u32[]{:S(2)}) %collective-permute-start.8) | collective-permute-done | bytes 524320 | tf_op jit(solution)/shard_map/ppermute | solution.py:224
  66.7 4.5 %shard_map.167 = (f32[1024,128]{1,0:T(8,128)S(1)}, f32[1024,128]{1,0:T(8,128)S(1)}, f32[1024,128]{1,0:T(8,128)S(1)}) custom-call(f32[2]{0:T(128)S(1)} %dynamic-slice_multiply_fusion.scale_ref, bf16[1024,128]{1,0:T(8,128)(2,1)S(1)} %get-tuple-element.43.q_ref, bf16[1024,128]{1,0:T(8,128)(2,1)S(1)} %get-tuple-element.62.refs_0_, ...), custom_call_target="tpu_custom_call" | custom-call | flops 536870912 | bytes 2359296 | tf_op jit(solution)/shard_map/pallas_call | solution.py:111
  71.3 6.5 %collective-permute-done.9 = bf16[2,1024,128]{2,1,0:T(8,128)(2,1)S(1)} collective-permute-done((bf16[2,1024,128]{2,1,0:T(8,128)(2,1)S(1)}, bf16[2,1024,128]{2,1,0:T(8,128)(2,1)S(1)}, u32[]{:S(2)}, u32[]{:S(2)}) %collective-permute-start.9) | collective-permute-done | bytes 524320 | tf_op jit(solution)/shard_map/ppermute | solution.py:224
  77.8 4.5 %shard_map.168 = (f32[1024,128]{1,0:T(8,128)S(1)}, f32[1024,128]{1,0:T(8,128)S(1)}, f32[1024,128]{1,0:T(8,128)S(1)}) custom-call(f32[2]{0:T(128)S(1)} %dynamic-slice_multiply_fusion.scale_ref, bf16[1024,128]{1,0:T(8,128)(2,1)S(1)} %get-tuple-element.43.q_ref, bf16[1024,128]{1,0:T(8,128)(2,1)S(1)} %get-tuple-element.64.refs_0_, ...), custom_call_target="tpu_custom_call" | custom-call | flops 536870912 | bytes 2359296 | tf_op jit(solution)/shard_map/pallas_call | solution.py:111
  82.4 4.8 %shard_map.169 = (f32[1024,128]{1,0:T(8,128)S(1)}, f32[1024,128]{1,0:T(8,128)S(1)}, f32[1024,128]{1,0:T(8,128)S(1)}) custom-call(f32[2]{0:T(128)S(1)} %dynamic-slice_multiply_fusion.scale_ref, bf16[1024,128]{1,0:T(8,128)(2,1)S(1)} %get-tuple-element.43.q_ref, bf16[1024,128]{1,0:T(8,128)(2,1)S(1)} %get-tuple-element.66.refs_0_, ...), custom_call_target="tpu_custom_call" | custom-call | flops 536870912 | bytes 2359296 | tf_op jit(solution)/shard_map/pallas_call | solution.py:111
  89.5 5.6 %collective-permute-start.12 = (bf16[128,256]{1,0:T(8,128)(2,1)S(1)}, bf16[128,256]{1,0:T(8,128)(2,1)S(1)}, u32[]{:S(2)}, u32[]{:S(2)}) collective-permute-start(bf16[128,256]{1,0:T(8,128)(2,1)S(1)} %get-tuple-element.71), channel_id=1, source_target_pairs={{1,0},{2,1},{3,2},{0,3},{5,4},{6,5},{7,6},{4,7},{9,8},{10,9},{11,1... | collective-permute-start | bytes 196616 | tf_op jit(solution)/shard_map/ppermute | solution.py:153
  95.8 1.8 %collective-permute-done.12 = bf16[128,256]{1,0:T(8,128)(2,1)S(1)} collective-permute-done((bf16[128,256]{1,0:T(8,128)(2,1)S(1)}, bf16[128,256]{1,0:T(8,128)(2,1)S(1)}, u32[]{:S(2)}, u32[]{:S(2)}) %collective-permute-start.12) | collective-permute-done | bytes 65568 | tf_op jit(solution)/shard_map/ppermute | solution.py:153
  97.6 4.6 %collective-permute-done.13 = bf16[128,256]{1,0:T(8,128)(2,1)S(1)} collective-permute-done((bf16[128,256]{1,0:T(8,128)(2,1)S(1)}, bf16[128,256]{1,0:T(8,128)(2,1)S(1)}, u32[]{:S(2)}, u32[]{:S(2)}) %collective-permute-start.13) | collective-permute-done | bytes 65568 | tf_op jit(solution)/shard_map/ppermute | solution.py:153
  103.0 3.4 %fusion.58 = bf16[128,4,4,32,4]{0,3,4,2,1:T(8,128)(2,1)S(1)} fusion(bf16[4,32,1024,1,1]{2,1,4,3,0:T(8,128)(2,1)S(1)} %bitcast.271, bf16[1024,4,4,128]{3,2,1,0:T(4,128)(2,1)} %param.28), kind=kOutput, calls=%fused_computation.74 | convolution fusion | flops 539230208 | bytes 4980736 | tf_op jit(solution)/shard_map/pqd,dabh->hpaqb/dot_general | solution.py:261
  109.6 2.3 %collective-permute-done.16 = bf16[128,1,128]{2,0,1:T(8,128)(2,1)S(1)} collective-permute-done((bf16[128,1,128]{2,0,1:T(8,128)(2,1)S(1)}, bf16[128,1,128]{2,0,1:T(8,128)(2,1)S(1)}, u32[]{:S(2)}, u32[]{:S(2)}) %collective-permute-start.16) | collective-permute-done | bytes 32800 | tf_op jit(solution)/shard_map/ppermute | solution.py:21
  113.0 3.8 %collective-permute-start.18 = (bf16[128,18,1]{0,1,2:T(8,128)(2,1)S(1)}, bf16[128,18,1]{0,1,2:T(8,128)(2,1)S(1)}, u32[]{:S(2)}, u32[]{:S(2)}) collective-permute-start(bf16[128,18,1]{0,1,2:T(8,128)(2,1)S(1)} %copy.65), channel_id=1, source_target_pairs={{1,0},{2,1},{3,2},{0,3},{5,4},{6,5},{7,6},{4,7},{9,8},{10,9},{11,1... | collective-permute-start | bytes 13832 | tf_op jit(solution)/shard_map/ppermute | solution.py:26
  119.6 1.8 %maximum_maximum_fusion = (bf16[128,18,129]{2,0,1:T(8,128)(2,1)S(1)}, bf16[128,18,129]{2,0,1:T(8,128)(2,1)S(1)}) fusion(bf16[128,1,128]{2,0,1:T(8,128)(2,1)S(1)} %collective-permute-done.16, bf16[128,16,128]{2,0,1:T(8,128)(2,1)S(1)} %copy.59, bf16[128,1,128]{2,0,1:T(8,128)(2,1)S(1)} %collective-permute-done.15, bf16[128,18,1]{2,0,1:T(8,128)(2,1)S(1)} %copy.63, ...), kind=kLoop, calls=%fused_computation.54 | loop fusion | flops 4755456 | bytes 1787904 | tf_op jit(solution)/shard_map/concatenate | solution.py:27
  124.9 3.4 %collective-permute-done.19 = f32[64]{0:T(128)S(1)} collective-permute-done((f32[64]{0:T(128)S(1)}, f32[64]{0:T(128)S(1)}, u32[]{:S(2)}, u32[]{:S(2)}) %collective-permute-start.19) | collective-permute-done | bytes 288 | tf_op jit(solution)/shard_map/ppermute | solution.py:34
  128.3 2.3 %collective-permute-start.20 = (f32[64]{0:T(128)S(1)}, f32[64]{0:T(128)S(1)}, u32[]{:S(2)}, u32[]{:S(2)}) collective-permute-start(f32[64]{0:T(128)S(1)} %add.311), channel_id=1, source_target_pairs={{0,2},{1,3},{2,0},{3,1},{4,6},{5,7},{6,4},{7,5},{8,10},{9,11},{10,... | collective-permute-start | bytes 776 | tf_op jit(solution)/shard_map/ppermute | solution.py:34
  130.6 2.1 %collective-permute-done.20 = f32[64]{0:T(128)S(1)} collective-permute-done((f32[64]{0:T(128)S(1)}, f32[64]{0:T(128)S(1)}, u32[]{:S(2)}, u32[]{:S(2)}) %collective-permute-start.20) | collective-permute-done | bytes 288 | tf_op jit(solution)/shard_map/ppermute | solution.py:34
  133.9 2.5 %collective-permute-start.22 = (f32[64]{0:T(128)S(1)}, f32[64]{0:T(128)S(1)}, u32[]{:S(2)}, u32[]{:S(2)}) collective-permute-start(f32[64]{0:T(128)S(1)} %add.313), channel_id=1, source_target_pairs={{0,8},{4,12},{8,0},{12,4},{16,24},{20,28},{24,16},{28,20},{1,9},{5... | collective-permute-start | bytes 776 | tf_op jit(solution)/shard_map/ppermute | solution.py:34
  136.4 1.5 %collective-permute-done.22 = f32[64]{0:T(128)S(1)} collective-permute-done((f32[64]{0:T(128)S(1)}, f32[64]{0:T(128)S(1)}, u32[]{:S(2)}, u32[]{:S(2)}) %collective-permute-start.22) | collective-permute-done | bytes 288 | tf_op jit(solution)/shard_map/ppermute | solution.py:34
  137.9 2.8 %collective-permute-start.23 = (f32[64]{0:T(128)S(1)}, f32[64]{0:T(128)S(1)}, u32[]{:S(2)}, u32[]{:S(2)}) collective-permute-start(f32[64]{0:T(128)S(1)} %add.314), channel_id=1, source_target_pairs={{0,16},{4,20},{8,24},{12,28},{16,0},{20,4},{24,8},{28,12},{1,17},{... | collective-permute-start | bytes 776 | tf_op jit(solution)/shard_map/ppermute | solution.py:34
  (139 shorter events, 35.4 us)
Async XLA Ops:
  0.6 25.5 %copy-start = (bf16[1024,1024]{1,0:T(8,128)(2,1)S(1)}, bf16[1024,1024]{1,0:T(8,128)(2,1)}, u32[]{:S(2)}) copy-start(bf16[1024,1024]{1,0:T(8,128)(2,1)} %param.25) | copy-start | bytes 6291460
  2.1 13.6 %copy-start.10 = (bf16[9,128,69]{1,2,0:T(8,128)(2,1)S(1)}, bf16[9,128,69]{1,2,0:T(8,128)(2,1)}, u32[]{:S(2)}) copy-start(bf16[9,128,69]{1,2,0:T(8,128)(2,1)} %param.19) | copy-start | bytes 476932
  2.2 3.8 %collective-permute-start = (bf16[69,2,128]{0,2,1:T(8,128)(2,1)S(1)}, bf16[69,2,128]{0,2,1:T(8,128)(2,1)S(1)}, u32[]{:S(2)}, u32[]{:S(2)}) collective-permute-start(bf16[69,2,128]{0,2,1:T(8,128)(2,1)S(1)} %get-tuple-element.67), channel_id=1, source_target_pairs={{0,4},{4,8},{8,12},{12,16},{16,20},{20,24},{24,28},{1,5},{5,9},{9,... | collective-permute-start | bytes 105992 | tf_op jit(solution)/shard_map/ppermute | solution.py:20
  4.7 5.3 %collective-permute-start.1 = (bf16[69,2,128]{0,2,1:T(8,128)(2,1)S(1)}, bf16[69,2,128]{0,2,1:T(8,128)(2,1)S(1)}, u32[]{:S(2)}, u32[]{:S(2)}) collective-permute-start(bf16[69,2,128]{0,2,1:T(8,128)(2,1)S(1)} %get-tuple-element.68), channel_id=1, source_target_pairs={{4,0},{8,4},{12,8},{16,12},{20,16},{24,20},{28,24},{5,1},{9,5},{13... | collective-permute-start | bytes 105992 | tf_op jit(solution)/shard_map/ppermute | solution.py:21
  9.9 5.5 %collective-permute-start.2 = (bf16[69,20,2]{0,2,1:T(2,128)(2,1)S(1)}, bf16[69,20,2]{0,2,1:T(2,128)(2,1)S(1)}, u32[]{:S(2)}, u32[]{:S(2)}) collective-permute-start(bf16[69,20,2]{0,2,1:T(2,128)(2,1)S(1)} %get-tuple-element.51), channel_id=1, source_target_pairs={{0,1},{1,2},{2,3},{3,0},{4,5},{5,6},{6,7},{7,4},{8,9},{9,10},{10,1... | collective-permute-start | bytes 16568 | tf_op jit(solution)/shard_map/ppermute | solution.py:25
  11.6 3.9 %collective-permute-start.3 = (bf16[69,20,2]{0,2,1:T(2,128)(2,1)S(1)}, bf16[69,20,2]{0,2,1:T(2,128)(2,1)S(1)}, u32[]{:S(2)}, u32[]{:S(2)}) collective-permute-start(bf16[69,20,2]{0,2,1:T(2,128)(2,1)S(1)} %get-tuple-element.52), channel_id=1, source_target_pairs={{1,0},{2,1},{3,2},{0,3},{5,4},{6,5},{7,6},{4,7},{9,8},{10,9},{11,1... | collective-permute-start | bytes 16568 | tf_op jit(solution)/shard_map/ppermute | solution.py:26
  22.9 2.2 %copy-start.2 = (bf16[4,4,128,1024]{3,2,1,0:T(8,128)(2,1)S(1)}, bf16[4,4,128,1024]{3,2,1,0:T(8,128)(2,1)}, u32[]{:S(2)}) copy-start(bf16[4,4,128,1024]{3,2,1,0:T(8,128)(2,1)} %param.21) | copy-start | bytes 12582916
  30.0 9.0 %collective-permute-start.4 = (bf16[3,128,256]{2,1,0:T(8,128)(2,1)S(1)}, bf16[3,128,256]{2,1,0:T(8,128)(2,1)S(1)}, u32[]{:S(2)}, u32[]{:S(2)}) collective-permute-start(bf16[3,128,256]{2,1,0:T(8,128)(2,1)S(1)} %get-tuple-element.50), channel_id=1, source_target_pairs={{0,1},{1,2},{2,3},{3,0},{4,5},{5,6},{6,7},{7,4},{8,9},{9,10},{10,1... | collective-permute-start | bytes 589832 | tf_op jit(solution)/shard_map/ppermute | solution.py:145
  31.4 16.6 %collective-permute-start.5 = (bf16[3,128,256]{2,1,0:T(8,128)(2,1)S(1)}, bf16[3,128,256]{2,1,0:T(8,128)(2,1)S(1)}, u32[]{:S(2)}, u32[]{:S(2)}) collective-permute-start(bf16[3,128,256]{2,1,0:T(8,128)(2,1)S(1)} %get-tuple-element.49), channel_id=1, source_target_pairs={{0,2},{1,3},{2,0},{3,1},{4,6},{5,7},{6,4},{7,5},{8,10},{9,11},{10,... | collective-permute-start | bytes 589832 | tf_op jit(solution)/shard_map/ppermute | solution.py:145
  34.5 13.6 %collective-permute-start.6 = (bf16[3,128,256]{2,1,0:T(8,128)(2,1)S(1)}, bf16[3,128,256]{2,1,0:T(8,128)(2,1)S(1)}, u32[]{:S(2)}, u32[]{:S(2)}) collective-permute-start(bf16[3,128,256]{2,1,0:T(8,128)(2,1)S(1)} %get-tuple-element.48), channel_id=1, source_target_pairs={{0,3},{1,0},{2,1},{3,2},{4,7},{5,4},{6,5},{7,6},{8,11},{9,8},{10,9... | collective-permute-start | bytes 589832 | tf_op jit(solution)/shard_map/ppermute | solution.py:145
  48.1 4.7 %copy-start.13 = (f32[16]{0:T(128)S(1)}, f32[16]{0:T(128)}, u32[]{:S(2)}) copy-start(f32[16]{0:T(128)} %param.27) | copy-start | bytes 196
  48.2 1.8 %collective-permute-start.7 = (bf16[3,512,128]{2,1,0:T(8,128)(2,1)S(1)}, bf16[3,512,128]{2,1,0:T(8,128)(2,1)S(1)}, u32[]{:S(2)}, u32[]{:S(2)}) collective-permute-start(bf16[3,512,128]{2,1,0:T(8,128)(2,1)S(1)} %get-tuple-element.45), channel_id=1, source_target_pairs={{0,4},{4,0},{8,12},{12,8},{16,20},{20,16},{24,28},{28,24},{1,5},{5... | collective-permute-start | bytes 1179656 | tf_op jit(solution)/shard_map/ppermute | solution.py:219
  50.0 15.7 %collective-permute-start.8 = (bf16[2,1024,128]{2,1,0:T(8,128)(2,1)S(1)}, bf16[2,1024,128]{2,1,0:T(8,128)(2,1)}, u32[]{:S(2)}, u32[]{:S(2)}) collective-permute-start(bf16[2,1024,128]{2,1,0:T(8,128)(2,1)S(1)} %pad_maximum_fusion.6), channel_id=1, source_target_pairs={{0,8},{4,12},{8,0},{12,4},{16,24},{20,28},{24,16},{28,20},{1,9},{5... | collective-permute-start | bytes 1572872 | tf_op jit(solution)/shard_map/ppermute | solution.py:224
  52.9 24.9 %collective-permute-start.9 = (bf16[2,1024,128]{2,1,0:T(8,128)(2,1)S(1)}, bf16[2,1024,128]{2,1,0:T(8,128)(2,1)S(1)}, u32[]{:S(2)}, u32[]{:S(2)}) collective-permute-start(bf16[2,1024,128]{2,1,0:T(8,128)(2,1)S(1)} %pad_maximum_fusion.6), channel_id=1, source_target_pairs={{0,16},{4,20},{8,24},{12,28},{16,0},{20,4},{24,8},{28,12},{1,17},{... | collective-permute-start | bytes 1572872 | tf_op jit(solution)/shard_map/ppermute | solution.py:224
  52.9 29.4 %collective-permute-start.10 = (bf16[2,1024,128]{2,1,0:T(8,128)(2,1)S(1)}, bf16[2,1024,128]{2,1,0:T(8,128)(2,1)S(1)}, u32[]{:S(2)}, u32[]{:S(2)}) collective-permute-start(bf16[2,1024,128]{2,1,0:T(8,128)(2,1)S(1)} %pad_maximum_fusion.6), channel_id=1, source_target_pairs={{0,24},{4,28},{8,16},{12,20},{16,8},{20,12},{24,0},{28,4},{1,25},{... | collective-permute-start | bytes 1572872 | tf_op jit(solution)/shard_map/ppermute | solution.py:224
  87.9 1.4 collective-permute-start.11
  89.4 13.2 %copy-start.5 = (bf16[1024,1024]{1,0:T(8,128)(2,1)S(1)}, bf16[1024,1024]{1,0:T(8,128)(2,1)}, u32[]{:S(2)}) copy-start(bf16[1024,1024]{1,0:T(8,128)(2,1)} %param.26) | copy-start | bytes 6291460
  89.5 8.1 %collective-permute-start.12 = (bf16[128,256]{1,0:T(8,128)(2,1)S(1)}, bf16[128,256]{1,0:T(8,128)(2,1)S(1)}, u32[]{:S(2)}, u32[]{:S(2)}) collective-permute-start(bf16[128,256]{1,0:T(8,128)(2,1)S(1)} %get-tuple-element.71), channel_id=1, source_target_pairs={{1,0},{2,1},{3,2},{0,3},{5,4},{6,5},{7,6},{4,7},{9,8},{10,9},{11,1... | collective-permute-start | bytes 196616 | tf_op jit(solution)/shard_map/ppermute | solution.py:153
  95.1 7.1 %collective-permute-start.13 = (bf16[128,256]{1,0:T(8,128)(2,1)S(1)}, bf16[128,256]{1,0:T(8,128)(2,1)S(1)}, u32[]{:S(2)}, u32[]{:S(2)}) collective-permute-start(bf16[128,256]{1,0:T(8,128)(2,1)S(1)} %get-tuple-element.70), channel_id=1, source_target_pairs={{2,0},{3,1},{0,2},{1,3},{6,4},{7,5},{4,6},{5,7},{10,8},{11,9},{8,1... | collective-permute-start | bytes 196616 | tf_op jit(solution)/shard_map/ppermute | solution.py:153
  95.8 6.5 %collective-permute-start.14 = (bf16[128,256]{1,0:T(8,128)(2,1)S(1)}, bf16[128,256]{1,0:T(8,128)(2,1)S(1)}, u32[]{:S(2)}, u32[]{:S(2)}) collective-permute-start(bf16[128,256]{1,0:T(8,128)(2,1)S(1)} %get-tuple-element.69), channel_id=1, source_target_pairs={{3,0},{0,1},{1,2},{2,3},{7,4},{4,5},{5,6},{6,7},{11,8},{8,9},{9,10... | collective-permute-start | bytes 196616 | tf_op jit(solution)/shard_map/ppermute | solution.py:153
  107.0 2.6 %collective-permute-start.15 = (bf16[128,1,128]{2,0,1:T(8,128)(2,1)S(1)}, bf16[128,1,128]{2,0,1:T(8,128)(2,1)S(1)}, u32[]{:S(2)}, u32[]{:S(2)}) collective-permute-start(bf16[128,1,128]{2,0,1:T(8,128)(2,1)S(1)} %get-tuple-element.59), channel_id=1, source_target_pairs={{0,4},{4,8},{8,12},{12,16},{16,20},{20,24},{24,28},{1,5},{5,9},{9,... | collective-permute-start | bytes 98312 | tf_op jit(solution)/shard_map/ppermute | solution.py:20
  108.3 3.7 %collective-permute-start.16 = (bf16[128,1,128]{2,0,1:T(8,128)(2,1)S(1)}, bf16[128,1,128]{2,0,1:T(8,128)(2,1)S(1)}, u32[]{:S(2)}, u32[]{:S(2)}) collective-permute-start(bf16[128,1,128]{2,0,1:T(8,128)(2,1)S(1)} %get-tuple-element.60), channel_id=1, source_target_pairs={{4,0},{8,4},{12,8},{16,12},{20,16},{24,20},{28,24},{5,1},{9,5},{13... | collective-permute-start | bytes 98312 | tf_op jit(solution)/shard_map/ppermute | solution.py:21
  112.0 4.8 %copy-start.9 = (bf16[9,69,128]{2,1,0:T(8,128)(2,1)S(1)}, bf16[9,69,128]{2,1,0:T(8,128)(2,1)}, u32[]{:S(2)}) copy-start(bf16[9,69,128]{2,1,0:T(8,128)(2,1)} %param.29) | copy-start | bytes 476932
  112.6 5.5 %collective-permute-start.17 = (bf16[128,18,1]{0,1,2:T(8,128)(2,1)S(1)}, bf16[128,18,1]{0,1,2:T(8,128)(2,1)S(1)}, u32[]{:S(2)}, u32[]{:S(2)}) collective-permute-start(bf16[128,18,1]{0,1,2:T(8,128)(2,1)S(1)} %copy.62), channel_id=1, source_target_pairs={{0,1},{1,2},{2,3},{3,0},{4,5},{5,6},{6,7},{7,4},{8,9},{9,10},{10,1... | collective-permute-start | bytes 13832 | tf_op jit(solution)/shard_map/ppermute | solution.py:25
  113.0 5.5 %collective-permute-start.18 = (bf16[128,18,1]{0,1,2:T(8,128)(2,1)S(1)}, bf16[128,18,1]{0,1,2:T(8,128)(2,1)S(1)}, u32[]{:S(2)}, u32[]{:S(2)}) collective-permute-start(bf16[128,18,1]{0,1,2:T(8,128)(2,1)S(1)} %copy.65), channel_id=1, source_target_pairs={{1,0},{2,1},{3,2},{0,3},{5,4},{6,5},{7,6},{4,7},{9,8},{10,9},{11,1... | collective-permute-start | bytes 13832 | tf_op jit(solution)/shard_map/ppermute | solution.py:26
  123.1 19.9 %copy-start.1 = (bf16[1024,1024]{1,0:T(8,128)(2,1)S(1)}, bf16[1024,1024]{1,0:T(8,128)(2,1)}, u32[]{:S(2)}) copy-start(bf16[1024,1024]{1,0:T(8,128)(2,1)} %param.25) | copy-start | bytes 6291460
  123.6 18.6 %copy-start.14 = (s32[64]{0:T(128)S(1)}, s32[64]{0:T(128)}, u32[]{:S(2)}) copy-start(s32[64]{0:T(128)} %param.18) | copy-start | bytes 772
  124.7 3.6 %collective-permute-start.19 = (f32[64]{0:T(128)S(1)}, f32[64]{0:T(128)S(1)}, u32[]{:S(2)}, u32[]{:S(2)}) collective-permute-start(f32[64]{0:T(128)S(1)} %fusion.40), channel_id=1, source_target_pairs={{0,1},{1,0},{2,3},{3,2},{4,5},{5,4},{6,7},{7,6},{8,9},{9,8},{10,11... | collective-permute-start | bytes 776 | tf_op jit(solution)/shard_map/ppermute | solution.py:34
  128.3 4.4 %collective-permute-start.20 = (f32[64]{0:T(128)S(1)}, f32[64]{0:T(128)S(1)}, u32[]{:S(2)}, u32[]{:S(2)}) collective-permute-start(f32[64]{0:T(128)S(1)} %add.311), channel_id=1, source_target_pairs={{0,2},{1,3},{2,0},{3,1},{4,6},{5,7},{6,4},{7,5},{8,10},{9,11},{10,... | collective-permute-start | bytes 776 | tf_op jit(solution)/shard_map/ppermute | solution.py:34
  132.7 1.1 collective-permute-start.21
  133.9 4.1 %collective-permute-start.22 = (f32[64]{0:T(128)S(1)}, f32[64]{0:T(128)S(1)}, u32[]{:S(2)}, u32[]{:S(2)}) collective-permute-start(f32[64]{0:T(128)S(1)} %add.313), channel_id=1, source_target_pairs={{0,8},{4,12},{8,0},{12,4},{16,24},{20,28},{24,16},{28,20},{1,9},{5... | collective-permute-start | bytes 776 | tf_op jit(solution)/shard_map/ppermute | solution.py:34
  137.9 4.3 %collective-permute-start.23 = (f32[64]{0:T(128)S(1)}, f32[64]{0:T(128)S(1)}, u32[]{:S(2)}, u32[]{:S(2)}) collective-permute-start(f32[64]{0:T(128)S(1)} %add.314), channel_id=1, source_target_pairs={{0,16},{4,20},{8,24},{12,28},{16,0},{20,4},{24,8},{28,12},{1,17},{... | collective-permute-start | bytes 776 | tf_op jit(solution)/shard_map/ppermute | solution.py:34
  (8 other events, 8.7 us)

commit v10 on v9

--- a/solution.py
+++ b/solution.py
@@ -99,7 +99,7 @@
 def attend_part(queries, key_chunks, value_chunks, scales, head_size):
     query_count, width = queries.shape
     key_count = sum(chunk.shape[0] for chunk in key_chunks)
-    cap = 1 << (max(8, (1 << 20) // key_count).bit_length() - 1)
+    cap = 1 << (max(8, (1 << 18) // key_count).bit_length() - 1)
     block = math.gcd(query_count, cap)
     heads = width // head_size
     part = jax.ShapeDtypeStruct((query_count, width), jnp.float32)

time: 143 us -> 144 us (level)
  Pallas kernels: 18.4 us -> 20.4 us
  waiting for transfers between devices: 52.8 us -> 51 us
    pallas_call x4, Pallas kernels: 18.4 us -> 20.4 us  [attend_part(): pl.pallas_call(functools.partial(attention_kernel, head_size=head_size, c...]
  transfers between devices with their start and end apart: 24 -> 24, of which waited for: 17 -> 17; matrix products, arithmetic and copies ran while one was open for 2% -> 2% of each run, Pallas kernels for 10% -> 11%
where the time goes in v10:
time: 144 us
  waiting for transfers between devices  51 us (35%)
  starting transfers between devices  38.9 us (27%)
  Pallas kernels  20.4 us (14%)
  matrix products  17.7 us (12%)
  local copies, waits for them, and re-layouts  10.9 us (8%)
  other arithmetic  3.6 us (2%)
    pallas_call x4, Pallas kernels, attend_part(): pl.pallas_call(functools.partial(attention_kernel, head_size=head_size, c...  20.4 us
    ppermute x3, waiting for transfers between devices, exchange_blocks(): lax.ppermute(outgoing, axis, [(i, (i + shift) % size) for i in range(size)])  12.7 us
    ppermute x3, waiting for transfers between devices, on_device(): lax.ppermute(key_value, 'lat', [(i, i ^ 2 * d) for i in range(lat_size)])  12 us
    dot_general x27, matrix products, convolution_kernel_taps(): jnp.einsum('oc,cyx->oyx', weight[tap_index], window, preferred_element_ty...  10.7 us
    ppermute x5, waiting for transfers between devices, butterfly_sum(): value = value + lax.ppermute(value, axis, partner)  8.49 us
    ppermute x5, starting transfers between devices, butterfly_sum(): value = value + lax.ppermute(value, axis, partner)  8.27 us
    ppermute x3, waiting for transfers between devices, return_blocks(): lax.ppermute(blocks[shift], axis, [((i + shift) % size, i) for i in range...  6.44 us
    unnamed x41, local copies, waits for them, and re-layouts  6.4 us
  transfers between devices with their start and end apart: 24, of which 17 were waited for; matrix products, arithmetic and copies ran while one was open for 2% of the time, Pallas kernels for 11%

profile of v10, /device:TPU:0, one launch (start us, length us, event | category | flops | bytes accessed | tf_op | source)
XLA Modules:
  0.0 143.9 jit_solution(15328402270299849404)
XLA Ops:
  0.6 1.5 %copy.49 = bf16[69,16,128]{0,2,1:T(8,128)(2,1)S(1)} copy(bf16[69,16,128]{2,1,0:T(8,128)(2,1)} %param.15) | data formatting | bytes 565248 | tf_op args[0]
  2.2 2.5 %collective-permute-start = (bf16[69,2,128]{0,2,1:T(8,128)(2,1)S(1)}, bf16[69,2,128]{0,2,1:T(8,128)(2,1)S(1)}, u32[]{:S(2)}, u32[]{:S(2)}) collective-permute-start(bf16[69,2,128]{0,2,1:T(8,128)(2,1)S(1)} %get-tuple-element.67), channel_id=1, source_target_pairs={{0,4},{4,8},{8,12},{12,16},{16,20},{20,24},{24,28},{1,5},{5,9},{9,... | collective-permute-start | bytes 105992 | tf_op jit(solution)/shard_map/ppermute | solution.py:20
  6.0 3.9 %collective-permute-done.1 = bf16[69,2,128]{0,2,1:T(8,128)(2,1)S(1)} collective-permute-done((bf16[69,2,128]{0,2,1:T(8,128)(2,1)S(1)}, bf16[69,2,128]{0,2,1:T(8,128)(2,1)S(1)}, u32[]{:S(2)}, u32[]{:S(2)}) %collective-permute-start.1) | collective-permute-done | bytes 35360 | tf_op jit(solution)/shard_map/ppermute | solution.py:21
  9.9 1.6 %collective-permute-start.2 = (bf16[69,20,2]{0,2,1:T(2,128)(2,1)S(1)}, bf16[69,20,2]{0,2,1:T(2,128)(2,1)S(1)}, u32[]{:S(2)}, u32[]{:S(2)}) collective-permute-start(bf16[69,20,2]{0,2,1:T(2,128)(2,1)S(1)} %get-tuple-element.51), channel_id=1, source_target_pairs={{0,1},{1,2},{2,3},{3,0},{4,5},{5,6},{6,7},{7,4},{8,9},{9,10},{10,1... | collective-permute-start | bytes 16568 | tf_op jit(solution)/shard_map/ppermute | solution.py:25
  11.6 2.2 %collective-permute-start.3 = (bf16[69,20,2]{0,2,1:T(2,128)(2,1)S(1)}, bf16[69,20,2]{0,2,1:T(2,128)(2,1)S(1)}, u32[]{:S(2)}, u32[]{:S(2)}) collective-permute-start(bf16[69,20,2]{0,2,1:T(2,128)(2,1)S(1)} %get-tuple-element.52), channel_id=1, source_target_pairs={{1,0},{2,1},{3,2},{0,3},{5,4},{6,5},{7,6},{4,7},{9,8},{10,9},{11,1... | collective-permute-start | bytes 16568 | tf_op jit(solution)/shard_map/ppermute | solution.py:26
  13.8 1.6 %collective-permute-done.2 = bf16[69,20,2]{0,2,1:T(2,128)(2,1)S(1)} collective-permute-done((bf16[69,20,2]{0,2,1:T(2,128)(2,1)S(1)}, bf16[69,20,2]{0,2,1:T(2,128)(2,1)S(1)}, u32[]{:S(2)}, u32[]{:S(2)}) %collective-permute-start.2) | collective-permute-done | bytes 5552 | tf_op jit(solution)/shard_map/ppermute | solution.py:25
  30.0 1.4 collective-permute-start.4
  31.4 3.1 %collective-permute-start.5 = (bf16[3,128,256]{2,1,0:T(8,128)(2,1)S(1)}, bf16[3,128,256]{2,1,0:T(8,128)(2,1)S(1)}, u32[]{:S(2)}, u32[]{:S(2)}) collective-permute-start(bf16[3,128,256]{2,1,0:T(8,128)(2,1)S(1)} %get-tuple-element.49), channel_id=1, source_target_pairs={{0,2},{1,3},{2,0},{3,1},{4,6},{5,7},{6,4},{7,5},{8,10},{9,11},{10,... | collective-permute-start | bytes 589832 | tf_op jit(solution)/shard_map/ppermute | solution.py:145
  35.3 3.6 %collective-permute-done.4 = bf16[3,128,256]{2,1,0:T(8,128)(2,1)S(1)} collective-permute-done((bf16[3,128,256]{2,1,0:T(8,128)(2,1)S(1)}, bf16[3,128,256]{2,1,0:T(8,128)(2,1)S(1)}, u32[]{:S(2)}, u32[]{:S(2)}) %collective-permute-start.4) | collective-permute-done | bytes 196640 | tf_op jit(solution)/shard_map/ppermute | solution.py:145
  39.0 9.1 %collective-permute-done.5 = bf16[3,128,256]{2,1,0:T(8,128)(2,1)S(1)} collective-permute-done((bf16[3,128,256]{2,1,0:T(8,128)(2,1)S(1)}, bf16[3,128,256]{2,1,0:T(8,128)(2,1)S(1)}, u32[]{:S(2)}, u32[]{:S(2)}) %collective-permute-start.5) | collective-permute-done | bytes 196640 | tf_op jit(solution)/shard_map/ppermute | solution.py:145
  48.4 1.6 %collective-permute-done.7 = bf16[3,512,128]{2,1,0:T(8,128)(2,1)S(1)} collective-permute-done((bf16[3,512,128]{2,1,0:T(8,128)(2,1)S(1)}, bf16[3,512,128]{2,1,0:T(8,128)(2,1)S(1)}, u32[]{:S(2)}, u32[]{:S(2)}) %collective-permute-start.7) | collective-permute-done | bytes 393248 | tf_op jit(solution)/shard_map/ppermute | solution.py:219
  50.0 2.8 %collective-permute-start.8 = (bf16[2,1024,128]{2,1,0:T(8,128)(2,1)S(1)}, bf16[2,1024,128]{2,1,0:T(8,128)(2,1)}, u32[]{:S(2)}, u32[]{:S(2)}) collective-permute-start(bf16[2,1024,128]{2,1,0:T(8,128)(2,1)S(1)} %pad_maximum_fusion.6), channel_id=1, source_target_pairs={{0,8},{4,12},{8,0},{12,4},{16,24},{20,28},{24,16},{28,20},{1,9},{5... | collective-permute-start | bytes 1572872 | tf_op jit(solution)/shard_map/ppermute | solution.py:224
  52.9 1.6 %collective-permute-start.10 = (bf16[2,1024,128]{2,1,0:T(8,128)(2,1)S(1)}, bf16[2,1024,128]{2,1,0:T(8,128)(2,1)S(1)}, u32[]{:S(2)}, u32[]{:S(2)}) collective-permute-start(bf16[2,1024,128]{2,1,0:T(8,128)(2,1)S(1)} %pad_maximum_fusion.6), channel_id=1, source_target_pairs={{0,24},{4,28},{8,16},{12,20},{16,8},{20,12},{24,0},{28,4},{1,25},{... | collective-permute-start | bytes 1572872 | tf_op jit(solution)/shard_map/ppermute | solution.py:224
  54.5 5.1 %shard_map.166 = (f32[1024,128]{1,0:T(8,128)S(1)}, f32[1024,128]{1,0:T(8,128)S(1)}, f32[1024,128]{1,0:T(8,128)S(1)}) custom-call(f32[2]{0:T(128)S(1)} %dynamic-slice_multiply_fusion.scale_ref, bf16[1024,128]{1,0:T(8,128)(2,1)S(1)} %get-tuple-element.43.q_ref, bf16[1024,128]{1,0:T(8,128)(2,1)S(1)} %get-tuple-element.44.refs_0_, ...), custom_call_target="tpu_custom_call" | custom-call | flops 536870912 | bytes 2359296 | tf_op jit(solution)/shard_map/pallas_call | solution.py:111
  59.6 6.0 %collective-permute-done.8 = bf16[2,1024,128]{2,1,0:T(8,128)(2,1)} collective-permute-done((bf16[2,1024,128]{2,1,0:T(8,128)(2,1)S(1)}, bf16[2,1024,128]{2,1,0:T(8,128)(2,1)}, u32[]{:S(2)}, u32[]{:S(2)}) %collective-permute-start.8) | collective-permute-done | bytes 524320 | tf_op jit(solution)/shard_map/ppermute | solution.py:224
  66.7 5.1 %shard_map.167 = (f32[1024,128]{1,0:T(8,128)S(1)}, f32[1024,128]{1,0:T(8,128)S(1)}, f32[1024,128]{1,0:T(8,128)S(1)}) custom-call(f32[2]{0:T(128)S(1)} %dynamic-slice_multiply_fusion.scale_ref, bf16[1024,128]{1,0:T(8,128)(2,1)S(1)} %get-tuple-element.43.q_ref, bf16[1024,128]{1,0:T(8,128)(2,1)S(1)} %get-tuple-element.62.refs_0_, ...), custom_call_target="tpu_custom_call" | custom-call | flops 536870912 | bytes 2359296 | tf_op jit(solution)/shard_map/pallas_call | solution.py:111
  71.9 5.9 %collective-permute-done.9 = bf16[2,1024,128]{2,1,0:T(8,128)(2,1)S(1)} collective-permute-done((bf16[2,1024,128]{2,1,0:T(8,128)(2,1)S(1)}, bf16[2,1024,128]{2,1,0:T(8,128)(2,1)S(1)}, u32[]{:S(2)}, u32[]{:S(2)}) %collective-permute-start.9) | collective-permute-done | bytes 524320 | tf_op jit(solution)/shard_map/ppermute | solution.py:224
  77.8 5.1 %shard_map.168 = (f32[1024,128]{1,0:T(8,128)S(1)}, f32[1024,128]{1,0:T(8,128)S(1)}, f32[1024,128]{1,0:T(8,128)S(1)}) custom-call(f32[2]{0:T(128)S(1)} %dynamic-slice_multiply_fusion.scale_ref, bf16[1024,128]{1,0:T(8,128)(2,1)S(1)} %get-tuple-element.43.q_ref, bf16[1024,128]{1,0:T(8,128)(2,1)S(1)} %get-tuple-element.64.refs_0_, ...), custom_call_target="tpu_custom_call" | custom-call | flops 536870912 | bytes 2359296 | tf_op jit(solution)/shard_map/pallas_call | solution.py:111
  83.0 5.1 %shard_map.169 = (f32[1024,128]{1,0:T(8,128)S(1)}, f32[1024,128]{1,0:T(8,128)S(1)}, f32[1024,128]{1,0:T(8,128)S(1)}) custom-call(f32[2]{0:T(128)S(1)} %dynamic-slice_multiply_fusion.scale_ref, bf16[1024,128]{1,0:T(8,128)(2,1)S(1)} %get-tuple-element.43.q_ref, bf16[1024,128]{1,0:T(8,128)(2,1)S(1)} %get-tuple-element.66.refs_0_, ...), custom_call_target="tpu_custom_call" | custom-call | flops 536870912 | bytes 2359296 | tf_op jit(solution)/shard_map/pallas_call | solution.py:111
  90.4 5.6 %collective-permute-start.12 = (bf16[128,256]{1,0:T(8,128)(2,1)S(1)}, bf16[128,256]{1,0:T(8,128)(2,1)S(1)}, u32[]{:S(2)}, u32[]{:S(2)}) collective-permute-start(bf16[128,256]{1,0:T(8,128)(2,1)S(1)} %get-tuple-element.71), channel_id=1, source_target_pairs={{1,0},{2,1},{3,2},{0,3},{5,4},{6,5},{7,6},{4,7},{9,8},{10,9},{11,1... | collective-permute-start | bytes 196616 | tf_op jit(solution)/shard_map/ppermute | solution.py:153
  96.7 1.8 %collective-permute-done.12 = bf16[128,256]{1,0:T(8,128)(2,1)S(1)} collective-permute-done((bf16[128,256]{1,0:T(8,128)(2,1)S(1)}, bf16[128,256]{1,0:T(8,128)(2,1)S(1)}, u32[]{:S(2)}, u32[]{:S(2)}) %collective-permute-start.12) | collective-permute-done | bytes 65568 | tf_op jit(solution)/shard_map/ppermute | solution.py:153
  98.5 4.6 %collective-permute-done.13 = bf16[128,256]{1,0:T(8,128)(2,1)S(1)} collective-permute-done((bf16[128,256]{1,0:T(8,128)(2,1)S(1)}, bf16[128,256]{1,0:T(8,128)(2,1)S(1)}, u32[]{:S(2)}, u32[]{:S(2)}) %collective-permute-start.13) | collective-permute-done | bytes 65568 | tf_op jit(solution)/shard_map/ppermute | solution.py:153
  103.9 3.4 %fusion.58 = bf16[128,4,4,32,4]{0,3,4,2,1:T(8,128)(2,1)S(1)} fusion(bf16[4,32,1024,1,1]{2,1,4,3,0:T(8,128)(2,1)S(1)} %bitcast.271, bf16[1024,4,4,128]{3,2,1,0:T(4,128)(2,1)} %param.28), kind=kOutput, calls=%fused_computation.74 | convolution fusion | flops 539230208 | bytes 4980736 | tf_op jit(solution)/shard_map/pqd,dabh->hpaqb/dot_general | solution.py:261
  110.6 2.4 %collective-permute-done.16 = bf16[128,1,128]{2,0,1:T(8,128)(2,1)S(1)} collective-permute-done((bf16[128,1,128]{2,0,1:T(8,128)(2,1)S(1)}, bf16[128,1,128]{2,0,1:T(8,128)(2,1)S(1)}, u32[]{:S(2)}, u32[]{:S(2)}) %collective-permute-start.16) | collective-permute-done | bytes 32800 | tf_op jit(solution)/shard_map/ppermute | solution.py:21
  113.9 4.1 %collective-permute-start.18 = (bf16[128,18,1]{0,1,2:T(8,128)(2,1)S(1)}, bf16[128,18,1]{0,1,2:T(8,128)(2,1)S(1)}, u32[]{:S(2)}, u32[]{:S(2)}) collective-permute-start(bf16[128,18,1]{0,1,2:T(8,128)(2,1)S(1)} %copy.65), channel_id=1, source_target_pairs={{1,0},{2,1},{3,2},{0,3},{5,4},{6,5},{7,6},{4,7},{9,8},{10,9},{11,1... | collective-permute-start | bytes 13832 | tf_op jit(solution)/shard_map/ppermute | solution.py:26
  120.5 1.8 %maximum_maximum_fusion = (bf16[128,18,129]{2,0,1:T(8,128)(2,1)S(1)}, bf16[128,18,129]{2,0,1:T(8,128)(2,1)S(1)}) fusion(bf16[128,1,128]{2,0,1:T(8,128)(2,1)S(1)} %collective-permute-done.16, bf16[128,16,128]{2,0,1:T(8,128)(2,1)S(1)} %copy.59, bf16[128,1,128]{2,0,1:T(8,128)(2,1)S(1)} %collective-permute-done.15, bf16[128,18,1]{2,0,1:T(8,128)(2,1)S(1)} %copy.63, ...), kind=kLoop, calls=%fused_computation.54 | loop fusion | flops 4755456 | bytes 1787904 | tf_op jit(solution)/shard_map/concatenate | solution.py:27
  126.0 3.2 %collective-permute-done.19 = f32[64]{0:T(128)S(1)} collective-permute-done((f32[64]{0:T(128)S(1)}, f32[64]{0:T(128)S(1)}, u32[]{:S(2)}, u32[]{:S(2)}) %collective-permute-start.19) | collective-permute-done | bytes 288 | tf_op jit(solution)/shard_map/ppermute | solution.py:34
  129.2 2.6 %collective-permute-start.20 = (f32[64]{0:T(128)S(1)}, f32[64]{0:T(128)S(1)}, u32[]{:S(2)}, u32[]{:S(2)}) collective-permute-start(f32[64]{0:T(128)S(1)} %add.311), channel_id=1, source_target_pairs={{0,2},{1,3},{2,0},{3,1},{4,6},{5,7},{6,4},{7,5},{8,10},{9,11},{10,... | collective-permute-start | bytes 776 | tf_op jit(solution)/shard_map/ppermute | solution.py:34
  131.8 1.9 %collective-permute-done.20 = f32[64]{0:T(128)S(1)} collective-permute-done((f32[64]{0:T(128)S(1)}, f32[64]{0:T(128)S(1)}, u32[]{:S(2)}, u32[]{:S(2)}) %collective-permute-start.20) | collective-permute-done | bytes 288 | tf_op jit(solution)/shard_map/ppermute | solution.py:34
  134.8 2.5 %collective-permute-start.22 = (f32[64]{0:T(128)S(1)}, f32[64]{0:T(128)S(1)}, u32[]{:S(2)}, u32[]{:S(2)}) collective-permute-start(f32[64]{0:T(128)S(1)} %add.313), channel_id=1, source_target_pairs={{0,8},{4,12},{8,0},{12,4},{16,24},{20,28},{24,16},{28,20},{1,9},{5... | collective-permute-start | bytes 776 | tf_op jit(solution)/shard_map/ppermute | solution.py:34
  137.3 1.5 %collective-permute-done.22 = f32[64]{0:T(128)S(1)} collective-permute-done((f32[64]{0:T(128)S(1)}, f32[64]{0:T(128)S(1)}, u32[]{:S(2)}, u32[]{:S(2)}) %collective-permute-start.22) | collective-permute-done | bytes 288 | tf_op jit(solution)/shard_map/ppermute | solution.py:34
  138.9 2.8 %collective-permute-start.23 = (f32[64]{0:T(128)S(1)}, f32[64]{0:T(128)S(1)}, u32[]{:S(2)}, u32[]{:S(2)}) collective-permute-start(f32[64]{0:T(128)S(1)} %add.314), channel_id=1, source_target_pairs={{0,16},{4,20},{8,24},{12,28},{16,0},{20,4},{24,8},{28,12},{1,17},{... | collective-permute-start | bytes 776 | tf_op jit(solution)/shard_map/ppermute | solution.py:34
  (139 shorter events, 35.4 us)
Async XLA Ops:
  0.6 25.5 %copy-start = (bf16[1024,1024]{1,0:T(8,128)(2,1)S(1)}, bf16[1024,1024]{1,0:T(8,128)(2,1)}, u32[]{:S(2)}) copy-start(bf16[1024,1024]{1,0:T(8,128)(2,1)} %param.25) | copy-start | bytes 6291460
  2.1 13.6 %copy-start.10 = (bf16[9,128,69]{1,2,0:T(8,128)(2,1)S(1)}, bf16[9,128,69]{1,2,0:T(8,128)(2,1)}, u32[]{:S(2)}) copy-start(bf16[9,128,69]{1,2,0:T(8,128)(2,1)} %param.19) | copy-start | bytes 476932
  2.2 3.8 %collective-permute-start = (bf16[69,2,128]{0,2,1:T(8,128)(2,1)S(1)}, bf16[69,2,128]{0,2,1:T(8,128)(2,1)S(1)}, u32[]{:S(2)}, u32[]{:S(2)}) collective-permute-start(bf16[69,2,128]{0,2,1:T(8,128)(2,1)S(1)} %get-tuple-element.67), channel_id=1, source_target_pairs={{0,4},{4,8},{8,12},{12,16},{16,20},{20,24},{24,28},{1,5},{5,9},{9,... | collective-permute-start | bytes 105992 | tf_op jit(solution)/shard_map/ppermute | solution.py:20
  4.7 5.3 %collective-permute-start.1 = (bf16[69,2,128]{0,2,1:T(8,128)(2,1)S(1)}, bf16[69,2,128]{0,2,1:T(8,128)(2,1)S(1)}, u32[]{:S(2)}, u32[]{:S(2)}) collective-permute-start(bf16[69,2,128]{0,2,1:T(8,128)(2,1)S(1)} %get-tuple-element.68), channel_id=1, source_target_pairs={{4,0},{8,4},{12,8},{16,12},{20,16},{24,20},{28,24},{5,1},{9,5},{13... | collective-permute-start | bytes 105992 | tf_op jit(solution)/shard_map/ppermute | solution.py:21
  9.9 5.5 %collective-permute-start.2 = (bf16[69,20,2]{0,2,1:T(2,128)(2,1)S(1)}, bf16[69,20,2]{0,2,1:T(2,128)(2,1)S(1)}, u32[]{:S(2)}, u32[]{:S(2)}) collective-permute-start(bf16[69,20,2]{0,2,1:T(2,128)(2,1)S(1)} %get-tuple-element.51), channel_id=1, source_target_pairs={{0,1},{1,2},{2,3},{3,0},{4,5},{5,6},{6,7},{7,4},{8,9},{9,10},{10,1... | collective-permute-start | bytes 16568 | tf_op jit(solution)/shard_map/ppermute | solution.py:25
  11.6 3.9 %collective-permute-start.3 = (bf16[69,20,2]{0,2,1:T(2,128)(2,1)S(1)}, bf16[69,20,2]{0,2,1:T(2,128)(2,1)S(1)}, u32[]{:S(2)}, u32[]{:S(2)}) collective-permute-start(bf16[69,20,2]{0,2,1:T(2,128)(2,1)S(1)} %get-tuple-element.52), channel_id=1, source_target_pairs={{1,0},{2,1},{3,2},{0,3},{5,4},{6,5},{7,6},{4,7},{9,8},{10,9},{11,1... | collective-permute-start | bytes 16568 | tf_op jit(solution)/shard_map/ppermute | solution.py:26
  22.9 2.2 %copy-start.2 = (bf16[4,4,128,1024]{3,2,1,0:T(8,128)(2,1)S(1)}, bf16[4,4,128,1024]{3,2,1,0:T(8,128)(2,1)}, u32[]{:S(2)}) copy-start(bf16[4,4,128,1024]{3,2,1,0:T(8,128)(2,1)} %param.21) | copy-start | bytes 12582916
  30.0 9.0 %collective-permute-start.4 = (bf16[3,128,256]{2,1,0:T(8,128)(2,1)S(1)}, bf16[3,128,256]{2,1,0:T(8,128)(2,1)S(1)}, u32[]{:S(2)}, u32[]{:S(2)}) collective-permute-start(bf16[3,128,256]{2,1,0:T(8,128)(2,1)S(1)} %get-tuple-element.50), channel_id=1, source_target_pairs={{0,1},{1,2},{2,3},{3,0},{4,5},{5,6},{6,7},{7,4},{8,9},{9,10},{10,1... | collective-permute-start | bytes 589832 | tf_op jit(solution)/shard_map/ppermute | solution.py:145
  31.4 16.6 %collective-permute-start.5 = (bf16[3,128,256]{2,1,0:T(8,128)(2,1)S(1)}, bf16[3,128,256]{2,1,0:T(8,128)(2,1)S(1)}, u32[]{:S(2)}, u32[]{:S(2)}) collective-permute-start(bf16[3,128,256]{2,1,0:T(8,128)(2,1)S(1)} %get-tuple-element.49), channel_id=1, source_target_pairs={{0,2},{1,3},{2,0},{3,1},{4,6},{5,7},{6,4},{7,5},{8,10},{9,11},{10,... | collective-permute-start | bytes 589832 | tf_op jit(solution)/shard_map/ppermute | solution.py:145
  34.5 13.6 %collective-permute-start.6 = (bf16[3,128,256]{2,1,0:T(8,128)(2,1)S(1)}, bf16[3,128,256]{2,1,0:T(8,128)(2,1)S(1)}, u32[]{:S(2)}, u32[]{:S(2)}) collective-permute-start(bf16[3,128,256]{2,1,0:T(8,128)(2,1)S(1)} %get-tuple-element.48), channel_id=1, source_target_pairs={{0,3},{1,0},{2,1},{3,2},{4,7},{5,4},{6,5},{7,6},{8,11},{9,8},{10,9... | collective-permute-start | bytes 589832 | tf_op jit(solution)/shard_map/ppermute | solution.py:145
  48.1 4.7 %copy-start.13 = (f32[16]{0:T(128)S(1)}, f32[16]{0:T(128)}, u32[]{:S(2)}) copy-start(f32[16]{0:T(128)} %param.27) | copy-start | bytes 196
  48.2 1.8 %collective-permute-start.7 = (bf16[3,512,128]{2,1,0:T(8,128)(2,1)S(1)}, bf16[3,512,128]{2,1,0:T(8,128)(2,1)S(1)}, u32[]{:S(2)}, u32[]{:S(2)}) collective-permute-start(bf16[3,512,128]{2,1,0:T(8,128)(2,1)S(1)} %get-tuple-element.45), channel_id=1, source_target_pairs={{0,4},{4,0},{8,12},{12,8},{16,20},{20,16},{24,28},{28,24},{1,5},{5... | collective-permute-start | bytes 1179656 | tf_op jit(solution)/shard_map/ppermute | solution.py:219
  50.0 15.7 %collective-permute-start.8 = (bf16[2,1024,128]{2,1,0:T(8,128)(2,1)S(1)}, bf16[2,1024,128]{2,1,0:T(8,128)(2,1)}, u32[]{:S(2)}, u32[]{:S(2)}) collective-permute-start(bf16[2,1024,128]{2,1,0:T(8,128)(2,1)S(1)} %pad_maximum_fusion.6), channel_id=1, source_target_pairs={{0,8},{4,12},{8,0},{12,4},{16,24},{20,28},{24,16},{28,20},{1,9},{5... | collective-permute-start | bytes 1572872 | tf_op jit(solution)/shard_map/ppermute | solution.py:224
  52.9 24.9 %collective-permute-start.9 = (bf16[2,1024,128]{2,1,0:T(8,128)(2,1)S(1)}, bf16[2,1024,128]{2,1,0:T(8,128)(2,1)S(1)}, u32[]{:S(2)}, u32[]{:S(2)}) collective-permute-start(bf16[2,1024,128]{2,1,0:T(8,128)(2,1)S(1)} %pad_maximum_fusion.6), channel_id=1, source_target_pairs={{0,16},{4,20},{8,24},{12,28},{16,0},{20,4},{24,8},{28,12},{1,17},{... | collective-permute-start | bytes 1572872 | tf_op jit(solution)/shard_map/ppermute | solution.py:224
  52.9 30.0 %collective-permute-start.10 = (bf16[2,1024,128]{2,1,0:T(8,128)(2,1)S(1)}, bf16[2,1024,128]{2,1,0:T(8,128)(2,1)S(1)}, u32[]{:S(2)}, u32[]{:S(2)}) collective-permute-start(bf16[2,1024,128]{2,1,0:T(8,128)(2,1)S(1)} %pad_maximum_fusion.6), channel_id=1, source_target_pairs={{0,24},{4,28},{8,16},{12,20},{16,8},{20,12},{24,0},{28,4},{1,25},{... | collective-permute-start | bytes 1572872 | tf_op jit(solution)/shard_map/ppermute | solution.py:224
  88.9 1.4 collective-permute-start.11
  90.3 13.2 %copy-start.5 = (bf16[1024,1024]{1,0:T(8,128)(2,1)S(1)}, bf16[1024,1024]{1,0:T(8,128)(2,1)}, u32[]{:S(2)}) copy-start(bf16[1024,1024]{1,0:T(8,128)(2,1)} %param.26) | copy-start | bytes 6291460
  90.4 8.1 %collective-permute-start.12 = (bf16[128,256]{1,0:T(8,128)(2,1)S(1)}, bf16[128,256]{1,0:T(8,128)(2,1)S(1)}, u32[]{:S(2)}, u32[]{:S(2)}) collective-permute-start(bf16[128,256]{1,0:T(8,128)(2,1)S(1)} %get-tuple-element.71), channel_id=1, source_target_pairs={{1,0},{2,1},{3,2},{0,3},{5,4},{6,5},{7,6},{4,7},{9,8},{10,9},{11,1... | collective-permute-start | bytes 196616 | tf_op jit(solution)/shard_map/ppermute | solution.py:153
  96.0 7.1 %collective-permute-start.13 = (bf16[128,256]{1,0:T(8,128)(2,1)S(1)}, bf16[128,256]{1,0:T(8,128)(2,1)S(1)}, u32[]{:S(2)}, u32[]{:S(2)}) collective-permute-start(bf16[128,256]{1,0:T(8,128)(2,1)S(1)} %get-tuple-element.70), channel_id=1, source_target_pairs={{2,0},{3,1},{0,2},{1,3},{6,4},{7,5},{4,6},{5,7},{10,8},{11,9},{8,1... | collective-permute-start | bytes 196616 | tf_op jit(solution)/shard_map/ppermute | solution.py:153
  96.7 6.5 %collective-permute-start.14 = (bf16[128,256]{1,0:T(8,128)(2,1)S(1)}, bf16[128,256]{1,0:T(8,128)(2,1)S(1)}, u32[]{:S(2)}, u32[]{:S(2)}) collective-permute-start(bf16[128,256]{1,0:T(8,128)(2,1)S(1)} %get-tuple-element.69), channel_id=1, source_target_pairs={{3,0},{0,1},{1,2},{2,3},{7,4},{4,5},{5,6},{6,7},{11,8},{8,9},{9,10... | collective-permute-start | bytes 196616 | tf_op jit(solution)/shard_map/ppermute | solution.py:153
  107.9 2.6 %collective-permute-start.15 = (bf16[128,1,128]{2,0,1:T(8,128)(2,1)S(1)}, bf16[128,1,128]{2,0,1:T(8,128)(2,1)S(1)}, u32[]{:S(2)}, u32[]{:S(2)}) collective-permute-start(bf16[128,1,128]{2,0,1:T(8,128)(2,1)S(1)} %get-tuple-element.59), channel_id=1, source_target_pairs={{0,4},{4,8},{8,12},{12,16},{16,20},{20,24},{24,28},{1,5},{5,9},{9,... | collective-permute-start | bytes 98312 | tf_op jit(solution)/shard_map/ppermute | solution.py:20
  109.2 3.7 %collective-permute-start.16 = (bf16[128,1,128]{2,0,1:T(8,128)(2,1)S(1)}, bf16[128,1,128]{2,0,1:T(8,128)(2,1)S(1)}, u32[]{:S(2)}, u32[]{:S(2)}) collective-permute-start(bf16[128,1,128]{2,0,1:T(8,128)(2,1)S(1)} %get-tuple-element.60), channel_id=1, source_target_pairs={{4,0},{8,4},{12,8},{16,12},{20,16},{24,20},{28,24},{5,1},{9,5},{13... | collective-permute-start | bytes 98312 | tf_op jit(solution)/shard_map/ppermute | solution.py:21
  113.0 5.0 %copy-start.9 = (bf16[9,69,128]{2,1,0:T(8,128)(2,1)S(1)}, bf16[9,69,128]{2,1,0:T(8,128)(2,1)}, u32[]{:S(2)}) copy-start(bf16[9,69,128]{2,1,0:T(8,128)(2,1)} %param.29) | copy-start | bytes 476932
  113.6 5.5 %collective-permute-start.17 = (bf16[128,18,1]{0,1,2:T(8,128)(2,1)S(1)}, bf16[128,18,1]{0,1,2:T(8,128)(2,1)S(1)}, u32[]{:S(2)}, u32[]{:S(2)}) collective-permute-start(bf16[128,18,1]{0,1,2:T(8,128)(2,1)S(1)} %copy.62), channel_id=1, source_target_pairs={{0,1},{1,2},{2,3},{3,0},{4,5},{5,6},{6,7},{7,4},{8,9},{9,10},{10,1... | collective-permute-start | bytes 13832 | tf_op jit(solution)/shard_map/ppermute | solution.py:25
  113.9 5.5 %collective-permute-start.18 = (bf16[128,18,1]{0,1,2:T(8,128)(2,1)S(1)}, bf16[128,18,1]{0,1,2:T(8,128)(2,1)S(1)}, u32[]{:S(2)}, u32[]{:S(2)}) collective-permute-start(bf16[128,18,1]{0,1,2:T(8,128)(2,1)S(1)} %copy.65), channel_id=1, source_target_pairs={{1,0},{2,1},{3,2},{0,3},{5,4},{6,5},{7,6},{4,7},{9,8},{10,9},{11,1... | collective-permute-start | bytes 13832 | tf_op jit(solution)/shard_map/ppermute | solution.py:26
  124.0 19.8 %copy-start.1 = (bf16[1024,1024]{1,0:T(8,128)(2,1)S(1)}, bf16[1024,1024]{1,0:T(8,128)(2,1)}, u32[]{:S(2)}) copy-start(bf16[1024,1024]{1,0:T(8,128)(2,1)} %param.25) | copy-start | bytes 6291460
  124.6 18.6 %copy-start.14 = (s32[64]{0:T(128)S(1)}, s32[64]{0:T(128)}, u32[]{:S(2)}) copy-start(s32[64]{0:T(128)} %param.18) | copy-start | bytes 772
  125.7 3.6 %collective-permute-start.19 = (f32[64]{0:T(128)S(1)}, f32[64]{0:T(128)S(1)}, u32[]{:S(2)}, u32[]{:S(2)}) collective-permute-start(f32[64]{0:T(128)S(1)} %fusion.40), channel_id=1, source_target_pairs={{0,1},{1,0},{2,3},{3,2},{4,5},{5,4},{6,7},{7,6},{8,9},{9,8},{10,11... | collective-permute-start | bytes 776 | tf_op jit(solution)/shard_map/ppermute | solution.py:34
  129.2 4.4 %collective-permute-start.20 = (f32[64]{0:T(128)S(1)}, f32[64]{0:T(128)S(1)}, u32[]{:S(2)}, u32[]{:S(2)}) collective-permute-start(f32[64]{0:T(128)S(1)} %add.311), channel_id=1, source_target_pairs={{0,2},{1,3},{2,0},{3,1},{4,6},{5,7},{6,4},{7,5},{8,10},{9,11},{10,... | collective-permute-start | bytes 776 | tf_op jit(solution)/shard_map/ppermute | solution.py:34
  133.7 1.1 collective-permute-start.21
  134.8 4.0 %collective-permute-start.22 = (f32[64]{0:T(128)S(1)}, f32[64]{0:T(128)S(1)}, u32[]{:S(2)}, u32[]{:S(2)}) collective-permute-start(f32[64]{0:T(128)S(1)} %add.313), channel_id=1, source_target_pairs={{0,8},{4,12},{8,0},{12,4},{16,24},{20,28},{24,16},{28,20},{1,9},{5... | collective-permute-start | bytes 776 | tf_op jit(solution)/shard_map/ppermute | solution.py:34
  138.9 4.4 %collective-permute-start.23 = (f32[64]{0:T(128)S(1)}, f32[64]{0:T(128)S(1)}, u32[]{:S(2)}, u32[]{:S(2)}) collective-permute-start(f32[64]{0:T(128)S(1)} %add.314), channel_id=1, source_target_pairs={{0,16},{4,20},{8,24},{12,28},{16,0},{20,4},{24,8},{28,12},{1,17},{... | collective-permute-start | bytes 776 | tf_op jit(solution)/shard_map/ppermute | solution.py:34
  (8 other events, 8.7 us)

commit v11 on v9

--- a/solution.py
+++ b/solution.py
@@ -257,11 +257,31 @@
         latent_wide + jnp.dot(attended, output_weight, preferred_element_type=jnp.float32)
     ).astype(jnp.bfloat16)
     latent_grid = latent_two.reshape(lat_rows // 4, lon_cols // 4, model_width)
-    decoder_output = jax.nn.gelu(
-        jnp.einsum("pqd,dabh->hpaqb", latent_grid, patch_out, preferred_element_type=jnp.float32)
-    )
-    decoder_output = decoder_output.reshape(conv_count, lat_rows, lon_cols).astype(jnp.bfloat16)
-    decoder_output_padded = halo_padded(decoder_output, 1)
+
+    def decode(token_grid):
+        decoded = jax.nn.gelu(
+            jnp.einsum(
+                "pqd,dabh->hpaqb", token_grid, patch_out, preferred_element_type=jnp.float32
+            )
+        )
+        return decoded.reshape(conv_count, lat_rows, -1).astype(jnp.bfloat16)
+
+    lon_size = lax.axis_size("lon")
+    first_column = decode(latent_grid[:, :1])[:, :, :1]
+    last_column = decode(latent_grid[:, -1:])[:, :, -1:]
+    from_left = lax.ppermute(last_column, "lon", [(j, (j + 1) % lon_size) for j in range(lon_size)])
+    from_right = lax.ppermute(first_column, "lon", [((j + 1) % lon_size, j) for j in range(lon_size)])
+    decoder_output = jnp.concatenate([from_left, decode(latent_grid), from_right], axis=2)
+    down = [(i, i + 1) for i in range(lat_size - 1)]
+    up = [(i + 1, i) for i in range(lat_size - 1)]
+    decoder_output_padded = jnp.concatenate(
+        [
+            lax.ppermute(decoder_output[:, -1:], "lat", down),
+            decoder_output,
+            lax.ppermute(decoder_output[:, :1], "lat", up),
+        ],
+        axis=1,
+    )
     estimated_maps = fields.astype(jnp.float32) + convolution_kernel_taps(
         decoder_output_padded, final_convolution_result
     )

time: 143 us -> 163 us (1.14)
  waiting for transfers between devices: 52.8 us -> 70.3 us
  matrix products: 17.7 us -> 22.1 us
    ppermute x0 -> x4, waiting for transfers between devices: none -> 18.7 us  [the longest x1 9.15 us: on_device(): lax.ppermute(first_column, 'lon', [((j + 1) % lon_size, j) for j in range...]
    ppermute x0 -> x4, starting transfers between devices: none -> 7.3 us  [the longest x1 3.82 us: on_device(): lax.ppermute(first_column, 'lon', [((j + 1) % lon_size, j) for j in range...]
    ppermute x2 -> x1, starting transfers between devices: 6.09 us -> 2.25 us  [halo_padded(): from_right = lax.ppermute(array[:, :, :width], 'lon', left)]
    dot_general x1 -> x3, matrix products: 3.39 us -> 7.14 us  [decode(): jnp.einsum('pqd,dabh->hpaqb', token_grid, patch_out, preferred_element_ty...]
    unnamed x41 -> x45, local copies, waits for them, and re-layouts: 6.4 us -> 8.78 us
    ppermute x2 -> x1, waiting for transfers between devices: 6.27 us -> 3.93 us  [halo_padded(): from_below = lax.ppermute(array[:, :width], 'lat', up)]
    concatenate x2 -> x1, other arithmetic: 2.04 us -> 0.25 us  [halo_padded(): return jnp.concatenate([from_left, array, from_right], axis=2)]
    ppermute x2 -> x1, starting transfers between devices: 3.78 us -> 2.49 us  [halo_padded(): from_above = lax.ppermute(array[:, -width:], 'lat', down)]
  transfers between devices with their start and end apart: 24 -> 24, of which waited for: 17 -> 18; matrix products, arithmetic and copies ran while one was open for 2% -> 4% of each run, Pallas kernels for 10% -> 8%
where the time goes in v11:
time: 163 us
  waiting for transfers between devices  70.3 us (43%)
  starting transfers between devices  38.3 us (23%)
  matrix products  22.1 us (14%)
  Pallas kernels  18.4 us (11%)
  local copies, waits for them, and re-layouts  9.95 us (6%)
  other arithmetic  2.66 us (2%)
    pallas_call x4, Pallas kernels, attend_part(): pl.pallas_call(functools.partial(attention_kernel, head_size=head_size, c...  18.4 us
    ppermute x3, waiting for transfers between devices, on_device(): lax.ppermute(key_value, 'lat', [(i, i ^ 2 * d) for i in range(lat_size)])  14.1 us
    ppermute x3, waiting for transfers between devices, exchange_blocks(): lax.ppermute(outgoing, axis, [(i, (i + shift) % size) for i in range(size)])  12.7 us
    dot_general x27, matrix products, convolution_kernel_taps(): jnp.einsum('oc,cyx->oyx', weight[tap_index], window, preferred_element_ty...  11.4 us
    ppermute x5, waiting for transfers between devices, butterfly_sum(): value = value + lax.ppermute(value, axis, partner)  9.93 us
    ppermute x1, waiting for transfers between devices, on_device(): lax.ppermute(first_column, 'lon', [((j + 1) % lon_size, j) for j in range...  9.15 us
    unnamed x45, local copies, waits for them, and re-layouts  8.78 us
    ppermute x1, waiting for transfers between devices, on_device(): lax.ppermute(last_column, 'lon', [(j, (j + 1) % lon_size) for j in range(...  8.35 us
  transfers between devices with their start and end apart: 24, of which 18 were waited for; matrix products, arithmetic and copies ran while one was open for 4% of the time, Pallas kernels for 8%

profile of v11, /device:TPU:0, one launch (start us, length us, event | category | flops | bytes accessed | tf_op | source)
XLA Modules:
  0.0 163.0 jit_solution(5549303372168372457)
XLA Ops:
  2.2 2.5 %collective-permute-start = (bf16[69,2,128]{0,2,1:T(8,128)(2,1)S(1)}, bf16[69,2,128]{0,2,1:T(8,128)(2,1)S(1)}, u32[]{:S(2)}, u32[]{:S(2)}) collective-permute-start(bf16[69,2,128]{0,2,1:T(8,128)(2,1)S(1)} %get-tuple-element.62), channel_id=1, source_target_pairs={{0,4},{4,8},{8,12},{12,16},{16,20},{20,24},{24,28},{1,5},{5,9},{9,... | collective-permute-start | bytes 105992 | tf_op jit(solution)/shard_map/ppermute | solution.py:20
  6.0 3.9 %collective-permute-done.1 = bf16[69,2,128]{0,2,1:T(8,128)(2,1)S(1)} collective-permute-done((bf16[69,2,128]{0,2,1:T(8,128)(2,1)S(1)}, bf16[69,2,128]{0,2,1:T(8,128)(2,1)S(1)}, u32[]{:S(2)}, u32[]{:S(2)}) %collective-permute-start.1) | collective-permute-done | bytes 35360 | tf_op jit(solution)/shard_map/ppermute | solution.py:21
  9.9 1.6 collective-permute-start.2
  11.6 2.2 %collective-permute-start.3 = (bf16[69,20,2]{0,2,1:T(2,128)(2,1)S(1)}, bf16[69,20,2]{0,2,1:T(2,128)(2,1)S(1)}, u32[]{:S(2)}, u32[]{:S(2)}) collective-permute-start(bf16[69,20,2]{0,2,1:T(2,128)(2,1)S(1)} %get-tuple-element.53), channel_id=1, source_target_pairs={{1,0},{2,1},{3,2},{0,3},{5,4},{6,5},{7,6},{4,7},{9,8},{10,9},{11,1... | collective-permute-start | bytes 16568 | tf_op jit(solution)/shard_map/ppermute | solution.py:26
  13.8 1.6 %collective-permute-done.2 = bf16[69,20,2]{0,2,1:T(2,128)(2,1)S(1)} collective-permute-done((bf16[69,20,2]{0,2,1:T(2,128)(2,1)S(1)}, bf16[69,20,2]{0,2,1:T(2,128)(2,1)S(1)}, u32[]{:S(2)}, u32[]{:S(2)}) %collective-permute-start.2) | collective-permute-done | bytes 5552 | tf_op jit(solution)/shard_map/ppermute | solution.py:25
  31.4 3.1 %collective-permute-start.5 = (bf16[3,128,256]{2,1,0:T(8,128)(2,1)S(1)}, bf16[3,128,256]{2,1,0:T(8,128)(2,1)S(1)}, u32[]{:S(2)}, u32[]{:S(2)}) collective-permute-start(bf16[3,128,256]{2,1,0:T(8,128)(2,1)S(1)} %get-tuple-element.50), channel_id=1, source_target_pairs={{0,2},{1,3},{2,0},{3,1},{4,6},{5,7},{6,4},{7,5},{8,10},{9,11},{10,... | collective-permute-start | bytes 589832 | tf_op jit(solution)/shard_map/ppermute | solution.py:145
  35.3 3.6 %collective-permute-done.4 = bf16[3,128,256]{2,1,0:T(8,128)(2,1)S(1)} collective-permute-done((bf16[3,128,256]{2,1,0:T(8,128)(2,1)S(1)}, bf16[3,128,256]{2,1,0:T(8,128)(2,1)S(1)}, u32[]{:S(2)}, u32[]{:S(2)}) %collective-permute-start.4) | collective-permute-done | bytes 196640 | tf_op jit(solution)/shard_map/ppermute | solution.py:145
  39.0 9.1 %collective-permute-done.5 = bf16[3,128,256]{2,1,0:T(8,128)(2,1)S(1)} collective-permute-done((bf16[3,128,256]{2,1,0:T(8,128)(2,1)S(1)}, bf16[3,128,256]{2,1,0:T(8,128)(2,1)S(1)}, u32[]{:S(2)}, u32[]{:S(2)}) %collective-permute-start.5) | collective-permute-done | bytes 196640 | tf_op jit(solution)/shard_map/ppermute | solution.py:145
  48.4 1.6 collective-permute-done.7
  50.0 2.8 %collective-permute-start.8 = (bf16[2,1024,128]{2,1,0:T(8,128)(2,1)S(1)}, bf16[2,1024,128]{2,1,0:T(8,128)(2,1)S(1)}, u32[]{:S(2)}, u32[]{:S(2)}) collective-permute-start(bf16[2,1024,128]{2,1,0:T(8,128)(2,1)S(1)} %pad_maximum_fusion.9), channel_id=1, source_target_pairs={{0,8},{4,12},{8,0},{12,4},{16,24},{20,28},{24,16},{28,20},{1,9},{5... | collective-permute-start | bytes 1572872 | tf_op jit(solution)/shard_map/ppermute | solution.py:224
  52.9 1.6 collective-permute-start.10
  54.5 4.5 %shard_map.166 = (f32[1024,128]{1,0:T(8,128)S(1)}, f32[1024,128]{1,0:T(8,128)S(1)}, f32[1024,128]{1,0:T(8,128)S(1)}) custom-call(f32[2]{0:T(128)S(1)} %dynamic-slice_multiply_fusion.scale_ref, bf16[1024,128]{1,0:T(8,128)(2,1)S(1)} %get-tuple-element.44.q_ref, bf16[1024,128]{1,0:T(8,128)(2,1)S(1)} %get-tuple-element.45.refs_0_, ...), custom_call_target="tpu_custom_call" | custom-call | flops 536870912 | bytes 2359296 | tf_op jit(solution)/shard_map/pallas_call | solution.py:111
  59.1 6.5 %collective-permute-done.8 = bf16[2,1024,128]{2,1,0:T(8,128)(2,1)S(1)} collective-permute-done((bf16[2,1024,128]{2,1,0:T(8,128)(2,1)S(1)}, bf16[2,1024,128]{2,1,0:T(8,128)(2,1)S(1)}, u32[]{:S(2)}, u32[]{:S(2)}) %collective-permute-start.8) | collective-permute-done | bytes 524320 | tf_op jit(solution)/shard_map/ppermute | solution.py:224
  65.6 4.5 %shard_map.167 = (f32[1024,128]{1,0:T(8,128)S(1)}, f32[1024,128]{1,0:T(8,128)S(1)}, f32[1024,128]{1,0:T(8,128)S(1)}) custom-call(f32[2]{0:T(128)S(1)} %dynamic-slice_multiply_fusion.scale_ref, bf16[1024,128]{1,0:T(8,128)(2,1)S(1)} %get-tuple-element.44.q_ref, bf16[1024,128]{1,0:T(8,128)(2,1)S(1)} %get-tuple-element.57.refs_0_, ...), custom_call_target="tpu_custom_call" | custom-call | flops 536870912 | bytes 2359296 | tf_op jit(solution)/shard_map/pallas_call | solution.py:111
  70.1 7.6 %collective-permute-done.9 = bf16[2,1024,128]{2,1,0:T(8,128)(2,1)S(1)} collective-permute-done((bf16[2,1024,128]{2,1,0:T(8,128)(2,1)S(1)}, bf16[2,1024,128]{2,1,0:T(8,128)(2,1)S(1)}, u32[]{:S(2)}, u32[]{:S(2)}) %collective-permute-start.9) | collective-permute-done | bytes 524320 | tf_op jit(solution)/shard_map/ppermute | solution.py:224
  77.8 4.5 %shard_map.168 = (f32[1024,128]{1,0:T(8,128)S(1)}, f32[1024,128]{1,0:T(8,128)S(1)}, f32[1024,128]{1,0:T(8,128)S(1)}) custom-call(f32[2]{0:T(128)S(1)} %dynamic-slice_multiply_fusion.scale_ref, bf16[1024,128]{1,0:T(8,128)(2,1)S(1)} %get-tuple-element.44.q_ref, bf16[1024,128]{1,0:T(8,128)(2,1)S(1)} %get-tuple-element.59.refs_0_, ...), custom_call_target="tpu_custom_call" | custom-call | flops 536870912 | bytes 2359296 | tf_op jit(solution)/shard_map/pallas_call | solution.py:111
  82.4 4.8 %shard_map.169 = (f32[1024,128]{1,0:T(8,128)S(1)}, f32[1024,128]{1,0:T(8,128)S(1)}, f32[1024,128]{1,0:T(8,128)S(1)}) custom-call(f32[2]{0:T(128)S(1)} %dynamic-slice_multiply_fusion.scale_ref, bf16[1024,128]{1,0:T(8,128)(2,1)S(1)} %get-tuple-element.44.q_ref, bf16[1024,128]{1,0:T(8,128)(2,1)S(1)} %get-tuple-element.61.refs_0_, ...), custom_call_target="tpu_custom_call" | custom-call | flops 536870912 | bytes 2359296 | tf_op jit(solution)/shard_map/pallas_call | solution.py:111
  89.3 5.6 %collective-permute-start.12 = (bf16[128,256]{1,0:T(8,128)(2,1)S(1)}, bf16[128,256]{1,0:T(8,128)(2,1)S(1)}, u32[]{:S(2)}, u32[]{:S(2)}) collective-permute-start(bf16[128,256]{1,0:T(8,128)(2,1)S(1)} %get-tuple-element.68), channel_id=1, source_target_pairs={{1,0},{2,1},{3,2},{0,3},{5,4},{6,5},{7,6},{4,7},{9,8},{10,9},{11,1... | collective-permute-start | bytes 196616 | tf_op jit(solution)/shard_map/ppermute | solution.py:153
  95.6 1.8 %collective-permute-done.12 = bf16[128,256]{1,0:T(8,128)(2,1)S(1)} collective-permute-done((bf16[128,256]{1,0:T(8,128)(2,1)S(1)}, bf16[128,256]{1,0:T(8,128)(2,1)S(1)}, u32[]{:S(2)}, u32[]{:S(2)}) %collective-permute-start.12) | collective-permute-done | bytes 65568 | tf_op jit(solution)/shard_map/ppermute | solution.py:153
  97.4 4.6 %collective-permute-done.13 = bf16[128,256]{1,0:T(8,128)(2,1)S(1)} collective-permute-done((bf16[128,256]{1,0:T(8,128)(2,1)S(1)}, bf16[128,256]{1,0:T(8,128)(2,1)S(1)}, u32[]{:S(2)}, u32[]{:S(2)}) %collective-permute-start.13) | collective-permute-done | bytes 65568 | tf_op jit(solution)/shard_map/ppermute | solution.py:153
  102.8 3.5 %fusion.72 = bf16[128,4,4,32,4]{0,3,4,2,1:T(8,128)(2,1)S(1)} fusion(bf16[4,32,1024,1,1]{2,1,4,3,0:T(8,128)(2,1)S(1)} %bitcast.307, bf16[1024,4,4,128]{3,2,1,0:T(4,128)(2,1)} %param.28), kind=kOutput, calls=%fused_computation.80 | convolution fusion | flops 539230208 | bytes 4980736 | tf_op jit(solution)/shard_map/pqd,dabh->hpaqb/dot_general | solution.py:263
  108.5 2.9 %fusion.138 = bf16[128,4,4,1,4]{0,1,4,2,3:T(4,128)(2,1)S(1)} fusion(bf16[1024,4,4,128]{3,2,1,0:T(4,128)(2,1)} %param.28, bf16[4,1,1024]{2,1,0:T(2,128)(2,1)S(1)} %get-tuple-element.65), kind=kOutput, calls=%fused_computation.186 | convolution fusion | flops 16850944 | bytes 4218880 | tf_op jit(solution)/shard_map/pqd,dabh->hpaqb/dot_general | solution.py:263
  112.5 3.8 %collective-permute-start.16 = (bf16[128,16,1]{2,0,1:T(8,128)(2,1)}, bf16[128,16,1]{2,0,1:T(8,128)(2,1)S(1)}, u32[]{:S(2)}, u32[]{:S(2)}) collective-permute-start(bf16[128,16,1]{2,0,1:T(8,128)(2,1)} %copy.66), channel_id=1, source_target_pairs={{1,0},{2,1},{3,2},{0,3},{5,4},{6,5},{7,6},{4,7},{9,8},{10,9},{11,1... | collective-permute-start | bytes 12296 | tf_op jit(solution)/shard_map/ppermute | solution.py:273
  117.1 8.3 %collective-permute-done.15 = bf16[128,16,1]{2,0,1:T(8,128)(2,1)S(1)} collective-permute-done((bf16[128,16,1]{2,0,1:T(8,128)(2,1)}, bf16[128,16,1]{2,0,1:T(8,128)(2,1)S(1)}, u32[]{:S(2)}, u32[]{:S(2)}) %collective-permute-start.15) | collective-permute-done | bytes 4128 | tf_op jit(solution)/shard_map/ppermute | solution.py:272
  125.4 9.2 %collective-permute-done.16 = bf16[128,16,1]{2,0,1:T(8,128)(2,1)S(1)} collective-permute-done((bf16[128,16,1]{2,0,1:T(8,128)(2,1)}, bf16[128,16,1]{2,0,1:T(8,128)(2,1)S(1)}, u32[]{:S(2)}, u32[]{:S(2)}) %collective-permute-start.16) | collective-permute-done | bytes 4128 | tf_op jit(solution)/shard_map/ppermute | solution.py:273
  134.7 1.9 %collective-permute-start.17 = (bf16[128,1,130]{2,0,1:T(8,128)(2,1)S(1)}, bf16[128,1,130]{2,0,1:T(8,128)(2,1)S(1)}, u32[]{:S(2)}, u32[]{:S(2)}) collective-permute-start(bf16[128,1,130]{2,0,1:T(8,128)(2,1)S(1)} %get-tuple-element.41), channel_id=1, source_target_pairs={{0,4},{4,8},{8,12},{12,16},{16,20},{20,24},{24,28},{1,5},{5,9},{9,... | collective-permute-start | bytes 99848 | tf_op jit(solution)/shard_map/ppermute | solution.py:279
  136.6 1.6 collective-permute-start.18
  145.2 3.0 %collective-permute-done.19 = f32[64]{0:T(128)S(1)} collective-permute-done((f32[64]{0:T(128)S(1)}, f32[64]{0:T(128)S(1)}, u32[]{:S(2)}, u32[]{:S(2)}) %collective-permute-start.19) | collective-permute-done | bytes 288 | tf_op jit(solution)/shard_map/ppermute | solution.py:34
  148.8 3.9 %collective-permute-done.20 = f32[64]{0:T(128)S(1)} collective-permute-done((f32[64]{0:T(128)S(1)}, f32[64]{0:T(128)S(1)}, u32[]{:S(2)}, u32[]{:S(2)}) %collective-permute-start.20) | collective-permute-done | bytes 288 | tf_op jit(solution)/shard_map/ppermute | solution.py:34
  154.1 2.4 %collective-permute-start.22 = (f32[64]{0:T(128)S(1)}, f32[64]{0:T(128)S(1)}, u32[]{:S(2)}, u32[]{:S(2)}) collective-permute-start(f32[64]{0:T(128)S(1)} %add.329), channel_id=1, source_target_pairs={{0,8},{4,12},{8,0},{12,4},{16,24},{20,28},{24,16},{28,20},{1,9},{5... | collective-permute-start | bytes 776 | tf_op jit(solution)/shard_map/ppermute | solution.py:34
  156.5 1.5 collective-permute-done.22
  158.0 2.8 %collective-permute-start.23 = (f32[64]{0:T(128)S(1)}, f32[64]{0:T(128)S(1)}, u32[]{:S(2)}, u32[]{:S(2)}) collective-permute-start(f32[64]{0:T(128)S(1)} %add.330), channel_id=1, source_target_pairs={{0,16},{4,20},{8,24},{12,28},{16,0},{20,4},{24,8},{28,12},{1,17},{... | collective-permute-start | bytes 776 | tf_op jit(solution)/shard_map/ppermute | solution.py:34
  (144 shorter events, 38.6 us)
Async XLA Ops:
  0.6 25.5 %copy-start = (bf16[1024,1024]{1,0:T(8,128)(2,1)S(1)}, bf16[1024,1024]{1,0:T(8,128)(2,1)}, u32[]{:S(2)}) copy-start(bf16[1024,1024]{1,0:T(8,128)(2,1)} %param.25) | copy-start | bytes 6291460
  2.1 13.6 %copy-start.10 = (bf16[9,128,69]{1,2,0:T(8,128)(2,1)S(1)}, bf16[9,128,69]{1,2,0:T(8,128)(2,1)}, u32[]{:S(2)}) copy-start(bf16[9,128,69]{1,2,0:T(8,128)(2,1)} %param.19) | copy-start | bytes 476932
  2.2 3.8 %collective-permute-start = (bf16[69,2,128]{0,2,1:T(8,128)(2,1)S(1)}, bf16[69,2,128]{0,2,1:T(8,128)(2,1)S(1)}, u32[]{:S(2)}, u32[]{:S(2)}) collective-permute-start(bf16[69,2,128]{0,2,1:T(8,128)(2,1)S(1)} %get-tuple-element.62), channel_id=1, source_target_pairs={{0,4},{4,8},{8,12},{12,16},{16,20},{20,24},{24,28},{1,5},{5,9},{9,... | collective-permute-start | bytes 105992 | tf_op jit(solution)/shard_map/ppermute | solution.py:20
  4.7 5.3 %collective-permute-start.1 = (bf16[69,2,128]{0,2,1:T(8,128)(2,1)S(1)}, bf16[69,2,128]{0,2,1:T(8,128)(2,1)S(1)}, u32[]{:S(2)}, u32[]{:S(2)}) collective-permute-start(bf16[69,2,128]{0,2,1:T(8,128)(2,1)S(1)} %get-tuple-element.63), channel_id=1, source_target_pairs={{4,0},{8,4},{12,8},{16,12},{20,16},{24,20},{28,24},{5,1},{9,5},{13... | collective-permute-start | bytes 105992 | tf_op jit(solution)/shard_map/ppermute | solution.py:21
  9.9 5.5 %collective-permute-start.2 = (bf16[69,20,2]{0,2,1:T(2,128)(2,1)S(1)}, bf16[69,20,2]{0,2,1:T(2,128)(2,1)S(1)}, u32[]{:S(2)}, u32[]{:S(2)}) collective-permute-start(bf16[69,20,2]{0,2,1:T(2,128)(2,1)S(1)} %get-tuple-element.52), channel_id=1, source_target_pairs={{0,1},{1,2},{2,3},{3,0},{4,5},{5,6},{6,7},{7,4},{8,9},{9,10},{10,1... | collective-permute-start | bytes 16568 | tf_op jit(solution)/shard_map/ppermute | solution.py:25
  11.6 3.9 %collective-permute-start.3 = (bf16[69,20,2]{0,2,1:T(2,128)(2,1)S(1)}, bf16[69,20,2]{0,2,1:T(2,128)(2,1)S(1)}, u32[]{:S(2)}, u32[]{:S(2)}) collective-permute-start(bf16[69,20,2]{0,2,1:T(2,128)(2,1)S(1)} %get-tuple-element.53), channel_id=1, source_target_pairs={{1,0},{2,1},{3,2},{0,3},{5,4},{6,5},{7,6},{4,7},{9,8},{10,9},{11,1... | collective-permute-start | bytes 16568 | tf_op jit(solution)/shard_map/ppermute | solution.py:26
  30.0 9.0 %collective-permute-start.4 = (bf16[3,128,256]{2,1,0:T(8,128)(2,1)S(1)}, bf16[3,128,256]{2,1,0:T(8,128)(2,1)S(1)}, u32[]{:S(2)}, u32[]{:S(2)}) collective-permute-start(bf16[3,128,256]{2,1,0:T(8,128)(2,1)S(1)} %get-tuple-element.51), channel_id=1, source_target_pairs={{0,1},{1,2},{2,3},{3,0},{4,5},{5,6},{6,7},{7,4},{8,9},{9,10},{10,1... | collective-permute-start | bytes 589832 | tf_op jit(solution)/shard_map/ppermute | solution.py:145
  31.4 16.6 %collective-permute-start.5 = (bf16[3,128,256]{2,1,0:T(8,128)(2,1)S(1)}, bf16[3,128,256]{2,1,0:T(8,128)(2,1)S(1)}, u32[]{:S(2)}, u32[]{:S(2)}) collective-permute-start(bf16[3,128,256]{2,1,0:T(8,128)(2,1)S(1)} %get-tuple-element.50), channel_id=1, source_target_pairs={{0,2},{1,3},{2,0},{3,1},{4,6},{5,7},{6,4},{7,5},{8,10},{9,11},{10,... | collective-permute-start | bytes 589832 | tf_op jit(solution)/shard_map/ppermute | solution.py:145
  34.5 13.6 %collective-permute-start.6 = (bf16[3,128,256]{2,1,0:T(8,128)(2,1)S(1)}, bf16[3,128,256]{2,1,0:T(8,128)(2,1)S(1)}, u32[]{:S(2)}, u32[]{:S(2)}) collective-permute-start(bf16[3,128,256]{2,1,0:T(8,128)(2,1)S(1)} %get-tuple-element.49), channel_id=1, source_target_pairs={{0,3},{1,0},{2,1},{3,2},{4,7},{5,4},{6,5},{7,6},{8,11},{9,8},{10,9... | collective-permute-start | bytes 589832 | tf_op jit(solution)/shard_map/ppermute | solution.py:145
  48.1 4.7 %copy-start.14 = (f32[16]{0:T(128)S(1)}, f32[16]{0:T(128)}, u32[]{:S(2)}) copy-start(f32[16]{0:T(128)} %param.27) | copy-start | bytes 196
  48.2 1.8 %collective-permute-start.7 = (bf16[3,512,128]{2,1,0:T(8,128)(2,1)S(1)}, bf16[3,512,128]{2,1,0:T(8,128)(2,1)S(1)}, u32[]{:S(2)}, u32[]{:S(2)}) collective-permute-start(bf16[3,512,128]{2,1,0:T(8,128)(2,1)S(1)} %get-tuple-element.46), channel_id=1, source_target_pairs={{0,4},{4,0},{8,12},{12,8},{16,20},{20,16},{24,28},{28,24},{1,5},{5... | collective-permute-start | bytes 1179656 | tf_op jit(solution)/shard_map/ppermute | solution.py:219
  50.0 15.5 %collective-permute-start.8 = (bf16[2,1024,128]{2,1,0:T(8,128)(2,1)S(1)}, bf16[2,1024,128]{2,1,0:T(8,128)(2,1)S(1)}, u32[]{:S(2)}, u32[]{:S(2)}) collective-permute-start(bf16[2,1024,128]{2,1,0:T(8,128)(2,1)S(1)} %pad_maximum_fusion.9), channel_id=1, source_target_pairs={{0,8},{4,12},{8,0},{12,4},{16,24},{20,28},{24,16},{28,20},{1,9},{5... | collective-permute-start | bytes 1572872 | tf_op jit(solution)/shard_map/ppermute | solution.py:224
  52.9 24.9 %collective-permute-start.9 = (bf16[2,1024,128]{2,1,0:T(8,128)(2,1)S(1)}, bf16[2,1024,128]{2,1,0:T(8,128)(2,1)S(1)}, u32[]{:S(2)}, u32[]{:S(2)}) collective-permute-start(bf16[2,1024,128]{2,1,0:T(8,128)(2,1)S(1)} %pad_maximum_fusion.9), channel_id=1, source_target_pairs={{0,16},{4,20},{8,24},{12,28},{16,0},{20,4},{24,8},{28,12},{1,17},{... | collective-permute-start | bytes 1572872 | tf_op jit(solution)/shard_map/ppermute | solution.py:224
  52.9 29.4 %collective-permute-start.10 = (bf16[2,1024,128]{2,1,0:T(8,128)(2,1)S(1)}, bf16[2,1024,128]{2,1,0:T(8,128)(2,1)S(1)}, u32[]{:S(2)}, u32[]{:S(2)}) collective-permute-start(bf16[2,1024,128]{2,1,0:T(8,128)(2,1)S(1)} %pad_maximum_fusion.9), channel_id=1, source_target_pairs={{0,24},{4,28},{8,16},{12,20},{16,8},{20,12},{24,0},{28,4},{1,25},{... | collective-permute-start | bytes 1572872 | tf_op jit(solution)/shard_map/ppermute | solution.py:224
  87.8 1.4 collective-permute-start.11
  89.2 13.2 %copy-start.5 = (bf16[1024,1024]{1,0:T(8,128)(2,1)S(1)}, bf16[1024,1024]{1,0:T(8,128)(2,1)}, u32[]{:S(2)}) copy-start(bf16[1024,1024]{1,0:T(8,128)(2,1)} %param.26) | copy-start | bytes 6291460
  89.3 8.1 %collective-permute-start.12 = (bf16[128,256]{1,0:T(8,128)(2,1)S(1)}, bf16[128,256]{1,0:T(8,128)(2,1)S(1)}, u32[]{:S(2)}, u32[]{:S(2)}) collective-permute-start(bf16[128,256]{1,0:T(8,128)(2,1)S(1)} %get-tuple-element.68), channel_id=1, source_target_pairs={{1,0},{2,1},{3,2},{0,3},{5,4},{6,5},{7,6},{4,7},{9,8},{10,9},{11,1... | collective-permute-start | bytes 196616 | tf_op jit(solution)/shard_map/ppermute | solution.py:153
  94.9 7.1 %collective-permute-start.13 = (bf16[128,256]{1,0:T(8,128)(2,1)S(1)}, bf16[128,256]{1,0:T(8,128)(2,1)S(1)}, u32[]{:S(2)}, u32[]{:S(2)}) collective-permute-start(bf16[128,256]{1,0:T(8,128)(2,1)S(1)} %get-tuple-element.67), channel_id=1, source_target_pairs={{2,0},{3,1},{0,2},{1,3},{6,4},{7,5},{4,6},{5,7},{10,8},{11,9},{8,1... | collective-permute-start | bytes 196616 | tf_op jit(solution)/shard_map/ppermute | solution.py:153
  95.6 6.5 %collective-permute-start.14 = (bf16[128,256]{1,0:T(8,128)(2,1)S(1)}, bf16[128,256]{1,0:T(8,128)(2,1)S(1)}, u32[]{:S(2)}, u32[]{:S(2)}) collective-permute-start(bf16[128,256]{1,0:T(8,128)(2,1)S(1)} %get-tuple-element.66), channel_id=1, source_target_pairs={{3,0},{0,1},{1,2},{2,3},{7,4},{4,5},{5,6},{6,7},{11,8},{8,9},{9,10... | collective-permute-start | bytes 196616 | tf_op jit(solution)/shard_map/ppermute | solution.py:153
  102.8 3.9 %copy-start.12 = (bf16[1024,4,4,128]{3,2,1,0:T(4,128)(2,1)S(1)}, bf16[1024,4,4,128]{3,2,1,0:T(4,128)(2,1)}, u32[]{:S(2)}) copy-start(bf16[1024,4,4,128]{3,2,1,0:T(4,128)(2,1)} %param.28) | copy-start | bytes 12582916
  108.5 16.9 %collective-permute-start.15 = (bf16[128,16,1]{2,0,1:T(8,128)(2,1)}, bf16[128,16,1]{2,0,1:T(8,128)(2,1)S(1)}, u32[]{:S(2)}, u32[]{:S(2)}) collective-permute-start(bf16[128,16,1]{2,0,1:T(8,128)(2,1)} %copy.64), channel_id=1, source_target_pairs={{0,1},{1,2},{2,3},{3,0},{4,5},{5,6},{6,7},{7,4},{8,9},{9,10},{10,1... | collective-permute-start | bytes 12296 | tf_op jit(solution)/shard_map/ppermute | solution.py:272
  108.5 7.8 %copy-start.9 = (bf16[9,69,128]{2,1,0:T(8,128)(2,1)S(1)}, bf16[9,69,128]{2,1,0:T(8,128)(2,1)}, u32[]{:S(2)}) copy-start(bf16[9,69,128]{2,1,0:T(8,128)(2,1)} %param.29) | copy-start | bytes 476932
  112.5 22.1 %collective-permute-start.16 = (bf16[128,16,1]{2,0,1:T(8,128)(2,1)}, bf16[128,16,1]{2,0,1:T(8,128)(2,1)S(1)}, u32[]{:S(2)}, u32[]{:S(2)}) collective-permute-start(bf16[128,16,1]{2,0,1:T(8,128)(2,1)} %copy.66), channel_id=1, source_target_pairs={{1,0},{2,1},{3,2},{0,3},{5,4},{6,5},{7,6},{4,7},{9,8},{10,9},{11,1... | collective-permute-start | bytes 12296 | tf_op jit(solution)/shard_map/ppermute | solution.py:273
  134.7 3.9 %collective-permute-start.17 = (bf16[128,1,130]{2,0,1:T(8,128)(2,1)S(1)}, bf16[128,1,130]{2,0,1:T(8,128)(2,1)S(1)}, u32[]{:S(2)}, u32[]{:S(2)}) collective-permute-start(bf16[128,1,130]{2,0,1:T(8,128)(2,1)S(1)} %get-tuple-element.41), channel_id=1, source_target_pairs={{0,4},{4,8},{8,12},{12,16},{16,20},{20,24},{24,28},{1,5},{5,9},{9,... | collective-permute-start | bytes 99848 | tf_op jit(solution)/shard_map/ppermute | solution.py:279
  136.6 3.1 %collective-permute-start.18 = (bf16[128,1,130]{2,0,1:T(8,128)(2,1)S(1)}, bf16[128,1,130]{2,0,1:T(8,128)(2,1)S(1)}, u32[]{:S(2)}, u32[]{:S(2)}) collective-permute-start(bf16[128,1,130]{2,0,1:T(8,128)(2,1)S(1)} %get-tuple-element.42), channel_id=1, source_target_pairs={{4,0},{8,4},{12,8},{16,12},{20,16},{24,20},{28,24},{5,1},{9,5},{13... | collective-permute-start | bytes 99848 | tf_op jit(solution)/shard_map/ppermute | solution.py:281
  143.5 18.9 %copy-start.15 = (s32[64]{0:T(128)S(1)}, s32[64]{0:T(128)}, u32[]{:S(2)}) copy-start(s32[64]{0:T(128)} %param.18) | copy-start | bytes 772
  143.6 19.5 %copy-start.1 = (bf16[1024,1024]{1,0:T(8,128)(2,1)S(1)}, bf16[1024,1024]{1,0:T(8,128)(2,1)}, u32[]{:S(2)}) copy-start(bf16[1024,1024]{1,0:T(8,128)(2,1)} %param.25) | copy-start | bytes 6291460
  144.6 3.6 %collective-permute-start.19 = (f32[64]{0:T(128)S(1)}, f32[64]{0:T(128)S(1)}, u32[]{:S(2)}, u32[]{:S(2)}) collective-permute-start(f32[64]{0:T(128)S(1)} %fusion.54), channel_id=1, source_target_pairs={{0,1},{1,0},{2,3},{3,2},{4,5},{5,4},{6,7},{7,6},{8,9},{9,8},{10,11... | collective-permute-start | bytes 776 | tf_op jit(solution)/shard_map/ppermute | solution.py:34
  148.2 4.4 %collective-permute-start.20 = (f32[64]{0:T(128)S(1)}, f32[64]{0:T(128)S(1)}, u32[]{:S(2)}, u32[]{:S(2)}) collective-permute-start(f32[64]{0:T(128)S(1)} %add.327), channel_id=1, source_target_pairs={{0,2},{1,3},{2,0},{3,1},{4,6},{5,7},{6,4},{7,5},{8,10},{9,11},{10,... | collective-permute-start | bytes 776 | tf_op jit(solution)/shard_map/ppermute | solution.py:34
  152.6 1.4 collective-permute-start.21
  154.1 4.0 %collective-permute-start.22 = (f32[64]{0:T(128)S(1)}, f32[64]{0:T(128)S(1)}, u32[]{:S(2)}, u32[]{:S(2)}) collective-permute-start(f32[64]{0:T(128)S(1)} %add.329), channel_id=1, source_target_pairs={{0,8},{4,12},{8,0},{12,4},{16,24},{20,28},{24,16},{28,20},{1,9},{5... | collective-permute-start | bytes 776 | tf_op jit(solution)/shard_map/ppermute | solution.py:34
  158.0 4.4 %collective-permute-start.23 = (f32[64]{0:T(128)S(1)}, f32[64]{0:T(128)S(1)}, u32[]{:S(2)}, u32[]{:S(2)}) collective-permute-start(f32[64]{0:T(128)S(1)} %add.330), channel_id=1, source_target_pairs={{0,16},{4,20},{8,24},{12,28},{16,0},{20,4},{24,8},{28,12},{1,17},{... | collective-permute-start | bytes 776 | tf_op jit(solution)/shard_map/ppermute | solution.py:34
  (9 other events, 10.8 us)

commit v12 on v9

--- a/solution.py
+++ b/solution.py
@@ -220,14 +220,24 @@
 
     pair_spread = with_partner(spread)
     pair_queries, key_value = pair_spread[0], pair_spread[1:]
-    remote_chunks = [
-        lax.ppermute(key_value, "lat", [(i, i ^ (2 * d)) for i in range(lat_size)])
-        for d in range(1, lat_size // 2)
-    ]
+    if lat_size == 8:
+        across_x = [(i, i ^ 2) for i in range(lat_size)]
+        across_y = [(i, i ^ 4) for i in range(lat_size)]
+        from_x = lax.ppermute(key_value, "lat", across_x)
+        from_y = lax.ppermute(key_value, "lat", across_y)
+        middle = key_value.shape[1] // 2
+        diagonal_low = lax.ppermute(from_y[:, :middle], "lat", across_x)
+        diagonal_high = lax.ppermute(from_x[:, middle:], "lat", across_y)
+        key_groups = [[key_value], [from_x], [from_y], [diagonal_low, diagonal_high]]
+    else:
+        remote_chunks = [
+            lax.ppermute(key_value, "lat", [(i, i ^ (2 * d)) for i in range(lat_size)])
+            for d in range(1, lat_size // 2)
+        ]
+        key_groups = [[key_value]] + [[chunk] for chunk in remote_chunks]
     local_heads = half // head_size
     head_first = (lax.axis_index("lon") * 2 + core) * local_heads
     scales = lax.dynamic_slice_in_dim(head_scale, head_first, local_heads) / math.sqrt(head_size)
-    key_groups = [[key_value]] + [[chunk] for chunk in remote_chunks]
     parts = [
         attend_part(
             pair_queries,

time: 143 us -> 142 us (level)
  waiting for transfers between devices: 52.8 us -> 49.1 us
    ppermute x3 -> x4, waiting for transfers between devices: 13.1 us -> 7.89 us  [the longest x1 7.88 us: on_device(): from_x = lax.ppermute(key_value, 'lat', across_x)]
    ppermute x3 -> x4, starting transfers between devices: 4.39 us -> 4.72 us  [the longest x1 2.77 us: on_device(): from_x = lax.ppermute(key_value, 'lat', across_x)]
  transfers between devices with their start and end apart: 24 -> 25, of which waited for: 17 -> 16; matrix products, arithmetic and copies ran while one was open for 2% -> 3% of each run, Pallas kernels for 10% -> 10%
where the time goes in v12:
time: 142 us; the launch traced here: 141 us
  waiting for transfers between devices  49.1 us (35%)
  starting transfers between devices  38.8 us (27%)
  Pallas kernels  18.1 us (13%)
  matrix products  17.7 us (12%)
  local copies, waits for them, and re-layouts  11.9 us (8%)
  other arithmetic  4.24 us (3%)
    pallas_call x4, Pallas kernels, attend_part(): pl.pallas_call(functools.partial(attention_kernel, head_size=head_size, c...  18.1 us
    ppermute x3, waiting for transfers between devices, exchange_blocks(): lax.ppermute(outgoing, axis, [(i, (i + shift) % size) for i in range(size)])  12.7 us
    dot_general x27, matrix products, convolution_kernel_taps(): jnp.einsum('oc,cyx->oyx', weight[tap_index], window, preferred_element_ty...  10.7 us
    ppermute x5, waiting for transfers between devices, butterfly_sum(): value = value + lax.ppermute(value, axis, partner)  9.06 us
    ppermute x5, starting transfers between devices, butterfly_sum(): value = value + lax.ppermute(value, axis, partner)  8.08 us
    ppermute x1, waiting for transfers between devices, on_device(): from_x = lax.ppermute(key_value, 'lat', across_x)  7.88 us
    ppermute x2, waiting for transfers between devices, halo_padded(): from_below = lax.ppermute(array[:, :width], 'lat', up)  7.62 us
    ppermute x3, waiting for transfers between devices, return_blocks(): lax.ppermute(blocks[shift], axis, [((i + shift) % size, i) for i in range...  6.44 us
  transfers between devices with their start and end apart: 25, of which 16 were waited for; matrix products, arithmetic and copies ran while one was open for 3% of the time, Pallas kernels for 10%

profile of v12, /device:TPU:0, one launch (start us, length us, event | category | flops | bytes accessed | tf_op | source)
XLA Modules:
  0.0 141.1 jit_solution(11172397654238519048)
XLA Ops:
  0.6 1.5 %copy.49 = bf16[69,16,128]{0,2,1:T(8,128)(2,1)S(1)} copy(bf16[69,16,128]{2,1,0:T(8,128)(2,1)} %param.15) | data formatting | bytes 565248 | tf_op args[0]
  2.2 2.5 %collective-permute-start = (bf16[69,2,128]{0,2,1:T(8,128)(2,1)S(1)}, bf16[69,2,128]{0,2,1:T(8,128)(2,1)S(1)}, u32[]{:S(2)}, u32[]{:S(2)}) collective-permute-start(bf16[69,2,128]{0,2,1:T(8,128)(2,1)S(1)} %get-tuple-element.65), channel_id=1, source_target_pairs={{0,4},{4,8},{8,12},{12,16},{16,20},{20,24},{24,28},{1,5},{5,9},{9,... | collective-permute-start | bytes 105992 | tf_op jit(solution)/shard_map/ppermute | solution.py:20
  6.0 3.9 %collective-permute-done.1 = bf16[69,2,128]{0,2,1:T(8,128)(2,1)S(1)} collective-permute-done((bf16[69,2,128]{0,2,1:T(8,128)(2,1)S(1)}, bf16[69,2,128]{0,2,1:T(8,128)(2,1)S(1)}, u32[]{:S(2)}, u32[]{:S(2)}) %collective-permute-start.1) | collective-permute-done | bytes 35360 | tf_op jit(solution)/shard_map/ppermute | solution.py:21
  9.9 1.6 %collective-permute-start.2 = (bf16[69,20,2]{0,2,1:T(2,128)(2,1)S(1)}, bf16[69,20,2]{0,2,1:T(2,128)(2,1)S(1)}, u32[]{:S(2)}, u32[]{:S(2)}) collective-permute-start(bf16[69,20,2]{0,2,1:T(2,128)(2,1)S(1)} %get-tuple-element.51), channel_id=1, source_target_pairs={{0,1},{1,2},{2,3},{3,0},{4,5},{5,6},{6,7},{7,4},{8,9},{9,10},{10,1... | collective-permute-start | bytes 16568 | tf_op jit(solution)/shard_map/ppermute | solution.py:25
  11.6 2.2 %collective-permute-start.3 = (bf16[69,20,2]{0,2,1:T(2,128)(2,1)S(1)}, bf16[69,20,2]{0,2,1:T(2,128)(2,1)S(1)}, u32[]{:S(2)}, u32[]{:S(2)}) collective-permute-start(bf16[69,20,2]{0,2,1:T(2,128)(2,1)S(1)} %get-tuple-element.52), channel_id=1, source_target_pairs={{1,0},{2,1},{3,2},{0,3},{5,4},{6,5},{7,6},{4,7},{9,8},{10,9},{11,1... | collective-permute-start | bytes 16568 | tf_op jit(solution)/shard_map/ppermute | solution.py:26
  13.8 1.6 %collective-permute-done.2 = bf16[69,20,2]{0,2,1:T(2,128)(2,1)S(1)} collective-permute-done((bf16[69,20,2]{0,2,1:T(2,128)(2,1)S(1)}, bf16[69,20,2]{0,2,1:T(2,128)(2,1)S(1)}, u32[]{:S(2)}, u32[]{:S(2)}) %collective-permute-start.2) | collective-permute-done | bytes 5552 | tf_op jit(solution)/shard_map/ppermute | solution.py:25
  30.0 1.4 collective-permute-start.4
  31.4 3.1 %collective-permute-start.5 = (bf16[3,128,256]{2,1,0:T(8,128)(2,1)S(1)}, bf16[3,128,256]{2,1,0:T(8,128)(2,1)S(1)}, u32[]{:S(2)}, u32[]{:S(2)}) collective-permute-start(bf16[3,128,256]{2,1,0:T(8,128)(2,1)S(1)} %get-tuple-element.49), channel_id=1, source_target_pairs={{0,2},{1,3},{2,0},{3,1},{4,6},{5,7},{6,4},{7,5},{8,10},{9,11},{10,... | collective-permute-start | bytes 589832 | tf_op jit(solution)/shard_map/ppermute | solution.py:145
  35.3 3.6 %collective-permute-done.4 = bf16[3,128,256]{2,1,0:T(8,128)(2,1)S(1)} collective-permute-done((bf16[3,128,256]{2,1,0:T(8,128)(2,1)S(1)}, bf16[3,128,256]{2,1,0:T(8,128)(2,1)S(1)}, u32[]{:S(2)}, u32[]{:S(2)}) %collective-permute-start.4) | collective-permute-done | bytes 196640 | tf_op jit(solution)/shard_map/ppermute | solution.py:145
  39.0 9.1 %collective-permute-done.5 = bf16[3,128,256]{2,1,0:T(8,128)(2,1)S(1)} collective-permute-done((bf16[3,128,256]{2,1,0:T(8,128)(2,1)S(1)}, bf16[3,128,256]{2,1,0:T(8,128)(2,1)S(1)}, u32[]{:S(2)}, u32[]{:S(2)}) %collective-permute-start.5) | collective-permute-done | bytes 196640 | tf_op jit(solution)/shard_map/ppermute | solution.py:145
  48.4 1.6 %collective-permute-done.7 = bf16[3,512,128]{2,1,0:T(8,128)(2,1)S(1)} collective-permute-done((bf16[3,512,128]{2,1,0:T(8,128)(2,1)S(1)}, bf16[3,512,128]{2,1,0:T(8,128)(2,1)S(1)}, u32[]{:S(2)}, u32[]{:S(2)}) %collective-permute-start.7) | collective-permute-done | bytes 393248 | tf_op jit(solution)/shard_map/ppermute | solution.py:219
  50.8 2.8 %collective-permute-start.8 = (bf16[2,1024,128]{2,1,0:T(8,128)(2,1)}, bf16[2,1024,128]{2,1,0:T(8,128)(2,1)}, u32[]{:S(2)}, u32[]{:S(2)}) collective-permute-start(bf16[2,1024,128]{2,1,0:T(8,128)(2,1)} %pad_maximum_fusion.6), channel_id=1, source_target_pairs={{0,8},{4,12},{8,0},{12,4},{16,24},{20,28},{24,16},{28,20},{1,9},{5... | collective-permute-start | bytes 1572872 | tf_op jit(solution)/shard_map/ppermute | solution.py:226
  53.7 4.5 %shard_map.166 = (f32[1024,128]{1,0:T(8,128)S(1)}, f32[1024,128]{1,0:T(8,128)S(1)}, f32[1024,128]{1,0:T(8,128)S(1)}) custom-call(f32[2]{0:T(128)S(1)} %dynamic-slice_multiply_fusion.scale_ref, bf16[1024,128]{1,0:T(8,128)(2,1)S(1)} %get-tuple-element.43.q_ref, bf16[1024,128]{1,0:T(8,128)(2,1)S(1)} %get-tuple-element.44.refs_0_, ...), custom_call_target="tpu_custom_call" | custom-call | flops 536870912 | bytes 2359296 | tf_op jit(solution)/shard_map/pallas_call | solution.py:111
  58.3 7.9 %collective-permute-done.8 = bf16[2,1024,128]{2,1,0:T(8,128)(2,1)} collective-permute-done((bf16[2,1024,128]{2,1,0:T(8,128)(2,1)}, bf16[2,1024,128]{2,1,0:T(8,128)(2,1)}, u32[]{:S(2)}, u32[]{:S(2)}) %collective-permute-start.8) | collective-permute-done | bytes 524320 | tf_op jit(solution)/shard_map/ppermute | solution.py:226
  67.1 1.6 %collective-permute-start.11 = (bf16[2,512,128]{2,1,0:T(8,128)(2,1)S(1)}, bf16[2,512,128]{2,1,0:T(8,128)(2,1)S(1)}, u32[]{:S(2)}, u32[]{:S(2)}) collective-permute-start(bf16[2,512,128]{2,1,0:T(8,128)(2,1)S(1)} %slice.376), channel_id=1, source_target_pairs={{0,16},{4,20},{8,24},{12,28},{16,0},{20,4},{24,8},{28,12},{1,17},{... | collective-permute-start | bytes 786440 | tf_op jit(solution)/shard_map/ppermute | solution.py:230
  70.1 4.5 %shard_map.167 = (f32[1024,128]{1,0:T(8,128)S(1)}, f32[1024,128]{1,0:T(8,128)S(1)}, f32[1024,128]{1,0:T(8,128)S(1)}) custom-call(f32[2]{0:T(128)S(1)} %dynamic-slice_multiply_fusion.scale_ref, bf16[1024,128]{1,0:T(8,128)(2,1)S(1)} %get-tuple-element.43.q_ref, bf16[1024,128]{1,0:T(8,128)(2,1)S(1)} %get-tuple-element.62.refs_0_, ...), custom_call_target="tpu_custom_call" | custom-call | flops 536870912 | bytes 2359296 | tf_op jit(solution)/shard_map/pallas_call | solution.py:111
  74.7 4.5 %shard_map.168 = (f32[1024,128]{1,0:T(8,128)S(1)}, f32[1024,128]{1,0:T(8,128)S(1)}, f32[1024,128]{1,0:T(8,128)S(1)}) custom-call(f32[2]{0:T(128)S(1)} %dynamic-slice_multiply_fusion.scale_ref, bf16[1024,128]{1,0:T(8,128)(2,1)S(1)} %get-tuple-element.43.q_ref, bf16[1024,128]{1,0:T(8,128)(2,1)S(1)} %get-tuple-element.64.refs_0_, ...), custom_call_target="tpu_custom_call" | custom-call | flops 536870912 | bytes 2359296 | tf_op jit(solution)/shard_map/pallas_call | solution.py:111
  79.3 4.6 %shard_map.169 = (f32[1024,128]{1,0:T(8,128)S(1)}, f32[1024,128]{1,0:T(8,128)S(1)}, f32[1024,128]{1,0:T(8,128)S(1)}) custom-call(f32[2]{0:T(128)S(1)} %dynamic-slice_multiply_fusion.scale_ref, bf16[1024,128]{1,0:T(8,128)(2,1)S(1)} %get-tuple-element.43.q_ref, bf16[512,128]{1,0:T(8,128)(2,1)S(1)} %get-tuple-element.75.refs_0_, ...), custom_call_target="tpu_custom_call" | custom-call | flops 536870912 | bytes 2359296 | tf_op jit(solution)/shard_map/pallas_call | solution.py:111
  84.6 1.3 collective-permute-done.12
  86.0 5.6 %collective-permute-start.13 = (bf16[128,256]{1,0:T(8,128)(2,1)S(1)}, bf16[128,256]{1,0:T(8,128)(2,1)S(1)}, u32[]{:S(2)}, u32[]{:S(2)}) collective-permute-start(bf16[128,256]{1,0:T(8,128)(2,1)S(1)} %get-tuple-element.69), channel_id=1, source_target_pairs={{1,0},{2,1},{3,2},{0,3},{5,4},{6,5},{7,6},{4,7},{9,8},{10,9},{11,1... | collective-permute-start | bytes 196616 | tf_op jit(solution)/shard_map/ppermute | solution.py:153
  92.3 1.8 %collective-permute-done.13 = bf16[128,256]{1,0:T(8,128)(2,1)S(1)} collective-permute-done((bf16[128,256]{1,0:T(8,128)(2,1)S(1)}, bf16[128,256]{1,0:T(8,128)(2,1)S(1)}, u32[]{:S(2)}, u32[]{:S(2)}) %collective-permute-start.13) | collective-permute-done | bytes 65568 | tf_op jit(solution)/shard_map/ppermute | solution.py:153
  94.1 4.6 %collective-permute-done.14 = bf16[128,256]{1,0:T(8,128)(2,1)S(1)} collective-permute-done((bf16[128,256]{1,0:T(8,128)(2,1)S(1)}, bf16[128,256]{1,0:T(8,128)(2,1)S(1)}, u32[]{:S(2)}, u32[]{:S(2)}) %collective-permute-start.14) | collective-permute-done | bytes 65568 | tf_op jit(solution)/shard_map/ppermute | solution.py:153
  99.5 3.4 %fusion.58 = bf16[128,4,4,32,4]{0,3,4,2,1:T(8,128)(2,1)S(1)} fusion(bf16[4,32,1024,1,1]{2,1,4,3,0:T(8,128)(2,1)S(1)} %bitcast.275, bf16[1024,4,4,128]{3,2,1,0:T(4,128)(2,1)} %param.28), kind=kOutput, calls=%fused_computation.74 | convolution fusion | flops 539230208 | bytes 4980736 | tf_op jit(solution)/shard_map/pqd,dabh->hpaqb/dot_general | solution.py:271
  106.1 3.7 %collective-permute-done.17 = bf16[128,1,128]{2,0,1:T(8,128)(2,1)S(1)} collective-permute-done((bf16[128,1,128]{2,0,1:T(8,128)(2,1)S(1)}, bf16[128,1,128]{2,0,1:T(8,128)(2,1)S(1)}, u32[]{:S(2)}, u32[]{:S(2)}) %collective-permute-start.17) | collective-permute-done | bytes 32800 | tf_op jit(solution)/shard_map/ppermute | solution.py:21
  110.8 3.8 %collective-permute-start.19 = (bf16[128,18,1]{0,1,2:T(8,128)(2,1)S(1)}, bf16[128,18,1]{0,1,2:T(8,128)(2,1)S(1)}, u32[]{:S(2)}, u32[]{:S(2)}) collective-permute-start(bf16[128,18,1]{0,1,2:T(8,128)(2,1)S(1)} %copy.65), channel_id=1, source_target_pairs={{1,0},{2,1},{3,2},{0,3},{5,4},{6,5},{7,6},{4,7},{9,8},{10,9},{11,1... | collective-permute-start | bytes 13832 | tf_op jit(solution)/shard_map/ppermute | solution.py:26
  117.4 1.8 %maximum_maximum_fusion = (bf16[128,18,129]{2,0,1:T(8,128)(2,1)S(1)}, bf16[128,18,129]{2,0,1:T(8,128)(2,1)S(1)}) fusion(bf16[128,1,128]{2,0,1:T(8,128)(2,1)S(1)} %collective-permute-done.17, bf16[128,16,128]{2,0,1:T(8,128)(2,1)S(1)} %copy.59, bf16[128,1,128]{2,0,1:T(8,128)(2,1)S(1)} %collective-permute-done.16, bf16[128,18,1]{2,0,1:T(8,128)(2,1)S(1)} %copy.63, ...), kind=kLoop, calls=%fused_computation.54 | loop fusion | flops 4755456 | bytes 1787904 | tf_op jit(solution)/shard_map/concatenate | solution.py:27
  122.6 3.6 %collective-permute-done.20 = f32[64]{0:T(128)S(1)} collective-permute-done((f32[64]{0:T(128)S(1)}, f32[64]{0:T(128)S(1)}, u32[]{:S(2)}, u32[]{:S(2)}) %collective-permute-start.20) | collective-permute-done | bytes 288 | tf_op jit(solution)/shard_map/ppermute | solution.py:34
  126.1 2.3 %collective-permute-start.21 = (f32[64]{0:T(128)S(1)}, f32[64]{0:T(128)S(1)}, u32[]{:S(2)}, u32[]{:S(2)}) collective-permute-start(f32[64]{0:T(128)S(1)} %add.311), channel_id=1, source_target_pairs={{0,2},{1,3},{2,0},{3,1},{4,6},{5,7},{6,4},{7,5},{8,10},{9,11},{10,... | collective-permute-start | bytes 776 | tf_op jit(solution)/shard_map/ppermute | solution.py:34
  128.5 2.1 %collective-permute-done.21 = f32[64]{0:T(128)S(1)} collective-permute-done((f32[64]{0:T(128)S(1)}, f32[64]{0:T(128)S(1)}, u32[]{:S(2)}, u32[]{:S(2)}) %collective-permute-start.21) | collective-permute-done | bytes 288 | tf_op jit(solution)/shard_map/ppermute | solution.py:34
  131.7 2.5 %collective-permute-start.23 = (f32[64]{0:T(128)S(1)}, f32[64]{0:T(128)S(1)}, u32[]{:S(2)}, u32[]{:S(2)}) collective-permute-start(f32[64]{0:T(128)S(1)} %add.313), channel_id=1, source_target_pairs={{0,8},{4,12},{8,0},{12,4},{16,24},{20,28},{24,16},{28,20},{1,9},{5... | collective-permute-start | bytes 776 | tf_op jit(solution)/shard_map/ppermute | solution.py:34
  134.2 1.5 %collective-permute-done.23 = f32[64]{0:T(128)S(1)} collective-permute-done((f32[64]{0:T(128)S(1)}, f32[64]{0:T(128)S(1)}, u32[]{:S(2)}, u32[]{:S(2)}) %collective-permute-start.23) | collective-permute-done | bytes 288 | tf_op jit(solution)/shard_map/ppermute | solution.py:34
  135.7 3.2 %collective-permute-start.24 = (f32[64]{0:T(128)S(1)}, f32[64]{0:T(128)S(1)}, u32[]{:S(2)}, u32[]{:S(2)}) collective-permute-start(f32[64]{0:T(128)S(1)} %add.314), channel_id=1, source_target_pairs={{0,16},{4,20},{8,24},{12,28},{16,0},{20,4},{24,8},{28,12},{1,17},{... | collective-permute-start | bytes 776 | tf_op jit(solution)/shard_map/ppermute | solution.py:34
  (144 shorter events, 36.0 us)
Async XLA Ops:
  0.6 25.5 %copy-start = (bf16[1024,1024]{1,0:T(8,128)(2,1)S(1)}, bf16[1024,1024]{1,0:T(8,128)(2,1)}, u32[]{:S(2)}) copy-start(bf16[1024,1024]{1,0:T(8,128)(2,1)} %param.25) | copy-start | bytes 6291460
  2.1 13.6 %copy-start.10 = (bf16[9,128,69]{1,2,0:T(8,128)(2,1)S(1)}, bf16[9,128,69]{1,2,0:T(8,128)(2,1)}, u32[]{:S(2)}) copy-start(bf16[9,128,69]{1,2,0:T(8,128)(2,1)} %param.19) | copy-start | bytes 476932
  2.2 3.8 %collective-permute-start = (bf16[69,2,128]{0,2,1:T(8,128)(2,1)S(1)}, bf16[69,2,128]{0,2,1:T(8,128)(2,1)S(1)}, u32[]{:S(2)}, u32[]{:S(2)}) collective-permute-start(bf16[69,2,128]{0,2,1:T(8,128)(2,1)S(1)} %get-tuple-element.65), channel_id=1, source_target_pairs={{0,4},{4,8},{8,12},{12,16},{16,20},{20,24},{24,28},{1,5},{5,9},{9,... | collective-permute-start | bytes 105992 | tf_op jit(solution)/shard_map/ppermute | solution.py:20
  4.7 5.3 %collective-permute-start.1 = (bf16[69,2,128]{0,2,1:T(8,128)(2,1)S(1)}, bf16[69,2,128]{0,2,1:T(8,128)(2,1)S(1)}, u32[]{:S(2)}, u32[]{:S(2)}) collective-permute-start(bf16[69,2,128]{0,2,1:T(8,128)(2,1)S(1)} %get-tuple-element.66), channel_id=1, source_target_pairs={{4,0},{8,4},{12,8},{16,12},{20,16},{24,20},{28,24},{5,1},{9,5},{13... | collective-permute-start | bytes 105992 | tf_op jit(solution)/shard_map/ppermute | solution.py:21
  9.9 5.5 %collective-permute-start.2 = (bf16[69,20,2]{0,2,1:T(2,128)(2,1)S(1)}, bf16[69,20,2]{0,2,1:T(2,128)(2,1)S(1)}, u32[]{:S(2)}, u32[]{:S(2)}) collective-permute-start(bf16[69,20,2]{0,2,1:T(2,128)(2,1)S(1)} %get-tuple-element.51), channel_id=1, source_target_pairs={{0,1},{1,2},{2,3},{3,0},{4,5},{5,6},{6,7},{7,4},{8,9},{9,10},{10,1... | collective-permute-start | bytes 16568 | tf_op jit(solution)/shard_map/ppermute | solution.py:25
  11.6 3.9 %collective-permute-start.3 = (bf16[69,20,2]{0,2,1:T(2,128)(2,1)S(1)}, bf16[69,20,2]{0,2,1:T(2,128)(2,1)S(1)}, u32[]{:S(2)}, u32[]{:S(2)}) collective-permute-start(bf16[69,20,2]{0,2,1:T(2,128)(2,1)S(1)} %get-tuple-element.52), channel_id=1, source_target_pairs={{1,0},{2,1},{3,2},{0,3},{5,4},{6,5},{7,6},{4,7},{9,8},{10,9},{11,1... | collective-permute-start | bytes 16568 | tf_op jit(solution)/shard_map/ppermute | solution.py:26
  30.0 9.0 %collective-permute-start.4 = (bf16[3,128,256]{2,1,0:T(8,128)(2,1)S(1)}, bf16[3,128,256]{2,1,0:T(8,128)(2,1)S(1)}, u32[]{:S(2)}, u32[]{:S(2)}) collective-permute-start(bf16[3,128,256]{2,1,0:T(8,128)(2,1)S(1)} %get-tuple-element.50), channel_id=1, source_target_pairs={{0,1},{1,2},{2,3},{3,0},{4,5},{5,6},{6,7},{7,4},{8,9},{9,10},{10,1... | collective-permute-start | bytes 589832 | tf_op jit(solution)/shard_map/ppermute | solution.py:145
  31.4 16.6 %collective-permute-start.5 = (bf16[3,128,256]{2,1,0:T(8,128)(2,1)S(1)}, bf16[3,128,256]{2,1,0:T(8,128)(2,1)S(1)}, u32[]{:S(2)}, u32[]{:S(2)}) collective-permute-start(bf16[3,128,256]{2,1,0:T(8,128)(2,1)S(1)} %get-tuple-element.49), channel_id=1, source_target_pairs={{0,2},{1,3},{2,0},{3,1},{4,6},{5,7},{6,4},{7,5},{8,10},{9,11},{10,... | collective-permute-start | bytes 589832 | tf_op jit(solution)/shard_map/ppermute | solution.py:145
  34.5 13.6 %collective-permute-start.6 = (bf16[3,128,256]{2,1,0:T(8,128)(2,1)S(1)}, bf16[3,128,256]{2,1,0:T(8,128)(2,1)S(1)}, u32[]{:S(2)}, u32[]{:S(2)}) collective-permute-start(bf16[3,128,256]{2,1,0:T(8,128)(2,1)S(1)} %get-tuple-element.48), channel_id=1, source_target_pairs={{0,3},{1,0},{2,1},{3,2},{4,7},{5,4},{6,5},{7,6},{8,11},{9,8},{10,9... | collective-permute-start | bytes 589832 | tf_op jit(solution)/shard_map/ppermute | solution.py:145
  48.1 5.5 %copy-start.13 = (f32[16]{0:T(128)S(1)}, f32[16]{0:T(128)}, u32[]{:S(2)}) copy-start(f32[16]{0:T(128)} %param.27) | copy-start | bytes 196
  48.2 1.8 %collective-permute-start.7 = (bf16[3,512,128]{2,1,0:T(8,128)(2,1)S(1)}, bf16[3,512,128]{2,1,0:T(8,128)(2,1)S(1)}, u32[]{:S(2)}, u32[]{:S(2)}) collective-permute-start(bf16[3,512,128]{2,1,0:T(8,128)(2,1)S(1)} %get-tuple-element.45), channel_id=1, source_target_pairs={{0,4},{4,0},{8,12},{12,8},{16,20},{20,16},{24,28},{28,24},{1,5},{5... | collective-permute-start | bytes 1179656 | tf_op jit(solution)/shard_map/ppermute | solution.py:219
  50.8 15.3 %collective-permute-start.8 = (bf16[2,1024,128]{2,1,0:T(8,128)(2,1)}, bf16[2,1024,128]{2,1,0:T(8,128)(2,1)}, u32[]{:S(2)}, u32[]{:S(2)}) collective-permute-start(bf16[2,1024,128]{2,1,0:T(8,128)(2,1)} %pad_maximum_fusion.6), channel_id=1, source_target_pairs={{0,8},{4,12},{8,0},{12,4},{16,24},{20,28},{24,16},{28,20},{1,9},{5... | collective-permute-start | bytes 1572872 | tf_op jit(solution)/shard_map/ppermute | solution.py:226
  53.6 15.1 %collective-permute-start.9 = (bf16[2,1024,128]{2,1,0:T(8,128)(2,1)}, bf16[2,1024,128]{2,1,0:T(8,128)(2,1)S(1)}, u32[]{:S(2)}, u32[]{:S(2)}) collective-permute-start(bf16[2,1024,128]{2,1,0:T(8,128)(2,1)} %pad_maximum_fusion.6), channel_id=1, source_target_pairs={{0,16},{4,20},{8,24},{12,28},{16,0},{20,4},{24,8},{28,12},{1,17},{... | collective-permute-start | bytes 1572872 | tf_op jit(solution)/shard_map/ppermute | solution.py:227
  67.1 12.1 %collective-permute-start.11 = (bf16[2,512,128]{2,1,0:T(8,128)(2,1)S(1)}, bf16[2,512,128]{2,1,0:T(8,128)(2,1)S(1)}, u32[]{:S(2)}, u32[]{:S(2)}) collective-permute-start(bf16[2,512,128]{2,1,0:T(8,128)(2,1)S(1)} %slice.376), channel_id=1, source_target_pairs={{0,16},{4,20},{8,24},{12,28},{16,0},{20,4},{24,8},{28,12},{1,17},{... | collective-permute-start | bytes 786440 | tf_op jit(solution)/shard_map/ppermute | solution.py:230
  68.7 10.5 %collective-permute-start.10 = (bf16[2,512,128]{2,1,0:T(8,128)(2,1)S(1)}, bf16[2,512,128]{2,1,0:T(8,128)(2,1)S(1)}, u32[]{:S(2)}, u32[]{:S(2)}) collective-permute-start(bf16[2,512,128]{2,1,0:T(8,128)(2,1)S(1)} %slice.374), channel_id=1, source_target_pairs={{0,8},{4,12},{8,0},{12,4},{16,24},{20,28},{24,16},{28,20},{1,9},{5... | collective-permute-start | bytes 786440 | tf_op jit(solution)/shard_map/ppermute | solution.py:229
  84.5 1.4 %collective-permute-start.12 = (bf16[512,128]{1,0:T(8,128)(2,1)S(1)}, bf16[512,128]{1,0:T(8,128)(2,1)S(1)}, u32[]{:S(2)}, u32[]{:S(2)}) collective-permute-start(bf16[512,128]{1,0:T(8,128)(2,1)S(1)} %get-tuple-element.71), channel_id=1, source_target_pairs={{0,4},{4,0},{8,12},{12,8},{16,20},{20,16},{24,28},{28,24},{1,5},{5... | collective-permute-start | bytes 393224 | tf_op jit(solution)/shard_map/ppermute | solution.py:255
  85.9 13.1 %copy-start.5 = (bf16[1024,1024]{1,0:T(8,128)(2,1)S(1)}, bf16[1024,1024]{1,0:T(8,128)(2,1)}, u32[]{:S(2)}) copy-start(bf16[1024,1024]{1,0:T(8,128)(2,1)} %param.26) | copy-start | bytes 6291460
  86.0 8.1 %collective-permute-start.13 = (bf16[128,256]{1,0:T(8,128)(2,1)S(1)}, bf16[128,256]{1,0:T(8,128)(2,1)S(1)}, u32[]{:S(2)}, u32[]{:S(2)}) collective-permute-start(bf16[128,256]{1,0:T(8,128)(2,1)S(1)} %get-tuple-element.69), channel_id=1, source_target_pairs={{1,0},{2,1},{3,2},{0,3},{5,4},{6,5},{7,6},{4,7},{9,8},{10,9},{11,1... | collective-permute-start | bytes 196616 | tf_op jit(solution)/shard_map/ppermute | solution.py:153
  91.6 7.1 %collective-permute-start.14 = (bf16[128,256]{1,0:T(8,128)(2,1)S(1)}, bf16[128,256]{1,0:T(8,128)(2,1)S(1)}, u32[]{:S(2)}, u32[]{:S(2)}) collective-permute-start(bf16[128,256]{1,0:T(8,128)(2,1)S(1)} %get-tuple-element.68), channel_id=1, source_target_pairs={{2,0},{3,1},{0,2},{1,3},{6,4},{7,5},{4,6},{5,7},{10,8},{11,9},{8,1... | collective-permute-start | bytes 196616 | tf_op jit(solution)/shard_map/ppermute | solution.py:153
  92.2 6.5 %collective-permute-start.15 = (bf16[128,256]{1,0:T(8,128)(2,1)S(1)}, bf16[128,256]{1,0:T(8,128)(2,1)S(1)}, u32[]{:S(2)}, u32[]{:S(2)}) collective-permute-start(bf16[128,256]{1,0:T(8,128)(2,1)S(1)} %get-tuple-element.67), channel_id=1, source_target_pairs={{3,0},{0,1},{1,2},{2,3},{7,4},{4,5},{5,6},{6,7},{11,8},{8,9},{9,10... | collective-permute-start | bytes 196616 | tf_op jit(solution)/shard_map/ppermute | solution.py:153
  103.4 2.6 %collective-permute-start.16 = (bf16[128,1,128]{2,0,1:T(8,128)(2,1)S(1)}, bf16[128,1,128]{2,0,1:T(8,128)(2,1)S(1)}, u32[]{:S(2)}, u32[]{:S(2)}) collective-permute-start(bf16[128,1,128]{2,0,1:T(8,128)(2,1)S(1)} %get-tuple-element.59), channel_id=1, source_target_pairs={{0,4},{4,8},{8,12},{12,16},{16,20},{20,24},{24,28},{1,5},{5,9},{9,... | collective-permute-start | bytes 98312 | tf_op jit(solution)/shard_map/ppermute | solution.py:20
  104.7 5.0 %collective-permute-start.17 = (bf16[128,1,128]{2,0,1:T(8,128)(2,1)S(1)}, bf16[128,1,128]{2,0,1:T(8,128)(2,1)S(1)}, u32[]{:S(2)}, u32[]{:S(2)}) collective-permute-start(bf16[128,1,128]{2,0,1:T(8,128)(2,1)S(1)} %get-tuple-element.60), channel_id=1, source_target_pairs={{4,0},{8,4},{12,8},{16,12},{20,16},{24,20},{28,24},{5,1},{9,5},{13... | collective-permute-start | bytes 98312 | tf_op jit(solution)/shard_map/ppermute | solution.py:21
  109.9 4.8 %copy-start.9 = (bf16[9,69,128]{2,1,0:T(8,128)(2,1)S(1)}, bf16[9,69,128]{2,1,0:T(8,128)(2,1)}, u32[]{:S(2)}) copy-start(bf16[9,69,128]{2,1,0:T(8,128)(2,1)} %param.29) | copy-start | bytes 476932
  110.5 5.5 %collective-permute-start.18 = (bf16[128,18,1]{0,1,2:T(8,128)(2,1)S(1)}, bf16[128,18,1]{0,1,2:T(8,128)(2,1)S(1)}, u32[]{:S(2)}, u32[]{:S(2)}) collective-permute-start(bf16[128,18,1]{0,1,2:T(8,128)(2,1)S(1)} %copy.62), channel_id=1, source_target_pairs={{0,1},{1,2},{2,3},{3,0},{4,5},{5,6},{6,7},{7,4},{8,9},{9,10},{10,1... | collective-permute-start | bytes 13832 | tf_op jit(solution)/shard_map/ppermute | solution.py:25
  110.8 5.5 %collective-permute-start.19 = (bf16[128,18,1]{0,1,2:T(8,128)(2,1)S(1)}, bf16[128,18,1]{0,1,2:T(8,128)(2,1)S(1)}, u32[]{:S(2)}, u32[]{:S(2)}) collective-permute-start(bf16[128,18,1]{0,1,2:T(8,128)(2,1)S(1)} %copy.65), channel_id=1, source_target_pairs={{1,0},{2,1},{3,2},{0,3},{5,4},{6,5},{7,6},{4,7},{9,8},{10,9},{11,1... | collective-permute-start | bytes 13832 | tf_op jit(solution)/shard_map/ppermute | solution.py:26
  120.9 20.2 %copy-start.1 = (bf16[1024,1024]{1,0:T(8,128)(2,1)S(1)}, bf16[1024,1024]{1,0:T(8,128)(2,1)}, u32[]{:S(2)}) copy-start(bf16[1024,1024]{1,0:T(8,128)(2,1)} %param.25) | copy-start | bytes 6291460
  121.5 19.0 %copy-start.14 = (s32[64]{0:T(128)S(1)}, s32[64]{0:T(128)}, u32[]{:S(2)}) copy-start(s32[64]{0:T(128)} %param.18) | copy-start | bytes 772
  122.6 3.6 %collective-permute-start.20 = (f32[64]{0:T(128)S(1)}, f32[64]{0:T(128)S(1)}, u32[]{:S(2)}, u32[]{:S(2)}) collective-permute-start(f32[64]{0:T(128)S(1)} %fusion.40), channel_id=1, source_target_pairs={{0,1},{1,0},{2,3},{3,2},{4,5},{5,4},{6,7},{7,6},{8,9},{9,8},{10,11... | collective-permute-start | bytes 776 | tf_op jit(solution)/shard_map/ppermute | solution.py:34
  126.1 4.4 %collective-permute-start.21 = (f32[64]{0:T(128)S(1)}, f32[64]{0:T(128)S(1)}, u32[]{:S(2)}, u32[]{:S(2)}) collective-permute-start(f32[64]{0:T(128)S(1)} %add.311), channel_id=1, source_target_pairs={{0,2},{1,3},{2,0},{3,1},{4,6},{5,7},{6,4},{7,5},{8,10},{9,11},{10,... | collective-permute-start | bytes 776 | tf_op jit(solution)/shard_map/ppermute | solution.py:34
  130.6 1.1 collective-permute-start.22
  131.7 4.0 %collective-permute-start.23 = (f32[64]{0:T(128)S(1)}, f32[64]{0:T(128)S(1)}, u32[]{:S(2)}, u32[]{:S(2)}) collective-permute-start(f32[64]{0:T(128)S(1)} %add.313), channel_id=1, source_target_pairs={{0,8},{4,12},{8,0},{12,4},{16,24},{20,28},{24,16},{28,20},{1,9},{5... | collective-permute-start | bytes 776 | tf_op jit(solution)/shard_map/ppermute | solution.py:34
  135.7 4.7 %collective-permute-start.24 = (f32[64]{0:T(128)S(1)}, f32[64]{0:T(128)S(1)}, u32[]{:S(2)}, u32[]{:S(2)}) collective-permute-start(f32[64]{0:T(128)S(1)} %add.314), channel_id=1, source_target_pairs={{0,16},{4,20},{8,24},{12,28},{16,0},{20,4},{24,8},{28,12},{1,17},{... | collective-permute-start | bytes 776 | tf_op jit(solution)/shard_map/ppermute | solution.py:34
  (9 other events, 10.9 us)

commit v13 on v12

--- a/solution.py
+++ b/solution.py
@@ -63,8 +63,6 @@
     queries = q_ref[...]
     column_head = lax.broadcasted_iota(jnp.int32, queries.shape, 1) // head_size
     total = jnp.zeros(queries.shape, jnp.float32)
-    maxima = jnp.zeros(queries.shape, jnp.float32)
-    sums = jnp.zeros(queries.shape, jnp.float32)
     for head in range(queries.shape[1] // head_size):
         in_head = column_head == head
         masked = jnp.where(in_head, queries, jnp.zeros_like(queries))
@@ -89,11 +87,9 @@
             weight_sum = chunk_sum if weight_sum is None else weight_sum + chunk_sum
             weighted = chunk_weighted if weighted is None else weighted + chunk_weighted
         total = jnp.where(in_head, weighted, total)
-        maxima = jnp.where(in_head, row_max, maxima)
-        sums = jnp.where(in_head, weight_sum, sums)
+        m_ref[:, head : head + 1] = row_max
+        l_ref[:, head : head + 1] = weight_sum
     o_ref[...] = total
-    m_ref[...] = maxima
-    l_ref[...] = sums
 
 
 def attend_part(queries, key_chunks, value_chunks, scales, head_size):
@@ -104,31 +100,37 @@
     heads = width // head_size
     part = jax.ShapeDtypeStruct((query_count, width), jnp.float32)
     part_spec = pl.BlockSpec((block, width), lambda i: (i, 0))
+    stat = jax.ShapeDtypeStruct((query_count, heads), jnp.float32)
+    stat_spec = pl.BlockSpec((block, heads), lambda i: (i, 0))
     chunk_specs = [
         pl.BlockSpec((chunk.shape[0], width), lambda i: (0, 0))
         for chunk in list(key_chunks) + list(value_chunks)
     ]
     return pl.pallas_call(
         functools.partial(attention_kernel, head_size=head_size, chunk_count=len(key_chunks)),
-        out_shape=(part, part, part),
+        out_shape=(part, stat, stat),
         grid=(query_count // block,),
         in_specs=[
             pl.BlockSpec(memory_space=pltpu.SMEM),
             pl.BlockSpec((block, width), lambda i: (i, 0)),
         ]
         + chunk_specs,
-        out_specs=(part_spec, part_spec, part_spec),
+        out_specs=(part_spec, stat_spec, stat_spec),
         compiler_params=pltpu.CompilerParams(vmem_limit_bytes=48 * 1024 * 1024),
         cost_estimate=pl.CostEstimate(
             flops=4 * query_count * key_count * width,
             transcendentals=query_count * key_count * heads,
             bytes_accessed=2 * (query_count * width + 2 * key_count * width)
-            + 12 * query_count * width,
+            + 4 * query_count * (width + 2 * heads),
         ),
     )(scales, queries, *key_chunks, *value_chunks)
 
 
-def merge_parts(parts):
+def merge_parts(parts, head_size):
+    parts = [
+        (total, jnp.repeat(maxima, head_size, axis=1), jnp.repeat(sums, head_size, axis=1))
+        for total, maxima, sums in parts
+    ]
     joint = functools.reduce(jnp.maximum, [maxima for total, maxima, sums in parts])
     rescales = [jnp.exp(maxima - joint) for total, maxima, sums in parts]
     total = sum(part[0] * rescale for part, rescale in zip(parts, rescales))
@@ -249,7 +251,7 @@
         for group in key_groups
         if group
     ]
-    pair_attended = merge_parts(parts)
+    pair_attended = merge_parts(parts, head_size)
     token_count = spread.shape[1]
     own_part = pair_attended[:token_count]
     returned = lax.ppermute(pair_attended[token_count:], "lat", partner)

time: 142 us -> 157 us (1.11)
  local copies, waits for them, and re-layouts: 11.9 us -> 28 us
  waiting for transfers between devices: 49.1 us -> 45.9 us
  other arithmetic: 4.24 us -> 6.02 us
    reshape x0 -> x8, local copies, waits for them, and re-layouts: none -> 10.2 us  [the longest x4 5.12 us: merge_parts(): jnp.repeat(maxima, head_size, axis=1)]
    ppermute x1, waiting for transfers between devices: 7.88 us -> 5.33 us  [on_device(): from_x = lax.ppermute(key_value, 'lat', across_x)]
    broadcast_in_dim x0 -> x8, local copies, waits for them, and re-layouts: none -> 2.09 us  [the longest x4 1.05 us: merge_parts(): jnp.repeat(sums, head_size, axis=1)]
    convert_element_type x1, other arithmetic: 0.56 us -> 2.39 us  [merge_parts(): return (total / weight_sum).astype(jnp.bfloat16)]
    slice x1, local copies, waits for them, and re-layouts: 0.02 us -> 1.67 us  [on_device(): diagonal_low = lax.ppermute(from_y[:, :middle], 'lat', across_x)]
    unnamed x41 -> x49, local copies, waits for them, and re-layouts: 6.4 us -> 6.41 us
  transfers between devices with their start and end apart: 25 -> 25, of which waited for: 16 -> 16; matrix products, arithmetic and copies ran while one was open for 3% -> 8% of each run, Pallas kernels for 10% -> 9%
where the time goes in v13:
time: 157 us; the launch traced here: 156 us
  waiting for transfers between devices  45.9 us (29%)
  starting transfers between devices  39.3 us (25%)
  local copies, waits for them, and re-layouts  28 us (18%)
  Pallas kernels  17.9 us (11%)
  matrix products  17.7 us (11%)
  other arithmetic  6.02 us (4%)
    pallas_call x4, Pallas kernels, attend_part(): pl.pallas_call(functools.partial(attention_kernel, head_size=head_size, c...  17.9 us
    ppermute x3, waiting for transfers between devices, exchange_blocks(): lax.ppermute(outgoing, axis, [(i, (i + shift) % size) for i in range(size)])  12.7 us
    dot_general x27, matrix products, convolution_kernel_taps(): jnp.einsum('oc,cyx->oyx', weight[tap_index], window, preferred_element_ty...  10.7 us
    ppermute x5, waiting for transfers between devices, butterfly_sum(): value = value + lax.ppermute(value, axis, partner)  8.67 us
    ppermute x5, starting transfers between devices, butterfly_sum(): value = value + lax.ppermute(value, axis, partner)  8.46 us
    ppermute x2, waiting for transfers between devices, halo_padded(): from_below = lax.ppermute(array[:, :width], 'lat', up)  7.65 us
    ppermute x3, waiting for transfers between devices, return_blocks(): lax.ppermute(blocks[shift], axis, [((i + shift) % size, i) for i in range...  6.44 us
    unnamed x49, local copies, waits for them, and re-layouts  6.41 us
  transfers between devices with their start and end apart: 25, of which 16 were waited for; matrix products, arithmetic and copies ran while one was open for 8% of the time, Pallas kernels for 9%

profile of v13, /device:TPU:0, one launch (start us, length us, event | category | flops | bytes accessed | tf_op | source)
XLA Modules:
  0.0 156.2 jit_solution(7343137386968399793)
XLA Ops:
  2.2 2.5 %collective-permute-start = (bf16[69,2,128]{0,2,1:T(8,128)(2,1)S(1)}, bf16[69,2,128]{0,2,1:T(8,128)(2,1)S(1)}, u32[]{:S(2)}, u32[]{:S(2)}) collective-permute-start(bf16[69,2,128]{0,2,1:T(8,128)(2,1)S(1)} %get-tuple-element.65), channel_id=1, source_target_pairs={{0,4},{4,8},{8,12},{12,16},{16,20},{20,24},{24,28},{1,5},{5,9},{9,... | collective-permute-start | bytes 105992 | tf_op jit(solution)/shard_map/ppermute | solution.py:20
  6.0 3.9 %collective-permute-done.1 = bf16[69,2,128]{0,2,1:T(8,128)(2,1)S(1)} collective-permute-done((bf16[69,2,128]{0,2,1:T(8,128)(2,1)S(1)}, bf16[69,2,128]{0,2,1:T(8,128)(2,1)S(1)}, u32[]{:S(2)}, u32[]{:S(2)}) %collective-permute-start.1) | collective-permute-done | bytes 35360 | tf_op jit(solution)/shard_map/ppermute | solution.py:21
  9.9 1.6 %collective-permute-start.2 = (bf16[69,20,2]{0,2,1:T(2,128)(2,1)S(1)}, bf16[69,20,2]{0,2,1:T(2,128)(2,1)S(1)}, u32[]{:S(2)}, u32[]{:S(2)}) collective-permute-start(bf16[69,20,2]{0,2,1:T(2,128)(2,1)S(1)} %get-tuple-element.51), channel_id=1, source_target_pairs={{0,1},{1,2},{2,3},{3,0},{4,5},{5,6},{6,7},{7,4},{8,9},{9,10},{10,1... | collective-permute-start | bytes 16568 | tf_op jit(solution)/shard_map/ppermute | solution.py:25
  11.6 2.2 %collective-permute-start.3 = (bf16[69,20,2]{0,2,1:T(2,128)(2,1)S(1)}, bf16[69,20,2]{0,2,1:T(2,128)(2,1)S(1)}, u32[]{:S(2)}, u32[]{:S(2)}) collective-permute-start(bf16[69,20,2]{0,2,1:T(2,128)(2,1)S(1)} %get-tuple-element.52), channel_id=1, source_target_pairs={{1,0},{2,1},{3,2},{0,3},{5,4},{6,5},{7,6},{4,7},{9,8},{10,9},{11,1... | collective-permute-start | bytes 16568 | tf_op jit(solution)/shard_map/ppermute | solution.py:26
  13.8 1.6 %collective-permute-done.2 = bf16[69,20,2]{0,2,1:T(2,128)(2,1)S(1)} collective-permute-done((bf16[69,20,2]{0,2,1:T(2,128)(2,1)S(1)}, bf16[69,20,2]{0,2,1:T(2,128)(2,1)S(1)}, u32[]{:S(2)}, u32[]{:S(2)}) %collective-permute-start.2) | collective-permute-done | bytes 5552 | tf_op jit(solution)/shard_map/ppermute | solution.py:25
  31.4 3.1 %collective-permute-start.5 = (bf16[3,128,256]{2,1,0:T(8,128)(2,1)S(1)}, bf16[3,128,256]{2,1,0:T(8,128)(2,1)S(1)}, u32[]{:S(2)}, u32[]{:S(2)}) collective-permute-start(bf16[3,128,256]{2,1,0:T(8,128)(2,1)S(1)} %get-tuple-element.49), channel_id=1, source_target_pairs={{0,2},{1,3},{2,0},{3,1},{4,6},{5,7},{6,4},{7,5},{8,10},{9,11},{10,... | collective-permute-start | bytes 589832 | tf_op jit(solution)/shard_map/ppermute | solution.py:147
  35.3 3.6 %collective-permute-done.4 = bf16[3,128,256]{2,1,0:T(8,128)(2,1)S(1)} collective-permute-done((bf16[3,128,256]{2,1,0:T(8,128)(2,1)S(1)}, bf16[3,128,256]{2,1,0:T(8,128)(2,1)S(1)}, u32[]{:S(2)}, u32[]{:S(2)}) %collective-permute-start.4) | collective-permute-done | bytes 196640 | tf_op jit(solution)/shard_map/ppermute | solution.py:147
  39.0 9.1 %collective-permute-done.5 = bf16[3,128,256]{2,1,0:T(8,128)(2,1)S(1)} collective-permute-done((bf16[3,128,256]{2,1,0:T(8,128)(2,1)S(1)}, bf16[3,128,256]{2,1,0:T(8,128)(2,1)S(1)}, u32[]{:S(2)}, u32[]{:S(2)}) %collective-permute-start.5) | collective-permute-done | bytes 196640 | tf_op jit(solution)/shard_map/ppermute | solution.py:147
  48.4 1.6 %collective-permute-done.7 = bf16[3,512,128]{2,1,0:T(8,128)(2,1)S(1)} collective-permute-done((bf16[3,512,128]{2,1,0:T(8,128)(2,1)S(1)}, bf16[3,512,128]{2,1,0:T(8,128)(2,1)S(1)}, u32[]{:S(2)}, u32[]{:S(2)}) %collective-permute-start.7) | collective-permute-done | bytes 393248 | tf_op jit(solution)/shard_map/ppermute | solution.py:221
  50.8 2.8 %collective-permute-start.8 = (bf16[2,1024,128]{2,1,0:T(8,128)(2,1)}, bf16[2,1024,128]{2,1,0:T(8,128)(2,1)S(1)}, u32[]{:S(2)}, u32[]{:S(2)}) collective-permute-start(bf16[2,1024,128]{2,1,0:T(8,128)(2,1)} %pad_maximum_fusion.6), channel_id=1, source_target_pairs={{0,8},{4,12},{8,0},{12,4},{16,24},{20,28},{24,16},{28,20},{1,9},{5... | collective-permute-start | bytes 1572872 | tf_op jit(solution)/shard_map/ppermute | solution.py:228
  53.7 4.5 %shard_map.166 = (f32[1024,128]{1,0:T(8,128)S(1)}, f32[1024,2]{1,0:T(8,128)S(1)}, f32[1024,2]{1,0:T(8,128)S(1)}) custom-call(f32[2]{0:T(128)S(1)} %dynamic-slice_multiply_fusion.scale_ref, bf16[1024,128]{1,0:T(8,128)(2,1)S(1)} %get-tuple-element.43.q_ref, bf16[1024,128]{1,0:T(8,128)(2,1)S(1)} %get-tuple-element.44.refs_0_, ...), custom_call_target="tpu_custom_call" | custom-call | flops 536870912 | bytes 1327104 | tf_op jit(solution)/shard_map/pallas_call | solution.py:109
  60.7 5.3 %collective-permute-done.8 = bf16[2,1024,128]{2,1,0:T(8,128)(2,1)S(1)} collective-permute-done((bf16[2,1024,128]{2,1,0:T(8,128)(2,1)}, bf16[2,1024,128]{2,1,0:T(8,128)(2,1)S(1)}, u32[]{:S(2)}, u32[]{:S(2)}) %collective-permute-start.8) | collective-permute-done | bytes 524320 | tf_op jit(solution)/shard_map/ppermute | solution.py:228
  66.0 4.5 %shard_map.167 = (f32[1024,128]{1,0:T(8,128)S(1)}, f32[1024,2]{1,0:T(8,128)S(1)}, f32[1024,2]{1,0:T(8,128)S(1)}) custom-call(f32[2]{0:T(128)S(1)} %dynamic-slice_multiply_fusion.scale_ref, bf16[1024,128]{1,0:T(8,128)(2,1)S(1)} %get-tuple-element.43.q_ref, bf16[1024,128]{1,0:T(8,128)(2,1)S(1)} %get-tuple-element.62.refs_0_, ...), custom_call_target="tpu_custom_call" | custom-call | flops 536870912 | bytes 1327104 | tf_op jit(solution)/shard_map/pallas_call | solution.py:109
  73.7 1.5 collective-permute-start.11
  75.3 1.7 %slice.374 = bf16[2,512,128]{2,1,0:T(8,128)(2,1)} slice(bf16[2,1024,128]{2,1,0:T(8,128)(2,1)} %collective-permute-done.9), slice={[0:2], [0:512], [0:128]} | slice | bytes 524288 | tf_op jit(solution)/shard_map/slice | solution.py:231
  78.3 4.7 %shard_map.168 = (f32[1024,128]{1,0:T(8,128)S(1)}, f32[1024,2]{1,0:T(8,128)S(1)}, f32[1024,2]{1,0:T(8,128)S(1)}) custom-call(f32[2]{0:T(128)S(1)} %dynamic-slice_multiply_fusion.scale_ref, bf16[1024,128]{1,0:T(8,128)(2,1)S(1)} %get-tuple-element.43.q_ref, bf16[1024,128]{1,0:T(8,128)(2,1)S(1)} %get-tuple-element.64.refs_0_, ...), custom_call_target="tpu_custom_call" | custom-call | flops 536870912 | bytes 1327104 | tf_op jit(solution)/shard_map/pallas_call | solution.py:109
  86.5 4.3 %shard_map.169 = (f32[1024,128]{1,0:T(8,128)S(1)}, f32[1024,2]{1,0:T(8,128)S(1)}, f32[1024,2]{1,0:T(8,128)S(1)}) custom-call(f32[2]{0:T(128)S(1)} %dynamic-slice_multiply_fusion.scale_ref, bf16[1024,128]{1,0:T(8,128)(2,1)S(1)} %get-tuple-element.43.q_ref, bf16[512,128]{1,0:T(8,128)(2,1)S(1)} %get-tuple-element.75.refs_0_, ...), custom_call_target="tpu_custom_call" | custom-call | flops 536870912 | bytes 1327104 | tf_op jit(solution)/shard_map/pallas_call | solution.py:109
  91.9 2.1 %copy.83 = f32[1024,128]{1,0:T(8,128)} copy(f32[1024,128]{0,1:T(8,128)} %bitcast.283) | data formatting | bytes 1048576 | tf_op jit(solution)/shard_map/reshape | solution.py:131
  95.0 2.0 %copy.95 = f32[1024,128]{1,0:T(8,128)} copy(f32[1024,128]{0,1:T(8,128)} %bitcast.284) | data formatting | bytes 1048576 | tf_op jit(solution)/shard_map/reshape | solution.py:131
  97.1 2.4 %divide_convert_fusion = bf16[1024,128]{1,0:T(8,128)(2,1)S(1)} fusion(f32[1024,128]{1,0:T(8,128)} %copy.95, f32[1024,128]{1,0:T(8,128)} %copy.93, f32[1024,128]{1,0:T(8,128)} %copy.91, f32[1024,128]{1,0:T(8,128)S(1)} %copy-done.8, f32[1024,128]{1,0:T(8,128)S(1)} %get-tuple-element.28, f32[1024,128]{1,0:T(8,128)} %copy.83, ...), kind=kLoop, calls=%fused_computation.125 | loop fusion | flops 3014656 | bytes 6553600 | tf_op jit(solution)/shard_map/convert_element_type | solution.py:138
  101.0 5.5 %collective-permute-start.13 = (bf16[128,256]{1,0:T(8,128)(2,1)S(1)}, bf16[128,256]{1,0:T(8,128)(2,1)S(1)}, u32[]{:S(2)}, u32[]{:S(2)}) collective-permute-start(bf16[128,256]{1,0:T(8,128)(2,1)S(1)} %get-tuple-element.69), channel_id=1, source_target_pairs={{1,0},{2,1},{3,2},{0,3},{5,4},{6,5},{7,6},{4,7},{9,8},{10,9},{11,1... | collective-permute-start | bytes 196616 | tf_op jit(solution)/shard_map/ppermute | solution.py:155
  107.3 1.8 %collective-permute-done.13 = bf16[128,256]{1,0:T(8,128)(2,1)S(1)} collective-permute-done((bf16[128,256]{1,0:T(8,128)(2,1)S(1)}, bf16[128,256]{1,0:T(8,128)(2,1)S(1)}, u32[]{:S(2)}, u32[]{:S(2)}) %collective-permute-start.13) | collective-permute-done | bytes 65568 | tf_op jit(solution)/shard_map/ppermute | solution.py:155
  109.1 4.6 %collective-permute-done.14 = bf16[128,256]{1,0:T(8,128)(2,1)S(1)} collective-permute-done((bf16[128,256]{1,0:T(8,128)(2,1)S(1)}, bf16[128,256]{1,0:T(8,128)(2,1)S(1)}, u32[]{:S(2)}, u32[]{:S(2)}) %collective-permute-start.14) | collective-permute-done | bytes 65568 | tf_op jit(solution)/shard_map/ppermute | solution.py:155
  114.5 3.4 %fusion.58 = bf16[128,4,4,32,4]{0,3,4,2,1:T(8,128)(2,1)S(1)} fusion(bf16[4,32,1024,1,1]{2,1,4,3,0:T(8,128)(2,1)S(1)} %bitcast.291, bf16[1024,4,4,128]{3,2,1,0:T(4,128)(2,1)} %param.28), kind=kOutput, calls=%fused_computation.74 | convolution fusion | flops 539230208 | bytes 4980736 | tf_op jit(solution)/shard_map/pqd,dabh->hpaqb/dot_general | solution.py:273
  121.1 3.7 %collective-permute-done.17 = bf16[128,1,128]{2,0,1:T(8,128)(2,1)S(1)} collective-permute-done((bf16[128,1,128]{2,0,1:T(8,128)(2,1)S(1)}, bf16[128,1,128]{2,0,1:T(8,128)(2,1)S(1)}, u32[]{:S(2)}, u32[]{:S(2)}) %collective-permute-start.17) | collective-permute-done | bytes 32800 | tf_op jit(solution)/shard_map/ppermute | solution.py:21
  125.9 4.1 %collective-permute-start.19 = (bf16[128,18,1]{0,1,2:T(8,128)(2,1)S(1)}, bf16[128,18,1]{0,1,2:T(8,128)(2,1)S(1)}, u32[]{:S(2)}, u32[]{:S(2)}) collective-permute-start(bf16[128,18,1]{0,1,2:T(8,128)(2,1)S(1)} %copy.105), channel_id=1, source_target_pairs={{1,0},{2,1},{3,2},{0,3},{5,4},{6,5},{7,6},{4,7},{9,8},{10,9},{11,1... | collective-permute-start | bytes 13832 | tf_op jit(solution)/shard_map/ppermute | solution.py:26
  132.4 1.8 %maximum_maximum_fusion = (bf16[128,18,129]{2,0,1:T(8,128)(2,1)S(1)}, bf16[128,18,129]{2,0,1:T(8,128)(2,1)S(1)}) fusion(bf16[128,1,128]{2,0,1:T(8,128)(2,1)S(1)} %collective-permute-done.17, bf16[128,16,128]{2,0,1:T(8,128)(2,1)S(1)} %copy.99, bf16[128,1,128]{2,0,1:T(8,128)(2,1)S(1)} %collective-permute-done.16, bf16[128,18,1]{2,0,1:T(8,128)(2,1)S(1)} %copy.103, ...), kind=kLoop, calls=%fused_computation.54 | loop fusion | flops 4755456 | bytes 1787904 | tf_op jit(solution)/shard_map/concatenate | solution.py:27
  137.7 3.4 %collective-permute-done.20 = f32[64]{0:T(128)S(1)} collective-permute-done((f32[64]{0:T(128)S(1)}, f32[64]{0:T(128)S(1)}, u32[]{:S(2)}, u32[]{:S(2)}) %collective-permute-start.20) | collective-permute-done | bytes 288 | tf_op jit(solution)/shard_map/ppermute | solution.py:34
  141.2 2.6 %collective-permute-start.21 = (f32[64]{0:T(128)S(1)}, f32[64]{0:T(128)S(1)}, u32[]{:S(2)}, u32[]{:S(2)}) collective-permute-start(f32[64]{0:T(128)S(1)} %add.311), channel_id=1, source_target_pairs={{0,2},{1,3},{2,0},{3,1},{4,6},{5,7},{6,4},{7,5},{8,10},{9,11},{10,... | collective-permute-start | bytes 776 | tf_op jit(solution)/shard_map/ppermute | solution.py:34
  143.8 1.8 %collective-permute-done.21 = f32[64]{0:T(128)S(1)} collective-permute-done((f32[64]{0:T(128)S(1)}, f32[64]{0:T(128)S(1)}, u32[]{:S(2)}, u32[]{:S(2)}) %collective-permute-start.21) | collective-permute-done | bytes 288 | tf_op jit(solution)/shard_map/ppermute | solution.py:34
  146.7 2.5 %collective-permute-start.23 = (f32[64]{0:T(128)S(1)}, f32[64]{0:T(128)S(1)}, u32[]{:S(2)}, u32[]{:S(2)}) collective-permute-start(f32[64]{0:T(128)S(1)} %add.313), channel_id=1, source_target_pairs={{0,8},{4,12},{8,0},{12,4},{16,24},{20,28},{24,16},{28,20},{1,9},{5... | collective-permute-start | bytes 776 | tf_op jit(solution)/shard_map/ppermute | solution.py:34
  150.8 3.2 %collective-permute-start.24 = (f32[64]{0:T(128)S(1)}, f32[64]{0:T(128)S(1)}, u32[]{:S(2)}, u32[]{:S(2)}) collective-permute-start(f32[64]{0:T(128)S(1)} %add.314), channel_id=1, source_target_pairs={{0,16},{4,20},{8,24},{12,28},{16,0},{20,4},{24,8},{28,12},{1,17},{... | collective-permute-start | bytes 776 | tf_op jit(solution)/shard_map/ppermute | solution.py:34
  (176 shorter events, 51.1 us)
Async XLA Ops:
  0.6 25.5 %copy-start = (bf16[1024,1024]{1,0:T(8,128)(2,1)S(1)}, bf16[1024,1024]{1,0:T(8,128)(2,1)}, u32[]{:S(2)}) copy-start(bf16[1024,1024]{1,0:T(8,128)(2,1)} %param.25) | copy-start | bytes 6291460
  2.1 13.6 %copy-start.14 = (bf16[9,128,69]{1,2,0:T(8,128)(2,1)S(1)}, bf16[9,128,69]{1,2,0:T(8,128)(2,1)}, u32[]{:S(2)}) copy-start(bf16[9,128,69]{1,2,0:T(8,128)(2,1)} %param.19) | copy-start | bytes 476932
  2.2 3.8 %collective-permute-start = (bf16[69,2,128]{0,2,1:T(8,128)(2,1)S(1)}, bf16[69,2,128]{0,2,1:T(8,128)(2,1)S(1)}, u32[]{:S(2)}, u32[]{:S(2)}) collective-permute-start(bf16[69,2,128]{0,2,1:T(8,128)(2,1)S(1)} %get-tuple-element.65), channel_id=1, source_target_pairs={{0,4},{4,8},{8,12},{12,16},{16,20},{20,24},{24,28},{1,5},{5,9},{9,... | collective-permute-start | bytes 105992 | tf_op jit(solution)/shard_map/ppermute | solution.py:20
  4.7 5.3 %collective-permute-start.1 = (bf16[69,2,128]{0,2,1:T(8,128)(2,1)S(1)}, bf16[69,2,128]{0,2,1:T(8,128)(2,1)S(1)}, u32[]{:S(2)}, u32[]{:S(2)}) collective-permute-start(bf16[69,2,128]{0,2,1:T(8,128)(2,1)S(1)} %get-tuple-element.66), channel_id=1, source_target_pairs={{4,0},{8,4},{12,8},{16,12},{20,16},{24,20},{28,24},{5,1},{9,5},{13... | collective-permute-start | bytes 105992 | tf_op jit(solution)/shard_map/ppermute | solution.py:21
  9.9 5.5 %collective-permute-start.2 = (bf16[69,20,2]{0,2,1:T(2,128)(2,1)S(1)}, bf16[69,20,2]{0,2,1:T(2,128)(2,1)S(1)}, u32[]{:S(2)}, u32[]{:S(2)}) collective-permute-start(bf16[69,20,2]{0,2,1:T(2,128)(2,1)S(1)} %get-tuple-element.51), channel_id=1, source_target_pairs={{0,1},{1,2},{2,3},{3,0},{4,5},{5,6},{6,7},{7,4},{8,9},{9,10},{10,1... | collective-permute-start | bytes 16568 | tf_op jit(solution)/shard_map/ppermute | solution.py:25
  11.6 3.9 %collective-permute-start.3 = (bf16[69,20,2]{0,2,1:T(2,128)(2,1)S(1)}, bf16[69,20,2]{0,2,1:T(2,128)(2,1)S(1)}, u32[]{:S(2)}, u32[]{:S(2)}) collective-permute-start(bf16[69,20,2]{0,2,1:T(2,128)(2,1)S(1)} %get-tuple-element.52), channel_id=1, source_target_pairs={{1,0},{2,1},{3,2},{0,3},{5,4},{6,5},{7,6},{4,7},{9,8},{10,9},{11,1... | collective-permute-start | bytes 16568 | tf_op jit(solution)/shard_map/ppermute | solution.py:26
  30.0 9.0 %collective-permute-start.4 = (bf16[3,128,256]{2,1,0:T(8,128)(2,1)S(1)}, bf16[3,128,256]{2,1,0:T(8,128)(2,1)S(1)}, u32[]{:S(2)}, u32[]{:S(2)}) collective-permute-start(bf16[3,128,256]{2,1,0:T(8,128)(2,1)S(1)} %get-tuple-element.50), channel_id=1, source_target_pairs={{0,1},{1,2},{2,3},{3,0},{4,5},{5,6},{6,7},{7,4},{8,9},{9,10},{10,1... | collective-permute-start | bytes 589832 | tf_op jit(solution)/shard_map/ppermute | solution.py:147
  31.4 16.6 %collective-permute-start.5 = (bf16[3,128,256]{2,1,0:T(8,128)(2,1)S(1)}, bf16[3,128,256]{2,1,0:T(8,128)(2,1)S(1)}, u32[]{:S(2)}, u32[]{:S(2)}) collective-permute-start(bf16[3,128,256]{2,1,0:T(8,128)(2,1)S(1)} %get-tuple-element.49), channel_id=1, source_target_pairs={{0,2},{1,3},{2,0},{3,1},{4,6},{5,7},{6,4},{7,5},{8,10},{9,11},{10,... | collective-permute-start | bytes 589832 | tf_op jit(solution)/shard_map/ppermute | solution.py:147
  34.5 13.6 %collective-permute-start.6 = (bf16[3,128,256]{2,1,0:T(8,128)(2,1)S(1)}, bf16[3,128,256]{2,1,0:T(8,128)(2,1)S(1)}, u32[]{:S(2)}, u32[]{:S(2)}) collective-permute-start(bf16[3,128,256]{2,1,0:T(8,128)(2,1)S(1)} %get-tuple-element.48), channel_id=1, source_target_pairs={{0,3},{1,0},{2,1},{3,2},{4,7},{5,4},{6,5},{7,6},{8,11},{9,8},{10,9... | collective-permute-start | bytes 589832 | tf_op jit(solution)/shard_map/ppermute | solution.py:147
  48.1 5.5 %copy-start.17 = (f32[16]{0:T(128)S(1)}, f32[16]{0:T(128)}, u32[]{:S(2)}) copy-start(f32[16]{0:T(128)} %param.27) | copy-start | bytes 196
  48.2 1.8 %collective-permute-start.7 = (bf16[3,512,128]{2,1,0:T(8,128)(2,1)S(1)}, bf16[3,512,128]{2,1,0:T(8,128)(2,1)S(1)}, u32[]{:S(2)}, u32[]{:S(2)}) collective-permute-start(bf16[3,512,128]{2,1,0:T(8,128)(2,1)S(1)} %get-tuple-element.45), channel_id=1, source_target_pairs={{0,4},{4,0},{8,12},{12,8},{16,20},{20,16},{24,28},{28,24},{1,5},{5... | collective-permute-start | bytes 1179656 | tf_op jit(solution)/shard_map/ppermute | solution.py:221
  50.8 15.2 %collective-permute-start.8 = (bf16[2,1024,128]{2,1,0:T(8,128)(2,1)}, bf16[2,1024,128]{2,1,0:T(8,128)(2,1)S(1)}, u32[]{:S(2)}, u32[]{:S(2)}) collective-permute-start(bf16[2,1024,128]{2,1,0:T(8,128)(2,1)} %pad_maximum_fusion.6), channel_id=1, source_target_pairs={{0,8},{4,12},{8,0},{12,4},{16,24},{20,28},{24,16},{28,20},{1,9},{5... | collective-permute-start | bytes 1572872 | tf_op jit(solution)/shard_map/ppermute | solution.py:228
  53.6 21.7 %collective-permute-start.9 = (bf16[2,1024,128]{2,1,0:T(8,128)(2,1)}, bf16[2,1024,128]{2,1,0:T(8,128)(2,1)}, u32[]{:S(2)}, u32[]{:S(2)}) collective-permute-start(bf16[2,1024,128]{2,1,0:T(8,128)(2,1)} %pad_maximum_fusion.6), channel_id=1, source_target_pairs={{0,16},{4,20},{8,24},{12,28},{16,0},{20,4},{24,8},{28,12},{1,17},{... | collective-permute-start | bytes 1572872 | tf_op jit(solution)/shard_map/ppermute | solution.py:229
  73.7 11.7 %collective-permute-start.11 = (bf16[2,512,128]{2,1,0:T(8,128)(2,1)}, bf16[2,512,128]{2,1,0:T(8,128)(2,1)S(1)}, u32[]{:S(2)}, u32[]{:S(2)}) collective-permute-start(bf16[2,512,128]{2,1,0:T(8,128)(2,1)} %slice.376), channel_id=1, source_target_pairs={{0,16},{4,20},{8,24},{12,28},{16,0},{20,4},{24,8},{28,12},{1,17},{... | collective-permute-start | bytes 786440 | tf_op jit(solution)/shard_map/ppermute | solution.py:232
  76.9 8.6 %collective-permute-start.10 = (bf16[2,512,128]{2,1,0:T(8,128)(2,1)}, bf16[2,512,128]{2,1,0:T(8,128)(2,1)}, u32[]{:S(2)}, u32[]{:S(2)}) collective-permute-start(bf16[2,512,128]{2,1,0:T(8,128)(2,1)} %slice.374), channel_id=1, source_target_pairs={{0,8},{4,12},{8,0},{12,4},{16,24},{20,28},{24,16},{28,20},{1,9},{5... | collective-permute-start | bytes 786440 | tf_op jit(solution)/shard_map/ppermute | solution.py:231
  99.5 1.4 collective-permute-start.12
  100.9 13.1 %copy-start.3 = (f32[4,32,1024]{2,1,0:T(8,128)S(1)}, f32[4,32,1024]{2,1,0:T(8,128)}, u32[]{:S(2)}) copy-start(f32[4,32,1024]{2,1,0:T(8,128)} %copy-done.2) | copy-start | bytes 1572868
  100.9 13.1 %copy-start.9 = (bf16[1024,1024]{1,0:T(8,128)(2,1)S(1)}, bf16[1024,1024]{1,0:T(8,128)(2,1)}, u32[]{:S(2)}) copy-start(bf16[1024,1024]{1,0:T(8,128)(2,1)} %param.26) | copy-start | bytes 6291460
  101.0 8.0 %collective-permute-start.13 = (bf16[128,256]{1,0:T(8,128)(2,1)S(1)}, bf16[128,256]{1,0:T(8,128)(2,1)S(1)}, u32[]{:S(2)}, u32[]{:S(2)}) collective-permute-start(bf16[128,256]{1,0:T(8,128)(2,1)S(1)} %get-tuple-element.69), channel_id=1, source_target_pairs={{1,0},{2,1},{3,2},{0,3},{5,4},{6,5},{7,6},{4,7},{9,8},{10,9},{11,1... | collective-permute-start | bytes 196616 | tf_op jit(solution)/shard_map/ppermute | solution.py:155
  106.6 7.1 %collective-permute-start.14 = (bf16[128,256]{1,0:T(8,128)(2,1)S(1)}, bf16[128,256]{1,0:T(8,128)(2,1)S(1)}, u32[]{:S(2)}, u32[]{:S(2)}) collective-permute-start(bf16[128,256]{1,0:T(8,128)(2,1)S(1)} %get-tuple-element.68), channel_id=1, source_target_pairs={{2,0},{3,1},{0,2},{1,3},{6,4},{7,5},{4,6},{5,7},{10,8},{11,9},{8,1... | collective-permute-start | bytes 196616 | tf_op jit(solution)/shard_map/ppermute | solution.py:155
  107.3 6.5 %collective-permute-start.15 = (bf16[128,256]{1,0:T(8,128)(2,1)S(1)}, bf16[128,256]{1,0:T(8,128)(2,1)S(1)}, u32[]{:S(2)}, u32[]{:S(2)}) collective-permute-start(bf16[128,256]{1,0:T(8,128)(2,1)S(1)} %get-tuple-element.67), channel_id=1, source_target_pairs={{3,0},{0,1},{1,2},{2,3},{7,4},{4,5},{5,6},{6,7},{11,8},{8,9},{9,10... | collective-permute-start | bytes 196616 | tf_op jit(solution)/shard_map/ppermute | solution.py:155
  118.5 2.6 %collective-permute-start.16 = (bf16[128,1,128]{2,0,1:T(8,128)(2,1)S(1)}, bf16[128,1,128]{2,0,1:T(8,128)(2,1)S(1)}, u32[]{:S(2)}, u32[]{:S(2)}) collective-permute-start(bf16[128,1,128]{2,0,1:T(8,128)(2,1)S(1)} %get-tuple-element.59), channel_id=1, source_target_pairs={{0,4},{4,8},{8,12},{12,16},{16,20},{20,24},{24,28},{1,5},{5,9},{9,... | collective-permute-start | bytes 98312 | tf_op jit(solution)/shard_map/ppermute | solution.py:20
  119.8 5.1 %collective-permute-start.17 = (bf16[128,1,128]{2,0,1:T(8,128)(2,1)S(1)}, bf16[128,1,128]{2,0,1:T(8,128)(2,1)S(1)}, u32[]{:S(2)}, u32[]{:S(2)}) collective-permute-start(bf16[128,1,128]{2,0,1:T(8,128)(2,1)S(1)} %get-tuple-element.60), channel_id=1, source_target_pairs={{4,0},{8,4},{12,8},{16,12},{20,16},{24,20},{28,24},{5,1},{9,5},{13... | collective-permute-start | bytes 98312 | tf_op jit(solution)/shard_map/ppermute | solution.py:21
  125.5 5.5 %collective-permute-start.18 = (bf16[128,18,1]{0,1,2:T(8,128)(2,1)S(1)}, bf16[128,18,1]{0,1,2:T(8,128)(2,1)S(1)}, u32[]{:S(2)}, u32[]{:S(2)}) collective-permute-start(bf16[128,18,1]{0,1,2:T(8,128)(2,1)S(1)} %copy.102), channel_id=1, source_target_pairs={{0,1},{1,2},{2,3},{3,0},{4,5},{5,6},{6,7},{7,4},{8,9},{9,10},{10,1... | collective-permute-start | bytes 13832 | tf_op jit(solution)/shard_map/ppermute | solution.py:25
  125.9 5.5 %collective-permute-start.19 = (bf16[128,18,1]{0,1,2:T(8,128)(2,1)S(1)}, bf16[128,18,1]{0,1,2:T(8,128)(2,1)S(1)}, u32[]{:S(2)}, u32[]{:S(2)}) collective-permute-start(bf16[128,18,1]{0,1,2:T(8,128)(2,1)S(1)} %copy.105), channel_id=1, source_target_pairs={{1,0},{2,1},{3,2},{0,3},{5,4},{6,5},{7,6},{4,7},{9,8},{10,9},{11,1... | collective-permute-start | bytes 13832 | tf_op jit(solution)/shard_map/ppermute | solution.py:26
  135.9 20.2 %copy-start.1 = (bf16[1024,1024]{1,0:T(8,128)(2,1)S(1)}, bf16[1024,1024]{1,0:T(8,128)(2,1)}, u32[]{:S(2)}) copy-start(bf16[1024,1024]{1,0:T(8,128)(2,1)} %param.25) | copy-start | bytes 6291460
  136.5 19.0 %copy-start.18 = (s32[64]{0:T(128)S(1)}, s32[64]{0:T(128)}, u32[]{:S(2)}) copy-start(s32[64]{0:T(128)} %param.18) | copy-start | bytes 772
  137.6 3.6 %collective-permute-start.20 = (f32[64]{0:T(128)S(1)}, f32[64]{0:T(128)S(1)}, u32[]{:S(2)}, u32[]{:S(2)}) collective-permute-start(f32[64]{0:T(128)S(1)} %fusion.40), channel_id=1, source_target_pairs={{0,1},{1,0},{2,3},{3,2},{4,5},{5,4},{6,7},{7,6},{8,9},{9,8},{10,11... | collective-permute-start | bytes 776 | tf_op jit(solution)/shard_map/ppermute | solution.py:34
  141.2 4.4 %collective-permute-start.21 = (f32[64]{0:T(128)S(1)}, f32[64]{0:T(128)S(1)}, u32[]{:S(2)}, u32[]{:S(2)}) collective-permute-start(f32[64]{0:T(128)S(1)} %add.311), channel_id=1, source_target_pairs={{0,2},{1,3},{2,0},{3,1},{4,6},{5,7},{6,4},{7,5},{8,10},{9,11},{10,... | collective-permute-start | bytes 776 | tf_op jit(solution)/shard_map/ppermute | solution.py:34
  145.6 1.1 collective-permute-start.22
  146.7 4.0 %collective-permute-start.23 = (f32[64]{0:T(128)S(1)}, f32[64]{0:T(128)S(1)}, u32[]{:S(2)}, u32[]{:S(2)}) collective-permute-start(f32[64]{0:T(128)S(1)} %add.313), channel_id=1, source_target_pairs={{0,8},{4,12},{8,0},{12,4},{16,24},{20,28},{24,16},{28,20},{1,9},{5... | collective-permute-start | bytes 776 | tf_op jit(solution)/shard_map/ppermute | solution.py:34
  150.8 4.7 %collective-permute-start.24 = (f32[64]{0:T(128)S(1)}, f32[64]{0:T(128)S(1)}, u32[]{:S(2)}, u32[]{:S(2)}) collective-permute-start(f32[64]{0:T(128)S(1)} %add.314), channel_id=1, source_target_pairs={{0,16},{4,20},{8,24},{12,28},{16,0},{20,4},{24,8},{28,12},{1,17},{... | collective-permute-start | bytes 776 | tf_op jit(solution)/shard_map/ppermute | solution.py:34
  (13 other events, 24.9 us)

commit v14 on v12

--- a/solution.py
+++ b/solution.py
@@ -228,7 +228,7 @@
         middle = key_value.shape[1] // 2
         diagonal_low = lax.ppermute(from_y[:, :middle], "lat", across_x)
         diagonal_high = lax.ppermute(from_x[:, middle:], "lat", across_y)
-        key_groups = [[key_value], [from_x], [from_y], [diagonal_low, diagonal_high]]
+        key_groups = [[key_value], [from_x, from_y], [diagonal_low, diagonal_high]]
     else:
         remote_chunks = [
             lax.ppermute(key_value, "lat", [(i, i ^ (2 * d)) for i in range(lat_size)])

time: 142 us -> 141 us (level)
    pallas_call x4 -> x3, Pallas kernels: 18.1 us -> 17.9 us  [attend_part(): pl.pallas_call(functools.partial(attention_kernel, head_size=head_size, c...]
where the time goes in v14:
time: 141 us
  waiting for transfers between devices  48.2 us (34%)
  starting transfers between devices  39.5 us (28%)
  Pallas kernels  17.9 us (13%)
  matrix products  17.7 us (13%)
  local copies, waits for them, and re-layouts  11.9 us (8%)
  other arithmetic  4.08 us (3%)
    pallas_call x3, Pallas kernels, attend_part(): pl.pallas_call(functools.partial(attention_kernel, head_size=head_size, c...  17.9 us
    ppermute x3, waiting for transfers between devices, exchange_blocks(): lax.ppermute(outgoing, axis, [(i, (i + shift) % size) for i in range(size)])  12.7 us
    dot_general x27, matrix products, convolution_kernel_taps(): jnp.einsum('oc,cyx->oyx', weight[tap_index], window, preferred_element_ty...  10.7 us
    ppermute x5, starting transfers between devices, butterfly_sum(): value = value + lax.ppermute(value, axis, partner)  8.63 us
    ppermute x5, waiting for transfers between devices, butterfly_sum(): value = value + lax.ppermute(value, axis, partner)  8.48 us
    ppermute x1, waiting for transfers between devices, on_device(): from_x = lax.ppermute(key_value, 'lat', across_x)  7.77 us
    ppermute x2, waiting for transfers between devices, halo_padded(): from_below = lax.ppermute(array[:, :width], 'lat', up)  7.65 us
    ppermute x3, waiting for transfers between devices, return_blocks(): lax.ppermute(blocks[shift], axis, [((i + shift) % size, i) for i in range...  6.44 us
  transfers between devices with their start and end apart: 25, of which 16 were waited for; matrix products, arithmetic and copies ran while one was open for 3% of the time, Pallas kernels for 10%

profile of v14, /device:TPU:0, one launch (start us, length us, event | category | flops | bytes accessed | tf_op | source)
XLA Modules:
  0.0 140.6 jit_solution(7516012783023641666)
XLA Ops:
  0.6 1.5 %copy.49 = bf16[69,16,128]{0,2,1:T(8,128)(2,1)S(1)} copy(bf16[69,16,128]{2,1,0:T(8,128)(2,1)} %param.15) | data formatting | bytes 565248 | tf_op args[0]
  2.2 2.5 %collective-permute-start = (bf16[69,2,128]{0,2,1:T(8,128)(2,1)S(1)}, bf16[69,2,128]{0,2,1:T(8,128)(2,1)S(1)}, u32[]{:S(2)}, u32[]{:S(2)}) collective-permute-start(bf16[69,2,128]{0,2,1:T(8,128)(2,1)S(1)} %get-tuple-element.59), channel_id=1, source_target_pairs={{0,4},{4,8},{8,12},{12,16},{16,20},{20,24},{24,28},{1,5},{5,9},{9,... | collective-permute-start | bytes 105992 | tf_op jit(solution)/shard_map/ppermute | solution.py:20
  4.7 1.3 collective-permute-start.1
  6.0 3.9 %collective-permute-done.1 = bf16[69,2,128]{0,2,1:T(8,128)(2,1)S(1)} collective-permute-done((bf16[69,2,128]{0,2,1:T(8,128)(2,1)S(1)}, bf16[69,2,128]{0,2,1:T(8,128)(2,1)S(1)}, u32[]{:S(2)}, u32[]{:S(2)}) %collective-permute-start.1) | collective-permute-done | bytes 35360 | tf_op jit(solution)/shard_map/ppermute | solution.py:21
  9.9 1.6 %collective-permute-start.2 = (bf16[69,20,2]{0,2,1:T(2,128)(2,1)S(1)}, bf16[69,20,2]{0,2,1:T(2,128)(2,1)S(1)}, u32[]{:S(2)}, u32[]{:S(2)}) collective-permute-start(bf16[69,20,2]{0,2,1:T(2,128)(2,1)S(1)} %get-tuple-element.45), channel_id=1, source_target_pairs={{0,1},{1,2},{2,3},{3,0},{4,5},{5,6},{6,7},{7,4},{8,9},{9,10},{10,1... | collective-permute-start | bytes 16568 | tf_op jit(solution)/shard_map/ppermute | solution.py:25
  11.6 2.2 %collective-permute-start.3 = (bf16[69,20,2]{0,2,1:T(2,128)(2,1)S(1)}, bf16[69,20,2]{0,2,1:T(2,128)(2,1)S(1)}, u32[]{:S(2)}, u32[]{:S(2)}) collective-permute-start(bf16[69,20,2]{0,2,1:T(2,128)(2,1)S(1)} %get-tuple-element.46), channel_id=1, source_target_pairs={{1,0},{2,1},{3,2},{0,3},{5,4},{6,5},{7,6},{4,7},{9,8},{10,9},{11,1... | collective-permute-start | bytes 16568 | tf_op jit(solution)/shard_map/ppermute | solution.py:26
  13.8 1.6 %collective-permute-done.2 = bf16[69,20,2]{0,2,1:T(2,128)(2,1)S(1)} collective-permute-done((bf16[69,20,2]{0,2,1:T(2,128)(2,1)S(1)}, bf16[69,20,2]{0,2,1:T(2,128)(2,1)S(1)}, u32[]{:S(2)}, u32[]{:S(2)}) %collective-permute-start.2) | collective-permute-done | bytes 5552 | tf_op jit(solution)/shard_map/ppermute | solution.py:25
  30.0 1.4 collective-permute-start.4
  31.4 3.1 %collective-permute-start.5 = (bf16[3,128,256]{2,1,0:T(8,128)(2,1)S(1)}, bf16[3,128,256]{2,1,0:T(8,128)(2,1)S(1)}, u32[]{:S(2)}, u32[]{:S(2)}) collective-permute-start(bf16[3,128,256]{2,1,0:T(8,128)(2,1)S(1)} %get-tuple-element.43), channel_id=1, source_target_pairs={{0,2},{1,3},{2,0},{3,1},{4,6},{5,7},{6,4},{7,5},{8,10},{9,11},{10,... | collective-permute-start | bytes 589832 | tf_op jit(solution)/shard_map/ppermute | solution.py:145
  35.3 3.6 %collective-permute-done.4 = bf16[3,128,256]{2,1,0:T(8,128)(2,1)S(1)} collective-permute-done((bf16[3,128,256]{2,1,0:T(8,128)(2,1)S(1)}, bf16[3,128,256]{2,1,0:T(8,128)(2,1)S(1)}, u32[]{:S(2)}, u32[]{:S(2)}) %collective-permute-start.4) | collective-permute-done | bytes 196640 | tf_op jit(solution)/shard_map/ppermute | solution.py:145
  39.0 9.1 %collective-permute-done.5 = bf16[3,128,256]{2,1,0:T(8,128)(2,1)S(1)} collective-permute-done((bf16[3,128,256]{2,1,0:T(8,128)(2,1)S(1)}, bf16[3,128,256]{2,1,0:T(8,128)(2,1)S(1)}, u32[]{:S(2)}, u32[]{:S(2)}) %collective-permute-start.5) | collective-permute-done | bytes 196640 | tf_op jit(solution)/shard_map/ppermute | solution.py:145
  48.4 1.6 %collective-permute-done.7 = bf16[3,512,128]{2,1,0:T(8,128)(2,1)S(1)} collective-permute-done((bf16[3,512,128]{2,1,0:T(8,128)(2,1)S(1)}, bf16[3,512,128]{2,1,0:T(8,128)(2,1)S(1)}, u32[]{:S(2)}, u32[]{:S(2)}) %collective-permute-start.7) | collective-permute-done | bytes 393248 | tf_op jit(solution)/shard_map/ppermute | solution.py:219
  50.8 2.8 %collective-permute-start.8 = (bf16[2,1024,128]{2,1,0:T(8,128)(2,1)}, bf16[2,1024,128]{2,1,0:T(8,128)(2,1)S(1)}, u32[]{:S(2)}, u32[]{:S(2)}) collective-permute-start(bf16[2,1024,128]{2,1,0:T(8,128)(2,1)} %pad_maximum_fusion.6), channel_id=1, source_target_pairs={{0,8},{4,12},{8,0},{12,4},{16,24},{20,28},{24,16},{28,20},{1,9},{5... | collective-permute-start | bytes 1572872 | tf_op jit(solution)/shard_map/ppermute | solution.py:226
  53.7 4.5 %shard_map.166 = (f32[1024,128]{1,0:T(8,128)S(1)}, f32[1024,128]{1,0:T(8,128)S(1)}, f32[1024,128]{1,0:T(8,128)S(1)}) custom-call(f32[2]{0:T(128)S(1)} %dynamic-slice_multiply_fusion.scale_ref, bf16[1024,128]{1,0:T(8,128)(2,1)S(1)} %get-tuple-element.37.q_ref, bf16[1024,128]{1,0:T(8,128)(2,1)S(1)} %get-tuple-element.38.refs_0_, ...), custom_call_target="tpu_custom_call" | custom-call | flops 536870912 | bytes 2359296 | tf_op jit(solution)/shard_map/pallas_call | solution.py:111
  58.2 7.8 %collective-permute-done.8 = bf16[2,1024,128]{2,1,0:T(8,128)(2,1)S(1)} collective-permute-done((bf16[2,1024,128]{2,1,0:T(8,128)(2,1)}, bf16[2,1024,128]{2,1,0:T(8,128)(2,1)S(1)}, u32[]{:S(2)}, u32[]{:S(2)}) %collective-permute-start.8) | collective-permute-done | bytes 524320 | tf_op jit(solution)/shard_map/ppermute | solution.py:226
  66.0 1.6 %collective-permute-start.11 = (bf16[2,512,128]{2,1,0:T(8,128)(2,1)S(1)}, bf16[2,512,128]{2,1,0:T(8,128)(2,1)S(1)}, u32[]{:S(2)}, u32[]{:S(2)}) collective-permute-start(bf16[2,512,128]{2,1,0:T(8,128)(2,1)S(1)} %slice.376), channel_id=1, source_target_pairs={{0,16},{4,20},{8,24},{12,28},{16,0},{20,4},{24,8},{28,12},{1,17},{... | collective-permute-start | bytes 786440 | tf_op jit(solution)/shard_map/ppermute | solution.py:230
  70.1 9.0 %shard_map.167 = (f32[1024,128]{1,0:T(8,128)S(1)}, f32[1024,128]{1,0:T(8,128)S(1)}, f32[1024,128]{1,0:T(8,128)S(1)}) custom-call(f32[2]{0:T(128)S(1)} %dynamic-slice_multiply_fusion.scale_ref, bf16[1024,128]{1,0:T(8,128)(2,1)S(1)} %get-tuple-element.37.q_ref, bf16[1024,128]{1,0:T(8,128)(2,1)S(1)} %get-tuple-element.58.refs_0_, ...), custom_call_target="tpu_custom_call" | custom-call | flops 1073741824 | bytes 2883584 | tf_op jit(solution)/shard_map/pallas_call | solution.py:111
  79.2 4.3 %shard_map.168 = (f32[1024,128]{1,0:T(8,128)S(1)}, f32[1024,128]{1,0:T(8,128)S(1)}, f32[1024,128]{1,0:T(8,128)S(1)}) custom-call(f32[2]{0:T(128)S(1)} %dynamic-slice_multiply_fusion.scale_ref, bf16[1024,128]{1,0:T(8,128)(2,1)S(1)} %get-tuple-element.37.q_ref, bf16[512,128]{1,0:T(8,128)(2,1)S(1)} %get-tuple-element.69.refs_0_, ...), custom_call_target="tpu_custom_call" | custom-call | flops 536870912 | bytes 2359296 | tf_op jit(solution)/shard_map/pallas_call | solution.py:111
  84.0 1.3 collective-permute-done.12
  85.5 5.6 %collective-permute-start.13 = (bf16[128,256]{1,0:T(8,128)(2,1)S(1)}, bf16[128,256]{1,0:T(8,128)(2,1)S(1)}, u32[]{:S(2)}, u32[]{:S(2)}) collective-permute-start(bf16[128,256]{1,0:T(8,128)(2,1)S(1)} %get-tuple-element.63), channel_id=1, source_target_pairs={{1,0},{2,1},{3,2},{0,3},{5,4},{6,5},{7,6},{4,7},{9,8},{10,9},{11,1... | collective-permute-start | bytes 196616 | tf_op jit(solution)/shard_map/ppermute | solution.py:153
  91.7 1.8 %collective-permute-done.13 = bf16[128,256]{1,0:T(8,128)(2,1)S(1)} collective-permute-done((bf16[128,256]{1,0:T(8,128)(2,1)S(1)}, bf16[128,256]{1,0:T(8,128)(2,1)S(1)}, u32[]{:S(2)}, u32[]{:S(2)}) %collective-permute-start.13) | collective-permute-done | bytes 65568 | tf_op jit(solution)/shard_map/ppermute | solution.py:153
  93.6 4.6 %collective-permute-done.14 = bf16[128,256]{1,0:T(8,128)(2,1)S(1)} collective-permute-done((bf16[128,256]{1,0:T(8,128)(2,1)S(1)}, bf16[128,256]{1,0:T(8,128)(2,1)S(1)}, u32[]{:S(2)}, u32[]{:S(2)}) %collective-permute-start.14) | collective-permute-done | bytes 65568 | tf_op jit(solution)/shard_map/ppermute | solution.py:153
  99.0 3.4 %fusion.58 = bf16[128,4,4,32,4]{0,3,4,2,1:T(8,128)(2,1)S(1)} fusion(bf16[4,32,1024,1,1]{2,1,4,3,0:T(8,128)(2,1)S(1)} %bitcast.275, bf16[1024,4,4,128]{3,2,1,0:T(4,128)(2,1)} %param.28), kind=kOutput, calls=%fused_computation.74 | convolution fusion | flops 539230208 | bytes 4980736 | tf_op jit(solution)/shard_map/pqd,dabh->hpaqb/dot_general | solution.py:271
  105.6 3.7 %collective-permute-done.17 = bf16[128,1,128]{2,0,1:T(8,128)(2,1)S(1)} collective-permute-done((bf16[128,1,128]{2,0,1:T(8,128)(2,1)S(1)}, bf16[128,1,128]{2,0,1:T(8,128)(2,1)S(1)}, u32[]{:S(2)}, u32[]{:S(2)}) %collective-permute-start.17) | collective-permute-done | bytes 32800 | tf_op jit(solution)/shard_map/ppermute | solution.py:21
  110.3 4.1 %collective-permute-start.19 = (bf16[128,18,1]{0,1,2:T(8,128)(2,1)S(1)}, bf16[128,18,1]{0,1,2:T(8,128)(2,1)S(1)}, u32[]{:S(2)}, u32[]{:S(2)}) collective-permute-start(bf16[128,18,1]{0,1,2:T(8,128)(2,1)S(1)} %copy.65), channel_id=1, source_target_pairs={{1,0},{2,1},{3,2},{0,3},{5,4},{6,5},{7,6},{4,7},{9,8},{10,9},{11,1... | collective-permute-start | bytes 13832 | tf_op jit(solution)/shard_map/ppermute | solution.py:26
  116.9 1.8 %maximum_maximum_fusion = (bf16[128,18,129]{2,0,1:T(8,128)(2,1)S(1)}, bf16[128,18,129]{2,0,1:T(8,128)(2,1)S(1)}) fusion(bf16[128,1,128]{2,0,1:T(8,128)(2,1)S(1)} %collective-permute-done.17, bf16[128,16,128]{2,0,1:T(8,128)(2,1)S(1)} %copy.59, bf16[128,1,128]{2,0,1:T(8,128)(2,1)S(1)} %collective-permute-done.16, bf16[128,18,1]{2,0,1:T(8,128)(2,1)S(1)} %copy.63, ...), kind=kLoop, calls=%fused_computation.54 | loop fusion | flops 4755456 | bytes 1787904 | tf_op jit(solution)/shard_map/concatenate | solution.py:27
  122.4 3.2 %collective-permute-done.20 = f32[64]{0:T(128)S(1)} collective-permute-done((f32[64]{0:T(128)S(1)}, f32[64]{0:T(128)S(1)}, u32[]{:S(2)}, u32[]{:S(2)}) %collective-permute-start.20) | collective-permute-done | bytes 288 | tf_op jit(solution)/shard_map/ppermute | solution.py:34
  125.6 2.6 %collective-permute-start.21 = (f32[64]{0:T(128)S(1)}, f32[64]{0:T(128)S(1)}, u32[]{:S(2)}, u32[]{:S(2)}) collective-permute-start(f32[64]{0:T(128)S(1)} %add.303), channel_id=1, source_target_pairs={{0,2},{1,3},{2,0},{3,1},{4,6},{5,7},{6,4},{7,5},{8,10},{9,11},{10,... | collective-permute-start | bytes 776 | tf_op jit(solution)/shard_map/ppermute | solution.py:34
  128.2 1.9 %collective-permute-done.21 = f32[64]{0:T(128)S(1)} collective-permute-done((f32[64]{0:T(128)S(1)}, f32[64]{0:T(128)S(1)}, u32[]{:S(2)}, u32[]{:S(2)}) %collective-permute-start.21) | collective-permute-done | bytes 288 | tf_op jit(solution)/shard_map/ppermute | solution.py:34
  131.2 2.5 %collective-permute-start.23 = (f32[64]{0:T(128)S(1)}, f32[64]{0:T(128)S(1)}, u32[]{:S(2)}, u32[]{:S(2)}) collective-permute-start(f32[64]{0:T(128)S(1)} %add.305), channel_id=1, source_target_pairs={{0,8},{4,12},{8,0},{12,4},{16,24},{20,28},{24,16},{28,20},{1,9},{5... | collective-permute-start | bytes 776 | tf_op jit(solution)/shard_map/ppermute | solution.py:34
  133.7 1.5 %collective-permute-done.23 = f32[64]{0:T(128)S(1)} collective-permute-done((f32[64]{0:T(128)S(1)}, f32[64]{0:T(128)S(1)}, u32[]{:S(2)}, u32[]{:S(2)}) %collective-permute-start.23) | collective-permute-done | bytes 288 | tf_op jit(solution)/shard_map/ppermute | solution.py:34
  135.2 3.2 %collective-permute-start.24 = (f32[64]{0:T(128)S(1)}, f32[64]{0:T(128)S(1)}, u32[]{:S(2)}, u32[]{:S(2)}) collective-permute-start(f32[64]{0:T(128)S(1)} %add.306), channel_id=1, source_target_pairs={{0,16},{4,20},{8,24},{12,28},{16,0},{20,4},{24,8},{28,12},{1,17},{... | collective-permute-start | bytes 776 | tf_op jit(solution)/shard_map/ppermute | solution.py:34
  (143 shorter events, 34.6 us)
Async XLA Ops:
  0.6 25.5 %copy-start = (bf16[1024,1024]{1,0:T(8,128)(2,1)S(1)}, bf16[1024,1024]{1,0:T(8,128)(2,1)}, u32[]{:S(2)}) copy-start(bf16[1024,1024]{1,0:T(8,128)(2,1)} %param.25) | copy-start | bytes 6291460
  2.1 13.6 %copy-start.10 = (bf16[9,128,69]{1,2,0:T(8,128)(2,1)S(1)}, bf16[9,128,69]{1,2,0:T(8,128)(2,1)}, u32[]{:S(2)}) copy-start(bf16[9,128,69]{1,2,0:T(8,128)(2,1)} %param.19) | copy-start | bytes 476932
  2.2 3.8 %collective-permute-start = (bf16[69,2,128]{0,2,1:T(8,128)(2,1)S(1)}, bf16[69,2,128]{0,2,1:T(8,128)(2,1)S(1)}, u32[]{:S(2)}, u32[]{:S(2)}) collective-permute-start(bf16[69,2,128]{0,2,1:T(8,128)(2,1)S(1)} %get-tuple-element.59), channel_id=1, source_target_pairs={{0,4},{4,8},{8,12},{12,16},{16,20},{20,24},{24,28},{1,5},{5,9},{9,... | collective-permute-start | bytes 105992 | tf_op jit(solution)/shard_map/ppermute | solution.py:20
  4.7 5.3 %collective-permute-start.1 = (bf16[69,2,128]{0,2,1:T(8,128)(2,1)S(1)}, bf16[69,2,128]{0,2,1:T(8,128)(2,1)S(1)}, u32[]{:S(2)}, u32[]{:S(2)}) collective-permute-start(bf16[69,2,128]{0,2,1:T(8,128)(2,1)S(1)} %get-tuple-element.60), channel_id=1, source_target_pairs={{4,0},{8,4},{12,8},{16,12},{20,16},{24,20},{28,24},{5,1},{9,5},{13... | collective-permute-start | bytes 105992 | tf_op jit(solution)/shard_map/ppermute | solution.py:21
  9.9 5.5 %collective-permute-start.2 = (bf16[69,20,2]{0,2,1:T(2,128)(2,1)S(1)}, bf16[69,20,2]{0,2,1:T(2,128)(2,1)S(1)}, u32[]{:S(2)}, u32[]{:S(2)}) collective-permute-start(bf16[69,20,2]{0,2,1:T(2,128)(2,1)S(1)} %get-tuple-element.45), channel_id=1, source_target_pairs={{0,1},{1,2},{2,3},{3,0},{4,5},{5,6},{6,7},{7,4},{8,9},{9,10},{10,1... | collective-permute-start | bytes 16568 | tf_op jit(solution)/shard_map/ppermute | solution.py:25
  11.6 3.9 %collective-permute-start.3 = (bf16[69,20,2]{0,2,1:T(2,128)(2,1)S(1)}, bf16[69,20,2]{0,2,1:T(2,128)(2,1)S(1)}, u32[]{:S(2)}, u32[]{:S(2)}) collective-permute-start(bf16[69,20,2]{0,2,1:T(2,128)(2,1)S(1)} %get-tuple-element.46), channel_id=1, source_target_pairs={{1,0},{2,1},{3,2},{0,3},{5,4},{6,5},{7,6},{4,7},{9,8},{10,9},{11,1... | collective-permute-start | bytes 16568 | tf_op jit(solution)/shard_map/ppermute | solution.py:26
  30.0 9.0 %collective-permute-start.4 = (bf16[3,128,256]{2,1,0:T(8,128)(2,1)S(1)}, bf16[3,128,256]{2,1,0:T(8,128)(2,1)S(1)}, u32[]{:S(2)}, u32[]{:S(2)}) collective-permute-start(bf16[3,128,256]{2,1,0:T(8,128)(2,1)S(1)} %get-tuple-element.44), channel_id=1, source_target_pairs={{0,1},{1,2},{2,3},{3,0},{4,5},{5,6},{6,7},{7,4},{8,9},{9,10},{10,1... | collective-permute-start | bytes 589832 | tf_op jit(solution)/shard_map/ppermute | solution.py:145
  31.4 16.6 %collective-permute-start.5 = (bf16[3,128,256]{2,1,0:T(8,128)(2,1)S(1)}, bf16[3,128,256]{2,1,0:T(8,128)(2,1)S(1)}, u32[]{:S(2)}, u32[]{:S(2)}) collective-permute-start(bf16[3,128,256]{2,1,0:T(8,128)(2,1)S(1)} %get-tuple-element.43), channel_id=1, source_target_pairs={{0,2},{1,3},{2,0},{3,1},{4,6},{5,7},{6,4},{7,5},{8,10},{9,11},{10,... | collective-permute-start | bytes 589832 | tf_op jit(solution)/shard_map/ppermute | solution.py:145
  34.5 13.6 %collective-permute-start.6 = (bf16[3,128,256]{2,1,0:T(8,128)(2,1)S(1)}, bf16[3,128,256]{2,1,0:T(8,128)(2,1)S(1)}, u32[]{:S(2)}, u32[]{:S(2)}) collective-permute-start(bf16[3,128,256]{2,1,0:T(8,128)(2,1)S(1)} %get-tuple-element.42), channel_id=1, source_target_pairs={{0,3},{1,0},{2,1},{3,2},{4,7},{5,4},{6,5},{7,6},{8,11},{9,8},{10,9... | collective-permute-start | bytes 589832 | tf_op jit(solution)/shard_map/ppermute | solution.py:145
  48.1 5.5 %copy-start.13 = (f32[16]{0:T(128)S(1)}, f32[16]{0:T(128)}, u32[]{:S(2)}) copy-start(f32[16]{0:T(128)} %param.27) | copy-start | bytes 196
  48.2 1.8 %collective-permute-start.7 = (bf16[3,512,128]{2,1,0:T(8,128)(2,1)S(1)}, bf16[3,512,128]{2,1,0:T(8,128)(2,1)S(1)}, u32[]{:S(2)}, u32[]{:S(2)}) collective-permute-start(bf16[3,512,128]{2,1,0:T(8,128)(2,1)S(1)} %get-tuple-element.39), channel_id=1, source_target_pairs={{0,4},{4,0},{8,12},{12,8},{16,20},{20,16},{24,28},{28,24},{1,5},{5... | collective-permute-start | bytes 1179656 | tf_op jit(solution)/shard_map/ppermute | solution.py:219
  50.8 15.2 %collective-permute-start.8 = (bf16[2,1024,128]{2,1,0:T(8,128)(2,1)}, bf16[2,1024,128]{2,1,0:T(8,128)(2,1)S(1)}, u32[]{:S(2)}, u32[]{:S(2)}) collective-permute-start(bf16[2,1024,128]{2,1,0:T(8,128)(2,1)} %pad_maximum_fusion.6), channel_id=1, source_target_pairs={{0,8},{4,12},{8,0},{12,4},{16,24},{20,28},{24,16},{28,20},{1,9},{5... | collective-permute-start | bytes 1572872 | tf_op jit(solution)/shard_map/ppermute | solution.py:226
  53.6 14.1 %collective-permute-start.9 = (bf16[2,1024,128]{2,1,0:T(8,128)(2,1)}, bf16[2,1024,128]{2,1,0:T(8,128)(2,1)}, u32[]{:S(2)}, u32[]{:S(2)}) collective-permute-start(bf16[2,1024,128]{2,1,0:T(8,128)(2,1)} %pad_maximum_fusion.6), channel_id=1, source_target_pairs={{0,16},{4,20},{8,24},{12,28},{16,0},{20,4},{24,8},{28,12},{1,17},{... | collective-permute-start | bytes 1572872 | tf_op jit(solution)/shard_map/ppermute | solution.py:227
  66.0 13.0 %collective-permute-start.11 = (bf16[2,512,128]{2,1,0:T(8,128)(2,1)S(1)}, bf16[2,512,128]{2,1,0:T(8,128)(2,1)S(1)}, u32[]{:S(2)}, u32[]{:S(2)}) collective-permute-start(bf16[2,512,128]{2,1,0:T(8,128)(2,1)S(1)} %slice.376), channel_id=1, source_target_pairs={{0,16},{4,20},{8,24},{12,28},{16,0},{20,4},{24,8},{28,12},{1,17},{... | collective-permute-start | bytes 786440 | tf_op jit(solution)/shard_map/ppermute | solution.py:230
  68.6 10.5 %collective-permute-start.10 = (bf16[2,512,128]{2,1,0:T(8,128)(2,1)S(1)}, bf16[2,512,128]{2,1,0:T(8,128)(2,1)S(1)}, u32[]{:S(2)}, u32[]{:S(2)}) collective-permute-start(bf16[2,512,128]{2,1,0:T(8,128)(2,1)S(1)} %slice.374), channel_id=1, source_target_pairs={{0,8},{4,12},{8,0},{12,4},{16,24},{20,28},{24,16},{28,20},{1,9},{5... | collective-permute-start | bytes 786440 | tf_op jit(solution)/shard_map/ppermute | solution.py:229
  84.0 1.4 %collective-permute-start.12 = (bf16[512,128]{1,0:T(8,128)(2,1)S(1)}, bf16[512,128]{1,0:T(8,128)(2,1)S(1)}, u32[]{:S(2)}, u32[]{:S(2)}) collective-permute-start(bf16[512,128]{1,0:T(8,128)(2,1)S(1)} %get-tuple-element.65), channel_id=1, source_target_pairs={{0,4},{4,0},{8,12},{12,8},{16,20},{20,16},{24,28},{28,24},{1,5},{5... | collective-permute-start | bytes 393224 | tf_op jit(solution)/shard_map/ppermute | solution.py:255
  85.4 13.1 %copy-start.5 = (bf16[1024,1024]{1,0:T(8,128)(2,1)S(1)}, bf16[1024,1024]{1,0:T(8,128)(2,1)}, u32[]{:S(2)}) copy-start(bf16[1024,1024]{1,0:T(8,128)(2,1)} %param.26) | copy-start | bytes 6291460
  85.5 8.1 %collective-permute-start.13 = (bf16[128,256]{1,0:T(8,128)(2,1)S(1)}, bf16[128,256]{1,0:T(8,128)(2,1)S(1)}, u32[]{:S(2)}, u32[]{:S(2)}) collective-permute-start(bf16[128,256]{1,0:T(8,128)(2,1)S(1)} %get-tuple-element.63), channel_id=1, source_target_pairs={{1,0},{2,1},{3,2},{0,3},{5,4},{6,5},{7,6},{4,7},{9,8},{10,9},{11,1... | collective-permute-start | bytes 196616 | tf_op jit(solution)/shard_map/ppermute | solution.py:153
  91.1 7.1 %collective-permute-start.14 = (bf16[128,256]{1,0:T(8,128)(2,1)S(1)}, bf16[128,256]{1,0:T(8,128)(2,1)S(1)}, u32[]{:S(2)}, u32[]{:S(2)}) collective-permute-start(bf16[128,256]{1,0:T(8,128)(2,1)S(1)} %get-tuple-element.62), channel_id=1, source_target_pairs={{2,0},{3,1},{0,2},{1,3},{6,4},{7,5},{4,6},{5,7},{10,8},{11,9},{8,1... | collective-permute-start | bytes 196616 | tf_op jit(solution)/shard_map/ppermute | solution.py:153
  91.7 6.5 %collective-permute-start.15 = (bf16[128,256]{1,0:T(8,128)(2,1)S(1)}, bf16[128,256]{1,0:T(8,128)(2,1)S(1)}, u32[]{:S(2)}, u32[]{:S(2)}) collective-permute-start(bf16[128,256]{1,0:T(8,128)(2,1)S(1)} %get-tuple-element.61), channel_id=1, source_target_pairs={{3,0},{0,1},{1,2},{2,3},{7,4},{4,5},{5,6},{6,7},{11,8},{8,9},{9,10... | collective-permute-start | bytes 196616 | tf_op jit(solution)/shard_map/ppermute | solution.py:153
  102.9 2.6 %collective-permute-start.16 = (bf16[128,1,128]{2,0,1:T(8,128)(2,1)S(1)}, bf16[128,1,128]{2,0,1:T(8,128)(2,1)S(1)}, u32[]{:S(2)}, u32[]{:S(2)}) collective-permute-start(bf16[128,1,128]{2,0,1:T(8,128)(2,1)S(1)} %get-tuple-element.53), channel_id=1, source_target_pairs={{0,4},{4,8},{8,12},{12,16},{16,20},{20,24},{24,28},{1,5},{5,9},{9,... | collective-permute-start | bytes 98312 | tf_op jit(solution)/shard_map/ppermute | solution.py:20
  104.2 5.1 %collective-permute-start.17 = (bf16[128,1,128]{2,0,1:T(8,128)(2,1)S(1)}, bf16[128,1,128]{2,0,1:T(8,128)(2,1)S(1)}, u32[]{:S(2)}, u32[]{:S(2)}) collective-permute-start(bf16[128,1,128]{2,0,1:T(8,128)(2,1)S(1)} %get-tuple-element.54), channel_id=1, source_target_pairs={{4,0},{8,4},{12,8},{16,12},{20,16},{24,20},{28,24},{5,1},{9,5},{13... | collective-permute-start | bytes 98312 | tf_op jit(solution)/shard_map/ppermute | solution.py:21
  109.4 5.0 %copy-start.9 = (bf16[9,69,128]{2,1,0:T(8,128)(2,1)S(1)}, bf16[9,69,128]{2,1,0:T(8,128)(2,1)}, u32[]{:S(2)}) copy-start(bf16[9,69,128]{2,1,0:T(8,128)(2,1)} %param.29) | copy-start | bytes 476932
  110.0 5.5 %collective-permute-start.18 = (bf16[128,18,1]{0,1,2:T(8,128)(2,1)S(1)}, bf16[128,18,1]{0,1,2:T(8,128)(2,1)S(1)}, u32[]{:S(2)}, u32[]{:S(2)}) collective-permute-start(bf16[128,18,1]{0,1,2:T(8,128)(2,1)S(1)} %copy.62), channel_id=1, source_target_pairs={{0,1},{1,2},{2,3},{3,0},{4,5},{5,6},{6,7},{7,4},{8,9},{9,10},{10,1... | collective-permute-start | bytes 13832 | tf_op jit(solution)/shard_map/ppermute | solution.py:25
  110.3 5.5 %collective-permute-start.19 = (bf16[128,18,1]{0,1,2:T(8,128)(2,1)S(1)}, bf16[128,18,1]{0,1,2:T(8,128)(2,1)S(1)}, u32[]{:S(2)}, u32[]{:S(2)}) collective-permute-start(bf16[128,18,1]{0,1,2:T(8,128)(2,1)S(1)} %copy.65), channel_id=1, source_target_pairs={{1,0},{2,1},{3,2},{0,3},{5,4},{6,5},{7,6},{4,7},{9,8},{10,9},{11,1... | collective-permute-start | bytes 13832 | tf_op jit(solution)/shard_map/ppermute | solution.py:26
  120.4 20.2 %copy-start.1 = (bf16[1024,1024]{1,0:T(8,128)(2,1)S(1)}, bf16[1024,1024]{1,0:T(8,128)(2,1)}, u32[]{:S(2)}) copy-start(bf16[1024,1024]{1,0:T(8,128)(2,1)} %param.25) | copy-start | bytes 6291460
  121.0 19.0 %copy-start.14 = (s32[64]{0:T(128)S(1)}, s32[64]{0:T(128)}, u32[]{:S(2)}) copy-start(s32[64]{0:T(128)} %param.18) | copy-start | bytes 772
  122.1 3.6 %collective-permute-start.20 = (f32[64]{0:T(128)S(1)}, f32[64]{0:T(128)S(1)}, u32[]{:S(2)}, u32[]{:S(2)}) collective-permute-start(f32[64]{0:T(128)S(1)} %fusion.40), channel_id=1, source_target_pairs={{0,1},{1,0},{2,3},{3,2},{4,5},{5,4},{6,7},{7,6},{8,9},{9,8},{10,11... | collective-permute-start | bytes 776 | tf_op jit(solution)/shard_map/ppermute | solution.py:34
  125.6 4.4 %collective-permute-start.21 = (f32[64]{0:T(128)S(1)}, f32[64]{0:T(128)S(1)}, u32[]{:S(2)}, u32[]{:S(2)}) collective-permute-start(f32[64]{0:T(128)S(1)} %add.303), channel_id=1, source_target_pairs={{0,2},{1,3},{2,0},{3,1},{4,6},{5,7},{6,4},{7,5},{8,10},{9,11},{10,... | collective-permute-start | bytes 776 | tf_op jit(solution)/shard_map/ppermute | solution.py:34
  130.1 1.1 collective-permute-start.22
  131.2 4.0 %collective-permute-start.23 = (f32[64]{0:T(128)S(1)}, f32[64]{0:T(128)S(1)}, u32[]{:S(2)}, u32[]{:S(2)}) collective-permute-start(f32[64]{0:T(128)S(1)} %add.305), channel_id=1, source_target_pairs={{0,8},{4,12},{8,0},{12,4},{16,24},{20,28},{24,16},{28,20},{1,9},{5... | collective-permute-start | bytes 776 | tf_op jit(solution)/shard_map/ppermute | solution.py:34
  135.2 4.7 %collective-permute-start.24 = (f32[64]{0:T(128)S(1)}, f32[64]{0:T(128)S(1)}, u32[]{:S(2)}, u32[]{:S(2)}) collective-permute-start(f32[64]{0:T(128)S(1)} %add.306), channel_id=1, source_target_pairs={{0,16},{4,20},{8,24},{12,28},{16,0},{20,4},{24,8},{28,12},{1,17},{... | collective-permute-start | bytes 776 | tf_op jit(solution)/shard_map/ppermute | solution.py:34
  (9 other events, 10.9 us)

commit v15 on v14

--- a/solution.py
+++ b/solution.py
@@ -96,20 +96,21 @@
     l_ref[...] = sums
 
 
-def attend_part(queries, key_chunks, value_chunks, scales, head_size):
+def attend_part(queries, chunks, scales, head_size):
     query_count, width = queries.shape
-    key_count = sum(chunk.shape[0] for chunk in key_chunks)
+    key_count = sum(chunk.shape[1] for chunk in chunks)
     cap = 1 << (max(8, (1 << 20) // key_count).bit_length() - 1)
     block = math.gcd(query_count, cap)
     heads = width // head_size
     part = jax.ShapeDtypeStruct((query_count, width), jnp.float32)
     part_spec = pl.BlockSpec((block, width), lambda i: (i, 0))
     chunk_specs = [
-        pl.BlockSpec((chunk.shape[0], width), lambda i: (0, 0))
-        for chunk in list(key_chunks) + list(value_chunks)
+        pl.BlockSpec((None, chunk.shape[1], width), lambda i, part=part: (part, 0, 0))
+        for part in (0, 1)
+        for chunk in chunks
     ]
     return pl.pallas_call(
-        functools.partial(attention_kernel, head_size=head_size, chunk_count=len(key_chunks)),
+        functools.partial(attention_kernel, head_size=head_size, chunk_count=len(chunks)),
         out_shape=(part, part, part),
         grid=(query_count // block,),
         in_specs=[
@@ -125,7 +126,7 @@
             bytes_accessed=2 * (query_count * width + 2 * key_count * width)
             + 12 * query_count * width,
         ),
-    )(scales, queries, *key_chunks, *value_chunks)
+    )(scales, queries, *chunks, *chunks)
 
 
 def merge_parts(parts):
@@ -239,13 +240,7 @@
     head_first = (lax.axis_index("lon") * 2 + core) * local_heads
     scales = lax.dynamic_slice_in_dim(head_scale, head_first, local_heads) / math.sqrt(head_size)
     parts = [
-        attend_part(
-            pair_queries,
-            [chunk[0] for chunk in group],
-            [chunk[1] for chunk in group],
-            scales,
-            head_size,
-        )
+        attend_part(pair_queries, group, scales, head_size)
         for group in key_groups
         if group
     ]

time: 141 us -> 142 us (level)
  waiting for transfers between devices: 48.2 us -> 52 us
  local copies, waits for them, and re-layouts: 11.9 us -> 9.78 us
    ppermute x1, waiting for transfers between devices: 0.01 us -> 11.9 us  [on_device(): from_y = lax.ppermute(key_value, 'lat', across_y)]
    ppermute x1, waiting for transfers between devices: 7.77 us -> 0.01 us  [on_device(): from_x = lax.ppermute(key_value, 'lat', across_x)]
    ppermute x1, starting transfers between devices: 0.01 us -> 2.63 us  [on_device(): from_y = lax.ppermute(key_value, 'lat', across_y)]
    ppermute x1, starting transfers between devices: 2.77 us -> 0.29 us  [on_device(): from_x = lax.ppermute(key_value, 'lat', across_x)]
    ppermute x1, starting transfers between devices: 0.35 us -> 2.02 us  [on_device(): diagonal_low = lax.ppermute(from_y[:, :middle], 'lat', across_x)]
  transfers between devices with their start and end apart: 25 -> 25, of which waited for: 16 -> 16; matrix products, arithmetic and copies ran while one was open for 3% -> 1% of each run, Pallas kernels for 10% -> 9%
where the time goes in v15:
time: 142 us
  waiting for transfers between devices  52 us (37%)
  starting transfers between devices  40.1 us (28%)
  Pallas kernels  17.8 us (13%)
  matrix products  17.7 us (12%)
  local copies, waits for them, and re-layouts  9.78 us (7%)
  other arithmetic  3.26 us (2%)
    pallas_call x3, Pallas kernels, attend_part(): pl.pallas_call(functools.partial(attention_kernel, head_size=head_size, c...  17.8 us
    ppermute x3, waiting for transfers between devices, exchange_blocks(): lax.ppermute(outgoing, axis, [(i, (i + shift) % size) for i in range(size)])  12.7 us
    ppermute x1, waiting for transfers between devices, on_device(): from_y = lax.ppermute(key_value, 'lat', across_y)  11.9 us
    dot_general x27, matrix products, convolution_kernel_taps(): jnp.einsum('oc,cyx->oyx', weight[tap_index], window, preferred_element_ty...  10.8 us
    ppermute x5, starting transfers between devices, butterfly_sum(): value = value + lax.ppermute(value, axis, partner)  8.62 us
    ppermute x5, waiting for transfers between devices, butterfly_sum(): value = value + lax.ppermute(value, axis, partner)  8.54 us
    ppermute x2, waiting for transfers between devices, halo_padded(): from_below = lax.ppermute(array[:, :width], 'lat', up)  7.33 us
    ppermute x3, waiting for transfers between devices, return_blocks(): lax.ppermute(blocks[shift], axis, [((i + shift) % size, i) for i in range...  6.44 us
  transfers between devices with their start and end apart: 25, of which 16 were waited for; matrix products, arithmetic and copies ran while one was open for 1% of the time, Pallas kernels for 9%

profile of v15, /device:TPU:0, one launch (start us, length us, event | category | flops | bytes accessed | tf_op | source)
XLA Modules:
  0.0 142.1 jit_solution(17041723938637866030)
XLA Ops:
  0.6 1.5 %copy.49 = bf16[69,16,128]{0,2,1:T(8,128)(2,1)S(1)} copy(bf16[69,16,128]{2,1,0:T(8,128)(2,1)} %param.15) | data formatting | bytes 565248 | tf_op args[0]
  2.2 2.5 %collective-permute-start = (bf16[69,2,128]{0,2,1:T(8,128)(2,1)S(1)}, bf16[69,2,128]{0,2,1:T(8,128)(2,1)S(1)}, u32[]{:S(2)}, u32[]{:S(2)}) collective-permute-start(bf16[69,2,128]{0,2,1:T(8,128)(2,1)S(1)} %get-tuple-element.52), channel_id=1, source_target_pairs={{0,4},{4,8},{8,12},{12,16},{16,20},{20,24},{24,28},{1,5},{5,9},{9,... | collective-permute-start | bytes 105992 | tf_op jit(solution)/shard_map/ppermute | solution.py:20
  4.7 1.3 collective-permute-start.1
  6.0 3.9 %collective-permute-done.1 = bf16[69,2,128]{0,2,1:T(8,128)(2,1)S(1)} collective-permute-done((bf16[69,2,128]{0,2,1:T(8,128)(2,1)S(1)}, bf16[69,2,128]{0,2,1:T(8,128)(2,1)S(1)}, u32[]{:S(2)}, u32[]{:S(2)}) %collective-permute-start.1) | collective-permute-done | bytes 35360 | tf_op jit(solution)/shard_map/ppermute | solution.py:21
  9.9 1.6 %collective-permute-start.2 = (bf16[69,20,2]{0,2,1:T(2,128)(2,1)S(1)}, bf16[69,20,2]{0,2,1:T(2,128)(2,1)S(1)}, u32[]{:S(2)}, u32[]{:S(2)}) collective-permute-start(bf16[69,20,2]{0,2,1:T(2,128)(2,1)S(1)} %get-tuple-element.42), channel_id=1, source_target_pairs={{0,1},{1,2},{2,3},{3,0},{4,5},{5,6},{6,7},{7,4},{8,9},{9,10},{10,1... | collective-permute-start | bytes 16568 | tf_op jit(solution)/shard_map/ppermute | solution.py:25
  11.6 2.2 %collective-permute-start.3 = (bf16[69,20,2]{0,2,1:T(2,128)(2,1)S(1)}, bf16[69,20,2]{0,2,1:T(2,128)(2,1)S(1)}, u32[]{:S(2)}, u32[]{:S(2)}) collective-permute-start(bf16[69,20,2]{0,2,1:T(2,128)(2,1)S(1)} %get-tuple-element.43), channel_id=1, source_target_pairs={{1,0},{2,1},{3,2},{0,3},{5,4},{6,5},{7,6},{4,7},{9,8},{10,9},{11,1... | collective-permute-start | bytes 16568 | tf_op jit(solution)/shard_map/ppermute | solution.py:26
  13.8 1.6 %collective-permute-done.2 = bf16[69,20,2]{0,2,1:T(2,128)(2,1)S(1)} collective-permute-done((bf16[69,20,2]{0,2,1:T(2,128)(2,1)S(1)}, bf16[69,20,2]{0,2,1:T(2,128)(2,1)S(1)}, u32[]{:S(2)}, u32[]{:S(2)}) %collective-permute-start.2) | collective-permute-done | bytes 5552 | tf_op jit(solution)/shard_map/ppermute | solution.py:25
  30.0 1.4 collective-permute-start.4
  31.4 3.1 %collective-permute-start.5 = (bf16[3,128,256]{2,1,0:T(8,128)(2,1)S(1)}, bf16[3,128,256]{2,1,0:T(8,128)(2,1)S(1)}, u32[]{:S(2)}, u32[]{:S(2)}) collective-permute-start(bf16[3,128,256]{2,1,0:T(8,128)(2,1)S(1)} %get-tuple-element.40), channel_id=1, source_target_pairs={{0,2},{1,3},{2,0},{3,1},{4,6},{5,7},{6,4},{7,5},{8,10},{9,11},{10,... | collective-permute-start | bytes 589832 | tf_op jit(solution)/shard_map/ppermute | solution.py:146
  35.3 3.6 %collective-permute-done.4 = bf16[3,128,256]{2,1,0:T(8,128)(2,1)S(1)} collective-permute-done((bf16[3,128,256]{2,1,0:T(8,128)(2,1)S(1)}, bf16[3,128,256]{2,1,0:T(8,128)(2,1)S(1)}, u32[]{:S(2)}, u32[]{:S(2)}) %collective-permute-start.4) | collective-permute-done | bytes 196640 | tf_op jit(solution)/shard_map/ppermute | solution.py:146
  39.0 9.1 %collective-permute-done.5 = bf16[3,128,256]{2,1,0:T(8,128)(2,1)S(1)} collective-permute-done((bf16[3,128,256]{2,1,0:T(8,128)(2,1)S(1)}, bf16[3,128,256]{2,1,0:T(8,128)(2,1)S(1)}, u32[]{:S(2)}, u32[]{:S(2)}) %collective-permute-start.5) | collective-permute-done | bytes 196640 | tf_op jit(solution)/shard_map/ppermute | solution.py:146
  48.4 1.6 %collective-permute-done.7 = bf16[3,512,128]{2,1,0:T(8,128)(2,1)S(1)} collective-permute-done((bf16[3,512,128]{2,1,0:T(8,128)(2,1)S(1)}, bf16[3,512,128]{2,1,0:T(8,128)(2,1)S(1)}, u32[]{:S(2)}, u32[]{:S(2)}) %collective-permute-start.7) | collective-permute-done | bytes 393248 | tf_op jit(solution)/shard_map/ppermute | solution.py:220
  50.0 2.6 %collective-permute-start.9 = (bf16[2,1024,128]{2,1,0:T(8,128)(2,1)S(1)}, bf16[2,1024,128]{2,1,0:T(8,128)(2,1)S(1)}, u32[]{:S(2)}, u32[]{:S(2)}) collective-permute-start(bf16[2,1024,128]{2,1,0:T(8,128)(2,1)S(1)} %pad_maximum_fusion.6.refs_0_.refs_1_), channel_id=1, source_target_pairs={{0,16},{4,20},{8,24},{12,28},{16,0},{20,4},{24,8},{28,12},{1,17},{... | collective-permute-start | bytes 1572872 | tf_op jit(solution)/shard_map/ppermute | solution.py:228
  53.0 11.9 %collective-permute-done.9.refs_1_.refs_3_ = bf16[2,1024,128]{2,1,0:T(8,128)(2,1)S(1)} collective-permute-done((bf16[2,1024,128]{2,1,0:T(8,128)(2,1)S(1)}, bf16[2,1024,128]{2,1,0:T(8,128)(2,1)S(1)}, u32[]{:S(2)}, u32[]{:S(2)}) %collective-permute-start.9) | collective-permute-done | bytes 524320 | tf_op jit(solution)/shard_map/ppermute | solution.py:228
  64.9 2.0 %collective-permute-start.10 = (bf16[2,512,128]{2,1,0:T(8,128)(2,1)S(1)}, bf16[2,512,128]{2,1,0:T(8,128)(2,1)S(1)}, u32[]{:S(2)}, u32[]{:S(2)}) collective-permute-start(bf16[2,512,128]{2,1,0:T(8,128)(2,1)S(1)} %slice.322), channel_id=1, source_target_pairs={{0,8},{4,12},{8,0},{12,4},{16,24},{20,28},{24,16},{28,20},{1,9},{5... | collective-permute-start | bytes 786440 | tf_op jit(solution)/shard_map/ppermute | solution.py:230
  67.3 4.5 %shard_map.166 = (f32[1024,128]{1,0:T(8,128)S(1)}, f32[1024,128]{1,0:T(8,128)S(1)}, f32[1024,128]{1,0:T(8,128)S(1)}) custom-call(f32[2]{0:T(128)S(1)} %dynamic-slice_multiply_fusion.scale_ref, bf16[1024,128]{1,0:T(8,128)(2,1)S(1)} %maximum_bitcast_fusion.q_ref, bf16[2,1024,128]{2,1,0:T(8,128)(2,1)S(1)} %pad_maximum_fusion.6.refs_0_.refs_1_, ...), custom_call_target="tpu_custom_call" | custom-call | flops 536870912 | bytes 2359296 | tf_op jit(solution)/shard_map/pallas_call | solution.py:112
  71.8 9.0 %shard_map.167 = (f32[1024,128]{1,0:T(8,128)S(1)}, f32[1024,128]{1,0:T(8,128)S(1)}, f32[1024,128]{1,0:T(8,128)S(1)}) custom-call(f32[2]{0:T(128)S(1)} %dynamic-slice_multiply_fusion.scale_ref, bf16[1024,128]{1,0:T(8,128)(2,1)S(1)} %maximum_bitcast_fusion.q_ref, bf16[2,1024,128]{2,1,0:T(8,128)(2,1)S(1)} %collective-permute-done.8.refs_0_.refs_2_, ...), custom_call_target="tpu_custom_call" | custom-call | flops 1073741824 | bytes 2883584 | tf_op jit(solution)/shard_map/pallas_call | solution.py:112
  80.8 4.3 %shard_map.168 = (f32[1024,128]{1,0:T(8,128)S(1)}, f32[1024,128]{1,0:T(8,128)S(1)}, f32[1024,128]{1,0:T(8,128)S(1)}) custom-call(f32[2]{0:T(128)S(1)} %dynamic-slice_multiply_fusion.scale_ref, bf16[1024,128]{1,0:T(8,128)(2,1)S(1)} %maximum_bitcast_fusion.q_ref, bf16[2,512,128]{2,1,0:T(8,128)(2,1)S(1)} %collective-permute-done.10.refs_0_.refs_2_, ...), custom_call_target="tpu_custom_call" | custom-call | flops 536870912 | bytes 2359296 | tf_op jit(solution)/shard_map/pallas_call | solution.py:112
  85.7 1.3 collective-permute-done.12
  87.2 5.6 %collective-permute-start.13 = (bf16[128,256]{1,0:T(8,128)(2,1)S(1)}, bf16[128,256]{1,0:T(8,128)(2,1)S(1)}, u32[]{:S(2)}, u32[]{:S(2)}) collective-permute-start(bf16[128,256]{1,0:T(8,128)(2,1)S(1)} %get-tuple-element.56), channel_id=1, source_target_pairs={{1,0},{2,1},{3,2},{0,3},{5,4},{6,5},{7,6},{4,7},{9,8},{10,9},{11,1... | collective-permute-start | bytes 196616 | tf_op jit(solution)/shard_map/ppermute | solution.py:154
  93.5 1.8 %collective-permute-done.13 = bf16[128,256]{1,0:T(8,128)(2,1)S(1)} collective-permute-done((bf16[128,256]{1,0:T(8,128)(2,1)S(1)}, bf16[128,256]{1,0:T(8,128)(2,1)S(1)}, u32[]{:S(2)}, u32[]{:S(2)}) %collective-permute-start.13) | collective-permute-done | bytes 65568 | tf_op jit(solution)/shard_map/ppermute | solution.py:154
  95.3 4.6 %collective-permute-done.14 = bf16[128,256]{1,0:T(8,128)(2,1)S(1)} collective-permute-done((bf16[128,256]{1,0:T(8,128)(2,1)S(1)}, bf16[128,256]{1,0:T(8,128)(2,1)S(1)}, u32[]{:S(2)}, u32[]{:S(2)}) %collective-permute-start.14) | collective-permute-done | bytes 65568 | tf_op jit(solution)/shard_map/ppermute | solution.py:154
  100.7 3.4 %fusion.58 = bf16[128,4,4,32,4]{0,3,4,2,1:T(8,128)(2,1)S(1)} fusion(bf16[4,32,1024,1,1]{2,1,4,3,0:T(8,128)(2,1)S(1)} %bitcast.255, bf16[1024,4,4,128]{3,2,1,0:T(4,128)(2,1)} %param.28), kind=kOutput, calls=%fused_computation.74 | convolution fusion | flops 539230208 | bytes 4980736 | tf_op jit(solution)/shard_map/pqd,dabh->hpaqb/dot_general | solution.py:266
  107.3 3.4 %collective-permute-done.17 = bf16[128,1,128]{2,0,1:T(8,128)(2,1)S(1)} collective-permute-done((bf16[128,1,128]{2,0,1:T(8,128)(2,1)S(1)}, bf16[128,1,128]{2,0,1:T(8,128)(2,1)S(1)}, u32[]{:S(2)}, u32[]{:S(2)}) %collective-permute-start.17) | collective-permute-done | bytes 32800 | tf_op jit(solution)/shard_map/ppermute | solution.py:21
  111.7 4.1 %collective-permute-start.19 = (bf16[128,18,1]{0,1,2:T(8,128)(2,1)S(1)}, bf16[128,18,1]{0,1,2:T(8,128)(2,1)S(1)}, u32[]{:S(2)}, u32[]{:S(2)}) collective-permute-start(bf16[128,18,1]{0,1,2:T(8,128)(2,1)S(1)} %copy.65), channel_id=1, source_target_pairs={{1,0},{2,1},{3,2},{0,3},{5,4},{6,5},{7,6},{4,7},{9,8},{10,9},{11,1... | collective-permute-start | bytes 13832 | tf_op jit(solution)/shard_map/ppermute | solution.py:26
  118.3 1.8 %maximum_maximum_fusion = (bf16[128,18,129]{2,0,1:T(8,128)(2,1)S(1)}, bf16[128,18,129]{2,0,1:T(8,128)(2,1)S(1)}) fusion(bf16[128,1,128]{2,0,1:T(8,128)(2,1)S(1)} %collective-permute-done.17, bf16[128,16,128]{2,0,1:T(8,128)(2,1)S(1)} %copy.59, bf16[128,1,128]{2,0,1:T(8,128)(2,1)S(1)} %collective-permute-done.16, bf16[128,18,1]{2,0,1:T(8,128)(2,1)S(1)} %copy.63, ...), kind=kLoop, calls=%fused_computation.54 | loop fusion | flops 4755456 | bytes 1787904 | tf_op jit(solution)/shard_map/concatenate | solution.py:27
  123.8 3.3 %collective-permute-done.20 = f32[64]{0:T(128)S(1)} collective-permute-done((f32[64]{0:T(128)S(1)}, f32[64]{0:T(128)S(1)}, u32[]{:S(2)}, u32[]{:S(2)}) %collective-permute-start.20) | collective-permute-done | bytes 288 | tf_op jit(solution)/shard_map/ppermute | solution.py:34
  127.0 2.6 %collective-permute-start.21 = (f32[64]{0:T(128)S(1)}, f32[64]{0:T(128)S(1)}, u32[]{:S(2)}, u32[]{:S(2)}) collective-permute-start(f32[64]{0:T(128)S(1)} %add.303), channel_id=1, source_target_pairs={{0,2},{1,3},{2,0},{3,1},{4,6},{5,7},{6,4},{7,5},{8,10},{9,11},{10,... | collective-permute-start | bytes 776 | tf_op jit(solution)/shard_map/ppermute | solution.py:34
  129.6 1.9 %collective-permute-done.21 = f32[64]{0:T(128)S(1)} collective-permute-done((f32[64]{0:T(128)S(1)}, f32[64]{0:T(128)S(1)}, u32[]{:S(2)}, u32[]{:S(2)}) %collective-permute-start.21) | collective-permute-done | bytes 288 | tf_op jit(solution)/shard_map/ppermute | solution.py:34
  132.6 2.5 %collective-permute-start.23 = (f32[64]{0:T(128)S(1)}, f32[64]{0:T(128)S(1)}, u32[]{:S(2)}, u32[]{:S(2)}) collective-permute-start(f32[64]{0:T(128)S(1)} %add.305), channel_id=1, source_target_pairs={{0,8},{4,12},{8,0},{12,4},{16,24},{20,28},{24,16},{28,20},{1,9},{5... | collective-permute-start | bytes 776 | tf_op jit(solution)/shard_map/ppermute | solution.py:34
  135.1 1.5 %collective-permute-done.23 = f32[64]{0:T(128)S(1)} collective-permute-done((f32[64]{0:T(128)S(1)}, f32[64]{0:T(128)S(1)}, u32[]{:S(2)}, u32[]{:S(2)}) %collective-permute-start.23) | collective-permute-done | bytes 288 | tf_op jit(solution)/shard_map/ppermute | solution.py:34
  136.7 3.2 %collective-permute-start.24 = (f32[64]{0:T(128)S(1)}, f32[64]{0:T(128)S(1)}, u32[]{:S(2)}, u32[]{:S(2)}) collective-permute-start(f32[64]{0:T(128)S(1)} %add.306), channel_id=1, source_target_pairs={{0,16},{4,20},{8,24},{12,28},{16,0},{20,4},{24,8},{28,12},{1,17},{... | collective-permute-start | bytes 776 | tf_op jit(solution)/shard_map/ppermute | solution.py:34
  (139 shorter events, 32.0 us)
Async XLA Ops:
  0.6 25.5 %copy-start = (bf16[1024,1024]{1,0:T(8,128)(2,1)S(1)}, bf16[1024,1024]{1,0:T(8,128)(2,1)}, u32[]{:S(2)}) copy-start(bf16[1024,1024]{1,0:T(8,128)(2,1)} %param.25) | copy-start | bytes 6291460
  2.1 13.6 %copy-start.10 = (bf16[9,128,69]{1,2,0:T(8,128)(2,1)S(1)}, bf16[9,128,69]{1,2,0:T(8,128)(2,1)}, u32[]{:S(2)}) copy-start(bf16[9,128,69]{1,2,0:T(8,128)(2,1)} %param.19) | copy-start | bytes 476932
  2.2 3.8 %collective-permute-start = (bf16[69,2,128]{0,2,1:T(8,128)(2,1)S(1)}, bf16[69,2,128]{0,2,1:T(8,128)(2,1)S(1)}, u32[]{:S(2)}, u32[]{:S(2)}) collective-permute-start(bf16[69,2,128]{0,2,1:T(8,128)(2,1)S(1)} %get-tuple-element.52), channel_id=1, source_target_pairs={{0,4},{4,8},{8,12},{12,16},{16,20},{20,24},{24,28},{1,5},{5,9},{9,... | collective-permute-start | bytes 105992 | tf_op jit(solution)/shard_map/ppermute | solution.py:20
  4.7 5.3 %collective-permute-start.1 = (bf16[69,2,128]{0,2,1:T(8,128)(2,1)S(1)}, bf16[69,2,128]{0,2,1:T(8,128)(2,1)S(1)}, u32[]{:S(2)}, u32[]{:S(2)}) collective-permute-start(bf16[69,2,128]{0,2,1:T(8,128)(2,1)S(1)} %get-tuple-element.53), channel_id=1, source_target_pairs={{4,0},{8,4},{12,8},{16,12},{20,16},{24,20},{28,24},{5,1},{9,5},{13... | collective-permute-start | bytes 105992 | tf_op jit(solution)/shard_map/ppermute | solution.py:21
  9.9 5.5 %collective-permute-start.2 = (bf16[69,20,2]{0,2,1:T(2,128)(2,1)S(1)}, bf16[69,20,2]{0,2,1:T(2,128)(2,1)S(1)}, u32[]{:S(2)}, u32[]{:S(2)}) collective-permute-start(bf16[69,20,2]{0,2,1:T(2,128)(2,1)S(1)} %get-tuple-element.42), channel_id=1, source_target_pairs={{0,1},{1,2},{2,3},{3,0},{4,5},{5,6},{6,7},{7,4},{8,9},{9,10},{10,1... | collective-permute-start | bytes 16568 | tf_op jit(solution)/shard_map/ppermute | solution.py:25
  11.6 3.9 %collective-permute-start.3 = (bf16[69,20,2]{0,2,1:T(2,128)(2,1)S(1)}, bf16[69,20,2]{0,2,1:T(2,128)(2,1)S(1)}, u32[]{:S(2)}, u32[]{:S(2)}) collective-permute-start(bf16[69,20,2]{0,2,1:T(2,128)(2,1)S(1)} %get-tuple-element.43), channel_id=1, source_target_pairs={{1,0},{2,1},{3,2},{0,3},{5,4},{6,5},{7,6},{4,7},{9,8},{10,9},{11,1... | collective-permute-start | bytes 16568 | tf_op jit(solution)/shard_map/ppermute | solution.py:26
  30.0 9.0 %collective-permute-start.4 = (bf16[3,128,256]{2,1,0:T(8,128)(2,1)S(1)}, bf16[3,128,256]{2,1,0:T(8,128)(2,1)S(1)}, u32[]{:S(2)}, u32[]{:S(2)}) collective-permute-start(bf16[3,128,256]{2,1,0:T(8,128)(2,1)S(1)} %get-tuple-element.41), channel_id=1, source_target_pairs={{0,1},{1,2},{2,3},{3,0},{4,5},{5,6},{6,7},{7,4},{8,9},{9,10},{10,1... | collective-permute-start | bytes 589832 | tf_op jit(solution)/shard_map/ppermute | solution.py:146
  31.4 16.6 %collective-permute-start.5 = (bf16[3,128,256]{2,1,0:T(8,128)(2,1)S(1)}, bf16[3,128,256]{2,1,0:T(8,128)(2,1)S(1)}, u32[]{:S(2)}, u32[]{:S(2)}) collective-permute-start(bf16[3,128,256]{2,1,0:T(8,128)(2,1)S(1)} %get-tuple-element.40), channel_id=1, source_target_pairs={{0,2},{1,3},{2,0},{3,1},{4,6},{5,7},{6,4},{7,5},{8,10},{9,11},{10,... | collective-permute-start | bytes 589832 | tf_op jit(solution)/shard_map/ppermute | solution.py:146
  34.5 13.6 %collective-permute-start.6 = (bf16[3,128,256]{2,1,0:T(8,128)(2,1)S(1)}, bf16[3,128,256]{2,1,0:T(8,128)(2,1)S(1)}, u32[]{:S(2)}, u32[]{:S(2)}) collective-permute-start(bf16[3,128,256]{2,1,0:T(8,128)(2,1)S(1)} %get-tuple-element.39), channel_id=1, source_target_pairs={{0,3},{1,0},{2,1},{3,2},{4,7},{5,4},{6,5},{7,6},{8,11},{9,8},{10,9... | collective-permute-start | bytes 589832 | tf_op jit(solution)/shard_map/ppermute | solution.py:146
  48.1 4.8 %copy-start.13 = (f32[16]{0:T(128)S(1)}, f32[16]{0:T(128)}, u32[]{:S(2)}) copy-start(f32[16]{0:T(128)} %param.27) | copy-start | bytes 196
  48.2 1.8 %collective-permute-start.7 = (bf16[3,512,128]{2,1,0:T(8,128)(2,1)S(1)}, bf16[3,512,128]{2,1,0:T(8,128)(2,1)S(1)}, u32[]{:S(2)}, u32[]{:S(2)}) collective-permute-start(bf16[3,512,128]{2,1,0:T(8,128)(2,1)S(1)} %get-tuple-element.37), channel_id=1, source_target_pairs={{0,4},{4,0},{8,12},{12,8},{16,20},{20,16},{24,28},{28,24},{1,5},{5... | collective-permute-start | bytes 1179656 | tf_op jit(solution)/shard_map/ppermute | solution.py:220
  50.0 14.9 %collective-permute-start.9 = (bf16[2,1024,128]{2,1,0:T(8,128)(2,1)S(1)}, bf16[2,1024,128]{2,1,0:T(8,128)(2,1)S(1)}, u32[]{:S(2)}, u32[]{:S(2)}) collective-permute-start(bf16[2,1024,128]{2,1,0:T(8,128)(2,1)S(1)} %pad_maximum_fusion.6.refs_0_.refs_1_), channel_id=1, source_target_pairs={{0,16},{4,20},{8,24},{12,28},{16,0},{20,4},{24,8},{28,12},{1,17},{... | collective-permute-start | bytes 1572872 | tf_op jit(solution)/shard_map/ppermute | solution.py:228
  52.6 14.3 %collective-permute-start.8 = (bf16[2,1024,128]{2,1,0:T(8,128)(2,1)S(1)}, bf16[2,1024,128]{2,1,0:T(8,128)(2,1)S(1)}, u32[]{:S(2)}, u32[]{:S(2)}) collective-permute-start(bf16[2,1024,128]{2,1,0:T(8,128)(2,1)S(1)} %pad_maximum_fusion.6.refs_0_.refs_1_), channel_id=1, source_target_pairs={{0,8},{4,12},{8,0},{12,4},{16,24},{20,28},{24,16},{28,20},{1,9},{5... | collective-permute-start | bytes 1572872 | tf_op jit(solution)/shard_map/ppermute | solution.py:227
  64.9 15.9 %collective-permute-start.10 = (bf16[2,512,128]{2,1,0:T(8,128)(2,1)S(1)}, bf16[2,512,128]{2,1,0:T(8,128)(2,1)S(1)}, u32[]{:S(2)}, u32[]{:S(2)}) collective-permute-start(bf16[2,512,128]{2,1,0:T(8,128)(2,1)S(1)} %slice.322), channel_id=1, source_target_pairs={{0,8},{4,12},{8,0},{12,4},{16,24},{20,28},{24,16},{28,20},{1,9},{5... | collective-permute-start | bytes 786440 | tf_op jit(solution)/shard_map/ppermute | solution.py:230
  66.9 13.9 %collective-permute-start.11 = (bf16[2,512,128]{2,1,0:T(8,128)(2,1)S(1)}, bf16[2,512,128]{2,1,0:T(8,128)(2,1)S(1)}, u32[]{:S(2)}, u32[]{:S(2)}) collective-permute-start(bf16[2,512,128]{2,1,0:T(8,128)(2,1)S(1)} %slice.323), channel_id=1, source_target_pairs={{0,16},{4,20},{8,24},{12,28},{16,0},{20,4},{24,8},{28,12},{1,17},{... | collective-permute-start | bytes 786440 | tf_op jit(solution)/shard_map/ppermute | solution.py:231
  85.6 1.4 collective-permute-start.12
  87.0 13.2 %copy-start.5 = (bf16[1024,1024]{1,0:T(8,128)(2,1)S(1)}, bf16[1024,1024]{1,0:T(8,128)(2,1)}, u32[]{:S(2)}) copy-start(bf16[1024,1024]{1,0:T(8,128)(2,1)} %param.26) | copy-start | bytes 6291460
  87.2 8.1 %collective-permute-start.13 = (bf16[128,256]{1,0:T(8,128)(2,1)S(1)}, bf16[128,256]{1,0:T(8,128)(2,1)S(1)}, u32[]{:S(2)}, u32[]{:S(2)}) collective-permute-start(bf16[128,256]{1,0:T(8,128)(2,1)S(1)} %get-tuple-element.56), channel_id=1, source_target_pairs={{1,0},{2,1},{3,2},{0,3},{5,4},{6,5},{7,6},{4,7},{9,8},{10,9},{11,1... | collective-permute-start | bytes 196616 | tf_op jit(solution)/shard_map/ppermute | solution.py:154
  92.8 7.1 %collective-permute-start.14 = (bf16[128,256]{1,0:T(8,128)(2,1)S(1)}, bf16[128,256]{1,0:T(8,128)(2,1)S(1)}, u32[]{:S(2)}, u32[]{:S(2)}) collective-permute-start(bf16[128,256]{1,0:T(8,128)(2,1)S(1)} %get-tuple-element.55), channel_id=1, source_target_pairs={{2,0},{3,1},{0,2},{1,3},{6,4},{7,5},{4,6},{5,7},{10,8},{11,9},{8,1... | collective-permute-start | bytes 196616 | tf_op jit(solution)/shard_map/ppermute | solution.py:154
  93.5 6.5 %collective-permute-start.15 = (bf16[128,256]{1,0:T(8,128)(2,1)S(1)}, bf16[128,256]{1,0:T(8,128)(2,1)S(1)}, u32[]{:S(2)}, u32[]{:S(2)}) collective-permute-start(bf16[128,256]{1,0:T(8,128)(2,1)S(1)} %get-tuple-element.54), channel_id=1, source_target_pairs={{3,0},{0,1},{1,2},{2,3},{7,4},{4,5},{5,6},{6,7},{11,8},{8,9},{9,10... | collective-permute-start | bytes 196616 | tf_op jit(solution)/shard_map/ppermute | solution.py:154
  104.7 2.6 %collective-permute-start.16 = (bf16[128,1,128]{2,0,1:T(8,128)(2,1)S(1)}, bf16[128,1,128]{2,0,1:T(8,128)(2,1)S(1)}, u32[]{:S(2)}, u32[]{:S(2)}) collective-permute-start(bf16[128,1,128]{2,0,1:T(8,128)(2,1)S(1)} %get-tuple-element.50), channel_id=1, source_target_pairs={{0,4},{4,8},{8,12},{12,16},{16,20},{20,24},{24,28},{1,5},{5,9},{9,... | collective-permute-start | bytes 98312 | tf_op jit(solution)/shard_map/ppermute | solution.py:20
  106.0 4.8 %collective-permute-start.17 = (bf16[128,1,128]{2,0,1:T(8,128)(2,1)S(1)}, bf16[128,1,128]{2,0,1:T(8,128)(2,1)S(1)}, u32[]{:S(2)}, u32[]{:S(2)}) collective-permute-start(bf16[128,1,128]{2,0,1:T(8,128)(2,1)S(1)} %get-tuple-element.51), channel_id=1, source_target_pairs={{4,0},{8,4},{12,8},{16,12},{20,16},{24,20},{28,24},{5,1},{9,5},{13... | collective-permute-start | bytes 98312 | tf_op jit(solution)/shard_map/ppermute | solution.py:21
  110.8 5.0 %copy-start.9 = (bf16[9,69,128]{2,1,0:T(8,128)(2,1)S(1)}, bf16[9,69,128]{2,1,0:T(8,128)(2,1)}, u32[]{:S(2)}) copy-start(bf16[9,69,128]{2,1,0:T(8,128)(2,1)} %param.29) | copy-start | bytes 476932
  111.4 5.5 %collective-permute-start.18 = (bf16[128,18,1]{0,1,2:T(8,128)(2,1)S(1)}, bf16[128,18,1]{0,1,2:T(8,128)(2,1)S(1)}, u32[]{:S(2)}, u32[]{:S(2)}) collective-permute-start(bf16[128,18,1]{0,1,2:T(8,128)(2,1)S(1)} %copy.62), channel_id=1, source_target_pairs={{0,1},{1,2},{2,3},{3,0},{4,5},{5,6},{6,7},{7,4},{8,9},{9,10},{10,1... | collective-permute-start | bytes 13832 | tf_op jit(solution)/shard_map/ppermute | solution.py:25
  111.7 5.5 %collective-permute-start.19 = (bf16[128,18,1]{0,1,2:T(8,128)(2,1)S(1)}, bf16[128,18,1]{0,1,2:T(8,128)(2,1)S(1)}, u32[]{:S(2)}, u32[]{:S(2)}) collective-permute-start(bf16[128,18,1]{0,1,2:T(8,128)(2,1)S(1)} %copy.65), channel_id=1, source_target_pairs={{1,0},{2,1},{3,2},{0,3},{5,4},{6,5},{7,6},{4,7},{9,8},{10,9},{11,1... | collective-permute-start | bytes 13832 | tf_op jit(solution)/shard_map/ppermute | solution.py:26
  121.8 20.2 %copy-start.1 = (bf16[1024,1024]{1,0:T(8,128)(2,1)S(1)}, bf16[1024,1024]{1,0:T(8,128)(2,1)}, u32[]{:S(2)}) copy-start(bf16[1024,1024]{1,0:T(8,128)(2,1)} %param.25) | copy-start | bytes 6291460
  122.4 19.0 %copy-start.14 = (s32[64]{0:T(128)S(1)}, s32[64]{0:T(128)}, u32[]{:S(2)}) copy-start(s32[64]{0:T(128)} %param.18) | copy-start | bytes 772
  123.5 3.6 %collective-permute-start.20 = (f32[64]{0:T(128)S(1)}, f32[64]{0:T(128)S(1)}, u32[]{:S(2)}, u32[]{:S(2)}) collective-permute-start(f32[64]{0:T(128)S(1)} %fusion.40), channel_id=1, source_target_pairs={{0,1},{1,0},{2,3},{3,2},{4,5},{5,4},{6,7},{7,6},{8,9},{9,8},{10,11... | collective-permute-start | bytes 776 | tf_op jit(solution)/shard_map/ppermute | solution.py:34
  127.0 4.4 %collective-permute-start.21 = (f32[64]{0:T(128)S(1)}, f32[64]{0:T(128)S(1)}, u32[]{:S(2)}, u32[]{:S(2)}) collective-permute-start(f32[64]{0:T(128)S(1)} %add.303), channel_id=1, source_target_pairs={{0,2},{1,3},{2,0},{3,1},{4,6},{5,7},{6,4},{7,5},{8,10},{9,11},{10,... | collective-permute-start | bytes 776 | tf_op jit(solution)/shard_map/ppermute | solution.py:34
  131.5 1.1 collective-permute-start.22
  132.6 4.0 %collective-permute-start.23 = (f32[64]{0:T(128)S(1)}, f32[64]{0:T(128)S(1)}, u32[]{:S(2)}, u32[]{:S(2)}) collective-permute-start(f32[64]{0:T(128)S(1)} %add.305), channel_id=1, source_target_pairs={{0,8},{4,12},{8,0},{12,4},{16,24},{20,28},{24,16},{28,20},{1,9},{5... | collective-permute-start | bytes 776 | tf_op jit(solution)/shard_map/ppermute | solution.py:34
  136.7 4.7 %collective-permute-start.24 = (f32[64]{0:T(128)S(1)}, f32[64]{0:T(128)S(1)}, u32[]{:S(2)}, u32[]{:S(2)}) collective-permute-start(f32[64]{0:T(128)S(1)} %add.306), channel_id=1, source_target_pairs={{0,16},{4,20},{8,24},{12,28},{16,0},{20,4},{24,8},{28,12},{1,17},{... | collective-permute-start | bytes 776 | tf_op jit(solution)/shard_map/ppermute | solution.py:34
  (9 other events, 10.9 us)

commit v16 on v14

--- a/solution.py
+++ b/solution.py
@@ -251,17 +251,37 @@
     ]
     pair_attended = merge_parts(parts)
     token_count = spread.shape[1]
-    own_part = pair_attended[:token_count]
-    returned = lax.ppermute(pair_attended[token_count:], "lat", partner)
-    attended_heads = jnp.where(
-        core == 0,
-        jnp.concatenate([own_part, returned], axis=1),
-        jnp.concatenate([returned, own_part], axis=1),
-    )
-    token_block = attended_heads.shape[0] // lon_size
-    attended = return_blocks(
-        [attended_heads[d * token_block : (d + 1) * token_block] for d in range(lon_size)], "lon"
-    )
+    token_block = token_count // lon_size
+    lon_index = lax.axis_index("lon")
+    own_blocks = [pair_attended[d * token_block : (d + 1) * token_block] for d in range(lon_size)]
+    partner_blocks = [
+        pair_attended[token_count + d * token_block : token_count + (d + 1) * token_block]
+        for d in range(lon_size)
+    ]
+    grid = ("lat", "lon")
+    by_shift = []
+    for shift in range(lon_size):
+        own = own_blocks[0] if shift == 0 else lax.ppermute(
+            own_blocks[shift], "lon", [((i + shift) % lon_size, i) for i in range(lon_size)]
+        )
+        other = lax.ppermute(
+            partner_blocks[shift],
+            grid,
+            [
+                (l * lon_size + j, (l ^ 1) * lon_size + (j - shift) % lon_size)
+                for l in range(lat_size)
+                for j in range(lon_size)
+            ],
+        )
+        by_shift.append(
+            jnp.where(
+                core == 0,
+                jnp.concatenate([own, other], axis=1),
+                jnp.concatenate([other, own], axis=1),
+            )
+        )
+    rotated = jnp.stack(by_shift + by_shift)
+    attended = lax.dynamic_slice_in_dim(rotated, lon_size - lon_index, lon_size, axis=0)
     attended = attended.transpose(1, 0, 2).reshape(token_block, model_width)
     latent_two = (
         latent_wide + jnp.dot(attended, output_weight, preferred_element_type=jnp.float32)

time: 141 us -> 142 us (level)
  starting transfers between devices: 39.5 us -> 43.7 us
  waiting for transfers between devices: 48.2 us -> 45.1 us
    ppermute x4 -> x7, starting transfers between devices: 6.32 us -> 10.1 us  [the longest x3 8.17 us: on_device(): lax.ppermute(own_blocks[shift], 'lon', [((i + shift) % lon_size, i) for i...]
    ppermute x4 -> x7, waiting for transfers between devices: 7.77 us -> 5.06 us  [the longest x3 3.1 us: on_device(): lax.ppermute(own_blocks[shift], 'lon', [((i + shift) % lon_size, i) for i...]
    unnamed x41 -> x34, local copies, waits for them, and re-layouts: 6.4 us -> 6.36 us
  transfers between devices with their start and end apart: 25 -> 28, of which waited for: 16 -> 17; matrix products, arithmetic and copies ran while one was open for 3% -> 3% of each run, Pallas kernels for 10% -> 10%
where the time goes in v16:
time: 142 us
  waiting for transfers between devices  45.1 us (32%)
  starting transfers between devices  43.7 us (31%)
  Pallas kernels  17.9 us (13%)
  matrix products  17.7 us (12%)
  local copies, waits for them, and re-layouts  11.8 us (8%)
  other arithmetic  4.14 us (3%)
    pallas_call x3, Pallas kernels, attend_part(): pl.pallas_call(functools.partial(attention_kernel, head_size=head_size, c...  17.9 us
    ppermute x3, waiting for transfers between devices, exchange_blocks(): lax.ppermute(outgoing, axis, [(i, (i + shift) % size) for i in range(size)])  12.7 us
    dot_general x27, matrix products, convolution_kernel_taps(): jnp.einsum('oc,cyx->oyx', weight[tap_index], window, preferred_element_ty...  10.7 us
    ppermute x5, waiting for transfers between devices, butterfly_sum(): value = value + lax.ppermute(value, axis, partner)  8.85 us
    ppermute x5, starting transfers between devices, butterfly_sum(): value = value + lax.ppermute(value, axis, partner)  8.26 us
    ppermute x3, starting transfers between devices, on_device(): lax.ppermute(own_blocks[shift], 'lon', [((i + shift) % lon_size, i) for i...  8.17 us
    ppermute x1, waiting for transfers between devices, on_device(): from_x = lax.ppermute(key_value, 'lat', across_x)  7.78 us
    ppermute x2, waiting for transfers between devices, halo_padded(): from_below = lax.ppermute(array[:, :width], 'lat', up)  6.87 us
  transfers between devices with their start and end apart: 28, of which 17 were waited for; matrix products, arithmetic and copies ran while one was open for 3% of the time, Pallas kernels for 10%

profile of v16, /device:TPU:0, one launch (start us, length us, event | category | flops | bytes accessed | tf_op | source)
XLA Modules:
  0.0 141.7 jit_solution(8019944407391574101)
XLA Ops:
  0.6 1.5 %copy.49 = bf16[69,16,128]{0,2,1:T(8,128)(2,1)S(1)} copy(bf16[69,16,128]{2,1,0:T(8,128)(2,1)} %param.15) | data formatting | bytes 565248 | tf_op args[0]
  2.2 2.5 %collective-permute-start = (bf16[69,2,128]{0,2,1:T(8,128)(2,1)S(1)}, bf16[69,2,128]{0,2,1:T(8,128)(2,1)S(1)}, u32[]{:S(2)}, u32[]{:S(2)}) collective-permute-start(bf16[69,2,128]{0,2,1:T(8,128)(2,1)S(1)} %get-tuple-element.59), channel_id=1, source_target_pairs={{0,4},{4,8},{8,12},{12,16},{16,20},{20,24},{24,28},{1,5},{5,9},{9,... | collective-permute-start | bytes 105992 | tf_op jit(solution)/shard_map/ppermute | solution.py:20
  6.0 3.9 %collective-permute-done.1 = bf16[69,2,128]{0,2,1:T(8,128)(2,1)S(1)} collective-permute-done((bf16[69,2,128]{0,2,1:T(8,128)(2,1)S(1)}, bf16[69,2,128]{0,2,1:T(8,128)(2,1)S(1)}, u32[]{:S(2)}, u32[]{:S(2)}) %collective-permute-start.1) | collective-permute-done | bytes 35360 | tf_op jit(solution)/shard_map/ppermute | solution.py:21
  9.9 1.6 %collective-permute-start.2 = (bf16[69,20,2]{0,2,1:T(2,128)(2,1)S(1)}, bf16[69,20,2]{0,2,1:T(2,128)(2,1)S(1)}, u32[]{:S(2)}, u32[]{:S(2)}) collective-permute-start(bf16[69,20,2]{0,2,1:T(2,128)(2,1)S(1)} %get-tuple-element.45), channel_id=1, source_target_pairs={{0,1},{1,2},{2,3},{3,0},{4,5},{5,6},{6,7},{7,4},{8,9},{9,10},{10,1... | collective-permute-start | bytes 16568 | tf_op jit(solution)/shard_map/ppermute | solution.py:25
  11.6 2.2 %collective-permute-start.3 = (bf16[69,20,2]{0,2,1:T(2,128)(2,1)S(1)}, bf16[69,20,2]{0,2,1:T(2,128)(2,1)S(1)}, u32[]{:S(2)}, u32[]{:S(2)}) collective-permute-start(bf16[69,20,2]{0,2,1:T(2,128)(2,1)S(1)} %get-tuple-element.46), channel_id=1, source_target_pairs={{1,0},{2,1},{3,2},{0,3},{5,4},{6,5},{7,6},{4,7},{9,8},{10,9},{11,1... | collective-permute-start | bytes 16568 | tf_op jit(solution)/shard_map/ppermute | solution.py:26
  13.8 1.6 %collective-permute-done.2 = bf16[69,20,2]{0,2,1:T(2,128)(2,1)S(1)} collective-permute-done((bf16[69,20,2]{0,2,1:T(2,128)(2,1)S(1)}, bf16[69,20,2]{0,2,1:T(2,128)(2,1)S(1)}, u32[]{:S(2)}, u32[]{:S(2)}) %collective-permute-start.2) | collective-permute-done | bytes 5552 | tf_op jit(solution)/shard_map/ppermute | solution.py:25
  31.4 3.1 %collective-permute-start.5 = (bf16[3,128,256]{2,1,0:T(8,128)(2,1)S(1)}, bf16[3,128,256]{2,1,0:T(8,128)(2,1)S(1)}, u32[]{:S(2)}, u32[]{:S(2)}) collective-permute-start(bf16[3,128,256]{2,1,0:T(8,128)(2,1)S(1)} %get-tuple-element.43), channel_id=1, source_target_pairs={{0,2},{1,3},{2,0},{3,1},{4,6},{5,7},{6,4},{7,5},{8,10},{9,11},{10,... | collective-permute-start | bytes 589832 | tf_op jit(solution)/shard_map/ppermute | solution.py:145
  35.3 3.6 %collective-permute-done.4 = bf16[3,128,256]{2,1,0:T(8,128)(2,1)S(1)} collective-permute-done((bf16[3,128,256]{2,1,0:T(8,128)(2,1)S(1)}, bf16[3,128,256]{2,1,0:T(8,128)(2,1)S(1)}, u32[]{:S(2)}, u32[]{:S(2)}) %collective-permute-start.4) | collective-permute-done | bytes 196640 | tf_op jit(solution)/shard_map/ppermute | solution.py:145
  39.0 9.1 %collective-permute-done.5 = bf16[3,128,256]{2,1,0:T(8,128)(2,1)S(1)} collective-permute-done((bf16[3,128,256]{2,1,0:T(8,128)(2,1)S(1)}, bf16[3,128,256]{2,1,0:T(8,128)(2,1)S(1)}, u32[]{:S(2)}, u32[]{:S(2)}) %collective-permute-start.5) | collective-permute-done | bytes 196640 | tf_op jit(solution)/shard_map/ppermute | solution.py:145
  48.4 1.6 %collective-permute-done.7 = bf16[3,512,128]{2,1,0:T(8,128)(2,1)S(1)} collective-permute-done((bf16[3,512,128]{2,1,0:T(8,128)(2,1)S(1)}, bf16[3,512,128]{2,1,0:T(8,128)(2,1)S(1)}, u32[]{:S(2)}, u32[]{:S(2)}) %collective-permute-start.7) | collective-permute-done | bytes 393248 | tf_op jit(solution)/shard_map/ppermute | solution.py:219
  50.8 2.8 %collective-permute-start.8 = (bf16[2,1024,128]{2,1,0:T(8,128)(2,1)}, bf16[2,1024,128]{2,1,0:T(8,128)(2,1)S(1)}, u32[]{:S(2)}, u32[]{:S(2)}) collective-permute-start(bf16[2,1024,128]{2,1,0:T(8,128)(2,1)} %pad_maximum_fusion.6), channel_id=1, source_target_pairs={{0,8},{4,12},{8,0},{12,4},{16,24},{20,28},{24,16},{28,20},{1,9},{5... | collective-permute-start | bytes 1572872 | tf_op jit(solution)/shard_map/ppermute | solution.py:226
  53.7 4.5 %shard_map.166 = (f32[1024,128]{1,0:T(8,128)S(1)}, f32[1024,128]{1,0:T(8,128)S(1)}, f32[1024,128]{1,0:T(8,128)S(1)}) custom-call(f32[2]{0:T(128)S(1)} %dynamic-slice_multiply_fusion.scale_ref, bf16[1024,128]{1,0:T(8,128)(2,1)S(1)} %get-tuple-element.37.q_ref, bf16[1024,128]{1,0:T(8,128)(2,1)S(1)} %get-tuple-element.38.refs_0_, ...), custom_call_target="tpu_custom_call" | custom-call | flops 536870912 | bytes 2359296 | tf_op jit(solution)/shard_map/pallas_call | solution.py:111
  58.2 7.8 %collective-permute-done.8 = bf16[2,1024,128]{2,1,0:T(8,128)(2,1)S(1)} collective-permute-done((bf16[2,1024,128]{2,1,0:T(8,128)(2,1)}, bf16[2,1024,128]{2,1,0:T(8,128)(2,1)S(1)}, u32[]{:S(2)}, u32[]{:S(2)}) %collective-permute-start.8) | collective-permute-done | bytes 524320 | tf_op jit(solution)/shard_map/ppermute | solution.py:226
  66.0 1.6 %collective-permute-start.11 = (bf16[2,512,128]{2,1,0:T(8,128)(2,1)S(1)}, bf16[2,512,128]{2,1,0:T(8,128)(2,1)S(1)}, u32[]{:S(2)}, u32[]{:S(2)}) collective-permute-start(bf16[2,512,128]{2,1,0:T(8,128)(2,1)S(1)} %slice.384), channel_id=1, source_target_pairs={{0,16},{4,20},{8,24},{12,28},{16,0},{20,4},{24,8},{28,12},{1,17},{... | collective-permute-start | bytes 786440 | tf_op jit(solution)/shard_map/ppermute | solution.py:230
  70.1 9.0 %shard_map.167 = (f32[1024,128]{1,0:T(8,128)S(1)}, f32[1024,128]{1,0:T(8,128)S(1)}, f32[1024,128]{1,0:T(8,128)S(1)}) custom-call(f32[2]{0:T(128)S(1)} %dynamic-slice_multiply_fusion.scale_ref, bf16[1024,128]{1,0:T(8,128)(2,1)S(1)} %get-tuple-element.37.q_ref, bf16[1024,128]{1,0:T(8,128)(2,1)S(1)} %get-tuple-element.58.refs_0_, ...), custom_call_target="tpu_custom_call" | custom-call | flops 1073741824 | bytes 2883584 | tf_op jit(solution)/shard_map/pallas_call | solution.py:111
  79.2 4.4 %shard_map.168 = (f32[1024,128]{1,0:T(8,128)S(1)}, f32[1024,128]{1,0:T(8,128)S(1)}, f32[1024,128]{1,0:T(8,128)S(1)}) custom-call(f32[2]{0:T(128)S(1)} %dynamic-slice_multiply_fusion.scale_ref, bf16[1024,128]{1,0:T(8,128)(2,1)S(1)} %get-tuple-element.37.q_ref, bf16[512,128]{1,0:T(8,128)(2,1)S(1)} %get-tuple-element.72.refs_0_, ...), custom_call_target="tpu_custom_call" | custom-call | flops 536870912 | bytes 2359296 | tf_op jit(solution)/shard_map/pallas_call | solution.py:111
  84.1 5.6 %collective-permute-start.13 = (bf16[128,128]{1,0:T(8,128)(2,1)S(1)}, bf16[128,128]{1,0:T(8,128)(2,1)S(1)}, u32[]{:S(2)}, u32[]{:S(2)}) collective-permute-start(bf16[128,128]{1,0:T(8,128)(2,1)S(1)} %get-tuple-element.66), channel_id=1, source_target_pairs={{1,0},{2,1},{3,2},{0,3},{5,4},{6,5},{7,6},{4,7},{9,8},{10,9},{11,1... | collective-permute-start | bytes 98312 | tf_op jit(solution)/shard_map/ppermute | solution.py:264
  90.4 1.7 %collective-permute-start.16 = (bf16[128,128]{1,0:T(8,128)(2,1)S(1)}, bf16[128,128]{1,0:T(8,128)(2,1)S(1)}, u32[]{:S(2)}, u32[]{:S(2)}) collective-permute-start(bf16[128,128]{1,0:T(8,128)(2,1)S(1)} %get-tuple-element.63), channel_id=1, source_target_pairs={{0,6},{1,7},{2,4},{3,5},{4,2},{5,3},{6,0},{7,1},{8,14},{9,15},{10,... | collective-permute-start | bytes 98312 | tf_op jit(solution)/shard_map/ppermute | solution.py:267
  92.1 1.9 %collective-permute-start.17 = (bf16[128,128]{1,0:T(8,128)(2,1)S(1)}, bf16[128,128]{1,0:T(8,128)(2,1)S(1)}, u32[]{:S(2)}, u32[]{:S(2)}) collective-permute-start(bf16[128,128]{1,0:T(8,128)(2,1)S(1)} %get-tuple-element.62), channel_id=1, source_target_pairs={{3,0},{0,1},{1,2},{2,3},{7,4},{4,5},{5,6},{6,7},{11,8},{8,9},{9,10... | collective-permute-start | bytes 98312 | tf_op jit(solution)/shard_map/ppermute | solution.py:264
  95.3 2.5 %collective-permute-done.17 = bf16[128,128]{1,0:T(8,128)(2,1)S(1)} collective-permute-done((bf16[128,128]{1,0:T(8,128)(2,1)S(1)}, bf16[128,128]{1,0:T(8,128)(2,1)S(1)}, u32[]{:S(2)}, u32[]{:S(2)}) %collective-permute-start.17) | collective-permute-done | bytes 32800 | tf_op jit(solution)/shard_map/ppermute | solution.py:264
  97.8 1.4 collective-permute-done.18
  100.1 3.4 %fusion.58 = bf16[128,4,4,32,4]{0,3,4,2,1:T(8,128)(2,1)S(1)} fusion(bf16[4,32,1024,1,1]{2,1,4,3,0:T(8,128)(2,1)S(1)} %bitcast.269, bf16[1024,4,4,128]{3,2,1,0:T(4,128)(2,1)} %param.28), kind=kOutput, calls=%fused_computation.74 | convolution fusion | flops 539230208 | bytes 4980736 | tf_op jit(solution)/shard_map/pqd,dabh->hpaqb/dot_general | solution.py:291
  104.1 2.1 %collective-permute-start.19 = (bf16[128,1,128]{2,0,1:T(8,128)(2,1)S(1)}, bf16[128,1,128]{2,0,1:T(8,128)(2,1)S(1)}, u32[]{:S(2)}, u32[]{:S(2)}) collective-permute-start(bf16[128,1,128]{2,0,1:T(8,128)(2,1)S(1)} %get-tuple-element.53), channel_id=1, source_target_pairs={{0,4},{4,8},{8,12},{12,16},{16,20},{20,24},{24,28},{1,5},{5,9},{9,... | collective-permute-start | bytes 98312 | tf_op jit(solution)/shard_map/ppermute | solution.py:20
  107.5 2.9 %collective-permute-done.20 = bf16[128,1,128]{2,0,1:T(8,128)(2,1)S(1)} collective-permute-done((bf16[128,1,128]{2,0,1:T(8,128)(2,1)S(1)}, bf16[128,1,128]{2,0,1:T(8,128)(2,1)S(1)}, u32[]{:S(2)}, u32[]{:S(2)}) %collective-permute-start.20) | collective-permute-done | bytes 32800 | tf_op jit(solution)/shard_map/ppermute | solution.py:21
  111.4 4.1 %collective-permute-start.22 = (bf16[128,18,1]{0,1,2:T(8,128)(2,1)S(1)}, bf16[128,18,1]{0,1,2:T(8,128)(2,1)S(1)}, u32[]{:S(2)}, u32[]{:S(2)}) collective-permute-start(bf16[128,18,1]{0,1,2:T(8,128)(2,1)S(1)} %copy.65), channel_id=1, source_target_pairs={{1,0},{2,1},{3,2},{0,3},{5,4},{6,5},{7,6},{4,7},{9,8},{10,9},{11,1... | collective-permute-start | bytes 13832 | tf_op jit(solution)/shard_map/ppermute | solution.py:26
  118.0 1.8 %maximum_maximum_fusion = (bf16[128,18,129]{2,0,1:T(8,128)(2,1)S(1)}, bf16[128,18,129]{2,0,1:T(8,128)(2,1)S(1)}) fusion(bf16[128,1,128]{2,0,1:T(8,128)(2,1)S(1)} %collective-permute-done.20, bf16[128,16,128]{2,0,1:T(8,128)(2,1)S(1)} %copy.59, bf16[128,1,128]{2,0,1:T(8,128)(2,1)S(1)} %collective-permute-done.19, bf16[128,18,1]{2,0,1:T(8,128)(2,1)S(1)} %copy.63, ...), kind=kLoop, calls=%fused_computation.54 | loop fusion | flops 4755456 | bytes 1787904 | tf_op jit(solution)/shard_map/concatenate | solution.py:27
  123.2 3.6 %collective-permute-done.23 = f32[64]{0:T(128)S(1)} collective-permute-done((f32[64]{0:T(128)S(1)}, f32[64]{0:T(128)S(1)}, u32[]{:S(2)}, u32[]{:S(2)}) %collective-permute-start.23) | collective-permute-done | bytes 288 | tf_op jit(solution)/shard_map/ppermute | solution.py:34
  126.7 2.6 %collective-permute-start.24 = (f32[64]{0:T(128)S(1)}, f32[64]{0:T(128)S(1)}, u32[]{:S(2)}, u32[]{:S(2)}) collective-permute-start(f32[64]{0:T(128)S(1)} %add.303), channel_id=1, source_target_pairs={{0,2},{1,3},{2,0},{3,1},{4,6},{5,7},{6,4},{7,5},{8,10},{9,11},{10,... | collective-permute-start | bytes 776 | tf_op jit(solution)/shard_map/ppermute | solution.py:34
  129.3 1.9 %collective-permute-done.24 = f32[64]{0:T(128)S(1)} collective-permute-done((f32[64]{0:T(128)S(1)}, f32[64]{0:T(128)S(1)}, u32[]{:S(2)}, u32[]{:S(2)}) %collective-permute-start.24) | collective-permute-done | bytes 288 | tf_op jit(solution)/shard_map/ppermute | solution.py:34
  132.3 2.5 %collective-permute-start.26 = (f32[64]{0:T(128)S(1)}, f32[64]{0:T(128)S(1)}, u32[]{:S(2)}, u32[]{:S(2)}) collective-permute-start(f32[64]{0:T(128)S(1)} %add.305), channel_id=1, source_target_pairs={{0,8},{4,12},{8,0},{12,4},{16,24},{20,28},{24,16},{28,20},{1,9},{5... | collective-permute-start | bytes 776 | tf_op jit(solution)/shard_map/ppermute | solution.py:34
  134.8 1.5 %collective-permute-done.26 = f32[64]{0:T(128)S(1)} collective-permute-done((f32[64]{0:T(128)S(1)}, f32[64]{0:T(128)S(1)}, u32[]{:S(2)}, u32[]{:S(2)}) %collective-permute-start.26) | collective-permute-done | bytes 288 | tf_op jit(solution)/shard_map/ppermute | solution.py:34
  136.4 3.2 %collective-permute-start.27 = (f32[64]{0:T(128)S(1)}, f32[64]{0:T(128)S(1)}, u32[]{:S(2)}, u32[]{:S(2)}) collective-permute-start(f32[64]{0:T(128)S(1)} %add.306), channel_id=1, source_target_pairs={{0,16},{4,20},{8,24},{12,28},{16,0},{20,4},{24,8},{28,12},{1,17},{... | collective-permute-start | bytes 776 | tf_op jit(solution)/shard_map/ppermute | solution.py:34
  (147 shorter events, 37.0 us)
Async XLA Ops:
  0.6 25.5 %copy-start = (bf16[1024,1024]{1,0:T(8,128)(2,1)S(1)}, bf16[1024,1024]{1,0:T(8,128)(2,1)}, u32[]{:S(2)}) copy-start(bf16[1024,1024]{1,0:T(8,128)(2,1)} %param.25) | copy-start | bytes 6291460
  2.2 3.8 %collective-permute-start = (bf16[69,2,128]{0,2,1:T(8,128)(2,1)S(1)}, bf16[69,2,128]{0,2,1:T(8,128)(2,1)S(1)}, u32[]{:S(2)}, u32[]{:S(2)}) collective-permute-start(bf16[69,2,128]{0,2,1:T(8,128)(2,1)S(1)} %get-tuple-element.59), channel_id=1, source_target_pairs={{0,4},{4,8},{8,12},{12,16},{16,20},{20,24},{24,28},{1,5},{5,9},{9,... | collective-permute-start | bytes 105992 | tf_op jit(solution)/shard_map/ppermute | solution.py:20
  4.7 5.3 %collective-permute-start.1 = (bf16[69,2,128]{0,2,1:T(8,128)(2,1)S(1)}, bf16[69,2,128]{0,2,1:T(8,128)(2,1)S(1)}, u32[]{:S(2)}, u32[]{:S(2)}) collective-permute-start(bf16[69,2,128]{0,2,1:T(8,128)(2,1)S(1)} %get-tuple-element.60), channel_id=1, source_target_pairs={{4,0},{8,4},{12,8},{16,12},{20,16},{24,20},{28,24},{5,1},{9,5},{13... | collective-permute-start | bytes 105992 | tf_op jit(solution)/shard_map/ppermute | solution.py:21
  9.9 5.5 %collective-permute-start.2 = (bf16[69,20,2]{0,2,1:T(2,128)(2,1)S(1)}, bf16[69,20,2]{0,2,1:T(2,128)(2,1)S(1)}, u32[]{:S(2)}, u32[]{:S(2)}) collective-permute-start(bf16[69,20,2]{0,2,1:T(2,128)(2,1)S(1)} %get-tuple-element.45), channel_id=1, source_target_pairs={{0,1},{1,2},{2,3},{3,0},{4,5},{5,6},{6,7},{7,4},{8,9},{9,10},{10,1... | collective-permute-start | bytes 16568 | tf_op jit(solution)/shard_map/ppermute | solution.py:25
  11.6 3.9 %collective-permute-start.3 = (bf16[69,20,2]{0,2,1:T(2,128)(2,1)S(1)}, bf16[69,20,2]{0,2,1:T(2,128)(2,1)S(1)}, u32[]{:S(2)}, u32[]{:S(2)}) collective-permute-start(bf16[69,20,2]{0,2,1:T(2,128)(2,1)S(1)} %get-tuple-element.46), channel_id=1, source_target_pairs={{1,0},{2,1},{3,2},{0,3},{5,4},{6,5},{7,6},{4,7},{9,8},{10,9},{11,1... | collective-permute-start | bytes 16568 | tf_op jit(solution)/shard_map/ppermute | solution.py:26
  30.0 9.0 %collective-permute-start.4 = (bf16[3,128,256]{2,1,0:T(8,128)(2,1)S(1)}, bf16[3,128,256]{2,1,0:T(8,128)(2,1)S(1)}, u32[]{:S(2)}, u32[]{:S(2)}) collective-permute-start(bf16[3,128,256]{2,1,0:T(8,128)(2,1)S(1)} %get-tuple-element.44), channel_id=1, source_target_pairs={{0,1},{1,2},{2,3},{3,0},{4,5},{5,6},{6,7},{7,4},{8,9},{9,10},{10,1... | collective-permute-start | bytes 589832 | tf_op jit(solution)/shard_map/ppermute | solution.py:145
  31.4 16.6 %collective-permute-start.5 = (bf16[3,128,256]{2,1,0:T(8,128)(2,1)S(1)}, bf16[3,128,256]{2,1,0:T(8,128)(2,1)S(1)}, u32[]{:S(2)}, u32[]{:S(2)}) collective-permute-start(bf16[3,128,256]{2,1,0:T(8,128)(2,1)S(1)} %get-tuple-element.43), channel_id=1, source_target_pairs={{0,2},{1,3},{2,0},{3,1},{4,6},{5,7},{6,4},{7,5},{8,10},{9,11},{10,... | collective-permute-start | bytes 589832 | tf_op jit(solution)/shard_map/ppermute | solution.py:145
  34.5 13.6 %collective-permute-start.6 = (bf16[3,128,256]{2,1,0:T(8,128)(2,1)S(1)}, bf16[3,128,256]{2,1,0:T(8,128)(2,1)S(1)}, u32[]{:S(2)}, u32[]{:S(2)}) collective-permute-start(bf16[3,128,256]{2,1,0:T(8,128)(2,1)S(1)} %get-tuple-element.42), channel_id=1, source_target_pairs={{0,3},{1,0},{2,1},{3,2},{4,7},{5,4},{6,5},{7,6},{8,11},{9,8},{10,9... | collective-permute-start | bytes 589832 | tf_op jit(solution)/shard_map/ppermute | solution.py:145
  48.2 1.8 %collective-permute-start.7 = (bf16[3,512,128]{2,1,0:T(8,128)(2,1)S(1)}, bf16[3,512,128]{2,1,0:T(8,128)(2,1)S(1)}, u32[]{:S(2)}, u32[]{:S(2)}) collective-permute-start(bf16[3,512,128]{2,1,0:T(8,128)(2,1)S(1)} %get-tuple-element.39), channel_id=1, source_target_pairs={{0,4},{4,0},{8,12},{12,8},{16,20},{20,16},{24,28},{28,24},{1,5},{5... | collective-permute-start | bytes 1179656 | tf_op jit(solution)/shard_map/ppermute | solution.py:219
  50.8 15.2 %collective-permute-start.8 = (bf16[2,1024,128]{2,1,0:T(8,128)(2,1)}, bf16[2,1024,128]{2,1,0:T(8,128)(2,1)S(1)}, u32[]{:S(2)}, u32[]{:S(2)}) collective-permute-start(bf16[2,1024,128]{2,1,0:T(8,128)(2,1)} %pad_maximum_fusion.6), channel_id=1, source_target_pairs={{0,8},{4,12},{8,0},{12,4},{16,24},{20,28},{24,16},{28,20},{1,9},{5... | collective-permute-start | bytes 1572872 | tf_op jit(solution)/shard_map/ppermute | solution.py:226
  53.6 14.1 %collective-permute-start.9 = (bf16[2,1024,128]{2,1,0:T(8,128)(2,1)}, bf16[2,1024,128]{2,1,0:T(8,128)(2,1)}, u32[]{:S(2)}, u32[]{:S(2)}) collective-permute-start(bf16[2,1024,128]{2,1,0:T(8,128)(2,1)} %pad_maximum_fusion.6), channel_id=1, source_target_pairs={{0,16},{4,20},{8,24},{12,28},{16,0},{20,4},{24,8},{28,12},{1,17},{... | collective-permute-start | bytes 1572872 | tf_op jit(solution)/shard_map/ppermute | solution.py:227
  66.0 13.0 %collective-permute-start.11 = (bf16[2,512,128]{2,1,0:T(8,128)(2,1)S(1)}, bf16[2,512,128]{2,1,0:T(8,128)(2,1)S(1)}, u32[]{:S(2)}, u32[]{:S(2)}) collective-permute-start(bf16[2,512,128]{2,1,0:T(8,128)(2,1)S(1)} %slice.384), channel_id=1, source_target_pairs={{0,16},{4,20},{8,24},{12,28},{16,0},{20,4},{24,8},{28,12},{1,17},{... | collective-permute-start | bytes 786440 | tf_op jit(solution)/shard_map/ppermute | solution.py:230
  68.6 10.5 %collective-permute-start.10 = (bf16[2,512,128]{2,1,0:T(8,128)(2,1)S(1)}, bf16[2,512,128]{2,1,0:T(8,128)(2,1)S(1)}, u32[]{:S(2)}, u32[]{:S(2)}) collective-permute-start(bf16[2,512,128]{2,1,0:T(8,128)(2,1)S(1)} %slice.382), channel_id=1, source_target_pairs={{0,8},{4,12},{8,0},{12,4},{16,24},{20,28},{24,16},{28,20},{1,9},{5... | collective-permute-start | bytes 786440 | tf_op jit(solution)/shard_map/ppermute | solution.py:229
  83.9 15.7 %copy-start.5 = (bf16[1024,1024]{1,0:T(8,128)(2,1)S(1)}, bf16[1024,1024]{1,0:T(8,128)(2,1)}, u32[]{:S(2)}) copy-start(bf16[1024,1024]{1,0:T(8,128)(2,1)} %param.26) | copy-start | bytes 6291460
  84.0 8.1 %collective-permute-start.12 = (bf16[128,128]{1,0:T(8,128)(2,1)S(1)}, bf16[128,128]{1,0:T(8,128)(2,1)S(1)}, u32[]{:S(2)}, u32[]{:S(2)}) collective-permute-start(bf16[128,128]{1,0:T(8,128)(2,1)S(1)} %get-tuple-element.67), channel_id=1, source_target_pairs={{0,4},{1,5},{2,6},{3,7},{4,0},{5,1},{6,2},{7,3},{8,12},{9,13},{10,... | collective-permute-start | bytes 98312 | tf_op jit(solution)/shard_map/ppermute | solution.py:267
  84.1 10.0 %collective-permute-start.13 = (bf16[128,128]{1,0:T(8,128)(2,1)S(1)}, bf16[128,128]{1,0:T(8,128)(2,1)S(1)}, u32[]{:S(2)}, u32[]{:S(2)}) collective-permute-start(bf16[128,128]{1,0:T(8,128)(2,1)S(1)} %get-tuple-element.66), channel_id=1, source_target_pairs={{1,0},{2,1},{3,2},{0,3},{5,4},{6,5},{7,6},{4,7},{9,8},{10,9},{11,1... | collective-permute-start | bytes 98312 | tf_op jit(solution)/shard_map/ppermute | solution.py:264
  89.6 4.5 %collective-permute-start.14 = (bf16[128,128]{1,0:T(8,128)(2,1)S(1)}, bf16[128,128]{1,0:T(8,128)(2,1)S(1)}, u32[]{:S(2)}, u32[]{:S(2)}) collective-permute-start(bf16[128,128]{1,0:T(8,128)(2,1)S(1)} %get-tuple-element.65), channel_id=1, source_target_pairs={{0,7},{1,4},{2,5},{3,6},{4,3},{5,0},{6,1},{7,2},{8,15},{9,12},{10,... | collective-permute-start | bytes 98312 | tf_op jit(solution)/shard_map/ppermute | solution.py:267
  89.7 5.1 %collective-permute-start.15 = (bf16[128,128]{1,0:T(8,128)(2,1)S(1)}, bf16[128,128]{1,0:T(8,128)(2,1)S(1)}, u32[]{:S(2)}, u32[]{:S(2)}) collective-permute-start(bf16[128,128]{1,0:T(8,128)(2,1)S(1)} %get-tuple-element.64), channel_id=1, source_target_pairs={{2,0},{3,1},{0,2},{1,3},{6,4},{7,5},{4,6},{5,7},{10,8},{11,9},{8,1... | collective-permute-start | bytes 98312 | tf_op jit(solution)/shard_map/ppermute | solution.py:264
  90.4 4.9 %collective-permute-start.16 = (bf16[128,128]{1,0:T(8,128)(2,1)S(1)}, bf16[128,128]{1,0:T(8,128)(2,1)S(1)}, u32[]{:S(2)}, u32[]{:S(2)}) collective-permute-start(bf16[128,128]{1,0:T(8,128)(2,1)S(1)} %get-tuple-element.63), channel_id=1, source_target_pairs={{0,6},{1,7},{2,4},{3,5},{4,2},{5,3},{6,0},{7,1},{8,14},{9,15},{10,... | collective-permute-start | bytes 98312 | tf_op jit(solution)/shard_map/ppermute | solution.py:267
  92.1 5.8 %collective-permute-start.17 = (bf16[128,128]{1,0:T(8,128)(2,1)S(1)}, bf16[128,128]{1,0:T(8,128)(2,1)S(1)}, u32[]{:S(2)}, u32[]{:S(2)}) collective-permute-start(bf16[128,128]{1,0:T(8,128)(2,1)S(1)} %get-tuple-element.62), channel_id=1, source_target_pairs={{3,0},{0,1},{1,2},{2,3},{7,4},{4,5},{5,6},{6,7},{11,8},{8,9},{9,10... | collective-permute-start | bytes 98312 | tf_op jit(solution)/shard_map/ppermute | solution.py:264
  94.1 5.2 %collective-permute-start.18 = (bf16[128,128]{1,0:T(8,128)(2,1)S(1)}, bf16[128,128]{1,0:T(8,128)(2,1)S(1)}, u32[]{:S(2)}, u32[]{:S(2)}) collective-permute-start(bf16[128,128]{1,0:T(8,128)(2,1)S(1)} %get-tuple-element.61), channel_id=1, source_target_pairs={{0,5},{1,6},{2,7},{3,4},{4,1},{5,2},{6,3},{7,0},{8,13},{9,14},{10,... | collective-permute-start | bytes 98312 | tf_op jit(solution)/shard_map/ppermute | solution.py:267
  104.1 3.4 %collective-permute-start.19 = (bf16[128,1,128]{2,0,1:T(8,128)(2,1)S(1)}, bf16[128,1,128]{2,0,1:T(8,128)(2,1)S(1)}, u32[]{:S(2)}, u32[]{:S(2)}) collective-permute-start(bf16[128,1,128]{2,0,1:T(8,128)(2,1)S(1)} %get-tuple-element.53), channel_id=1, source_target_pairs={{0,4},{4,8},{8,12},{12,16},{16,20},{20,24},{24,28},{1,5},{5,9},{9,... | collective-permute-start | bytes 98312 | tf_op jit(solution)/shard_map/ppermute | solution.py:20
  106.1 4.3 %collective-permute-start.20 = (bf16[128,1,128]{2,0,1:T(8,128)(2,1)S(1)}, bf16[128,1,128]{2,0,1:T(8,128)(2,1)S(1)}, u32[]{:S(2)}, u32[]{:S(2)}) collective-permute-start(bf16[128,1,128]{2,0,1:T(8,128)(2,1)S(1)} %get-tuple-element.54), channel_id=1, source_target_pairs={{4,0},{8,4},{12,8},{16,12},{20,16},{24,20},{28,24},{5,1},{9,5},{13... | collective-permute-start | bytes 98312 | tf_op jit(solution)/shard_map/ppermute | solution.py:21
  111.1 5.5 %collective-permute-start.21 = (bf16[128,18,1]{0,1,2:T(8,128)(2,1)S(1)}, bf16[128,18,1]{0,1,2:T(8,128)(2,1)S(1)}, u32[]{:S(2)}, u32[]{:S(2)}) collective-permute-start(bf16[128,18,1]{0,1,2:T(8,128)(2,1)S(1)} %copy.62), channel_id=1, source_target_pairs={{0,1},{1,2},{2,3},{3,0},{4,5},{5,6},{6,7},{7,4},{8,9},{9,10},{10,1... | collective-permute-start | bytes 13832 | tf_op jit(solution)/shard_map/ppermute | solution.py:25
  111.4 5.5 %collective-permute-start.22 = (bf16[128,18,1]{0,1,2:T(8,128)(2,1)S(1)}, bf16[128,18,1]{0,1,2:T(8,128)(2,1)S(1)}, u32[]{:S(2)}, u32[]{:S(2)}) collective-permute-start(bf16[128,18,1]{0,1,2:T(8,128)(2,1)S(1)} %copy.65), channel_id=1, source_target_pairs={{1,0},{2,1},{3,2},{0,3},{5,4},{6,5},{7,6},{4,7},{9,8},{10,9},{11,1... | collective-permute-start | bytes 13832 | tf_op jit(solution)/shard_map/ppermute | solution.py:26
  121.5 20.2 %copy-start.1 = (bf16[1024,1024]{1,0:T(8,128)(2,1)S(1)}, bf16[1024,1024]{1,0:T(8,128)(2,1)}, u32[]{:S(2)}) copy-start(bf16[1024,1024]{1,0:T(8,128)(2,1)} %param.25) | copy-start | bytes 6291460
  122.1 19.0 %copy-start.14 = (s32[64]{0:T(128)S(1)}, s32[64]{0:T(128)}, u32[]{:S(2)}) copy-start(s32[64]{0:T(128)} %param.18) | copy-start | bytes 772
  123.2 3.6 %collective-permute-start.23 = (f32[64]{0:T(128)S(1)}, f32[64]{0:T(128)S(1)}, u32[]{:S(2)}, u32[]{:S(2)}) collective-permute-start(f32[64]{0:T(128)S(1)} %fusion.40), channel_id=1, source_target_pairs={{0,1},{1,0},{2,3},{3,2},{4,5},{5,4},{6,7},{7,6},{8,9},{9,8},{10,11... | collective-permute-start | bytes 776 | tf_op jit(solution)/shard_map/ppermute | solution.py:34
  126.7 4.5 %collective-permute-start.24 = (f32[64]{0:T(128)S(1)}, f32[64]{0:T(128)S(1)}, u32[]{:S(2)}, u32[]{:S(2)}) collective-permute-start(f32[64]{0:T(128)S(1)} %add.303), channel_id=1, source_target_pairs={{0,2},{1,3},{2,0},{3,1},{4,6},{5,7},{6,4},{7,5},{8,10},{9,11},{10,... | collective-permute-start | bytes 776 | tf_op jit(solution)/shard_map/ppermute | solution.py:34
  131.2 1.1 collective-permute-start.25
  132.3 4.0 %collective-permute-start.26 = (f32[64]{0:T(128)S(1)}, f32[64]{0:T(128)S(1)}, u32[]{:S(2)}, u32[]{:S(2)}) collective-permute-start(f32[64]{0:T(128)S(1)} %add.305), channel_id=1, source_target_pairs={{0,8},{4,12},{8,0},{12,4},{16,24},{20,28},{24,16},{28,20},{1,9},{5... | collective-permute-start | bytes 776 | tf_op jit(solution)/shard_map/ppermute | solution.py:34
  136.4 4.7 %collective-permute-start.27 = (f32[64]{0:T(128)S(1)}, f32[64]{0:T(128)S(1)}, u32[]{:S(2)}, u32[]{:S(2)}) collective-permute-start(f32[64]{0:T(128)S(1)} %add.306), channel_id=1, source_target_pairs={{0,16},{4,20},{8,24},{12,28},{16,0},{20,4},{24,8},{28,12},{1,17},{... | collective-permute-start | bytes 776 | tf_op jit(solution)/shard_map/ppermute | solution.py:34
  (12 other events, 34.9 us)

commit v17 on v14

--- a/solution.py
+++ b/solution.py
@@ -249,7 +249,10 @@
         for group in key_groups
         if group
     ]
-    pair_attended = merge_parts(parts)
+    half_rows = pair_queries.shape[0] // 2
+    partner_rows = merge_parts([tuple(x[half_rows:] for x in part) for part in parts])
+    own_rows = merge_parts([tuple(x[:half_rows] for x in part) for part in parts])
+    pair_attended = jnp.concatenate([own_rows, partner_rows], axis=0)
     token_count = spread.shape[1]
     own_part = pair_attended[:token_count]
     returned = lax.ppermute(pair_attended[token_count:], "lat", partner)

time: 141 us -> 141 us (level)
  no operation moved by 1% of the time
where the time goes in v17:
time: 141 us
  waiting for transfers between devices  48.2 us (34%)
  starting transfers between devices  39.5 us (28%)
  Pallas kernels  17.9 us (13%)
  matrix products  17.7 us (13%)
  local copies, waits for them, and re-layouts  11.9 us (8%)
  other arithmetic  4.08 us (3%)
    pallas_call x3, Pallas kernels, attend_part(): pl.pallas_call(functools.partial(attention_kernel, head_size=head_size, c...  17.9 us
    ppermute x3, waiting for transfers between devices, exchange_blocks(): lax.ppermute(outgoing, axis, [(i, (i + shift) % size) for i in range(size)])  12.7 us
    dot_general x27, matrix products, convolution_kernel_taps(): jnp.einsum('oc,cyx->oyx', weight[tap_index], window, preferred_element_ty...  10.7 us
    ppermute x5, starting transfers between devices, butterfly_sum(): value = value + lax.ppermute(value, axis, partner)  8.63 us
    ppermute x5, waiting for transfers between devices, butterfly_sum(): value = value + lax.ppermute(value, axis, partner)  8.48 us
    ppermute x1, waiting for transfers between devices, on_device(): from_x = lax.ppermute(key_value, 'lat', across_x)  7.77 us
    ppermute x2, waiting for transfers between devices, halo_padded(): from_below = lax.ppermute(array[:, :width], 'lat', up)  7.65 us
    ppermute x3, waiting for transfers between devices, return_blocks(): lax.ppermute(blocks[shift], axis, [((i + shift) % size, i) for i in range...  6.44 us
  transfers between devices with their start and end apart: 25, of which 16 were waited for; matrix products, arithmetic and copies ran while one was open for 3% of the time, Pallas kernels for 10%

profile of v17, /device:TPU:0, one launch (start us, length us, event | category | flops | bytes accessed | tf_op | source)
XLA Modules:
  0.0 140.6 jit_solution(2895694924171753211)
XLA Ops:
  0.6 1.5 %copy.49 = bf16[69,16,128]{0,2,1:T(8,128)(2,1)S(1)} copy(bf16[69,16,128]{2,1,0:T(8,128)(2,1)} %param.15) | data formatting | bytes 565248 | tf_op args[0]
  2.2 2.5 %collective-permute-start = (bf16[69,2,128]{0,2,1:T(8,128)(2,1)S(1)}, bf16[69,2,128]{0,2,1:T(8,128)(2,1)S(1)}, u32[]{:S(2)}, u32[]{:S(2)}) collective-permute-start(bf16[69,2,128]{0,2,1:T(8,128)(2,1)S(1)} %get-tuple-element.61), channel_id=1, source_target_pairs={{0,4},{4,8},{8,12},{12,16},{16,20},{20,24},{24,28},{1,5},{5,9},{9,... | collective-permute-start | bytes 105992 | tf_op jit(solution)/shard_map/ppermute | solution.py:20
  4.7 1.3 collective-permute-start.1
  6.0 3.9 %collective-permute-done.1 = bf16[69,2,128]{0,2,1:T(8,128)(2,1)S(1)} collective-permute-done((bf16[69,2,128]{0,2,1:T(8,128)(2,1)S(1)}, bf16[69,2,128]{0,2,1:T(8,128)(2,1)S(1)}, u32[]{:S(2)}, u32[]{:S(2)}) %collective-permute-start.1) | collective-permute-done | bytes 35360 | tf_op jit(solution)/shard_map/ppermute | solution.py:21
  9.9 1.6 %collective-permute-start.2 = (bf16[69,20,2]{0,2,1:T(2,128)(2,1)S(1)}, bf16[69,20,2]{0,2,1:T(2,128)(2,1)S(1)}, u32[]{:S(2)}, u32[]{:S(2)}) collective-permute-start(bf16[69,20,2]{0,2,1:T(2,128)(2,1)S(1)} %get-tuple-element.47), channel_id=1, source_target_pairs={{0,1},{1,2},{2,3},{3,0},{4,5},{5,6},{6,7},{7,4},{8,9},{9,10},{10,1... | collective-permute-start | bytes 16568 | tf_op jit(solution)/shard_map/ppermute | solution.py:25
  11.6 2.2 %collective-permute-start.3 = (bf16[69,20,2]{0,2,1:T(2,128)(2,1)S(1)}, bf16[69,20,2]{0,2,1:T(2,128)(2,1)S(1)}, u32[]{:S(2)}, u32[]{:S(2)}) collective-permute-start(bf16[69,20,2]{0,2,1:T(2,128)(2,1)S(1)} %get-tuple-element.48), channel_id=1, source_target_pairs={{1,0},{2,1},{3,2},{0,3},{5,4},{6,5},{7,6},{4,7},{9,8},{10,9},{11,1... | collective-permute-start | bytes 16568 | tf_op jit(solution)/shard_map/ppermute | solution.py:26
  13.8 1.6 %collective-permute-done.2 = bf16[69,20,2]{0,2,1:T(2,128)(2,1)S(1)} collective-permute-done((bf16[69,20,2]{0,2,1:T(2,128)(2,1)S(1)}, bf16[69,20,2]{0,2,1:T(2,128)(2,1)S(1)}, u32[]{:S(2)}, u32[]{:S(2)}) %collective-permute-start.2) | collective-permute-done | bytes 5552 | tf_op jit(solution)/shard_map/ppermute | solution.py:25
  30.0 1.4 collective-permute-start.4
  31.4 3.1 %collective-permute-start.5 = (bf16[3,128,256]{2,1,0:T(8,128)(2,1)S(1)}, bf16[3,128,256]{2,1,0:T(8,128)(2,1)S(1)}, u32[]{:S(2)}, u32[]{:S(2)}) collective-permute-start(bf16[3,128,256]{2,1,0:T(8,128)(2,1)S(1)} %get-tuple-element.45), channel_id=1, source_target_pairs={{0,2},{1,3},{2,0},{3,1},{4,6},{5,7},{6,4},{7,5},{8,10},{9,11},{10,... | collective-permute-start | bytes 589832 | tf_op jit(solution)/shard_map/ppermute | solution.py:145
  35.3 3.6 %collective-permute-done.4 = bf16[3,128,256]{2,1,0:T(8,128)(2,1)S(1)} collective-permute-done((bf16[3,128,256]{2,1,0:T(8,128)(2,1)S(1)}, bf16[3,128,256]{2,1,0:T(8,128)(2,1)S(1)}, u32[]{:S(2)}, u32[]{:S(2)}) %collective-permute-start.4) | collective-permute-done | bytes 196640 | tf_op jit(solution)/shard_map/ppermute | solution.py:145
  39.0 9.1 %collective-permute-done.5 = bf16[3,128,256]{2,1,0:T(8,128)(2,1)S(1)} collective-permute-done((bf16[3,128,256]{2,1,0:T(8,128)(2,1)S(1)}, bf16[3,128,256]{2,1,0:T(8,128)(2,1)S(1)}, u32[]{:S(2)}, u32[]{:S(2)}) %collective-permute-start.5) | collective-permute-done | bytes 196640 | tf_op jit(solution)/shard_map/ppermute | solution.py:145
  48.4 1.6 %collective-permute-done.7 = bf16[3,512,128]{2,1,0:T(8,128)(2,1)S(1)} collective-permute-done((bf16[3,512,128]{2,1,0:T(8,128)(2,1)S(1)}, bf16[3,512,128]{2,1,0:T(8,128)(2,1)S(1)}, u32[]{:S(2)}, u32[]{:S(2)}) %collective-permute-start.7) | collective-permute-done | bytes 393248 | tf_op jit(solution)/shard_map/ppermute | solution.py:219
  50.8 2.8 %collective-permute-start.8 = (bf16[2,1024,128]{2,1,0:T(8,128)(2,1)}, bf16[2,1024,128]{2,1,0:T(8,128)(2,1)S(1)}, u32[]{:S(2)}, u32[]{:S(2)}) collective-permute-start(bf16[2,1024,128]{2,1,0:T(8,128)(2,1)} %pad_maximum_fusion.6), channel_id=1, source_target_pairs={{0,8},{4,12},{8,0},{12,4},{16,24},{20,28},{24,16},{28,20},{1,9},{5... | collective-permute-start | bytes 1572872 | tf_op jit(solution)/shard_map/ppermute | solution.py:226
  53.7 4.5 %shard_map.166 = (f32[1024,128]{1,0:T(8,128)S(1)}, f32[1024,128]{1,0:T(8,128)S(1)}, f32[1024,128]{1,0:T(8,128)S(1)}) custom-call(f32[2]{0:T(128)S(1)} %dynamic-slice_multiply_fusion.scale_ref, bf16[1024,128]{1,0:T(8,128)(2,1)S(1)} %get-tuple-element.39.q_ref, bf16[1024,128]{1,0:T(8,128)(2,1)S(1)} %get-tuple-element.40.refs_0_, ...), custom_call_target="tpu_custom_call" | custom-call | flops 536870912 | bytes 2359296 | tf_op jit(solution)/shard_map/pallas_call | solution.py:111
  58.2 7.8 %collective-permute-done.8 = bf16[2,1024,128]{2,1,0:T(8,128)(2,1)S(1)} collective-permute-done((bf16[2,1024,128]{2,1,0:T(8,128)(2,1)}, bf16[2,1024,128]{2,1,0:T(8,128)(2,1)S(1)}, u32[]{:S(2)}, u32[]{:S(2)}) %collective-permute-start.8) | collective-permute-done | bytes 524320 | tf_op jit(solution)/shard_map/ppermute | solution.py:226
  66.0 1.6 %collective-permute-start.11 = (bf16[2,512,128]{2,1,0:T(8,128)(2,1)S(1)}, bf16[2,512,128]{2,1,0:T(8,128)(2,1)S(1)}, u32[]{:S(2)}, u32[]{:S(2)}) collective-permute-start(bf16[2,512,128]{2,1,0:T(8,128)(2,1)S(1)} %slice.440), channel_id=1, source_target_pairs={{0,16},{4,20},{8,24},{12,28},{16,0},{20,4},{24,8},{28,12},{1,17},{... | collective-permute-start | bytes 786440 | tf_op jit(solution)/shard_map/ppermute | solution.py:230
  70.1 9.0 %shard_map.167 = (f32[1024,128]{1,0:T(8,128)S(1)}, f32[1024,128]{1,0:T(8,128)S(1)}, f32[1024,128]{1,0:T(8,128)S(1)}) custom-call(f32[2]{0:T(128)S(1)} %dynamic-slice_multiply_fusion.scale_ref, bf16[1024,128]{1,0:T(8,128)(2,1)S(1)} %get-tuple-element.39.q_ref, bf16[1024,128]{1,0:T(8,128)(2,1)S(1)} %get-tuple-element.60.refs_0_, ...), custom_call_target="tpu_custom_call" | custom-call | flops 1073741824 | bytes 2883584 | tf_op jit(solution)/shard_map/pallas_call | solution.py:111
  79.2 4.3 %shard_map.168 = (f32[1024,128]{1,0:T(8,128)S(1)}, f32[1024,128]{1,0:T(8,128)S(1)}, f32[1024,128]{1,0:T(8,128)S(1)}) custom-call(f32[2]{0:T(128)S(1)} %dynamic-slice_multiply_fusion.scale_ref, bf16[1024,128]{1,0:T(8,128)(2,1)S(1)} %get-tuple-element.39.q_ref, bf16[512,128]{1,0:T(8,128)(2,1)S(1)} %get-tuple-element.69.refs_0_, ...), custom_call_target="tpu_custom_call" | custom-call | flops 536870912 | bytes 2359296 | tf_op jit(solution)/shard_map/pallas_call | solution.py:111
  84.0 1.3 collective-permute-done.12
  85.5 5.6 %collective-permute-start.13 = (bf16[128,256]{1,0:T(8,128)(2,1)S(1)}, bf16[128,256]{1,0:T(8,128)(2,1)S(1)}, u32[]{:S(2)}, u32[]{:S(2)}) collective-permute-start(bf16[128,256]{1,0:T(8,128)(2,1)S(1)} %get-tuple-element.65), channel_id=1, source_target_pairs={{1,0},{2,1},{3,2},{0,3},{5,4},{6,5},{7,6},{4,7},{9,8},{10,9},{11,1... | collective-permute-start | bytes 196616 | tf_op jit(solution)/shard_map/ppermute | solution.py:153
  91.7 1.8 %collective-permute-done.13 = bf16[128,256]{1,0:T(8,128)(2,1)S(1)} collective-permute-done((bf16[128,256]{1,0:T(8,128)(2,1)S(1)}, bf16[128,256]{1,0:T(8,128)(2,1)S(1)}, u32[]{:S(2)}, u32[]{:S(2)}) %collective-permute-start.13) | collective-permute-done | bytes 65568 | tf_op jit(solution)/shard_map/ppermute | solution.py:153
  93.5 4.6 %collective-permute-done.14 = bf16[128,256]{1,0:T(8,128)(2,1)S(1)} collective-permute-done((bf16[128,256]{1,0:T(8,128)(2,1)S(1)}, bf16[128,256]{1,0:T(8,128)(2,1)S(1)}, u32[]{:S(2)}, u32[]{:S(2)}) %collective-permute-start.14) | collective-permute-done | bytes 65568 | tf_op jit(solution)/shard_map/ppermute | solution.py:153
  98.9 3.4 %fusion.58 = bf16[128,4,4,32,4]{0,3,4,2,1:T(8,128)(2,1)S(1)} fusion(bf16[4,32,1024,1,1]{2,1,4,3,0:T(8,128)(2,1)S(1)} %bitcast.275, bf16[1024,4,4,128]{3,2,1,0:T(4,128)(2,1)} %param.28), kind=kOutput, calls=%fused_computation.74 | convolution fusion | flops 539230208 | bytes 4980736 | tf_op jit(solution)/shard_map/pqd,dabh->hpaqb/dot_general | solution.py:274
  105.6 3.7 %collective-permute-done.17 = bf16[128,1,128]{2,0,1:T(8,128)(2,1)S(1)} collective-permute-done((bf16[128,1,128]{2,0,1:T(8,128)(2,1)S(1)}, bf16[128,1,128]{2,0,1:T(8,128)(2,1)S(1)}, u32[]{:S(2)}, u32[]{:S(2)}) %collective-permute-start.17) | collective-permute-done | bytes 32800 | tf_op jit(solution)/shard_map/ppermute | solution.py:21
  110.3 4.1 %collective-permute-start.19 = (bf16[128,18,1]{0,1,2:T(8,128)(2,1)S(1)}, bf16[128,18,1]{0,1,2:T(8,128)(2,1)S(1)}, u32[]{:S(2)}, u32[]{:S(2)}) collective-permute-start(bf16[128,18,1]{0,1,2:T(8,128)(2,1)S(1)} %copy.65), channel_id=1, source_target_pairs={{1,0},{2,1},{3,2},{0,3},{5,4},{6,5},{7,6},{4,7},{9,8},{10,9},{11,1... | collective-permute-start | bytes 13832 | tf_op jit(solution)/shard_map/ppermute | solution.py:26
  116.9 1.8 %maximum_maximum_fusion = (bf16[128,18,129]{2,0,1:T(8,128)(2,1)S(1)}, bf16[128,18,129]{2,0,1:T(8,128)(2,1)S(1)}) fusion(bf16[128,1,128]{2,0,1:T(8,128)(2,1)S(1)} %collective-permute-done.17, bf16[128,16,128]{2,0,1:T(8,128)(2,1)S(1)} %copy.59, bf16[128,1,128]{2,0,1:T(8,128)(2,1)S(1)} %collective-permute-done.16, bf16[128,18,1]{2,0,1:T(8,128)(2,1)S(1)} %copy.63, ...), kind=kLoop, calls=%fused_computation.54 | loop fusion | flops 4755456 | bytes 1787904 | tf_op jit(solution)/shard_map/concatenate | solution.py:27
  122.4 3.2 %collective-permute-done.20 = f32[64]{0:T(128)S(1)} collective-permute-done((f32[64]{0:T(128)S(1)}, f32[64]{0:T(128)S(1)}, u32[]{:S(2)}, u32[]{:S(2)}) %collective-permute-start.20) | collective-permute-done | bytes 288 | tf_op jit(solution)/shard_map/ppermute | solution.py:34
  125.6 2.6 %collective-permute-start.21 = (f32[64]{0:T(128)S(1)}, f32[64]{0:T(128)S(1)}, u32[]{:S(2)}, u32[]{:S(2)}) collective-permute-start(f32[64]{0:T(128)S(1)} %add.319), channel_id=1, source_target_pairs={{0,2},{1,3},{2,0},{3,1},{4,6},{5,7},{6,4},{7,5},{8,10},{9,11},{10,... | collective-permute-start | bytes 776 | tf_op jit(solution)/shard_map/ppermute | solution.py:34
  128.2 1.9 %collective-permute-done.21 = f32[64]{0:T(128)S(1)} collective-permute-done((f32[64]{0:T(128)S(1)}, f32[64]{0:T(128)S(1)}, u32[]{:S(2)}, u32[]{:S(2)}) %collective-permute-start.21) | collective-permute-done | bytes 288 | tf_op jit(solution)/shard_map/ppermute | solution.py:34
  131.2 2.5 %collective-permute-start.23 = (f32[64]{0:T(128)S(1)}, f32[64]{0:T(128)S(1)}, u32[]{:S(2)}, u32[]{:S(2)}) collective-permute-start(f32[64]{0:T(128)S(1)} %add.321), channel_id=1, source_target_pairs={{0,8},{4,12},{8,0},{12,4},{16,24},{20,28},{24,16},{28,20},{1,9},{5... | collective-permute-start | bytes 776 | tf_op jit(solution)/shard_map/ppermute | solution.py:34
  133.7 1.5 %collective-permute-done.23 = f32[64]{0:T(128)S(1)} collective-permute-done((f32[64]{0:T(128)S(1)}, f32[64]{0:T(128)S(1)}, u32[]{:S(2)}, u32[]{:S(2)}) %collective-permute-start.23) | collective-permute-done | bytes 288 | tf_op jit(solution)/shard_map/ppermute | solution.py:34
  135.2 3.2 %collective-permute-start.24 = (f32[64]{0:T(128)S(1)}, f32[64]{0:T(128)S(1)}, u32[]{:S(2)}, u32[]{:S(2)}) collective-permute-start(f32[64]{0:T(128)S(1)} %add.322), channel_id=1, source_target_pairs={{0,16},{4,20},{8,24},{12,28},{16,0},{20,4},{24,8},{28,12},{1,17},{... | collective-permute-start | bytes 776 | tf_op jit(solution)/shard_map/ppermute | solution.py:34
  (142 shorter events, 34.6 us)
Async XLA Ops:
  0.6 25.5 %copy-start = (bf16[1024,1024]{1,0:T(8,128)(2,1)S(1)}, bf16[1024,1024]{1,0:T(8,128)(2,1)}, u32[]{:S(2)}) copy-start(bf16[1024,1024]{1,0:T(8,128)(2,1)} %param.25) | copy-start | bytes 6291460
  2.1 13.6 %copy-start.10 = (bf16[9,128,69]{1,2,0:T(8,128)(2,1)S(1)}, bf16[9,128,69]{1,2,0:T(8,128)(2,1)}, u32[]{:S(2)}) copy-start(bf16[9,128,69]{1,2,0:T(8,128)(2,1)} %param.19) | copy-start | bytes 476932
  2.2 3.8 %collective-permute-start = (bf16[69,2,128]{0,2,1:T(8,128)(2,1)S(1)}, bf16[69,2,128]{0,2,1:T(8,128)(2,1)S(1)}, u32[]{:S(2)}, u32[]{:S(2)}) collective-permute-start(bf16[69,2,128]{0,2,1:T(8,128)(2,1)S(1)} %get-tuple-element.61), channel_id=1, source_target_pairs={{0,4},{4,8},{8,12},{12,16},{16,20},{20,24},{24,28},{1,5},{5,9},{9,... | collective-permute-start | bytes 105992 | tf_op jit(solution)/shard_map/ppermute | solution.py:20
  4.7 5.3 %collective-permute-start.1 = (bf16[69,2,128]{0,2,1:T(8,128)(2,1)S(1)}, bf16[69,2,128]{0,2,1:T(8,128)(2,1)S(1)}, u32[]{:S(2)}, u32[]{:S(2)}) collective-permute-start(bf16[69,2,128]{0,2,1:T(8,128)(2,1)S(1)} %get-tuple-element.62), channel_id=1, source_target_pairs={{4,0},{8,4},{12,8},{16,12},{20,16},{24,20},{28,24},{5,1},{9,5},{13... | collective-permute-start | bytes 105992 | tf_op jit(solution)/shard_map/ppermute | solution.py:21
  9.9 5.5 %collective-permute-start.2 = (bf16[69,20,2]{0,2,1:T(2,128)(2,1)S(1)}, bf16[69,20,2]{0,2,1:T(2,128)(2,1)S(1)}, u32[]{:S(2)}, u32[]{:S(2)}) collective-permute-start(bf16[69,20,2]{0,2,1:T(2,128)(2,1)S(1)} %get-tuple-element.47), channel_id=1, source_target_pairs={{0,1},{1,2},{2,3},{3,0},{4,5},{5,6},{6,7},{7,4},{8,9},{9,10},{10,1... | collective-permute-start | bytes 16568 | tf_op jit(solution)/shard_map/ppermute | solution.py:25
  11.6 3.9 %collective-permute-start.3 = (bf16[69,20,2]{0,2,1:T(2,128)(2,1)S(1)}, bf16[69,20,2]{0,2,1:T(2,128)(2,1)S(1)}, u32[]{:S(2)}, u32[]{:S(2)}) collective-permute-start(bf16[69,20,2]{0,2,1:T(2,128)(2,1)S(1)} %get-tuple-element.48), channel_id=1, source_target_pairs={{1,0},{2,1},{3,2},{0,3},{5,4},{6,5},{7,6},{4,7},{9,8},{10,9},{11,1... | collective-permute-start | bytes 16568 | tf_op jit(solution)/shard_map/ppermute | solution.py:26
  30.0 9.0 %collective-permute-start.4 = (bf16[3,128,256]{2,1,0:T(8,128)(2,1)S(1)}, bf16[3,128,256]{2,1,0:T(8,128)(2,1)S(1)}, u32[]{:S(2)}, u32[]{:S(2)}) collective-permute-start(bf16[3,128,256]{2,1,0:T(8,128)(2,1)S(1)} %get-tuple-element.46), channel_id=1, source_target_pairs={{0,1},{1,2},{2,3},{3,0},{4,5},{5,6},{6,7},{7,4},{8,9},{9,10},{10,1... | collective-permute-start | bytes 589832 | tf_op jit(solution)/shard_map/ppermute | solution.py:145
  31.4 16.6 %collective-permute-start.5 = (bf16[3,128,256]{2,1,0:T(8,128)(2,1)S(1)}, bf16[3,128,256]{2,1,0:T(8,128)(2,1)S(1)}, u32[]{:S(2)}, u32[]{:S(2)}) collective-permute-start(bf16[3,128,256]{2,1,0:T(8,128)(2,1)S(1)} %get-tuple-element.45), channel_id=1, source_target_pairs={{0,2},{1,3},{2,0},{3,1},{4,6},{5,7},{6,4},{7,5},{8,10},{9,11},{10,... | collective-permute-start | bytes 589832 | tf_op jit(solution)/shard_map/ppermute | solution.py:145
  34.5 13.6 %collective-permute-start.6 = (bf16[3,128,256]{2,1,0:T(8,128)(2,1)S(1)}, bf16[3,128,256]{2,1,0:T(8,128)(2,1)S(1)}, u32[]{:S(2)}, u32[]{:S(2)}) collective-permute-start(bf16[3,128,256]{2,1,0:T(8,128)(2,1)S(1)} %get-tuple-element.44), channel_id=1, source_target_pairs={{0,3},{1,0},{2,1},{3,2},{4,7},{5,4},{6,5},{7,6},{8,11},{9,8},{10,9... | collective-permute-start | bytes 589832 | tf_op jit(solution)/shard_map/ppermute | solution.py:145
  48.1 5.5 %copy-start.13 = (f32[16]{0:T(128)S(1)}, f32[16]{0:T(128)}, u32[]{:S(2)}) copy-start(f32[16]{0:T(128)} %param.27) | copy-start | bytes 196
  48.2 1.8 %collective-permute-start.7 = (bf16[3,512,128]{2,1,0:T(8,128)(2,1)S(1)}, bf16[3,512,128]{2,1,0:T(8,128)(2,1)S(1)}, u32[]{:S(2)}, u32[]{:S(2)}) collective-permute-start(bf16[3,512,128]{2,1,0:T(8,128)(2,1)S(1)} %get-tuple-element.41), channel_id=1, source_target_pairs={{0,4},{4,0},{8,12},{12,8},{16,20},{20,16},{24,28},{28,24},{1,5},{5... | collective-permute-start | bytes 1179656 | tf_op jit(solution)/shard_map/ppermute | solution.py:219
  50.8 15.2 %collective-permute-start.8 = (bf16[2,1024,128]{2,1,0:T(8,128)(2,1)}, bf16[2,1024,128]{2,1,0:T(8,128)(2,1)S(1)}, u32[]{:S(2)}, u32[]{:S(2)}) collective-permute-start(bf16[2,1024,128]{2,1,0:T(8,128)(2,1)} %pad_maximum_fusion.6), channel_id=1, source_target_pairs={{0,8},{4,12},{8,0},{12,4},{16,24},{20,28},{24,16},{28,20},{1,9},{5... | collective-permute-start | bytes 1572872 | tf_op jit(solution)/shard_map/ppermute | solution.py:226
  53.6 14.1 %collective-permute-start.9 = (bf16[2,1024,128]{2,1,0:T(8,128)(2,1)}, bf16[2,1024,128]{2,1,0:T(8,128)(2,1)}, u32[]{:S(2)}, u32[]{:S(2)}) collective-permute-start(bf16[2,1024,128]{2,1,0:T(8,128)(2,1)} %pad_maximum_fusion.6), channel_id=1, source_target_pairs={{0,16},{4,20},{8,24},{12,28},{16,0},{20,4},{24,8},{28,12},{1,17},{... | collective-permute-start | bytes 1572872 | tf_op jit(solution)/shard_map/ppermute | solution.py:227
  66.0 13.0 %collective-permute-start.11 = (bf16[2,512,128]{2,1,0:T(8,128)(2,1)S(1)}, bf16[2,512,128]{2,1,0:T(8,128)(2,1)S(1)}, u32[]{:S(2)}, u32[]{:S(2)}) collective-permute-start(bf16[2,512,128]{2,1,0:T(8,128)(2,1)S(1)} %slice.440), channel_id=1, source_target_pairs={{0,16},{4,20},{8,24},{12,28},{16,0},{20,4},{24,8},{28,12},{1,17},{... | collective-permute-start | bytes 786440 | tf_op jit(solution)/shard_map/ppermute | solution.py:230
  68.6 10.5 %collective-permute-start.10 = (bf16[2,512,128]{2,1,0:T(8,128)(2,1)S(1)}, bf16[2,512,128]{2,1,0:T(8,128)(2,1)S(1)}, u32[]{:S(2)}, u32[]{:S(2)}) collective-permute-start(bf16[2,512,128]{2,1,0:T(8,128)(2,1)S(1)} %slice.438), channel_id=1, source_target_pairs={{0,8},{4,12},{8,0},{12,4},{16,24},{20,28},{24,16},{28,20},{1,9},{5... | collective-permute-start | bytes 786440 | tf_op jit(solution)/shard_map/ppermute | solution.py:229
  83.9 1.4 %collective-permute-start.12 = (bf16[512,128]{1,0:T(8,128)(2,1)S(1)}, bf16[512,128]{1,0:T(8,128)(2,1)S(1)}, u32[]{:S(2)}, u32[]{:S(2)}) collective-permute-start(bf16[512,128]{1,0:T(8,128)(2,1)S(1)} %get-tuple-element.37), channel_id=1, source_target_pairs={{0,4},{4,0},{8,12},{12,8},{16,20},{20,16},{24,28},{28,24},{1,5},{5... | collective-permute-start | bytes 393224 | tf_op jit(solution)/shard_map/ppermute | solution.py:258
  85.4 13.1 %copy-start.5 = (bf16[1024,1024]{1,0:T(8,128)(2,1)S(1)}, bf16[1024,1024]{1,0:T(8,128)(2,1)}, u32[]{:S(2)}) copy-start(bf16[1024,1024]{1,0:T(8,128)(2,1)} %param.26) | copy-start | bytes 6291460
  85.5 8.1 %collective-permute-start.13 = (bf16[128,256]{1,0:T(8,128)(2,1)S(1)}, bf16[128,256]{1,0:T(8,128)(2,1)S(1)}, u32[]{:S(2)}, u32[]{:S(2)}) collective-permute-start(bf16[128,256]{1,0:T(8,128)(2,1)S(1)} %get-tuple-element.65), channel_id=1, source_target_pairs={{1,0},{2,1},{3,2},{0,3},{5,4},{6,5},{7,6},{4,7},{9,8},{10,9},{11,1... | collective-permute-start | bytes 196616 | tf_op jit(solution)/shard_map/ppermute | solution.py:153
  91.0 7.1 %collective-permute-start.14 = (bf16[128,256]{1,0:T(8,128)(2,1)S(1)}, bf16[128,256]{1,0:T(8,128)(2,1)S(1)}, u32[]{:S(2)}, u32[]{:S(2)}) collective-permute-start(bf16[128,256]{1,0:T(8,128)(2,1)S(1)} %get-tuple-element.64), channel_id=1, source_target_pairs={{2,0},{3,1},{0,2},{1,3},{6,4},{7,5},{4,6},{5,7},{10,8},{11,9},{8,1... | collective-permute-start | bytes 196616 | tf_op jit(solution)/shard_map/ppermute | solution.py:153
  91.7 6.5 %collective-permute-start.15 = (bf16[128,256]{1,0:T(8,128)(2,1)S(1)}, bf16[128,256]{1,0:T(8,128)(2,1)S(1)}, u32[]{:S(2)}, u32[]{:S(2)}) collective-permute-start(bf16[128,256]{1,0:T(8,128)(2,1)S(1)} %get-tuple-element.63), channel_id=1, source_target_pairs={{3,0},{0,1},{1,2},{2,3},{7,4},{4,5},{5,6},{6,7},{11,8},{8,9},{9,10... | collective-permute-start | bytes 196616 | tf_op jit(solution)/shard_map/ppermute | solution.py:153
  102.9 2.6 %collective-permute-start.16 = (bf16[128,1,128]{2,0,1:T(8,128)(2,1)S(1)}, bf16[128,1,128]{2,0,1:T(8,128)(2,1)S(1)}, u32[]{:S(2)}, u32[]{:S(2)}) collective-permute-start(bf16[128,1,128]{2,0,1:T(8,128)(2,1)S(1)} %get-tuple-element.55), channel_id=1, source_target_pairs={{0,4},{4,8},{8,12},{12,16},{16,20},{20,24},{24,28},{1,5},{5,9},{9,... | collective-permute-start | bytes 98312 | tf_op jit(solution)/shard_map/ppermute | solution.py:20
  104.2 5.1 %collective-permute-start.17 = (bf16[128,1,128]{2,0,1:T(8,128)(2,1)S(1)}, bf16[128,1,128]{2,0,1:T(8,128)(2,1)S(1)}, u32[]{:S(2)}, u32[]{:S(2)}) collective-permute-start(bf16[128,1,128]{2,0,1:T(8,128)(2,1)S(1)} %get-tuple-element.56), channel_id=1, source_target_pairs={{4,0},{8,4},{12,8},{16,12},{20,16},{24,20},{28,24},{5,1},{9,5},{13... | collective-permute-start | bytes 98312 | tf_op jit(solution)/shard_map/ppermute | solution.py:21
  109.4 5.0 %copy-start.9 = (bf16[9,69,128]{2,1,0:T(8,128)(2,1)S(1)}, bf16[9,69,128]{2,1,0:T(8,128)(2,1)}, u32[]{:S(2)}) copy-start(bf16[9,69,128]{2,1,0:T(8,128)(2,1)} %param.29) | copy-start | bytes 476932
  109.9 5.5 %collective-permute-start.18 = (bf16[128,18,1]{0,1,2:T(8,128)(2,1)S(1)}, bf16[128,18,1]{0,1,2:T(8,128)(2,1)S(1)}, u32[]{:S(2)}, u32[]{:S(2)}) collective-permute-start(bf16[128,18,1]{0,1,2:T(8,128)(2,1)S(1)} %copy.62), channel_id=1, source_target_pairs={{0,1},{1,2},{2,3},{3,0},{4,5},{5,6},{6,7},{7,4},{8,9},{9,10},{10,1... | collective-permute-start | bytes 13832 | tf_op jit(solution)/shard_map/ppermute | solution.py:25
  110.3 5.5 %collective-permute-start.19 = (bf16[128,18,1]{0,1,2:T(8,128)(2,1)S(1)}, bf16[128,18,1]{0,1,2:T(8,128)(2,1)S(1)}, u32[]{:S(2)}, u32[]{:S(2)}) collective-permute-start(bf16[128,18,1]{0,1,2:T(8,128)(2,1)S(1)} %copy.65), channel_id=1, source_target_pairs={{1,0},{2,1},{3,2},{0,3},{5,4},{6,5},{7,6},{4,7},{9,8},{10,9},{11,1... | collective-permute-start | bytes 13832 | tf_op jit(solution)/shard_map/ppermute | solution.py:26
  120.4 20.2 %copy-start.1 = (bf16[1024,1024]{1,0:T(8,128)(2,1)S(1)}, bf16[1024,1024]{1,0:T(8,128)(2,1)}, u32[]{:S(2)}) copy-start(bf16[1024,1024]{1,0:T(8,128)(2,1)} %param.25) | copy-start | bytes 6291460
  121.0 19.0 %copy-start.14 = (s32[64]{0:T(128)S(1)}, s32[64]{0:T(128)}, u32[]{:S(2)}) copy-start(s32[64]{0:T(128)} %param.18) | copy-start | bytes 772
  122.0 3.6 %collective-permute-start.20 = (f32[64]{0:T(128)S(1)}, f32[64]{0:T(128)S(1)}, u32[]{:S(2)}, u32[]{:S(2)}) collective-permute-start(f32[64]{0:T(128)S(1)} %fusion.40), channel_id=1, source_target_pairs={{0,1},{1,0},{2,3},{3,2},{4,5},{5,4},{6,7},{7,6},{8,9},{9,8},{10,11... | collective-permute-start | bytes 776 | tf_op jit(solution)/shard_map/ppermute | solution.py:34
  125.6 4.4 %collective-permute-start.21 = (f32[64]{0:T(128)S(1)}, f32[64]{0:T(128)S(1)}, u32[]{:S(2)}, u32[]{:S(2)}) collective-permute-start(f32[64]{0:T(128)S(1)} %add.319), channel_id=1, source_target_pairs={{0,2},{1,3},{2,0},{3,1},{4,6},{5,7},{6,4},{7,5},{8,10},{9,11},{10,... | collective-permute-start | bytes 776 | tf_op jit(solution)/shard_map/ppermute | solution.py:34
  130.0 1.1 collective-permute-start.22
  131.2 4.0 %collective-permute-start.23 = (f32[64]{0:T(128)S(1)}, f32[64]{0:T(128)S(1)}, u32[]{:S(2)}, u32[]{:S(2)}) collective-permute-start(f32[64]{0:T(128)S(1)} %add.321), channel_id=1, source_target_pairs={{0,8},{4,12},{8,0},{12,4},{16,24},{20,28},{24,16},{28,20},{1,9},{5... | collective-permute-start | bytes 776 | tf_op jit(solution)/shard_map/ppermute | solution.py:34
  135.2 4.7 %collective-permute-start.24 = (f32[64]{0:T(128)S(1)}, f32[64]{0:T(128)S(1)}, u32[]{:S(2)}, u32[]{:S(2)}) collective-permute-start(f32[64]{0:T(128)S(1)} %add.322), channel_id=1, source_target_pairs={{0,16},{4,20},{8,24},{12,28},{16,0},{20,4},{24,8},{28,12},{1,17},{... | collective-permute-start | bytes 776 | tf_op jit(solution)/shard_map/ppermute | solution.py:34
  (9 other events, 10.9 us)
